TPU v7x, 256 devices: a whole 4x4x8 slice. The times are simulated.
256 devices in a mesh: row: 16 (over x, y_lo, core), col: 16 (over y_hi, z).
Axes of the slice: x: 4, y: 4 (y_hi: 2, y_lo: 2; y = y_hi * 2 + y_lo), z: 8, core: 2. Of those that a mesh axis runs over, the one named last changes fastest.
Arguments:
- coeffs: bfloat16 [4096, 4096], P('row', 'col'), may hold values from -6 to 6
- block_tiles: bfloat16 [64, 48, 64, 64], P('col', 'row'), may hold values from -0.15625 to 0.15625
- neighbours: int32 [64, 48], P('col'), may hold values from 0 to 63, as said below
- density: int32 [32], replicated, may hold values from 6 to 48, as said below
Outputs:
- filtered: bfloat16 [4096, 4096], P('row', 'col')
Inputs may be any that keep to these rules, and one draw needn't show every extreme that they name: `neighbours`: slot 0 of block row b holds b itself. Where 48 <= 64 the slots of one block row name distinct block rows; otherwise every block row is named in each row and some more than once, whose tiles then add. `density`: the number of leading live slots of every block row of a region; some region has 48 and some has 6 in every draw.
All inputs are finite; a program needn't handle non-finite values.
Results may differ from a plain program's by a relative error of at most 0.0054.
Values may be sent and summed in bfloat16 or wider, within the bound.
No kernel may reach another device: no remote copies, remote signals or barrier semaphores. Data moves between devices by JAX's collectives and lax.ppermute only.
A program may use at most 64 MiB of HBM per device.

v0:
```python
import jax
import jax.numpy as jnp
from jax import lax
from jax.sharding import PartitionSpec as P

STEPS = 3
REG_BLK = 2


def body(coeffs, block_tiles, neighbours, density):
    local_width = coeffs.shape[0]
    block_rows = neighbours.shape[0]
    slot_count = neighbours.shape[1]
    block_size = block_tiles.shape[2]
    block_ids = lax.axis_index("col") * block_rows + jnp.arange(block_rows, dtype=jnp.int32)
    region_ids = block_ids // REG_BLK
    region_match = region_ids[:, None] == jnp.arange(density.shape[0], dtype=jnp.int32)[None, :]
    live_counts = jnp.sum(jnp.where(region_match, density[None, :], 0), axis=1)
    live_mask = jnp.arange(slot_count, dtype=jnp.int32)[None, :] < live_counts[:, None]

    def accumulate(blocks, tile_piece):
        piece_slots = tile_piece.shape[1]
        gathered = jnp.take(blocks, neighbours.reshape(-1), axis=1)
        gathered = gathered.reshape(local_width, block_rows, piece_slots, block_size)
        masked = jnp.where(live_mask[:, :, None, None], tile_piece, jnp.zeros((), tile_piece.dtype))
        return jnp.einsum("mbsj,bsij->mbi", gathered, masked, preferred_element_type=jnp.float32)

    def guarded(blocks, tile_piece):
        return accumulate(blocks, tile_piece)

    def apply_hamiltonian(current_field):
        all_coeffs = lax.all_gather(current_field, "col", axis=1, tiled=True)
        blocks = all_coeffs.reshape(local_width, -1, block_size)
        running = guarded(blocks, lax.all_gather(block_tiles, "row", axis=1, tiled=True))
        return running.reshape(local_width, block_rows * block_size)

    previous = coeffs
    current = apply_hamiltonian(coeffs).astype(jnp.bfloat16)
    for repeat in range(STEPS - 1):
        product = apply_hamiltonian(current)
        following = (2.0 * product - previous.astype(jnp.float32)).astype(jnp.bfloat16)
        previous = current
        current = following
    return current


def solution(mesh):
    placed = (P("row", "col"), P("col", "row", None, None), P("col", None), P())
    return jax.shard_map(
        body, mesh=mesh, in_specs=placed, out_specs=P("row", "col"), check_vma=False
    )
```

profile of v0, /device:TPU:2, one launch (start us, length us, event | category | flops | bytes accessed | tf_op | source)
XLA Modules:
  0.0 346.5 jit_solution(15413313421211487123)
XLA Ops:
  6.5 0.0 all-gather.7.cloned.1.call-start
  6.5 1.7 copy.14
  8.2 0.0 all-gather.7.cloned.1.call-update
  8.2 0.0 all-gather.5.cloned.1.call-start
  8.3 0.7 all-gather.5.cloned.1.call-update
  9.0 0.0 all-gather.9.cloned.1.call-start
  9.0 0.8 reshape.78
  9.8 0.8 select_reduce_fusion
  10.7 0.1 iota_compare_fusion.1
  10.8 87.5 %all-gather.7.cloned.1.call-done = bf16[256,4096]{0,1:T(8,128)(2,1)} async-done(((bf16[256,256]{0,1:T(8,128)(2,1)}), bf16[256,4096]{0,1:T(8,128)(2,1)}) %all-gather.7.cloned.1.call-update) | async-done | bytes 2097168 | tf_op jit(solution)/shard_map/all_gather | solution.py:32
  98.2 9.6 %gather_fusion = bf16[192,256,64]{1,2,0:T(8,128)(2,1)} fusion(bf16[256,64,64]{0,2,1:T(8,128)(2,1)} %bitcast.42, s32[1024]{0:T(1024)S(1)} %pad_clamp_fusion), kind=kCustom, calls=%fused_computation.clone | custom fusion | bytes 12583680 | tf_op jit(solution)/shard_map/jit(_take)/gather | solution.py:23
  107.8 6.2 %broadcast_select_fusion = bf16[192,256,64]{1,2,0:T(8,128)(2,1)} fusion(bf16[192,256,64]{1,2,0:T(8,128)(2,1)} %gather_fusion, pred[192]{0:T(512)(128)(4,1)S(1)} %compare_and_fusion), kind=kLoop, calls=%fused_computation.3 | loop fusion | flops 3145728 | bytes 12583104 | tf_op jit(solution)/shard_map/jit(_take)/select_n | solution.py:23
  114.0 20.3 %all-gather.5.cloned.1.call-done = bf16[4,48,64,64]{3,2,1,0:T(8,128)(2,1)} async-done(((bf16[4,3,64,64]{3,2,1,0:T(8,128)(2,1)}), bf16[4,48,64,64]{3,2,1,0:T(8,128)(2,1)}) %all-gather.5.cloned.1.call-update) | async-done | bytes 1572880 | tf_op jit(solution)/shard_map/all_gather | solution.py:34
  134.3 5.9 %fusion.11 = bf16[4,64,256]{2,1,0:T(8,128)(2,1)} fusion(bf16[256,4,48,64]{0,3,2,1:T(8,128)(2,1)} %bitcast.45, bf16[4,48,64,64]{3,2,1,0:T(8,128)(2,1)} %all-gather.5.cloned.1.call-done, pred[4,48]{1,0:T(4,128)(4,1)S(1)} %iota_compare_fusion.1), kind=kOutput, calls=%fused_computation.18 | convolution fusion | flops 403505152 | bytes 7995584 | tf_op jit(solution)/shard_map/mbsj,bsij->mbi/dot_general | solution.py:26
  140.2 0.0 all-gather.9.cloned.1.call-update
  140.3 0.2 all-gather.11.cloned.1.call-start
  140.5 85.6 %all-gather.9.cloned.1.call-done = bf16[256,4096]{0,1:T(8,128)(2,1)} async-done(((bf16[256,256]{0,1:T(8,128)(2,1)}), bf16[256,4096]{0,1:T(8,128)(2,1)}) %all-gather.9.cloned.1.call-update) | async-done | bytes 2097168 | tf_op jit(solution)/shard_map/all_gather | solution.py:32
  226.1 9.6 %gather_fusion.1 = bf16[192,256,64]{1,2,0:T(8,128)(2,1)} fusion(bf16[256,64,64]{0,2,1:T(8,128)(2,1)} %bitcast.44, s32[1024]{0:T(1024)S(1)} %pad_clamp_fusion), kind=kCustom, calls=%fused_computation.1.clone | custom fusion | bytes 12583680 | tf_op jit(solution)/shard_map/jit(_take)/gather | solution.py:23
  235.8 3.6 %broadcast_select_fusion.1 = bf16[192,256,64]{1,2,0:T(8,128)(2,1)S(1)} fusion(bf16[192,256,64]{1,2,0:T(8,128)(2,1)} %gather_fusion.1, pred[192]{0:T(512)(128)(4,1)S(1)} %compare_and_fusion), kind=kLoop, calls=%fused_computation.4 | loop fusion | flops 3145728 | bytes 12583104 | tf_op jit(solution)/shard_map/jit(_take)/select_n | solution.py:23
  239.3 0.0 copy-start
  239.4 0.1 copy-done.2
  239.5 1.7 fusion.10
  241.2 0.7 fusion.12
  241.9 0.0 all-gather.11.cloned.1.call-update
  241.9 0.1 copy.16
  242.0 82.1 %all-gather.11.cloned.1.call-done = bf16[256,4096]{0,1:T(8,128)(2,1)} async-done(((bf16[256,256]{0,1:T(8,128)(2,1)}), bf16[256,4096]{0,1:T(8,128)(2,1)}) %all-gather.11.cloned.1.call-update) | async-done | bytes 2097168 | tf_op jit(solution)/shard_map/all_gather | solution.py:32
  324.1 9.6 %gather_fusion.2 = bf16[192,256,64]{1,2,0:T(8,128)(2,1)} fusion(bf16[256,64,64]{0,2,1:T(8,128)(2,1)} %bitcast.43, s32[1024]{0:T(1024)S(1)} %pad_clamp_fusion), kind=kCustom, calls=%fused_computation.2.clone | custom fusion | bytes 12583680 | tf_op jit(solution)/shard_map/jit(_take)/gather | solution.py:23
  333.7 3.6 %broadcast_select_fusion.2 = bf16[192,256,64]{1,2,0:T(8,128)(2,1)S(1)} fusion(bf16[192,256,64]{1,2,0:T(8,128)(2,1)} %gather_fusion.2, pred[192]{0:T(512)(128)(4,1)S(1)} %compare_and_fusion), kind=kLoop, calls=%fused_computation.5 | loop fusion | flops 3145728 | bytes 12583104 | tf_op jit(solution)/shard_map/jit(_take)/select_n | solution.py:23
  337.3 0.1 copy-done.3
  337.4 1.7 fusion.9
  339.1 0.1 copy.17
  339.3 0.7 subtract_convert_fusion
  (9 shorter events, 0.0 us)
Async XLA Ops:
  6.5 91.7 %all-gather.7.cloned.1.call-start = ((), (), s32[]{:S(2)}) async-start(), calls=%async_computation.1 | async-start | bytes 2228224 | tf_op jit(solution)/shard_map/all_gather | solution.py:32
  8.2 126.1 %all-gather.5.cloned.1.call-start = ((), (), s32[]{:S(2)}) async-start(), calls=%async_computation | async-start | bytes 3342336 | tf_op jit(solution)/shard_map/all_gather | solution.py:34
  9.0 217.2 %all-gather.9.cloned.1.call-start = ((), (), s32[]{:S(2)}) async-start(), calls=%async_computation.2 | async-start | bytes 2228224 | tf_op jit(solution)/shard_map/all_gather | solution.py:32
  140.3 183.8 %all-gather.11.cloned.1.call-start = ((), (), s32[]{:S(2)}) async-start(), calls=%async_computation.3 | async-start | bytes 2228224 | tf_op jit(solution)/shard_map/all_gather | solution.py:32
  235.8 3.7 %copy-start.2 = (bf16[4,48,64,64]{3,2,1,0:T(8,128)(2,1)S(1)}, bf16[4,48,64,64]{3,2,1,0:T(8,128)(2,1)}, u32[]{:S(2)}) copy-start(bf16[4,48,64,64]{3,2,1,0:T(8,128)(2,1)} %all-gather.5.cloned.1.call-done) | copy-start | bytes 4718596
  239.3 1.8 copy-start
  239.4 2.5 copy-start.1
  333.7 3.7 %copy-start.3 = (bf16[4,48,64,64]{3,2,1,0:T(8,128)(2,1)S(1)}, bf16[4,48,64,64]{3,2,1,0:T(8,128)(2,1)}, u32[]{:S(2)}) copy-start(bf16[4,48,64,64]{3,2,1,0:T(8,128)(2,1)} %all-gather.5.cloned.1.call-done) | copy-start | bytes 4718596
Sparse Core Ops, SparseCore 0:
  9.9 88.2 all-gather.6
  100.0 34.2 all-gather.4
  140.4 85.6 all-gather.8
  242.0 82.0 all-gather.10
where the time goes:
time: 347 us; the launch traced here: 346 us
  waiting for transfers between devices  276 us (80%)
  local copies, waits for them, and re-layouts  31.8 us (9%)
  other arithmetic  15.7 us (5%)
  between operations  13.2 us (4%)
  matrix products  9.31 us (3%)
    all_gather x3, waiting for transfers between devices, apply_hamiltonian(): all_coeffs = lax.all_gather(current_field, 'col', axis=1, tiled=True)  255 us
    gather x3, local copies, waits for them, and re-layouts, accumulate(): gathered = jnp.take(blocks, neighbours.reshape(-1), axis=1)  28.9 us
    all_gather x1, waiting for transfers between devices, apply_hamiltonian(): lax.all_gather(block_tiles, 'row', axis=1, tiled=True)  20.3 us
    select_n x4, other arithmetic, accumulate(): gathered = jnp.take(blocks, neighbours.reshape(-1), axis=1)  13.4 us
    dot_general x3, matrix products, accumulate(): jnp.einsum('mbsj,bsij->mbi', gathered, masked, preferred_element_type=jnp...  9.31 us
  transfers between devices with their start and end apart: 4, of which 4 were waited for; matrix products, arithmetic and copies ran while one was open for 5% of the time, Pallas kernels for 0%

commit v1 on v0

v1 whole, which is shorter than its diff:
```python
import jax
import jax.numpy as jnp
from jax import lax
from jax.sharding import Mesh, PartitionSpec as P

STEPS = 3
REG_BLK = 2

ROW_AXES = ("x", "y_lo", "core")
COL_AXES = ("y_hi", "z")


def gather_col(field, y_count, z_count):
    y = lax.axis_index("y_hi")
    pairs = [field]
    for shift in range(1, y_count):
        pairs.append(lax.ppermute(field, "y_hi", [(i, (i + shift) % y_count) for i in range(y_count)]))
    pair = jnp.roll(jnp.stack(pairs)[::-1], y + 1, axis=0)
    fwd = [(i, (i + 1) % z_count) for i in range(z_count)]
    bwd = [(i, (i - 1) % z_count) for i in range(z_count)]
    blocks = [None] * z_count
    blocks[0] = pair
    right = pair
    left = pair
    half = z_count // 2
    for k in range(1, (z_count + 1) // 2):
        right = lax.ppermute(right, "z", fwd)
        left = lax.ppermute(left, "z", bwd)
        blocks[(-k) % z_count] = right
        blocks[k] = left
    if z_count % 2 == 0 and z_count > 1:
        split = y_count // 2
        if split == 0:
            blocks[half] = lax.ppermute(right, "z", fwd)
        else:
            lo = lax.ppermute(right[:split], "z", fwd)
            hi = lax.ppermute(left[split:], "z", bwd)
            blocks[half] = jnp.concatenate([lo, hi], axis=0)
    return blocks


def body(coeffs, block_tiles, neighbours, density):
    y_count = lax.axis_size("y_hi")
    z_count = lax.axis_size("z")
    local_width = coeffs.shape[1]
    block_rows = neighbours.shape[0]
    slot_count = neighbours.shape[1]
    block_size = block_tiles.shape[2]
    total_blocks = block_rows * y_count * z_count
    col = lax.axis_index("y_hi") * z_count + lax.axis_index("z")
    block_ids = col * block_rows + jnp.arange(block_rows, dtype=jnp.int32)
    region_ids = block_ids // REG_BLK
    region_match = region_ids[:, None] == jnp.arange(density.shape[0], dtype=jnp.int32)[None, :]
    live_counts = jnp.sum(jnp.where(region_match, density[None, :], 0), axis=1)
    live_mask = jnp.arange(slot_count, dtype=jnp.int32)[None, :] < live_counts[:, None]

    tiles = lax.all_gather(block_tiles, ROW_AXES, axis=1, tiled=True)
    pick = (neighbours[:, :, None] == jnp.arange(total_blocks, dtype=jnp.int32)[None, None, :]) & live_mask[:, :, None]
    dense = jnp.einsum("bsn,bsij->njbi", pick.astype(tiles.dtype), tiles, preferred_element_type=jnp.float32)
    dense = dense.astype(tiles.dtype).reshape(y_count, z_count, local_width, local_width)
    dense = jnp.roll(dense, -lax.axis_index("z"), axis=1)

    def apply_hamiltonian(field):
        blocks = gather_col(field, y_count, z_count)
        total = None
        for d, chunk in enumerate(blocks):
            part = jnp.einsum("ymj,yjo->mo", chunk, dense[:, d], preferred_element_type=jnp.float32)
            total = part if total is None else total + part
        return total

    previous = coeffs
    current = apply_hamiltonian(coeffs).astype(jnp.bfloat16)
    for repeat in range(STEPS - 1):
        product = apply_hamiltonian(current)
        following = (2.0 * product - previous.astype(jnp.float32)).astype(jnp.bfloat16)
        previous = current
        current = following
    return current


def solution(mesh):
    devices = mesh.devices.reshape(4, 2, 2, 2, 8)
    fine = Mesh(devices, ROW_AXES + COL_AXES)
    placed = (P(ROW_AXES, COL_AXES), P(COL_AXES, ROW_AXES, None, None), P(COL_AXES, None), P())
    return jax.shard_map(
        body, mesh=fine, in_specs=placed, out_specs=P(ROW_AXES, COL_AXES), check_vma=False
    )
```

time: 347 us -> 162 us (0.47)
  waiting for transfers between devices: 276 us -> 66.8 us
  starting transfers between devices: 0.3 us -> 52.5 us
  local copies, waits for them, and re-layouts: 31.8 us -> 10.9 us
  other arithmetic: 15.7 us -> 3.92 us
  matrix products: 9.31 us -> 13.9 us
    all_gather x4 -> x1, waiting for transfers between devices: 275 us -> 2.73 us  [body(): tiles = lax.all_gather(block_tiles, ROW_AXES, axis=1, tiled=True)]
    ppermute x0 -> x27, waiting for transfers between devices: none -> 64 us  [the longest x9 36.4 us: gather_col(): right = lax.ppermute(right, 'z', fwd)]
    ppermute x0 -> x27, starting transfers between devices: none -> 52.5 us  [the longest x9 31.3 us: gather_col(): left = lax.ppermute(left, 'z', bwd)]
    gather x3 -> x0, local copies, waits for them, and re-layouts: 28.9 us -> none  [accumulate(): gathered = jnp.take(blocks, neighbours.reshape(-1), axis=1)]
    select_n x4 -> x0, other arithmetic: 13.4 us -> none  [accumulate(): gathered = jnp.take(blocks, neighbours.reshape(-1), axis=1)]
    reshape x1 -> x2, local copies, waits for them, and re-layouts: 0.76 us -> 8.27 us  [body(): dense.astype(tiles.dtype)]
    dot_general x3 -> x25, matrix products: 9.31 us -> 13.9 us  [the longest x24 7.15 us: apply_hamiltonian(): jnp.einsum('ymj,yjo->mo', chunk, dense[:, d], preferred_element_type=jnp....]
  transfers between devices with their start and end apart: 4 -> 28, of which waited for: 4 -> 15; matrix products, arithmetic and copies ran while one was open for 5% -> 15% of each run, Pallas kernels for 0% -> 0%
where the time goes in v1:
time: 162 us
  waiting for transfers between devices  66.8 us (41%)
  starting transfers between devices  52.5 us (32%)
  matrix products  13.9 us (9%)
  between operations  13.8 us (9%)
  local copies, waits for them, and re-layouts  10.9 us (7%)
  other arithmetic  3.92 us (2%)
    ppermute x9, waiting for transfers between devices, gather_col(): right = lax.ppermute(right, 'z', fwd)  36.4 us
    ppermute x9, starting transfers between devices, gather_col(): left = lax.ppermute(left, 'z', bwd)  31.3 us
    ppermute x3, waiting for transfers between devices, gather_col(): lax.ppermute(field, 'y_hi', [(i, (i + shift) % y_count) for i in range(y_...  11.9 us
    ppermute x9, waiting for transfers between devices, gather_col(): left = lax.ppermute(left, 'z', bwd)  10.4 us
    ppermute x3, starting transfers between devices, gather_col(): hi = lax.ppermute(left[split:], 'z', bwd)  9.79 us
    ppermute x3, starting transfers between devices, gather_col(): lax.ppermute(field, 'y_hi', [(i, (i + shift) % y_count) for i in range(y_...  8.93 us
    reshape x2, local copies, waits for them, and re-layouts, body(): dense.astype(tiles.dtype)  8.27 us
    dot_general x24, matrix products, apply_hamiltonian(): jnp.einsum('ymj,yjo->mo', chunk, dense[:, d], preferred_element_type=jnp....  7.15 us
  transfers between devices with their start and end apart: 28, of which 15 were waited for; matrix products, arithmetic and copies ran while one was open for 15% of the time, Pallas kernels for 0%

profile of v1, /device:TPU:2, one launch (start us, length us, event | category | flops | bytes accessed | tf_op | source)
XLA Modules:
  0.0 161.8 jit_solution(8390986829544298298)
XLA Ops:
  8.2 3.3 %collective-permute-start = (bf16[256,256]{1,0:T(8,128)(2,1)}, bf16[256,256]{1,0:T(8,128)(2,1)S(1)}, u32[]{:S(2)}, u32[]{:S(2)}) collective-permute-start(bf16[256,256]{1,0:T(8,128)(2,1)} %param.6), channel_id=1, source_target_pairs={{0,8},{8,0},{1,9},{9,1},{2,10},{10,2},{3,11},{11,3},{4,12},{12,4},... | collective-permute-start | bytes 393224 | tf_op jit(solution)/shard_map/ppermute | solution.py:17
  11.5 3.8 %collective-permute-done = bf16[256,256]{1,0:T(8,128)(2,1)S(1)} collective-permute-done((bf16[256,256]{1,0:T(8,128)(2,1)}, bf16[256,256]{1,0:T(8,128)(2,1)S(1)}, u32[]{:S(2)}, u32[]{:S(2)}) %collective-permute-start) | collective-permute-done | bytes 131104 | tf_op jit(solution)/shard_map/ppermute | solution.py:17
  18.3 4.0 %collective-permute-start.1 = (bf16[2,256,256]{2,1,0:T(8,128)(2,1)S(1)}, bf16[2,256,256]{2,1,0:T(8,128)(2,1)S(1)}, u32[]{:S(2)}, u32[]{:S(2)}) collective-permute-start(bf16[2,256,256]{2,1,0:T(8,128)(2,1)S(1)} %fusion.35), channel_id=1, source_target_pairs={{0,7},{1,0},{2,1},{3,2},{4,3},{5,4},{6,5},{7,6},{8,15},{9,8},{10,9... | collective-permute-start | bytes 786440 | tf_op jit(solution)/shard_map/ppermute | solution.py:28
  22.3 5.4 %collective-permute-done.4 = bf16[2,256,256]{2,1,0:T(8,128)(2,1)S(1)} collective-permute-done((bf16[2,256,256]{2,1,0:T(8,128)(2,1)S(1)}, bf16[2,256,256]{2,1,0:T(8,128)(2,1)S(1)}, u32[]{:S(2)}, u32[]{:S(2)}) %collective-permute-start.4) | collective-permute-done | bytes 262176 | tf_op jit(solution)/shard_map/ppermute | solution.py:27
  27.7 3.2 %collective-permute-start.2 = (bf16[2,256,256]{2,1,0:T(8,128)(2,1)S(1)}, bf16[2,256,256]{2,1,0:T(8,128)(2,1)S(1)}, u32[]{:S(2)}, u32[]{:S(2)}) collective-permute-start(bf16[2,256,256]{2,1,0:T(8,128)(2,1)S(1)} %collective-permute-done.1), channel_id=1, source_target_pairs={{0,7},{1,0},{2,1},{3,2},{4,3},{5,4},{6,5},{7,6},{8,15},{9,8},{10,9... | collective-permute-start | bytes 786440 | tf_op jit(solution)/shard_map/ppermute | solution.py:28
  31.0 4.6 %collective-permute-done.5 = bf16[2,256,256]{2,1,0:T(8,128)(2,1)S(1)} collective-permute-done((bf16[2,256,256]{2,1,0:T(8,128)(2,1)S(1)}, bf16[2,256,256]{2,1,0:T(8,128)(2,1)S(1)}, u32[]{:S(2)}, u32[]{:S(2)}) %collective-permute-start.5) | collective-permute-done | bytes 262176 | tf_op jit(solution)/shard_map/ppermute | solution.py:27
  35.6 3.3 %collective-permute-start.3 = (bf16[2,256,256]{2,1,0:T(8,128)(2,1)S(1)}, bf16[2,256,256]{2,1,0:T(8,128)(2,1)S(1)}, u32[]{:S(2)}, u32[]{:S(2)}) collective-permute-start(bf16[2,256,256]{2,1,0:T(8,128)(2,1)S(1)} %collective-permute-done.2), channel_id=1, source_target_pairs={{0,7},{1,0},{2,1},{3,2},{4,3},{5,4},{6,5},{7,6},{8,15},{9,8},{10,9... | collective-permute-start | bytes 786440 | tf_op jit(solution)/shard_map/ppermute | solution.py:28
  39.1 4.0 %collective-permute-done.6 = bf16[2,256,256]{2,1,0:T(8,128)(2,1)S(1)} collective-permute-done((bf16[2,256,256]{2,1,0:T(8,128)(2,1)S(1)}, bf16[2,256,256]{2,1,0:T(8,128)(2,1)S(1)}, u32[]{:S(2)}, u32[]{:S(2)}) %collective-permute-start.6) | collective-permute-done | bytes 262176 | tf_op jit(solution)/shard_map/ppermute | solution.py:27
  43.9 3.2 %collective-permute-start.8 = (bf16[1,256,256]{2,1,0:T(8,128)(2,1)}, bf16[1,256,256]{2,1,0:T(8,128)(2,1)}, u32[]{:S(2)}, u32[]{:S(2)}) collective-permute-start(bf16[1,256,256]{2,1,0:T(8,128)(2,1)} %slice.77), channel_id=1, source_target_pairs={{0,7},{1,0},{2,1},{3,2},{4,3},{5,4},{6,5},{7,6},{8,15},{9,8},{10,9... | collective-permute-start | bytes 393224 | tf_op jit(solution)/shard_map/ppermute | solution.py:37
  47.1 2.7 %all-gather.2.cloned.1.call-done = bf16[4,48,64,64]{3,2,0,1:T(8,128)(2,1)} async-done(((bf16[4,3,64,64]{3,2,0,1:T(8,128)(2,1)}), bf16[4,48,64,64]{3,2,0,1:T(8,128)(2,1)}) %all-gather.2.cloned.1.call-update) | async-done | bytes 1572880 | tf_op jit(solution)/shard_map/all_gather | solution.py:57
  49.9 6.8 %convert_bitcast_fusion = bf16[64,64,4,64]{1,0,3,2:T(8,128)(2,1)} fusion(bf16[4,48,64,64]{3,2,0,1:T(8,128)(2,1)} %all-gather.2.cloned.1.call-done, s32[4,48]{1,0:T(4,128)S(1)} %copy-done.5, pred[4,48]{1,0:T(4,128)(4,1)S(1)} %iota_compare_fusion.2), kind=kOutput, calls=%fused_computation.2 | convolution fusion | flops 101736448 | bytes 3670976 | tf_op jit(solution)/shard_map/bsn,bsij->njbi/dot_general | solution.py:59
  56.6 5.5 %reshape.45 = bf16[2,8,256,256]{2,1,0,3:T(8,128)(2,1)S(1)} reshape(bf16[64,64,4,64]{1,0,3,2:T(8,128)(2,1)} %convert_bitcast_fusion) | data formatting | bytes 4194304 | tf_op jit(solution)/shard_map/reshape | solution.py:60
  62.1 2.8 %copy.14 = bf16[2,8,256,256]{3,2,0,1:T(8,128)(2,1)} copy(bf16[2,8,256,256]{2,1,0,3:T(8,128)(2,1)S(1)} %reshape.45) | data formatting | bytes 4194304 | tf_op jit(solution)/shard_map/reshape | solution.py:60
  70.4 2.9 %collective-permute-start.9 = (bf16[256,256]{1,0:T(8,128)(2,1)S(1)}, bf16[256,256]{1,0:T(8,128)(2,1)S(1)}, u32[]{:S(2)}, u32[]{:S(2)}) collective-permute-start(bf16[256,256]{1,0:T(8,128)(2,1)S(1)} %fusion.32), channel_id=1, source_target_pairs={{0,8},{8,0},{1,9},{9,1},{2,10},{10,2},{3,11},{11,3},{4,12},{12,4},... | collective-permute-start | bytes 393224 | tf_op jit(solution)/shard_map/ppermute | solution.py:17
  73.2 4.4 %collective-permute-done.9 = bf16[256,256]{1,0:T(8,128)(2,1)S(1)} collective-permute-done((bf16[256,256]{1,0:T(8,128)(2,1)S(1)}, bf16[256,256]{1,0:T(8,128)(2,1)S(1)}, u32[]{:S(2)}, u32[]{:S(2)}) %collective-permute-start.9) | collective-permute-done | bytes 131104 | tf_op jit(solution)/shard_map/ppermute | solution.py:17
  77.8 3.5 %collective-permute-start.10 = (bf16[2,256,256]{2,1,0:T(8,128)(2,1)S(1)}, bf16[2,256,256]{2,1,0:T(8,128)(2,1)S(1)}, u32[]{:S(2)}, u32[]{:S(2)}) collective-permute-start(bf16[2,256,256]{2,1,0:T(8,128)(2,1)S(1)} %fusion.34), channel_id=1, source_target_pairs={{0,7},{1,0},{2,1},{3,2},{4,3},{5,4},{6,5},{7,6},{8,15},{9,8},{10,9... | collective-permute-start | bytes 786440 | tf_op jit(solution)/shard_map/ppermute | solution.py:28
  81.5 4.9 %collective-permute-done.10 = bf16[2,256,256]{2,1,0:T(8,128)(2,1)S(1)} collective-permute-done((bf16[2,256,256]{2,1,0:T(8,128)(2,1)S(1)}, bf16[2,256,256]{2,1,0:T(8,128)(2,1)S(1)}, u32[]{:S(2)}, u32[]{:S(2)}) %collective-permute-start.10) | collective-permute-done | bytes 262176 | tf_op jit(solution)/shard_map/ppermute | solution.py:28
  86.3 3.7 %collective-permute-start.11 = (bf16[2,256,256]{2,1,0:T(8,128)(2,1)S(1)}, bf16[2,256,256]{2,1,0:T(8,128)(2,1)S(1)}, u32[]{:S(2)}, u32[]{:S(2)}) collective-permute-start(bf16[2,256,256]{2,1,0:T(8,128)(2,1)S(1)} %collective-permute-done.10), channel_id=1, source_target_pairs={{0,7},{1,0},{2,1},{3,2},{4,3},{5,4},{6,5},{7,6},{8,15},{9,8},{10,9... | collective-permute-start | bytes 786440 | tf_op jit(solution)/shard_map/ppermute | solution.py:28
  90.5 7.2 %collective-permute-done.14 = bf16[2,256,256]{2,1,0:T(8,128)(2,1)S(1)} collective-permute-done((bf16[2,256,256]{2,1,0:T(8,128)(2,1)S(1)}, bf16[2,256,256]{2,1,0:T(8,128)(2,1)S(1)}, u32[]{:S(2)}, u32[]{:S(2)}) %collective-permute-start.14) | collective-permute-done | bytes 262176 | tf_op jit(solution)/shard_map/ppermute | solution.py:27
  97.7 3.2 %collective-permute-start.12 = (bf16[2,256,256]{2,1,0:T(8,128)(2,1)S(1)}, bf16[2,256,256]{2,1,0:T(8,128)(2,1)S(1)}, u32[]{:S(2)}, u32[]{:S(2)}) collective-permute-start(bf16[2,256,256]{2,1,0:T(8,128)(2,1)S(1)} %collective-permute-done.11), channel_id=1, source_target_pairs={{0,7},{1,0},{2,1},{3,2},{4,3},{5,4},{6,5},{7,6},{8,15},{9,8},{10,9... | collective-permute-start | bytes 786440 | tf_op jit(solution)/shard_map/ppermute | solution.py:28
  101.4 3.9 %collective-permute-done.15 = bf16[2,256,256]{2,1,0:T(8,128)(2,1)S(1)} collective-permute-done((bf16[2,256,256]{2,1,0:T(8,128)(2,1)S(1)}, bf16[2,256,256]{2,1,0:T(8,128)(2,1)S(1)}, u32[]{:S(2)}, u32[]{:S(2)}) %collective-permute-start.15) | collective-permute-done | bytes 262176 | tf_op jit(solution)/shard_map/ppermute | solution.py:27
  105.6 3.3 %collective-permute-start.17 = (bf16[1,256,256]{2,1,0:T(8,128)(2,1)S(1)}, bf16[1,256,256]{2,1,0:T(8,128)(2,1)S(1)}, u32[]{:S(2)}, u32[]{:S(2)}) collective-permute-start(bf16[1,256,256]{2,1,0:T(8,128)(2,1)S(1)} %slice.83), channel_id=1, source_target_pairs={{0,7},{1,0},{2,1},{3,2},{4,3},{5,4},{6,5},{7,6},{8,15},{9,8},{10,9... | collective-permute-start | bytes 393224 | tf_op jit(solution)/shard_map/ppermute | solution.py:37
  109.1 2.6 %collective-permute-done.16 = bf16[1,256,256]{2,1,0:T(8,128)(2,1)S(1)} collective-permute-done((bf16[1,256,256]{2,1,0:T(8,128)(2,1)S(1)}, bf16[1,256,256]{2,1,0:T(8,128)(2,1)S(1)}, u32[]{:S(2)}, u32[]{:S(2)}) %collective-permute-start.16) | collective-permute-done | bytes 131104 | tf_op jit(solution)/shard_map/ppermute | solution.py:36
  112.3 2.8 %collective-permute-start.18 = (bf16[256,256]{1,0:T(8,128)(2,1)S(1)}, bf16[256,256]{1,0:T(8,128)(2,1)S(1)}, u32[]{:S(2)}, u32[]{:S(2)}) collective-permute-start(bf16[256,256]{1,0:T(8,128)(2,1)S(1)} %fusion.31), channel_id=1, source_target_pairs={{0,8},{8,0},{1,9},{9,1},{2,10},{10,2},{3,11},{11,3},{4,12},{12,4},... | collective-permute-start | bytes 393224 | tf_op jit(solution)/shard_map/ppermute | solution.py:17
  115.1 3.8 %collective-permute-done.18 = bf16[256,256]{1,0:T(8,128)(2,1)S(1)} collective-permute-done((bf16[256,256]{1,0:T(8,128)(2,1)S(1)}, bf16[256,256]{1,0:T(8,128)(2,1)S(1)}, u32[]{:S(2)}, u32[]{:S(2)}) %collective-permute-start.18) | collective-permute-done | bytes 131104 | tf_op jit(solution)/shard_map/ppermute | solution.py:17
  119.0 3.4 %collective-permute-start.19 = (bf16[2,256,256]{2,1,0:T(8,128)(2,1)S(1)}, bf16[2,256,256]{2,1,0:T(8,128)(2,1)S(1)}, u32[]{:S(2)}, u32[]{:S(2)}) collective-permute-start(bf16[2,256,256]{2,1,0:T(8,128)(2,1)S(1)} %fusion.33), channel_id=1, source_target_pairs={{0,7},{1,0},{2,1},{3,2},{4,3},{5,4},{6,5},{7,6},{8,15},{9,8},{10,9... | collective-permute-start | bytes 786440 | tf_op jit(solution)/shard_map/ppermute | solution.py:28
  122.6 5.6 %collective-permute-done.19 = bf16[2,256,256]{2,1,0:T(8,128)(2,1)S(1)} collective-permute-done((bf16[2,256,256]{2,1,0:T(8,128)(2,1)S(1)}, bf16[2,256,256]{2,1,0:T(8,128)(2,1)S(1)}, u32[]{:S(2)}, u32[]{:S(2)}) %collective-permute-start.19) | collective-permute-done | bytes 262176 | tf_op jit(solution)/shard_map/ppermute | solution.py:28
  128.2 3.7 %collective-permute-start.20 = (bf16[2,256,256]{2,1,0:T(8,128)(2,1)S(1)}, bf16[2,256,256]{2,1,0:T(8,128)(2,1)S(1)}, u32[]{:S(2)}, u32[]{:S(2)}) collective-permute-start(bf16[2,256,256]{2,1,0:T(8,128)(2,1)S(1)} %collective-permute-done.19), channel_id=1, source_target_pairs={{0,7},{1,0},{2,1},{3,2},{4,3},{5,4},{6,5},{7,6},{8,15},{9,8},{10,9... | collective-permute-start | bytes 786440 | tf_op jit(solution)/shard_map/ppermute | solution.py:28
  132.4 7.6 %collective-permute-done.23 = bf16[2,256,256]{2,1,0:T(8,128)(2,1)S(1)} collective-permute-done((bf16[2,256,256]{2,1,0:T(8,128)(2,1)S(1)}, bf16[2,256,256]{2,1,0:T(8,128)(2,1)S(1)}, u32[]{:S(2)}, u32[]{:S(2)}) %collective-permute-start.23) | collective-permute-done | bytes 262176 | tf_op jit(solution)/shard_map/ppermute | solution.py:27
  140.0 3.2 %collective-permute-start.21 = (bf16[2,256,256]{2,1,0:T(8,128)(2,1)S(1)}, bf16[2,256,256]{2,1,0:T(8,128)(2,1)S(1)}, u32[]{:S(2)}, u32[]{:S(2)}) collective-permute-start(bf16[2,256,256]{2,1,0:T(8,128)(2,1)S(1)} %collective-permute-done.20), channel_id=1, source_target_pairs={{0,7},{1,0},{2,1},{3,2},{4,3},{5,4},{6,5},{7,6},{8,15},{9,8},{10,9... | collective-permute-start | bytes 786440 | tf_op jit(solution)/shard_map/ppermute | solution.py:28
  143.7 3.9 %collective-permute-done.24 = bf16[2,256,256]{2,1,0:T(8,128)(2,1)S(1)} collective-permute-done((bf16[2,256,256]{2,1,0:T(8,128)(2,1)S(1)}, bf16[2,256,256]{2,1,0:T(8,128)(2,1)S(1)}, u32[]{:S(2)}, u32[]{:S(2)}) %collective-permute-start.24) | collective-permute-done | bytes 262176 | tf_op jit(solution)/shard_map/ppermute | solution.py:27
  147.7 3.3 %collective-permute-start.26 = (bf16[1,256,256]{2,1,0:T(8,128)(2,1)S(1)}, bf16[1,256,256]{2,1,0:T(8,128)(2,1)S(1)}, u32[]{:S(2)}, u32[]{:S(2)}) collective-permute-start(bf16[1,256,256]{2,1,0:T(8,128)(2,1)S(1)} %slice.85), channel_id=1, source_target_pairs={{0,7},{1,0},{2,1},{3,2},{4,3},{5,4},{6,5},{7,6},{8,15},{9,8},{10,9... | collective-permute-start | bytes 393224 | tf_op jit(solution)/shard_map/ppermute | solution.py:37
  (86 shorter events, 18.9 us)
Async XLA Ops:
  6.5 32.3 %copy-start.6 = (s32[32]{0:T(128)S(1)}, s32[32]{0:T(128)}, u32[]{:S(2)}) copy-start(s32[32]{0:T(128)} %param.9) | copy-start | bytes 388
  6.5 43.3 %copy-start.5 = (s32[4,48]{1,0:T(4,128)S(1)}, s32[4,48]{1,0:T(4,128)}, u32[]{:S(2)}) copy-start(s32[4,48]{1,0:T(4,128)} %param.8) | copy-start | bytes 2308
  6.5 43.3 %all-gather.2.cloned.1.call-start = ((), (), s32[]{:S(2)}) async-start(), calls=%async_computation | async-start | bytes 3342336 | tf_op jit(solution)/shard_map/all_gather | solution.py:57
  8.2 7.0 %collective-permute-start = (bf16[256,256]{1,0:T(8,128)(2,1)}, bf16[256,256]{1,0:T(8,128)(2,1)S(1)}, u32[]{:S(2)}, u32[]{:S(2)}) collective-permute-start(bf16[256,256]{1,0:T(8,128)(2,1)} %param.6), channel_id=1, source_target_pairs={{0,8},{8,0},{1,9},{9,1},{2,10},{10,2},{3,11},{11,3},{4,12},{12,4},... | collective-permute-start | bytes 393224 | tf_op jit(solution)/shard_map/ppermute | solution.py:17
  16.3 11.4 %collective-permute-start.4 = (bf16[2,256,256]{2,1,0:T(8,128)(2,1)S(1)}, bf16[2,256,256]{2,1,0:T(8,128)(2,1)S(1)}, u32[]{:S(2)}, u32[]{:S(2)}) collective-permute-start(bf16[2,256,256]{2,1,0:T(8,128)(2,1)S(1)} %fusion.35), channel_id=1, source_target_pairs={{0,1},{1,2},{2,3},{3,4},{4,5},{5,6},{6,7},{7,0},{8,9},{9,10},{10,1... | collective-permute-start | bytes 786440 | tf_op jit(solution)/shard_map/ppermute | solution.py:27
  18.3 9.4 %collective-permute-start.1 = (bf16[2,256,256]{2,1,0:T(8,128)(2,1)S(1)}, bf16[2,256,256]{2,1,0:T(8,128)(2,1)S(1)}, u32[]{:S(2)}, u32[]{:S(2)}) collective-permute-start(bf16[2,256,256]{2,1,0:T(8,128)(2,1)S(1)} %fusion.35), channel_id=1, source_target_pairs={{0,7},{1,0},{2,1},{3,2},{4,3},{5,4},{6,5},{7,6},{8,15},{9,8},{10,9... | collective-permute-start | bytes 786440 | tf_op jit(solution)/shard_map/ppermute | solution.py:28
  27.7 7.8 %collective-permute-start.5 = (bf16[2,256,256]{2,1,0:T(8,128)(2,1)S(1)}, bf16[2,256,256]{2,1,0:T(8,128)(2,1)S(1)}, u32[]{:S(2)}, u32[]{:S(2)}) collective-permute-start(bf16[2,256,256]{2,1,0:T(8,128)(2,1)S(1)} %collective-permute-done.4), channel_id=1, source_target_pairs={{0,1},{1,2},{2,3},{3,4},{4,5},{5,6},{6,7},{7,0},{8,9},{9,10},{10,1... | collective-permute-start | bytes 786440 | tf_op jit(solution)/shard_map/ppermute | solution.py:27
  27.7 7.8 %collective-permute-start.2 = (bf16[2,256,256]{2,1,0:T(8,128)(2,1)S(1)}, bf16[2,256,256]{2,1,0:T(8,128)(2,1)S(1)}, u32[]{:S(2)}, u32[]{:S(2)}) collective-permute-start(bf16[2,256,256]{2,1,0:T(8,128)(2,1)S(1)} %collective-permute-done.1), channel_id=1, source_target_pairs={{0,7},{1,0},{2,1},{3,2},{4,3},{5,4},{6,5},{7,6},{8,15},{9,8},{10,9... | collective-permute-start | bytes 786440 | tf_op jit(solution)/shard_map/ppermute | solution.py:28
  35.5 7.6 %collective-permute-start.6 = (bf16[2,256,256]{2,1,0:T(8,128)(2,1)S(1)}, bf16[2,256,256]{2,1,0:T(8,128)(2,1)S(1)}, u32[]{:S(2)}, u32[]{:S(2)}) collective-permute-start(bf16[2,256,256]{2,1,0:T(8,128)(2,1)S(1)} %collective-permute-done.5), channel_id=1, source_target_pairs={{0,1},{1,2},{2,3},{3,4},{4,5},{5,6},{6,7},{7,0},{8,9},{9,10},{10,1... | collective-permute-start | bytes 786440 | tf_op jit(solution)/shard_map/ppermute | solution.py:27
  35.5 14.3 %copy-start.3 = (bf16[2,256,256]{2,1,0:T(8,128)(2,1)}, bf16[2,256,256]{2,1,0:T(8,128)(2,1)S(1)}, u32[]{:S(2)}) copy-start(bf16[2,256,256]{2,1,0:T(8,128)(2,1)S(1)} %collective-permute-done.2) | copy-start | bytes 786436
  35.6 7.7 %collective-permute-start.3 = (bf16[2,256,256]{2,1,0:T(8,128)(2,1)S(1)}, bf16[2,256,256]{2,1,0:T(8,128)(2,1)S(1)}, u32[]{:S(2)}, u32[]{:S(2)}) collective-permute-start(bf16[2,256,256]{2,1,0:T(8,128)(2,1)S(1)} %collective-permute-done.2), channel_id=1, source_target_pairs={{0,7},{1,0},{2,1},{3,2},{4,3},{5,4},{6,5},{7,6},{8,15},{9,8},{10,9... | collective-permute-start | bytes 786440 | tf_op jit(solution)/shard_map/ppermute | solution.py:28
  43.1 25.8 %collective-permute-start.7 = (bf16[1,256,256]{2,1,0:T(8,128)(2,1)S(1)}, bf16[1,256,256]{2,1,0:T(8,128)(2,1)}, u32[]{:S(2)}, u32[]{:S(2)}) collective-permute-start(bf16[1,256,256]{2,1,0:T(8,128)(2,1)S(1)} %slice.76), channel_id=1, source_target_pairs={{0,1},{1,2},{2,3},{3,4},{4,5},{5,6},{6,7},{7,0},{8,9},{9,10},{10,1... | collective-permute-start | bytes 393224 | tf_op jit(solution)/shard_map/ppermute | solution.py:36
  43.9 25.0 %collective-permute-start.8 = (bf16[1,256,256]{2,1,0:T(8,128)(2,1)}, bf16[1,256,256]{2,1,0:T(8,128)(2,1)}, u32[]{:S(2)}, u32[]{:S(2)}) collective-permute-start(bf16[1,256,256]{2,1,0:T(8,128)(2,1)} %slice.77), channel_id=1, source_target_pairs={{0,7},{1,0},{2,1},{3,2},{4,3},{5,4},{6,5},{7,6},{8,15},{9,8},{10,9... | collective-permute-start | bytes 393224 | tf_op jit(solution)/shard_map/ppermute | solution.py:37
  70.4 7.2 %collective-permute-start.9 = (bf16[256,256]{1,0:T(8,128)(2,1)S(1)}, bf16[256,256]{1,0:T(8,128)(2,1)S(1)}, u32[]{:S(2)}, u32[]{:S(2)}) collective-permute-start(bf16[256,256]{1,0:T(8,128)(2,1)S(1)} %fusion.32), channel_id=1, source_target_pairs={{0,8},{8,0},{1,9},{9,1},{2,10},{10,2},{3,11},{11,3},{4,12},{12,4},... | collective-permute-start | bytes 393224 | tf_op jit(solution)/shard_map/ppermute | solution.py:17
  77.8 8.6 %collective-permute-start.10 = (bf16[2,256,256]{2,1,0:T(8,128)(2,1)S(1)}, bf16[2,256,256]{2,1,0:T(8,128)(2,1)S(1)}, u32[]{:S(2)}, u32[]{:S(2)}) collective-permute-start(bf16[2,256,256]{2,1,0:T(8,128)(2,1)S(1)} %fusion.34), channel_id=1, source_target_pairs={{0,7},{1,0},{2,1},{3,2},{4,3},{5,4},{6,5},{7,6},{8,15},{9,8},{10,9... | collective-permute-start | bytes 786440 | tf_op jit(solution)/shard_map/ppermute | solution.py:28
  81.2 8.8 %collective-permute-start.13 = (bf16[2,256,256]{2,1,0:T(8,128)(2,1)S(1)}, bf16[2,256,256]{2,1,0:T(8,128)(2,1)S(1)}, u32[]{:S(2)}, u32[]{:S(2)}) collective-permute-start(bf16[2,256,256]{2,1,0:T(8,128)(2,1)S(1)} %fusion.34), channel_id=1, source_target_pairs={{0,1},{1,2},{2,3},{3,4},{4,5},{5,6},{6,7},{7,0},{8,9},{9,10},{10,1... | collective-permute-start | bytes 786440 | tf_op jit(solution)/shard_map/ppermute | solution.py:27
  86.3 11.4 %collective-permute-start.11 = (bf16[2,256,256]{2,1,0:T(8,128)(2,1)S(1)}, bf16[2,256,256]{2,1,0:T(8,128)(2,1)S(1)}, u32[]{:S(2)}, u32[]{:S(2)}) collective-permute-start(bf16[2,256,256]{2,1,0:T(8,128)(2,1)S(1)} %collective-permute-done.10), channel_id=1, source_target_pairs={{0,7},{1,0},{2,1},{3,2},{4,3},{5,4},{6,5},{7,6},{8,15},{9,8},{10,9... | collective-permute-start | bytes 786440 | tf_op jit(solution)/shard_map/ppermute | solution.py:28
  90.0 7.7 %collective-permute-start.14 = (bf16[2,256,256]{2,1,0:T(8,128)(2,1)S(1)}, bf16[2,256,256]{2,1,0:T(8,128)(2,1)S(1)}, u32[]{:S(2)}, u32[]{:S(2)}) collective-permute-start(bf16[2,256,256]{2,1,0:T(8,128)(2,1)S(1)} %collective-permute-done.13), channel_id=1, source_target_pairs={{0,1},{1,2},{2,3},{3,4},{4,5},{5,6},{6,7},{7,0},{8,9},{9,10},{10,1... | collective-permute-start | bytes 786440 | tf_op jit(solution)/shard_map/ppermute | solution.py:27
  90.5 21.5 %copy-start = (bf16[256,256]{1,0:T(8,128)(2,1)S(1)}, bf16[256,256]{1,0:T(8,128)(2,1)}, u32[]{:S(2)}) copy-start(bf16[256,256]{1,0:T(8,128)(2,1)} %param.6) | copy-start | bytes 393220
  97.7 7.6 %collective-permute-start.15 = (bf16[2,256,256]{2,1,0:T(8,128)(2,1)S(1)}, bf16[2,256,256]{2,1,0:T(8,128)(2,1)S(1)}, u32[]{:S(2)}, u32[]{:S(2)}) collective-permute-start(bf16[2,256,256]{2,1,0:T(8,128)(2,1)S(1)} %collective-permute-done.14), channel_id=1, source_target_pairs={{0,1},{1,2},{2,3},{3,4},{4,5},{5,6},{6,7},{7,0},{8,9},{9,10},{10,1... | collective-permute-start | bytes 786440 | tf_op jit(solution)/shard_map/ppermute | solution.py:27
  97.7 7.9 %collective-permute-start.12 = (bf16[2,256,256]{2,1,0:T(8,128)(2,1)S(1)}, bf16[2,256,256]{2,1,0:T(8,128)(2,1)S(1)}, u32[]{:S(2)}, u32[]{:S(2)}) collective-permute-start(bf16[2,256,256]{2,1,0:T(8,128)(2,1)S(1)} %collective-permute-done.11), channel_id=1, source_target_pairs={{0,7},{1,0},{2,1},{3,2},{4,3},{5,4},{6,5},{7,6},{8,15},{9,8},{10,9... | collective-permute-start | bytes 786440 | tf_op jit(solution)/shard_map/ppermute | solution.py:28
  105.3 6.5 %collective-permute-start.16 = (bf16[1,256,256]{2,1,0:T(8,128)(2,1)S(1)}, bf16[1,256,256]{2,1,0:T(8,128)(2,1)S(1)}, u32[]{:S(2)}, u32[]{:S(2)}) collective-permute-start(bf16[1,256,256]{2,1,0:T(8,128)(2,1)S(1)} %slice.82), channel_id=1, source_target_pairs={{0,1},{1,2},{2,3},{3,4},{4,5},{5,6},{6,7},{7,0},{8,9},{9,10},{10,1... | collective-permute-start | bytes 393224 | tf_op jit(solution)/shard_map/ppermute | solution.py:36
  105.6 6.1 %collective-permute-start.17 = (bf16[1,256,256]{2,1,0:T(8,128)(2,1)S(1)}, bf16[1,256,256]{2,1,0:T(8,128)(2,1)S(1)}, u32[]{:S(2)}, u32[]{:S(2)}) collective-permute-start(bf16[1,256,256]{2,1,0:T(8,128)(2,1)S(1)} %slice.83), channel_id=1, source_target_pairs={{0,7},{1,0},{2,1},{3,2},{4,3},{5,4},{6,5},{7,6},{8,15},{9,8},{10,9... | collective-permute-start | bytes 393224 | tf_op jit(solution)/shard_map/ppermute | solution.py:37
  112.3 6.6 %collective-permute-start.18 = (bf16[256,256]{1,0:T(8,128)(2,1)S(1)}, bf16[256,256]{1,0:T(8,128)(2,1)S(1)}, u32[]{:S(2)}, u32[]{:S(2)}) collective-permute-start(bf16[256,256]{1,0:T(8,128)(2,1)S(1)} %fusion.31), channel_id=1, source_target_pairs={{0,8},{8,0},{1,9},{9,1},{2,10},{10,2},{3,11},{11,3},{4,12},{12,4},... | collective-permute-start | bytes 393224 | tf_op jit(solution)/shard_map/ppermute | solution.py:17
  119.0 9.2 %collective-permute-start.19 = (bf16[2,256,256]{2,1,0:T(8,128)(2,1)S(1)}, bf16[2,256,256]{2,1,0:T(8,128)(2,1)S(1)}, u32[]{:S(2)}, u32[]{:S(2)}) collective-permute-start(bf16[2,256,256]{2,1,0:T(8,128)(2,1)S(1)} %fusion.33), channel_id=1, source_target_pairs={{0,7},{1,0},{2,1},{3,2},{4,3},{5,4},{6,5},{7,6},{8,15},{9,8},{10,9... | collective-permute-start | bytes 786440 | tf_op jit(solution)/shard_map/ppermute | solution.py:28
  122.4 9.5 %collective-permute-start.22 = (bf16[2,256,256]{2,1,0:T(8,128)(2,1)S(1)}, bf16[2,256,256]{2,1,0:T(8,128)(2,1)S(1)}, u32[]{:S(2)}, u32[]{:S(2)}) collective-permute-start(bf16[2,256,256]{2,1,0:T(8,128)(2,1)S(1)} %fusion.33), channel_id=1, source_target_pairs={{0,1},{1,2},{2,3},{3,4},{4,5},{5,6},{6,7},{7,0},{8,9},{9,10},{10,1... | collective-permute-start | bytes 786440 | tf_op jit(solution)/shard_map/ppermute | solution.py:27
  128.2 11.8 %collective-permute-start.20 = (bf16[2,256,256]{2,1,0:T(8,128)(2,1)S(1)}, bf16[2,256,256]{2,1,0:T(8,128)(2,1)S(1)}, u32[]{:S(2)}, u32[]{:S(2)}) collective-permute-start(bf16[2,256,256]{2,1,0:T(8,128)(2,1)S(1)} %collective-permute-done.19), channel_id=1, source_target_pairs={{0,7},{1,0},{2,1},{3,2},{4,3},{5,4},{6,5},{7,6},{8,15},{9,8},{10,9... | collective-permute-start | bytes 786440 | tf_op jit(solution)/shard_map/ppermute | solution.py:28
  131.9 8.1 %collective-permute-start.23 = (bf16[2,256,256]{2,1,0:T(8,128)(2,1)S(1)}, bf16[2,256,256]{2,1,0:T(8,128)(2,1)S(1)}, u32[]{:S(2)}, u32[]{:S(2)}) collective-permute-start(bf16[2,256,256]{2,1,0:T(8,128)(2,1)S(1)} %collective-permute-done.22), channel_id=1, source_target_pairs={{0,1},{1,2},{2,3},{3,4},{4,5},{5,6},{6,7},{7,0},{8,9},{9,10},{10,1... | collective-permute-start | bytes 786440 | tf_op jit(solution)/shard_map/ppermute | solution.py:27
  140.0 7.6 %collective-permute-start.24 = (bf16[2,256,256]{2,1,0:T(8,128)(2,1)S(1)}, bf16[2,256,256]{2,1,0:T(8,128)(2,1)S(1)}, u32[]{:S(2)}, u32[]{:S(2)}) collective-permute-start(bf16[2,256,256]{2,1,0:T(8,128)(2,1)S(1)} %collective-permute-done.23), channel_id=1, source_target_pairs={{0,1},{1,2},{2,3},{3,4},{4,5},{5,6},{6,7},{7,0},{8,9},{9,10},{10,1... | collective-permute-start | bytes 786440 | tf_op jit(solution)/shard_map/ppermute | solution.py:27
  140.0 7.7 %collective-permute-start.21 = (bf16[2,256,256]{2,1,0:T(8,128)(2,1)S(1)}, bf16[2,256,256]{2,1,0:T(8,128)(2,1)S(1)}, u32[]{:S(2)}, u32[]{:S(2)}) collective-permute-start(bf16[2,256,256]{2,1,0:T(8,128)(2,1)S(1)} %collective-permute-done.20), channel_id=1, source_target_pairs={{0,7},{1,0},{2,1},{3,2},{4,3},{5,4},{6,5},{7,6},{8,15},{9,8},{10,9... | collective-permute-start | bytes 786440 | tf_op jit(solution)/shard_map/ppermute | solution.py:28
  147.6 6.3 %collective-permute-start.25 = (bf16[1,256,256]{2,1,0:T(8,128)(2,1)S(1)}, bf16[1,256,256]{2,1,0:T(8,128)(2,1)S(1)}, u32[]{:S(2)}, u32[]{:S(2)}) collective-permute-start(bf16[1,256,256]{2,1,0:T(8,128)(2,1)S(1)} %slice.84), channel_id=1, source_target_pairs={{0,1},{1,2},{2,3},{3,4},{4,5},{5,6},{6,7},{7,0},{8,9},{9,10},{10,1... | collective-permute-start | bytes 393224 | tf_op jit(solution)/shard_map/ppermute | solution.py:36
  147.7 6.1 %collective-permute-start.26 = (bf16[1,256,256]{2,1,0:T(8,128)(2,1)S(1)}, bf16[1,256,256]{2,1,0:T(8,128)(2,1)S(1)}, u32[]{:S(2)}, u32[]{:S(2)}) collective-permute-start(bf16[1,256,256]{2,1,0:T(8,128)(2,1)S(1)} %slice.85), channel_id=1, source_target_pairs={{0,7},{1,0},{2,1},{3,2},{4,3},{5,4},{6,5},{7,6},{8,15},{9,8},{10,9... | collective-permute-start | bytes 393224 | tf_op jit(solution)/shard_map/ppermute | solution.py:37
  (3 other events, 10.0 us)
Sparse Core Ops, SparseCore 0:
  9.2 40.6 all-gather.1

commit v2 on v1

v2 whole, which is shorter than its diff:
```python
import jax
import jax.numpy as jnp
from jax import lax
from jax.sharding import Mesh, PartitionSpec as P

STEPS = 3
REG_BLK = 2

ROW_AXES = ("x", "y_lo", "core")
COL_AXES = ("y_hi", "z")


def ring_blocks(piece, axis, count, split_dim):
    fwd = [(i, (i + 1) % count) for i in range(count)]
    bwd = [(i, (i - 1) % count) for i in range(count)]
    blocks = [None] * count
    blocks[0] = piece
    right = piece
    left = piece
    for k in range(1, (count + 1) // 2):
        right = lax.ppermute(right, axis, fwd)
        left = lax.ppermute(left, axis, bwd)
        blocks[(-k) % count] = right
        blocks[k] = left
    if count % 2 == 0 and count > 1:
        if count == 2:
            blocks[1] = lax.ppermute(piece, axis, fwd)
        else:
            split = piece.shape[split_dim] // 2
            lo = lax.ppermute(lax.slice_in_dim(right, 0, split, axis=split_dim), axis, fwd)
            hi = lax.ppermute(lax.slice_in_dim(left, split, None, axis=split_dim), axis, bwd)
            blocks[count // 2] = jnp.concatenate([lo, hi], axis=split_dim)
    return blocks


def in_order(blocks, axis):
    return jnp.roll(jnp.stack(blocks), lax.axis_index(axis), axis=0)


def gather_col(field, y_count, z_count):
    pair = in_order(ring_blocks(field, "y_hi", y_count, 0), "y_hi")
    return ring_blocks(pair, "z", z_count, 0)


def gather_slots(tiles):
    local_slots = tiles.shape[1]
    slot_map = jnp.arange(local_slots, dtype=jnp.int32)
    stride = 1
    for axis in ROW_AXES[::-1]:
        count = lax.axis_size(axis)
        stacked = jnp.stack(ring_blocks(tiles, axis, count, 0))
        tiles = jnp.moveaxis(stacked, 0, 1).reshape(tiles.shape[0], -1, *tiles.shape[2:])
        owner = (lax.axis_index(axis) + jnp.arange(count, dtype=jnp.int32)) % count
        slot_map = (owner[:, None] * (stride * local_slots) + slot_map[None, :]).reshape(-1)
        stride = stride * count
    return tiles, slot_map


def body(coeffs, block_tiles, neighbours, density):
    y_count = lax.axis_size("y_hi")
    z_count = lax.axis_size("z")
    local_width = coeffs.shape[1]
    block_rows = neighbours.shape[0]
    slot_count = neighbours.shape[1]
    block_size = block_tiles.shape[2]
    total_blocks = block_rows * y_count * z_count
    col = lax.axis_index("y_hi") * z_count + lax.axis_index("z")
    block_ids = col * block_rows + jnp.arange(block_rows, dtype=jnp.int32)
    region_ids = block_ids // REG_BLK
    region_match = region_ids[:, None] == jnp.arange(density.shape[0], dtype=jnp.int32)[None, :]
    live_counts = jnp.sum(jnp.where(region_match, density[None, :], 0), axis=1)
    live_mask = jnp.arange(slot_count, dtype=jnp.int32)[None, :] < live_counts[:, None]

    tiles, slot_map = gather_slots(block_tiles)
    ring_neighbours = neighbours[:, slot_map]
    ring_live = live_mask[:, slot_map]
    rows = jnp.arange(total_blocks, dtype=jnp.int32)
    per_col = block_rows
    row_y = rows // (z_count * per_col)
    row_d = (rows // per_col) % z_count
    row_block = (row_y * z_count + (row_d + lax.axis_index("z")) % z_count) * per_col + rows % per_col
    pick = (ring_neighbours[:, :, None] == row_block[None, None, :]) & ring_live[:, :, None]
    dense = jnp.einsum("bsn,bsij->njbi", pick.astype(tiles.dtype), tiles, preferred_element_type=tiles.dtype)
    dense = dense.reshape(y_count, z_count, local_width, local_width)

    def apply_hamiltonian(field):
        blocks = gather_col(field, y_count, z_count)
        total = None
        for d, chunk in enumerate(blocks):
            part = jnp.einsum("ymj,yjo->mo", chunk, dense[:, d], preferred_element_type=jnp.float32)
            total = part if total is None else total + part
        return total

    previous = coeffs
    current = apply_hamiltonian(coeffs).astype(jnp.bfloat16)

    def recurse(repeat, carry):
        previous, current = carry
        product = apply_hamiltonian(current)
        following = (2.0 * product - previous.astype(jnp.float32)).astype(jnp.bfloat16)
        return current, following

    previous, current = lax.fori_loop(0, STEPS - 1, recurse, (previous, current))
    return current


def solution(mesh):
    devices = mesh.devices.reshape(4, 2, 2, 2, 8)
    fine = Mesh(devices, ROW_AXES + COL_AXES)
    placed = (P(ROW_AXES, COL_AXES), P(COL_AXES, ROW_AXES, None, None), P(COL_AXES, None), P())
    return jax.shard_map(
        body, mesh=fine, in_specs=placed, out_specs=P(ROW_AXES, COL_AXES), check_vma=False
    )
```

time: 162 us -> 174 us (1.074); the launches traced: 162 us -> 172 us
  between operations: 13.8 us -> 0.23 us
  local copies, waits for them, and re-layouts: 10.9 us -> 21.8 us
  starting transfers between devices: 52.5 us -> 62.4 us
    ppermute x27 -> x33, starting transfers between devices: 52.5 us -> 62.4 us  [the longest x10 31.7 us: ring_blocks(): left = lax.ppermute(left, axis, bwd)]
    transpose x0 -> x3, local copies, waits for them, and re-layouts: none -> 7.09 us  [the longest x1 6.35 us: body(): jnp.einsum('bsn,bsij->njbi', pick.astype(tiles.dtype), tiles, preferred_e...]
    ppermute x27 -> x33, waiting for transfers between devices: 64 us -> 67.8 us  [the longest x10 26.5 us: ring_blocks(): left = lax.ppermute(left, axis, bwd)]
    all_gather x1 -> x0, waiting for transfers between devices: 2.73 us -> none  [body(): tiles = lax.all_gather(block_tiles, ROW_AXES, axis=1, tiled=True)]
    dot_general x24, matrix products: 7.15 us -> 9.33 us  [apply_hamiltonian(): jnp.einsum('ymj,yjo->mo', chunk, dense[:, d], preferred_element_type=jnp....]
    concatenate x4 -> x3, other arithmetic: 2.68 us -> 0.59 us  [in_order(): return jnp.roll(jnp.stack(blocks), lax.axis_index(axis), axis=0)]
    dot_general x1, matrix products: 6.78 us -> 4.81 us  [body(): jnp.einsum('bsn,bsij->njbi', pick.astype(tiles.dtype), tiles, preferred_e...]
  transfers between devices with their start and end apart: 28 -> 33, of which waited for: 15 -> 21; matrix products, arithmetic and copies ran while one was open for 15% -> 22% of each run, Pallas kernels for 0% -> 0%
where the time goes in v2:
time: 174 us; the launch traced here: 172 us
  waiting for transfers between devices  67.8 us (39%)
  starting transfers between devices  62.4 us (36%)
  local copies, waits for them, and re-layouts  21.8 us (13%)
  matrix products  14.1 us (8%)
  other arithmetic  5.11 us (3%)
    ppermute x10, starting transfers between devices, ring_blocks(): left = lax.ppermute(left, axis, bwd)  31.7 us
    ppermute x10, waiting for transfers between devices, ring_blocks(): left = lax.ppermute(left, axis, bwd)  26.5 us
    ppermute x5, waiting for transfers between devices, ring_blocks(): blocks[1] = lax.ppermute(piece, axis, fwd)  14.6 us
    ppermute x4, starting transfers between devices, ring_blocks(): lax.ppermute(lax.slice_in_dim(left, split, None, axis=split_dim), axis, bwd)  12.5 us
    ppermute x10, waiting for transfers between devices, ring_blocks(): right = lax.ppermute(right, axis, fwd)  12.3 us
    reshape x2, local copies, waits for them, and re-layouts, body(): dense = dense.reshape(y_count, z_count, local_width, local_width)  9.54 us
    dot_general x24, matrix products, apply_hamiltonian(): jnp.einsum('ymj,yjo->mo', chunk, dense[:, d], preferred_element_type=jnp....  9.33 us
    ppermute x4, waiting for transfers between devices, ring_blocks(): lax.ppermute(lax.slice_in_dim(right, 0, split, axis=split_dim), axis, fwd)  9.29 us
  transfers between devices with their start and end apart: 33, of which 21 were waited for; matrix products, arithmetic and copies ran while one was open for 22% of the time, Pallas kernels for 0%

profile of v2, /device:TPU:2, one launch (start us, length us, event | category | flops | bytes accessed | tf_op | source)
XLA Modules:
  0.0 171.8 jit_solution(13991234420912318099)
XLA Ops:
  0.9 3.2 %collective-permute-start.9 = (bf16[256,256]{1,0:T(8,128)(2,1)S(1)}, bf16[256,256]{1,0:T(8,128)(2,1)S(1)}, u32[]{:S(2)}, u32[]{:S(2)}) collective-permute-start(bf16[256,256]{1,0:T(8,128)(2,1)S(1)} %copy.59), channel_id=1, source_target_pairs={{0,8},{8,0},{1,9},{9,1},{2,10},{10,2},{3,11},{11,3},{4,12},{12,4},... | collective-permute-start | bytes 393224 | tf_op jit(solution)/shard_map/ppermute | solution.py:27
  8.6 5.9 %collective-permute-start.16 = (bf16[2,256,256]{2,1,0:T(8,128)(2,1)S(1)}, bf16[2,256,256]{2,1,0:T(8,128)(2,1)}, u32[]{:S(2)}, u32[]{:S(2)}) collective-permute-start(bf16[2,256,256]{2,1,0:T(8,128)(2,1)S(1)} %fusion.47), channel_id=1, source_target_pairs={{0,7},{1,0},{2,1},{3,2},{4,3},{5,4},{6,5},{7,6},{8,15},{9,8},{10,9... | collective-permute-start | bytes 786440 | tf_op jit(solution)/shard_map/ppermute | solution.py:22
  14.5 3.5 %collective-permute-done.11 = bf16[4,6,64,64]{3,2,1,0:T(8,128)(2,1)S(1)} collective-permute-done((bf16[4,6,64,64]{3,2,1,0:T(8,128)(2,1)S(1)}, bf16[4,6,64,64]{3,2,1,0:T(8,128)(2,1)S(1)}, u32[]{:S(2)}, u32[]{:S(2)}) %collective-permute-start.11) | collective-permute-done | bytes 196640 | tf_op jit(solution)/shard_map/ppermute | solution.py:27
  20.4 5.9 %collective-permute-start.17 = (bf16[2,256,256]{2,1,0:T(8,128)(2,1)}, bf16[2,256,256]{2,1,0:T(8,128)(2,1)}, u32[]{:S(2)}, u32[]{:S(2)}) collective-permute-start(bf16[2,256,256]{2,1,0:T(8,128)(2,1)} %collective-permute-done.16), channel_id=1, source_target_pairs={{0,7},{1,0},{2,1},{3,2},{4,3},{5,4},{6,5},{7,6},{8,15},{9,8},{10,9... | collective-permute-start | bytes 786440 | tf_op jit(solution)/shard_map/ppermute | solution.py:22
  26.3 10.7 %collective-permute-done.13 = bf16[4,12,64,64]{3,2,1,0:T(8,128)(2,1)S(1)} collective-permute-done((bf16[4,12,64,64]{3,2,1,0:T(8,128)(2,1)S(1)}, bf16[4,12,64,64]{3,2,1,0:T(8,128)(2,1)S(1)}, u32[]{:S(2)}, u32[]{:S(2)}) %collective-permute-start.13) | collective-permute-done | bytes 393248 | tf_op jit(solution)/shard_map/ppermute | solution.py:21
  41.5 2.0 %collective-permute-start.21 = (bf16[2,256,256]{2,1,0:T(8,128)(2,1)}, bf16[2,256,256]{2,1,0:T(8,128)(2,1)}, u32[]{:S(2)}, u32[]{:S(2)}) collective-permute-start(bf16[2,256,256]{2,1,0:T(8,128)(2,1)} %collective-permute-done.20), channel_id=1, source_target_pairs={{0,1},{1,2},{2,3},{3,4},{4,5},{5,6},{6,7},{7,0},{8,9},{9,10},{10,1... | collective-permute-start | bytes 786440 | tf_op jit(solution)/shard_map/ppermute | solution.py:21
  43.5 4.3 %collective-permute-start.18 = (bf16[2,256,256]{2,1,0:T(8,128)(2,1)}, bf16[2,256,256]{2,1,0:T(8,128)(2,1)S(1)}, u32[]{:S(2)}, u32[]{:S(2)}) collective-permute-start(bf16[2,256,256]{2,1,0:T(8,128)(2,1)} %collective-permute-done.17), channel_id=1, source_target_pairs={{0,7},{1,0},{2,1},{3,2},{4,3},{5,4},{6,5},{7,6},{8,15},{9,8},{10,9... | collective-permute-start | bytes 786440 | tf_op jit(solution)/shard_map/ppermute | solution.py:22
  51.9 4.8 %fusion.35 = bf16[64,64,4,64]{0,1,3,2:T(8,128)(2,1)} fusion(bf16[4,48,64,64]{3,2,1,0:T(8,128)(2,1)S(1)} %bitcast.219, s32[64]{0:T(128)S(1)} %fusion.58, s32[4,48]{1,0:T(4,128)S(1)} %copy.31, pred[4,48]{1,0:T(4,128)(4,1)S(1)} %copy.32), kind=kOutput, calls=%fused_computation.50 | convolution fusion | flops 100687872 | bytes 3671232 | tf_op jit(solution)/shard_map/bsn,bsij->njbi/dot_general | solution.py:83
  56.7 6.4 %copy.34 = bf16[64,64,4,64]{1,0,3,2:T(8,128)(2,1)} copy(bf16[64,64,4,64]{0,1,3,2:T(8,128)(2,1)} %fusion.35) | data formatting | bytes 4194304 | tf_op jit(solution)/shard_map/bsn,bsij->njbi/transpose | solution.py:83
  63.1 6.5 %reshape.202 = bf16[2,8,256,256]{2,1,0,3:T(8,128)(2,1)} reshape(bf16[64,64,4,64]{1,0,3,2:T(8,128)(2,1)} %copy.34) | data formatting | bytes 4194304 | tf_op jit(solution)/shard_map/reshape | solution.py:84
  69.6 3.0 %copy.35 = bf16[2,8,256,256]{3,2,0,1:T(8,128)(2,1)S(1)} copy(bf16[2,8,256,256]{2,1,0,3:T(8,128)(2,1)} %reshape.202) | data formatting | bytes 4194304 | tf_op jit(solution)/shard_map/reshape | solution.py:84
  77.6 2.0 %collective-permute-start.22 = (bf16[1,256,256]{2,1,0:T(8,128)(2,1)S(1)}, bf16[1,256,256]{2,1,0:T(8,128)(2,1)S(1)}, u32[]{:S(2)}, u32[]{:S(2)}) collective-permute-start(bf16[1,256,256]{2,1,0:T(8,128)(2,1)S(1)} %slice.90), channel_id=1, source_target_pairs={{0,1},{1,2},{2,3},{3,4},{4,5},{5,6},{6,7},{7,0},{8,9},{9,10},{10,1... | collective-permute-start | bytes 393224 | tf_op jit(solution)/shard_map/ppermute | solution.py:30
  79.6 4.5 %collective-permute-start.23 = (bf16[1,256,256]{2,1,0:T(8,128)(2,1)S(1)}, bf16[1,256,256]{2,1,0:T(8,128)(2,1)S(1)}, u32[]{:S(2)}, u32[]{:S(2)}) collective-permute-start(bf16[1,256,256]{2,1,0:T(8,128)(2,1)S(1)} %slice.91), channel_id=1, source_target_pairs={{0,7},{1,0},{2,1},{3,2},{4,3},{5,4},{6,5},{7,6},{8,15},{9,8},{10,9... | collective-permute-start | bytes 393224 | tf_op jit(solution)/shard_map/ppermute | solution.py:31
  87.2 83.9 %while.12 = (s32[]{:T(128)}, bf16[256,256]{1,0:T(8,128)(2,1)S(1)}, bf16[256,256]{1,0:T(8,128)(2,1)S(1)}, bf16[2,8,256,256]{3,2,0,1:T(8,128)(2,1)S(1)}, s32[]{:T(...) while((s32[]{:T(128)}, bf16[256,256]{1,0:T(8,128)(2,1)S(1)}, ...), condition=%wide.region_2.4_spmd, body=%wide.region_1.3_spmd.sunk | while | flops 538116096 | bytes 17564300 | solution.py:103
  88.7 5.1 %collective-permute-done = bf16[256,256]{1,0:T(8,128)(2,1)S(1)} collective-permute-done((bf16[256,256]{1,0:T(8,128)(2,1)S(1)}, bf16[256,256]{1,0:T(8,128)(2,1)S(1)}, u32[]{:S(2)}, u32[]{:S(2)}) %collective-permute-start) | collective-permute-done | bytes 131104 | tf_op jit(solution)/shard_map/while/body/eval_jaxpr/ppermute | solution.py:27
  94.0 3.6 %collective-permute-start.4 = (bf16[2,256,256]{2,1,0:T(8,128)(2,1)S(1)}, bf16[2,256,256]{2,1,0:T(8,128)(2,1)S(1)}, u32[]{:S(2)}, u32[]{:S(2)}) collective-permute-start(bf16[2,256,256]{2,1,0:T(8,128)(2,1)S(1)} %fusion.123), channel_id=1, source_target_pairs={{0,7},{1,0},{2,1},{3,2},{4,3},{5,4},{6,5},{7,6},{8,15},{9,8},{10,9... | collective-permute-start | bytes 786440 | tf_op jit(solution)/shard_map/while/body/eval_jaxpr/ppermute | solution.py:22
  97.9 5.9 %collective-permute-done.4 = bf16[2,256,256]{2,1,0:T(8,128)(2,1)S(1)} collective-permute-done((bf16[2,256,256]{2,1,0:T(8,128)(2,1)S(1)}, bf16[2,256,256]{2,1,0:T(8,128)(2,1)S(1)}, u32[]{:S(2)}, u32[]{:S(2)}) %collective-permute-start.4) | collective-permute-done | bytes 262176 | tf_op jit(solution)/shard_map/while/body/eval_jaxpr/ppermute | solution.py:22
  103.8 3.7 %collective-permute-start.5 = (bf16[2,256,256]{2,1,0:T(8,128)(2,1)S(1)}, bf16[2,256,256]{2,1,0:T(8,128)(2,1)S(1)}, u32[]{:S(2)}, u32[]{:S(2)}) collective-permute-start(bf16[2,256,256]{2,1,0:T(8,128)(2,1)S(1)} %collective-permute-done.4), channel_id=1, source_target_pairs={{0,7},{1,0},{2,1},{3,2},{4,3},{5,4},{6,5},{7,6},{8,15},{9,8},{10,9... | collective-permute-start | bytes 786440 | tf_op jit(solution)/shard_map/while/body/eval_jaxpr/ppermute | solution.py:22
  108.2 5.4 %collective-permute-done.5 = bf16[2,256,256]{2,1,0:T(8,128)(2,1)S(1)} collective-permute-done((bf16[2,256,256]{2,1,0:T(8,128)(2,1)S(1)}, bf16[2,256,256]{2,1,0:T(8,128)(2,1)S(1)}, u32[]{:S(2)}, u32[]{:S(2)}) %collective-permute-start.5) | collective-permute-done | bytes 262176 | tf_op jit(solution)/shard_map/while/body/eval_jaxpr/ppermute | solution.py:22
  113.6 3.7 %collective-permute-start.6 = (bf16[2,256,256]{2,1,0:T(8,128)(2,1)S(1)}, bf16[2,256,256]{2,1,0:T(8,128)(2,1)S(1)}, u32[]{:S(2)}, u32[]{:S(2)}) collective-permute-start(bf16[2,256,256]{2,1,0:T(8,128)(2,1)S(1)} %collective-permute-done.5), channel_id=1, source_target_pairs={{0,7},{1,0},{2,1},{3,2},{4,3},{5,4},{6,5},{7,6},{8,15},{9,8},{10,9... | collective-permute-start | bytes 786440 | tf_op jit(solution)/shard_map/while/body/eval_jaxpr/ppermute | solution.py:22
  117.7 3.5 %collective-permute-done.6 = bf16[2,256,256]{2,1,0:T(8,128)(2,1)S(1)} collective-permute-done((bf16[2,256,256]{2,1,0:T(8,128)(2,1)S(1)}, bf16[2,256,256]{2,1,0:T(8,128)(2,1)S(1)}, u32[]{:S(2)}, u32[]{:S(2)}) %collective-permute-start.6) | collective-permute-done | bytes 262176 | tf_op jit(solution)/shard_map/while/body/eval_jaxpr/ppermute | solution.py:22
  121.2 3.8 %collective-permute-start.7 = (bf16[1,256,256]{2,1,0:T(8,128)(2,1)S(1)}, bf16[1,256,256]{2,1,0:T(8,128)(2,1)S(1)}, u32[]{:S(2)}, u32[]{:S(2)}) collective-permute-start(bf16[1,256,256]{2,1,0:T(8,128)(2,1)S(1)} %slice.162), channel_id=1, source_target_pairs={{0,7},{1,0},{2,1},{3,2},{4,3},{5,4},{6,5},{7,6},{8,15},{9,8},{10,9... | collective-permute-start | bytes 393224 | tf_op jit(solution)/shard_map/while/body/eval_jaxpr/ppermute | solution.py:31
  125.3 2.2 %collective-permute-done.7 = bf16[1,256,256]{2,1,0:T(8,128)(2,1)S(1)} collective-permute-done((bf16[1,256,256]{2,1,0:T(8,128)(2,1)S(1)}, bf16[1,256,256]{2,1,0:T(8,128)(2,1)S(1)}, u32[]{:S(2)}, u32[]{:S(2)}) %collective-permute-start.7) | collective-permute-done | bytes 131104 | tf_op jit(solution)/shard_map/while/body/eval_jaxpr/ppermute | solution.py:31
  127.5 3.8 %collective-permute-done.8 = bf16[1,256,256]{2,1,0:T(8,128)(2,1)S(1)} collective-permute-done((bf16[1,256,256]{2,1,0:T(8,128)(2,1)S(1)}, bf16[1,256,256]{2,1,0:T(8,128)(2,1)S(1)}, u32[]{:S(2)}, u32[]{:S(2)}) %collective-permute-start.8) | collective-permute-done | bytes 131104 | tf_op jit(solution)/shard_map/while/body/eval_jaxpr/ppermute | solution.py:30
  133.5 4.9 %collective-permute-done = bf16[256,256]{1,0:T(8,128)(2,1)S(1)} collective-permute-done((bf16[256,256]{1,0:T(8,128)(2,1)S(1)}, bf16[256,256]{1,0:T(8,128)(2,1)S(1)}, u32[]{:S(2)}, u32[]{:S(2)}) %collective-permute-start) | collective-permute-done | bytes 131104 | tf_op jit(solution)/shard_map/while/body/eval_jaxpr/ppermute | solution.py:27
  138.7 2.0 %collective-permute-start.1 = (bf16[2,256,256]{2,1,0:T(8,128)(2,1)S(1)}, bf16[2,256,256]{2,1,0:T(8,128)(2,1)S(1)}, u32[]{:S(2)}, u32[]{:S(2)}) collective-permute-start(bf16[2,256,256]{2,1,0:T(8,128)(2,1)S(1)} %fusion.123), channel_id=1, source_target_pairs={{0,1},{1,2},{2,3},{3,4},{4,5},{5,6},{6,7},{7,0},{8,9},{9,10},{10,1... | collective-permute-start | bytes 786440 | tf_op jit(solution)/shard_map/while/body/eval_jaxpr/ppermute | solution.py:21
  140.9 5.8 %collective-permute-done.4 = bf16[2,256,256]{2,1,0:T(8,128)(2,1)S(1)} collective-permute-done((bf16[2,256,256]{2,1,0:T(8,128)(2,1)S(1)}, bf16[2,256,256]{2,1,0:T(8,128)(2,1)S(1)}, u32[]{:S(2)}, u32[]{:S(2)}) %collective-permute-start.4) | collective-permute-done | bytes 262176 | tf_op jit(solution)/shard_map/while/body/eval_jaxpr/ppermute | solution.py:22
  150.1 3.0 %collective-permute-done.5 = bf16[2,256,256]{2,1,0:T(8,128)(2,1)S(1)} collective-permute-done((bf16[2,256,256]{2,1,0:T(8,128)(2,1)S(1)}, bf16[2,256,256]{2,1,0:T(8,128)(2,1)S(1)}, u32[]{:S(2)}, u32[]{:S(2)}) %collective-permute-start.5) | collective-permute-done | bytes 262176 | tf_op jit(solution)/shard_map/while/body/eval_jaxpr/ppermute | solution.py:22
  153.1 3.2 %collective-permute-start.6 = (bf16[2,256,256]{2,1,0:T(8,128)(2,1)S(1)}, bf16[2,256,256]{2,1,0:T(8,128)(2,1)S(1)}, u32[]{:S(2)}, u32[]{:S(2)}) collective-permute-start(bf16[2,256,256]{2,1,0:T(8,128)(2,1)S(1)} %collective-permute-done.5), channel_id=1, source_target_pairs={{0,7},{1,0},{2,1},{3,2},{4,3},{5,4},{6,5},{7,6},{8,15},{9,8},{10,9... | collective-permute-start | bytes 786440 | tf_op jit(solution)/shard_map/while/body/eval_jaxpr/ppermute | solution.py:22
  157.2 3.0 %collective-permute-done.6 = bf16[2,256,256]{2,1,0:T(8,128)(2,1)S(1)} collective-permute-done((bf16[2,256,256]{2,1,0:T(8,128)(2,1)S(1)}, bf16[2,256,256]{2,1,0:T(8,128)(2,1)S(1)}, u32[]{:S(2)}, u32[]{:S(2)}) %collective-permute-start.6) | collective-permute-done | bytes 262176 | tf_op jit(solution)/shard_map/while/body/eval_jaxpr/ppermute | solution.py:22
  160.2 3.8 %collective-permute-start.7 = (bf16[1,256,256]{2,1,0:T(8,128)(2,1)S(1)}, bf16[1,256,256]{2,1,0:T(8,128)(2,1)S(1)}, u32[]{:S(2)}, u32[]{:S(2)}) collective-permute-start(bf16[1,256,256]{2,1,0:T(8,128)(2,1)S(1)} %slice.162), channel_id=1, source_target_pairs={{0,7},{1,0},{2,1},{3,2},{4,3},{5,4},{6,5},{7,6},{8,15},{9,8},{10,9... | collective-permute-start | bytes 393224 | tf_op jit(solution)/shard_map/while/body/eval_jaxpr/ppermute | solution.py:31
  166.5 4.1 %collective-permute-done.8 = bf16[1,256,256]{2,1,0:T(8,128)(2,1)S(1)} collective-permute-done((bf16[1,256,256]{2,1,0:T(8,128)(2,1)S(1)}, bf16[1,256,256]{2,1,0:T(8,128)(2,1)S(1)}, u32[]{:S(2)}, u32[]{:S(2)}) %collective-permute-start.8) | collective-permute-done | bytes 131104 | tf_op jit(solution)/shard_map/while/body/eval_jaxpr/ppermute | solution.py:30
  (115 shorter events, 38.2 us)
Async XLA Ops:
  0.9 7.5 %collective-permute-start.9 = (bf16[256,256]{1,0:T(8,128)(2,1)S(1)}, bf16[256,256]{1,0:T(8,128)(2,1)S(1)}, u32[]{:S(2)}, u32[]{:S(2)}) collective-permute-start(bf16[256,256]{1,0:T(8,128)(2,1)S(1)} %copy.59), channel_id=1, source_target_pairs={{0,8},{8,0},{1,9},{9,1},{2,10},{10,2},{3,11},{11,3},{4,12},{12,4},... | collective-permute-start | bytes 393224 | tf_op jit(solution)/shard_map/ppermute | solution.py:27
  6.8 11.2 %collective-permute-start.11 = (bf16[4,6,64,64]{3,2,1,0:T(8,128)(2,1)S(1)}, bf16[4,6,64,64]{3,2,1,0:T(8,128)(2,1)S(1)}, u32[]{:S(2)}, u32[]{:S(2)}) collective-permute-start(bf16[4,6,64,64]{3,2,1,0:T(8,128)(2,1)S(1)} %bitcast.227), channel_id=1, source_target_pairs={{0,32},{32,0},{1,33},{33,1},{2,34},{34,2},{3,35},{35,3},{4,36},{36... | collective-permute-start | bytes 589832 | tf_op jit(solution)/shard_map/ppermute | solution.py:27
  8.6 11.8 %collective-permute-start.16 = (bf16[2,256,256]{2,1,0:T(8,128)(2,1)S(1)}, bf16[2,256,256]{2,1,0:T(8,128)(2,1)}, u32[]{:S(2)}, u32[]{:S(2)}) collective-permute-start(bf16[2,256,256]{2,1,0:T(8,128)(2,1)S(1)} %fusion.47), channel_id=1, source_target_pairs={{0,7},{1,0},{2,1},{3,2},{4,3},{5,4},{6,5},{7,6},{8,15},{9,8},{10,9... | collective-permute-start | bytes 786440 | tf_op jit(solution)/shard_map/ppermute | solution.py:22
  14.5 11.8 %collective-permute-start.19 = (bf16[2,256,256]{2,1,0:T(8,128)(2,1)S(1)}, bf16[2,256,256]{2,1,0:T(8,128)(2,1)S(1)}, u32[]{:S(2)}, u32[]{:S(2)}) collective-permute-start(bf16[2,256,256]{2,1,0:T(8,128)(2,1)S(1)} %fusion.47), channel_id=1, source_target_pairs={{0,1},{1,2},{2,3},{3,4},{4,5},{5,6},{6,7},{7,0},{8,9},{9,10},{10,1... | collective-permute-start | bytes 786440 | tf_op jit(solution)/shard_map/ppermute | solution.py:21
  18.2 18.8 %collective-permute-start.13 = (bf16[4,12,64,64]{3,2,1,0:T(8,128)(2,1)S(1)}, bf16[4,12,64,64]{3,2,1,0:T(8,128)(2,1)S(1)}, u32[]{:S(2)}, u32[]{:S(2)}) collective-permute-start(bf16[4,12,64,64]{3,2,1,0:T(8,128)(2,1)S(1)} %bitcast.222), channel_id=1, source_target_pairs={{0,64},{64,128},{128,192},{192,0},{1,65},{65,129},{129,193},{193,1... | collective-permute-start | bytes 1179656 | tf_op jit(solution)/shard_map/ppermute | solution.py:21
  19.8 18.8 %collective-permute-start.12 = (bf16[4,12,64,64]{3,2,1,0:T(8,128)(2,1)S(1)}, bf16[4,12,64,64]{3,2,1,0:T(8,128)(2,1)S(1)}, u32[]{:S(2)}, u32[]{:S(2)}) collective-permute-start(bf16[4,12,64,64]{3,2,1,0:T(8,128)(2,1)S(1)} %bitcast.223), channel_id=1, source_target_pairs={{0,192},{64,0},{128,64},{192,128},{1,193},{65,1},{129,65},{193,129... | collective-permute-start | bytes 1179656 | tf_op jit(solution)/shard_map/ppermute | solution.py:22
  20.4 23.2 %collective-permute-start.17 = (bf16[2,256,256]{2,1,0:T(8,128)(2,1)}, bf16[2,256,256]{2,1,0:T(8,128)(2,1)}, u32[]{:S(2)}, u32[]{:S(2)}) collective-permute-start(bf16[2,256,256]{2,1,0:T(8,128)(2,1)} %collective-permute-done.16), channel_id=1, source_target_pairs={{0,7},{1,0},{2,1},{3,2},{4,3},{5,4},{6,5},{7,6},{8,15},{9,8},{10,9... | collective-permute-start | bytes 786440 | tf_op jit(solution)/shard_map/ppermute | solution.py:22
  26.3 15.2 %collective-permute-start.20 = (bf16[2,256,256]{2,1,0:T(8,128)(2,1)S(1)}, bf16[2,256,256]{2,1,0:T(8,128)(2,1)}, u32[]{:S(2)}, u32[]{:S(2)}) collective-permute-start(bf16[2,256,256]{2,1,0:T(8,128)(2,1)S(1)} %collective-permute-done.19), channel_id=1, source_target_pairs={{0,1},{1,2},{2,3},{3,4},{4,5},{5,6},{6,7},{7,0},{8,9},{9,10},{10,1... | collective-permute-start | bytes 786440 | tf_op jit(solution)/shard_map/ppermute | solution.py:21
  37.1 10.8 %collective-permute-start.14 = (bf16[2,12,64,64]{3,2,1,0:T(8,128)(2,1)S(1)}, bf16[2,12,64,64]{3,2,1,0:T(8,128)(2,1)}, u32[]{:S(2)}, u32[]{:S(2)}) collective-permute-start(bf16[2,12,64,64]{3,2,1,0:T(8,128)(2,1)S(1)} %slice.84), channel_id=1, source_target_pairs={{0,64},{64,128},{128,192},{192,0},{1,65},{65,129},{129,193},{193,1... | collective-permute-start | bytes 589832 | tf_op jit(solution)/shard_map/ppermute | solution.py:30
  39.5 9.5 %collective-permute-start.15 = (bf16[2,12,64,64]{3,2,1,0:T(8,128)(2,1)}, bf16[2,12,64,64]{3,2,1,0:T(8,128)(2,1)}, u32[]{:S(2)}, u32[]{:S(2)}) collective-permute-start(bf16[2,12,64,64]{3,2,1,0:T(8,128)(2,1)} %slice.85), channel_id=1, source_target_pairs={{0,192},{64,0},{128,64},{192,128},{1,193},{65,1},{129,65},{193,129... | collective-permute-start | bytes 589832 | tf_op jit(solution)/shard_map/ppermute | solution.py:31
  41.5 35.2 %collective-permute-start.21 = (bf16[2,256,256]{2,1,0:T(8,128)(2,1)}, bf16[2,256,256]{2,1,0:T(8,128)(2,1)}, u32[]{:S(2)}, u32[]{:S(2)}) collective-permute-start(bf16[2,256,256]{2,1,0:T(8,128)(2,1)} %collective-permute-done.20), channel_id=1, source_target_pairs={{0,1},{1,2},{2,3},{3,4},{4,5},{5,6},{6,7},{7,0},{8,9},{9,10},{10,1... | collective-permute-start | bytes 786440 | tf_op jit(solution)/shard_map/ppermute | solution.py:21
  43.5 36.1 %collective-permute-start.18 = (bf16[2,256,256]{2,1,0:T(8,128)(2,1)}, bf16[2,256,256]{2,1,0:T(8,128)(2,1)S(1)}, u32[]{:S(2)}, u32[]{:S(2)}) collective-permute-start(bf16[2,256,256]{2,1,0:T(8,128)(2,1)} %collective-permute-done.17), channel_id=1, source_target_pairs={{0,7},{1,0},{2,1},{3,2},{4,3},{5,4},{6,5},{7,6},{8,15},{9,8},{10,9... | collective-permute-start | bytes 786440 | tf_op jit(solution)/shard_map/ppermute | solution.py:22
  77.6 9.1 %collective-permute-start.22 = (bf16[1,256,256]{2,1,0:T(8,128)(2,1)S(1)}, bf16[1,256,256]{2,1,0:T(8,128)(2,1)S(1)}, u32[]{:S(2)}, u32[]{:S(2)}) collective-permute-start(bf16[1,256,256]{2,1,0:T(8,128)(2,1)S(1)} %slice.90), channel_id=1, source_target_pairs={{0,1},{1,2},{2,3},{3,4},{4,5},{5,6},{6,7},{7,0},{8,9},{9,10},{10,1... | collective-permute-start | bytes 393224 | tf_op jit(solution)/shard_map/ppermute | solution.py:30
  79.6 7.1 %collective-permute-start.23 = (bf16[1,256,256]{2,1,0:T(8,128)(2,1)S(1)}, bf16[1,256,256]{2,1,0:T(8,128)(2,1)S(1)}, u32[]{:S(2)}, u32[]{:S(2)}) collective-permute-start(bf16[1,256,256]{2,1,0:T(8,128)(2,1)S(1)} %slice.91), channel_id=1, source_target_pairs={{0,7},{1,0},{2,1},{3,2},{4,3},{5,4},{6,5},{7,6},{8,15},{9,8},{10,9... | collective-permute-start | bytes 393224 | tf_op jit(solution)/shard_map/ppermute | solution.py:31
  87.2 6.6 %collective-permute-start = (bf16[256,256]{1,0:T(8,128)(2,1)S(1)}, bf16[256,256]{1,0:T(8,128)(2,1)S(1)}, u32[]{:S(2)}, u32[]{:S(2)}) collective-permute-start(bf16[256,256]{1,0:T(8,128)(2,1)S(1)} %copy.54), channel_id=1, source_target_pairs={{0,8},{8,0},{1,9},{9,1},{2,10},{10,2},{3,11},{11,3},{4,12},{12,4},... | collective-permute-start | bytes 393224 | tf_op jit(solution)/shard_map/while/body/eval_jaxpr/ppermute | solution.py:27
  94.0 9.8 %collective-permute-start.4 = (bf16[2,256,256]{2,1,0:T(8,128)(2,1)S(1)}, bf16[2,256,256]{2,1,0:T(8,128)(2,1)S(1)}, u32[]{:S(2)}, u32[]{:S(2)}) collective-permute-start(bf16[2,256,256]{2,1,0:T(8,128)(2,1)S(1)} %fusion.123), channel_id=1, source_target_pairs={{0,7},{1,0},{2,1},{3,2},{4,3},{5,4},{6,5},{7,6},{8,15},{9,8},{10,9... | collective-permute-start | bytes 786440 | tf_op jit(solution)/shard_map/while/body/eval_jaxpr/ppermute | solution.py:22
  97.6 10.1 %collective-permute-start.1 = (bf16[2,256,256]{2,1,0:T(8,128)(2,1)S(1)}, bf16[2,256,256]{2,1,0:T(8,128)(2,1)S(1)}, u32[]{:S(2)}, u32[]{:S(2)}) collective-permute-start(bf16[2,256,256]{2,1,0:T(8,128)(2,1)S(1)} %fusion.123), channel_id=1, source_target_pairs={{0,1},{1,2},{2,3},{3,4},{4,5},{5,6},{6,7},{7,0},{8,9},{9,10},{10,1... | collective-permute-start | bytes 786440 | tf_op jit(solution)/shard_map/while/body/eval_jaxpr/ppermute | solution.py:21
  103.8 9.8 %collective-permute-start.5 = (bf16[2,256,256]{2,1,0:T(8,128)(2,1)S(1)}, bf16[2,256,256]{2,1,0:T(8,128)(2,1)S(1)}, u32[]{:S(2)}, u32[]{:S(2)}) collective-permute-start(bf16[2,256,256]{2,1,0:T(8,128)(2,1)S(1)} %collective-permute-done.4), channel_id=1, source_target_pairs={{0,7},{1,0},{2,1},{3,2},{4,3},{5,4},{6,5},{7,6},{8,15},{9,8},{10,9... | collective-permute-start | bytes 786440 | tf_op jit(solution)/shard_map/while/body/eval_jaxpr/ppermute | solution.py:22
  107.7 9.5 %collective-permute-start.2 = (bf16[2,256,256]{2,1,0:T(8,128)(2,1)S(1)}, bf16[2,256,256]{2,1,0:T(8,128)(2,1)S(1)}, u32[]{:S(2)}, u32[]{:S(2)}) collective-permute-start(bf16[2,256,256]{2,1,0:T(8,128)(2,1)S(1)} %collective-permute-done.1), channel_id=1, source_target_pairs={{0,1},{1,2},{2,3},{3,4},{4,5},{5,6},{6,7},{7,0},{8,9},{9,10},{10,1... | collective-permute-start | bytes 786440 | tf_op jit(solution)/shard_map/while/body/eval_jaxpr/ppermute | solution.py:21
  113.6 7.6 %collective-permute-start.6 = (bf16[2,256,256]{2,1,0:T(8,128)(2,1)S(1)}, bf16[2,256,256]{2,1,0:T(8,128)(2,1)S(1)}, u32[]{:S(2)}, u32[]{:S(2)}) collective-permute-start(bf16[2,256,256]{2,1,0:T(8,128)(2,1)S(1)} %collective-permute-done.5), channel_id=1, source_target_pairs={{0,7},{1,0},{2,1},{3,2},{4,3},{5,4},{6,5},{7,6},{8,15},{9,8},{10,9... | collective-permute-start | bytes 786440 | tf_op jit(solution)/shard_map/while/body/eval_jaxpr/ppermute | solution.py:22
  117.3 7.7 %collective-permute-start.3 = (bf16[2,256,256]{2,1,0:T(8,128)(2,1)S(1)}, bf16[2,256,256]{2,1,0:T(8,128)(2,1)S(1)}, u32[]{:S(2)}, u32[]{:S(2)}) collective-permute-start(bf16[2,256,256]{2,1,0:T(8,128)(2,1)S(1)} %collective-permute-done.2), channel_id=1, source_target_pairs={{0,1},{1,2},{2,3},{3,4},{4,5},{5,6},{6,7},{7,0},{8,9},{9,10},{10,1... | collective-permute-start | bytes 786440 | tf_op jit(solution)/shard_map/while/body/eval_jaxpr/ppermute | solution.py:21
  121.2 6.3 %collective-permute-start.7 = (bf16[1,256,256]{2,1,0:T(8,128)(2,1)S(1)}, bf16[1,256,256]{2,1,0:T(8,128)(2,1)S(1)}, u32[]{:S(2)}, u32[]{:S(2)}) collective-permute-start(bf16[1,256,256]{2,1,0:T(8,128)(2,1)S(1)} %slice.162), channel_id=1, source_target_pairs={{0,7},{1,0},{2,1},{3,2},{4,3},{5,4},{6,5},{7,6},{8,15},{9,8},{10,9... | collective-permute-start | bytes 393224 | tf_op jit(solution)/shard_map/while/body/eval_jaxpr/ppermute | solution.py:31
  125.0 6.3 %collective-permute-start.8 = (bf16[1,256,256]{2,1,0:T(8,128)(2,1)S(1)}, bf16[1,256,256]{2,1,0:T(8,128)(2,1)S(1)}, u32[]{:S(2)}, u32[]{:S(2)}) collective-permute-start(bf16[1,256,256]{2,1,0:T(8,128)(2,1)S(1)} %slice.163), channel_id=1, source_target_pairs={{0,1},{1,2},{2,3},{3,4},{4,5},{5,6},{6,7},{7,0},{8,9},{9,10},{10,1... | collective-permute-start | bytes 393224 | tf_op jit(solution)/shard_map/while/body/eval_jaxpr/ppermute | solution.py:30
  131.8 6.6 %collective-permute-start = (bf16[256,256]{1,0:T(8,128)(2,1)S(1)}, bf16[256,256]{1,0:T(8,128)(2,1)S(1)}, u32[]{:S(2)}, u32[]{:S(2)}) collective-permute-start(bf16[256,256]{1,0:T(8,128)(2,1)S(1)} %copy.54), channel_id=1, source_target_pairs={{0,8},{8,0},{1,9},{9,1},{2,10},{10,2},{3,11},{11,3},{4,12},{12,4},... | collective-permute-start | bytes 393224 | tf_op jit(solution)/shard_map/while/body/eval_jaxpr/ppermute | solution.py:27
  138.6 8.1 %collective-permute-start.4 = (bf16[2,256,256]{2,1,0:T(8,128)(2,1)S(1)}, bf16[2,256,256]{2,1,0:T(8,128)(2,1)S(1)}, u32[]{:S(2)}, u32[]{:S(2)}) collective-permute-start(bf16[2,256,256]{2,1,0:T(8,128)(2,1)S(1)} %fusion.123), channel_id=1, source_target_pairs={{0,7},{1,0},{2,1},{3,2},{4,3},{5,4},{6,5},{7,6},{8,15},{9,8},{10,9... | collective-permute-start | bytes 786440 | tf_op jit(solution)/shard_map/while/body/eval_jaxpr/ppermute | solution.py:22
  138.7 9.1 %collective-permute-start.1 = (bf16[2,256,256]{2,1,0:T(8,128)(2,1)S(1)}, bf16[2,256,256]{2,1,0:T(8,128)(2,1)S(1)}, u32[]{:S(2)}, u32[]{:S(2)}) collective-permute-start(bf16[2,256,256]{2,1,0:T(8,128)(2,1)S(1)} %fusion.123), channel_id=1, source_target_pairs={{0,1},{1,2},{2,3},{3,4},{4,5},{5,6},{6,7},{7,0},{8,9},{9,10},{10,1... | collective-permute-start | bytes 786440 | tf_op jit(solution)/shard_map/while/body/eval_jaxpr/ppermute | solution.py:21
  146.7 6.4 %collective-permute-start.5 = (bf16[2,256,256]{2,1,0:T(8,128)(2,1)S(1)}, bf16[2,256,256]{2,1,0:T(8,128)(2,1)S(1)}, u32[]{:S(2)}, u32[]{:S(2)}) collective-permute-start(bf16[2,256,256]{2,1,0:T(8,128)(2,1)S(1)} %collective-permute-done.4), channel_id=1, source_target_pairs={{0,7},{1,0},{2,1},{3,2},{4,3},{5,4},{6,5},{7,6},{8,15},{9,8},{10,9... | collective-permute-start | bytes 786440 | tf_op jit(solution)/shard_map/while/body/eval_jaxpr/ppermute | solution.py:22
  147.8 9.0 %collective-permute-start.2 = (bf16[2,256,256]{2,1,0:T(8,128)(2,1)S(1)}, bf16[2,256,256]{2,1,0:T(8,128)(2,1)S(1)}, u32[]{:S(2)}, u32[]{:S(2)}) collective-permute-start(bf16[2,256,256]{2,1,0:T(8,128)(2,1)S(1)} %collective-permute-done.1), channel_id=1, source_target_pairs={{0,1},{1,2},{2,3},{3,4},{4,5},{5,6},{6,7},{7,0},{8,9},{9,10},{10,1... | collective-permute-start | bytes 786440 | tf_op jit(solution)/shard_map/while/body/eval_jaxpr/ppermute | solution.py:21
  153.1 7.1 %collective-permute-start.6 = (bf16[2,256,256]{2,1,0:T(8,128)(2,1)S(1)}, bf16[2,256,256]{2,1,0:T(8,128)(2,1)S(1)}, u32[]{:S(2)}, u32[]{:S(2)}) collective-permute-start(bf16[2,256,256]{2,1,0:T(8,128)(2,1)S(1)} %collective-permute-done.5), channel_id=1, source_target_pairs={{0,7},{1,0},{2,1},{3,2},{4,3},{5,4},{6,5},{7,6},{8,15},{9,8},{10,9... | collective-permute-start | bytes 786440 | tf_op jit(solution)/shard_map/while/body/eval_jaxpr/ppermute | solution.py:22
  156.7 7.6 %collective-permute-start.3 = (bf16[2,256,256]{2,1,0:T(8,128)(2,1)S(1)}, bf16[2,256,256]{2,1,0:T(8,128)(2,1)S(1)}, u32[]{:S(2)}, u32[]{:S(2)}) collective-permute-start(bf16[2,256,256]{2,1,0:T(8,128)(2,1)S(1)} %collective-permute-done.2), channel_id=1, source_target_pairs={{0,1},{1,2},{2,3},{3,4},{4,5},{5,6},{6,7},{7,0},{8,9},{9,10},{10,1... | collective-permute-start | bytes 786440 | tf_op jit(solution)/shard_map/while/body/eval_jaxpr/ppermute | solution.py:21
  160.2 6.3 %collective-permute-start.7 = (bf16[1,256,256]{2,1,0:T(8,128)(2,1)S(1)}, bf16[1,256,256]{2,1,0:T(8,128)(2,1)S(1)}, u32[]{:S(2)}, u32[]{:S(2)}) collective-permute-start(bf16[1,256,256]{2,1,0:T(8,128)(2,1)S(1)} %slice.162), channel_id=1, source_target_pairs={{0,7},{1,0},{2,1},{3,2},{4,3},{5,4},{6,5},{7,6},{8,15},{9,8},{10,9... | collective-permute-start | bytes 393224 | tf_op jit(solution)/shard_map/while/body/eval_jaxpr/ppermute | solution.py:31
  164.3 6.3 %collective-permute-start.8 = (bf16[1,256,256]{2,1,0:T(8,128)(2,1)S(1)}, bf16[1,256,256]{2,1,0:T(8,128)(2,1)S(1)}, u32[]{:S(2)}, u32[]{:S(2)}) collective-permute-start(bf16[1,256,256]{2,1,0:T(8,128)(2,1)S(1)} %slice.163), channel_id=1, source_target_pairs={{0,1},{1,2},{2,3},{3,4},{4,5},{5,6},{6,7},{7,0},{8,9},{9,10},{10,1... | collective-permute-start | bytes 393224 | tf_op jit(solution)/shard_map/while/body/eval_jaxpr/ppermute | solution.py:30
  (7 other events, 55.5 us)

commit v3 on v2

--- a/solution.py
+++ b/solution.py
@@ -1,6 +1,8 @@
 import jax
 import jax.numpy as jnp
 from jax import lax
+from jax.experimental import pallas as pl
+from jax.experimental.pallas import tpu as pltpu
 from jax.sharding import Mesh, PartitionSpec as P
 
 STEPS = 3
@@ -46,14 +48,41 @@
     local_slots = tiles.shape[1]
     slot_map = jnp.arange(local_slots, dtype=jnp.int32)
     stride = 1
+    stacked = tiles[None]
     for axis in ROW_AXES[::-1]:
         count = lax.axis_size(axis)
-        stacked = jnp.stack(ring_blocks(tiles, axis, count, 0))
-        tiles = jnp.moveaxis(stacked, 0, 1).reshape(tiles.shape[0], -1, *tiles.shape[2:])
+        stacked = jnp.stack(ring_blocks(stacked, axis, count, 0)).reshape(-1, *tiles.shape)
         owner = (lax.axis_index(axis) + jnp.arange(count, dtype=jnp.int32)) % count
         slot_map = (owner[:, None] * (stride * local_slots) + slot_map[None, :]).reshape(-1)
         stride = stride * count
-    return tiles, slot_map
+    return stacked, slot_map
+
+
+def place_tiles(dest, tiles, rows):
+    positions, block_rows, local_slots, size, _ = tiles.shape
+    slots = positions * local_slots
+
+    def kernel(dest_ref, tiles_ref, out_ref):
+        out_ref[...] = jnp.zeros(out_ref.shape, out_ref.dtype)
+        for b in range(block_rows):
+            def place(p, carry):
+                target = dest_ref[b * slots + p]
+
+                @pl.when(target >= 0)
+                def _():
+                    start = pl.multiple_of(target * size, size)
+                    out_ref[pl.ds(start, size), b * size:(b + 1) * size] = tiles_ref[p // local_slots, b, p % local_slots]
+
+                return carry
+
+            lax.fori_loop(0, slots, place, 0)
+
+    return pl.pallas_call(
+        kernel,
+        out_shape=jax.ShapeDtypeStruct((rows * size, block_rows * size), tiles.dtype),
+        in_specs=[pl.BlockSpec(memory_space=pltpu.SMEM), pl.BlockSpec(memory_space=pltpu.VMEM)],
+        out_specs=pl.BlockSpec(memory_space=pltpu.VMEM),
+    )(dest.reshape(-1), tiles)
 
 
 def body(coeffs, block_tiles, neighbours, density):
@@ -71,23 +100,22 @@
     live_counts = jnp.sum(jnp.where(region_match, density[None, :], 0), axis=1)
     live_mask = jnp.arange(slot_count, dtype=jnp.int32)[None, :] < live_counts[:, None]
 
-    tiles, slot_map = gather_slots(block_tiles)
+    tiles, slot_map = gather_slots(jnp.swapaxes(block_tiles, 2, 3))
     ring_neighbours = neighbours[:, slot_map]
     ring_live = live_mask[:, slot_map]
-    rows = jnp.arange(total_blocks, dtype=jnp.int32)
     per_col = block_rows
-    row_y = rows // (z_count * per_col)
-    row_d = (rows // per_col) % z_count
-    row_block = (row_y * z_count + (row_d + lax.axis_index("z")) % z_count) * per_col + rows % per_col
-    pick = (ring_neighbours[:, :, None] == row_block[None, None, :]) & ring_live[:, :, None]
-    dense = jnp.einsum("bsn,bsij->njbi", pick.astype(tiles.dtype), tiles, preferred_element_type=tiles.dtype)
-    dense = dense.reshape(y_count, z_count, local_width, local_width)
+    owner = ring_neighbours // per_col
+    offset = (owner % z_count - lax.axis_index("z")) % z_count
+    target = (offset * y_count + owner // z_count) * per_col + ring_neighbours % per_col
+    dest = jnp.where(ring_live, target, -1)
+    dense = place_tiles(dest, tiles, total_blocks)
+    dense = dense.reshape(z_count, y_count, local_width, local_width)
 
     def apply_hamiltonian(field):
         blocks = gather_col(field, y_count, z_count)
         total = None
         for d, chunk in enumerate(blocks):
-            part = jnp.einsum("ymj,yjo->mo", chunk, dense[:, d], preferred_element_type=jnp.float32)
+            part = jnp.einsum("ymj,yjo->mo", chunk, dense[d], preferred_element_type=jnp.float32)
             total = part if total is None else total + part
         return total
 

time: 174 us -> 166 us (0.954)
  local copies, waits for them, and re-layouts: 21.8 us -> 8 us
  Pallas kernels: 0 us -> 7.08 us
  matrix products: 14.1 us -> 10.3 us
  starting transfers between devices: 62.4 us -> 65.6 us
    reshape x2 -> x1, local copies, waits for them, and re-layouts: 9.54 us -> 1.2 us  [gather_slots(): jnp.stack(ring_blocks(stacked, axis, count, 0)).reshape(-1, *tiles.shape)]
    transpose x3 -> x0, local copies, waits for them, and re-layouts: 7.09 us -> none  [the longest x1 6.35 us: body(): jnp.einsum('bsn,bsij->njbi', pick.astype(tiles.dtype), tiles, preferred_e...]
    pallas_call x0 -> x1, Pallas kernels: none -> 7.08 us  [place_tiles(): pl.pallas_call(kernel, out_shape=jax.ShapeDtypeStruct((rows * size, block...]
    dot_general x25 -> x24, matrix products: 14.1 us -> 10.3 us  [apply_hamiltonian(): jnp.einsum('ymj,yjo->mo', chunk, dense[d], preferred_element_type=jnp.flo...]
    ppermute x4, starting transfers between devices: 3.73 us -> 7.13 us  [ring_blocks(): lax.ppermute(lax.slice_in_dim(right, 0, split, axis=split_dim), axis, fwd)]
    another operation x2 -> x4, other arithmetic: 2.35 us -> 4.62 us  [gather_slots(): jnp.stack(ring_blocks(stacked, axis, count, 0)).reshape(-1, *tiles.shape)]
  transfers between devices with their start and end apart: 33 -> 33, of which waited for: 21 -> 25; matrix products, arithmetic and copies ran while one was open for 22% -> 12% of each run, Pallas kernels for 0% -> 4%
where the time goes in v3:
time: 166 us; the launch traced here: 164 us
  waiting for transfers between devices  66.7 us (40%)
  starting transfers between devices  65.6 us (40%)
  matrix products  10.3 us (6%)
  local copies, waits for them, and re-layouts  8 us (5%)
  Pallas kernels  7.08 us (4%)
  other arithmetic  6.24 us (4%)
    ppermute x10, starting transfers between devices, ring_blocks(): left = lax.ppermute(left, axis, bwd)  32 us
    ppermute x10, waiting for transfers between devices, ring_blocks(): left = lax.ppermute(left, axis, bwd)  26.5 us
    ppermute x5, waiting for transfers between devices, ring_blocks(): blocks[1] = lax.ppermute(piece, axis, fwd)  14.6 us
    ppermute x4, starting transfers between devices, ring_blocks(): lax.ppermute(lax.slice_in_dim(left, split, None, axis=split_dim), axis, bwd)  11.4 us
    ppermute x10, waiting for transfers between devices, ring_blocks(): right = lax.ppermute(right, axis, fwd)  10.6 us
    dot_general x24, matrix products, apply_hamiltonian(): jnp.einsum('ymj,yjo->mo', chunk, dense[d], preferred_element_type=jnp.flo...  10.3 us
    ppermute x4, waiting for transfers between devices, ring_blocks(): lax.ppermute(lax.slice_in_dim(right, 0, split, axis=split_dim), axis, fwd)  8.58 us
    ppermute x5, starting transfers between devices, ring_blocks(): blocks[1] = lax.ppermute(piece, axis, fwd)  7.92 us
  transfers between devices with their start and end apart: 33, of which 25 were waited for; matrix products, arithmetic and copies ran while one was open for 12% of the time, Pallas kernels for 4%

profile of v3, /device:TPU:2, one launch (start us, length us, event | category | flops | bytes accessed | tf_op | source)
XLA Modules:
  0.0 164.3 jit_solution(37719871066095777)
XLA Ops:
  0.9 3.2 %collective-permute-start.9 = (bf16[256,256]{1,0:T(8,128)(2,1)S(1)}, bf16[256,256]{1,0:T(8,128)(2,1)S(1)}, u32[]{:S(2)}, u32[]{:S(2)}) collective-permute-start(bf16[256,256]{1,0:T(8,128)(2,1)S(1)} %copy.31), channel_id=1, source_target_pairs={{0,8},{8,0},{1,9},{9,1},{2,10},{10,2},{3,11},{11,3},{4,12},{12,4},... | collective-permute-start | bytes 393224 | tf_op jit(solution)/shard_map/ppermute | solution.py:29
  7.8 5.9 %collective-permute-start.16 = (bf16[2,256,256]{2,1,0:T(8,128)(2,1)S(1)}, bf16[2,256,256]{2,1,0:T(8,128)(2,1)}, u32[]{:S(2)}, u32[]{:S(2)}) collective-permute-start(bf16[2,256,256]{2,1,0:T(8,128)(2,1)S(1)} %fusion.42), channel_id=1, source_target_pairs={{0,7},{1,0},{2,1},{3,2},{4,3},{5,4},{6,5},{7,6},{8,15},{9,8},{10,9... | collective-permute-start | bytes 786440 | tf_op jit(solution)/shard_map/ppermute | solution.py:24
  13.8 4.3 %collective-permute-done.11 = bf16[2,4,3,64,64]{3,4,2,1,0:T(8,128)(2,1)S(1)} collective-permute-done((bf16[2,4,3,64,64]{3,4,2,1,0:T(8,128)(2,1)S(1)}, bf16[2,4,3,64,64]{3,4,2,1,0:T(8,128)(2,1)S(1)}, u32[]{:S(2)}, u32[]{:S(2)}) %collective-permute-start.11) | collective-permute-done | bytes 196640 | tf_op jit(solution)/shard_map/ppermute | solution.py:29
  21.7 5.9 %collective-permute-start.17 = (bf16[2,256,256]{2,1,0:T(8,128)(2,1)}, bf16[2,256,256]{2,1,0:T(8,128)(2,1)}, u32[]{:S(2)}, u32[]{:S(2)}) collective-permute-start(bf16[2,256,256]{2,1,0:T(8,128)(2,1)} %collective-permute-done.16), channel_id=1, source_target_pairs={{0,7},{1,0},{2,1},{3,2},{4,3},{5,4},{6,5},{7,6},{8,15},{9,8},{10,9... | collective-permute-start | bytes 786440 | tf_op jit(solution)/shard_map/ppermute | solution.py:24
  29.3 9.1 %collective-permute-done.13 = bf16[4,4,3,64,64]{4,3,2,1,0:T(8,128)(2,1)S(1)} collective-permute-done((bf16[4,4,3,64,64]{4,3,2,1,0:T(8,128)(2,1)}, bf16[4,4,3,64,64]{4,3,2,1,0:T(8,128)(2,1)S(1)}, u32[]{:S(2)}, u32[]{:S(2)}) %collective-permute-start.13) | collective-permute-done | bytes 393248 | tf_op jit(solution)/shard_map/ppermute | solution.py:23
  42.3 2.0 %collective-permute-start.21 = (bf16[2,256,256]{2,1,0:T(8,128)(2,1)}, bf16[2,256,256]{2,1,0:T(8,128)(2,1)}, u32[]{:S(2)}, u32[]{:S(2)}) collective-permute-start(bf16[2,256,256]{2,1,0:T(8,128)(2,1)} %collective-permute-done.20), channel_id=1, source_target_pairs={{0,1},{1,2},{2,3},{3,4},{4,5},{5,6},{6,7},{7,0},{8,9},{9,10},{10,1... | collective-permute-start | bytes 786440 | tf_op jit(solution)/shard_map/ppermute | solution.py:23
  44.3 4.2 %collective-permute-start.18 = (bf16[2,256,256]{2,1,0:T(8,128)(2,1)}, bf16[2,256,256]{2,1,0:T(8,128)(2,1)}, u32[]{:S(2)}, u32[]{:S(2)}) collective-permute-start(bf16[2,256,256]{2,1,0:T(8,128)(2,1)} %collective-permute-done.17), channel_id=1, source_target_pairs={{0,7},{1,0},{2,1},{3,2},{4,3},{5,4},{6,5},{7,6},{8,15},{9,8},{10,9... | collective-permute-start | bytes 786440 | tf_op jit(solution)/shard_map/ppermute | solution.py:24
  51.7 2.1 %pad_maximum_fusion = bf16[4,4,4,3,64,64]{5,4,3,2,1,0:T(8,128)(2,1)} fusion(bf16[1,4,4,3,64,64]{5,4,3,2,1,0:T(8,128)(2,1)S(1)} %bitcast.206, bf16[1,4,4,3,64,64]{5,4,3,2,1,0:T(8,128)(2,1)S(1)} %maximum_bitcast_fusion, bf16[1,4,4,3,64,64]{5,4,3,2,1,0:T(8,128)(2,1)S(1)} %bitcast.207, bf16[1,4,4,3,64,64]{5,4,3,2,1,0:T(8,128)(2,1)S(1)} %copy.20), kind=kLoop, calls=%fused_computation.47 | loop fusion | flops 2359296 | bytes 3145728 | tf_op jit(solution)/shard_map/stack | solution.py:54
  53.7 7.1 %shard_map.46 = bf16[4096,256]{1,0:T(8,128)(2,1)S(1)} custom-call(s32[192]{0:T(256)} %fusion.53.dest_ref, bf16[16,4,3,64,64]{4,3,2,1,0:T(8,128)(2,1)} %bitcast.201), custom_call_target="tpu_custom_call" | custom-call | tf_op jit(solution)/shard_map/pallas_call | solution.py:80
  66.0 5.4 %collective-permute-start.22 = (bf16[1,256,256]{2,1,0:T(8,128)(2,1)S(1)}, bf16[1,256,256]{2,1,0:T(8,128)(2,1)S(1)}, u32[]{:S(2)}, u32[]{:S(2)}) collective-permute-start(bf16[1,256,256]{2,1,0:T(8,128)(2,1)S(1)} %slice.98), channel_id=1, source_target_pairs={{0,1},{1,2},{2,3},{3,4},{4,5},{5,6},{6,7},{7,0},{8,9},{9,10},{10,1... | collective-permute-start | bytes 393224 | tf_op jit(solution)/shard_map/ppermute | solution.py:32
  72.3 3.3 %collective-permute-start.23 = (bf16[1,256,256]{2,1,0:T(8,128)(2,1)S(1)}, bf16[1,256,256]{2,1,0:T(8,128)(2,1)S(1)}, u32[]{:S(2)}, u32[]{:S(2)}) collective-permute-start(bf16[1,256,256]{2,1,0:T(8,128)(2,1)S(1)} %slice.99), channel_id=1, source_target_pairs={{0,7},{1,0},{2,1},{3,2},{4,3},{5,4},{6,5},{7,6},{8,15},{9,8},{10,9... | collective-permute-start | bytes 393224 | tf_op jit(solution)/shard_map/ppermute | solution.py:33
  79.5 84.1 %while.12 = (s32[]{:T(128)}, bf16[256,256]{1,0:T(8,128)(2,1)S(1)}, bf16[256,256]{1,0:T(8,128)(2,1)S(1)}, bf16[8,2,256,256]{3,2,1,0:T(8,128)(2,1)S(1)}, s32[]{:T(...) while((s32[]{:T(128)}, bf16[256,256]{1,0:T(8,128)(2,1)S(1)}, ...), condition=%wide.region_2.4_spmd, body=%wide.region_1.3_spmd.sunk | while | flops 538116096 | bytes 17564300 | solution.py:131
  81.4 4.7 %collective-permute-done = bf16[256,256]{1,0:T(8,128)(2,1)S(1)} collective-permute-done((bf16[256,256]{1,0:T(8,128)(2,1)S(1)}, bf16[256,256]{1,0:T(8,128)(2,1)S(1)}, u32[]{:S(2)}, u32[]{:S(2)}) %collective-permute-start) | collective-permute-done | bytes 131104 | tf_op jit(solution)/shard_map/while/body/eval_jaxpr/ppermute | solution.py:29
  86.3 3.7 %collective-permute-start.4 = (bf16[2,256,256]{2,1,0:T(8,128)(2,1)S(1)}, bf16[2,256,256]{2,1,0:T(8,128)(2,1)S(1)}, u32[]{:S(2)}, u32[]{:S(2)}) collective-permute-start(bf16[2,256,256]{2,1,0:T(8,128)(2,1)S(1)} %fusion.122), channel_id=1, source_target_pairs={{0,7},{1,0},{2,1},{3,2},{4,3},{5,4},{6,5},{7,6},{8,15},{9,8},{10,9... | collective-permute-start | bytes 786440 | tf_op jit(solution)/shard_map/while/body/eval_jaxpr/ppermute | solution.py:24
  90.3 6.1 %collective-permute-done.4 = bf16[2,256,256]{2,1,0:T(8,128)(2,1)S(1)} collective-permute-done((bf16[2,256,256]{2,1,0:T(8,128)(2,1)S(1)}, bf16[2,256,256]{2,1,0:T(8,128)(2,1)S(1)}, u32[]{:S(2)}, u32[]{:S(2)}) %collective-permute-start.4) | collective-permute-done | bytes 262176 | tf_op jit(solution)/shard_map/while/body/eval_jaxpr/ppermute | solution.py:24
  96.3 3.7 %collective-permute-start.5 = (bf16[2,256,256]{2,1,0:T(8,128)(2,1)S(1)}, bf16[2,256,256]{2,1,0:T(8,128)(2,1)S(1)}, u32[]{:S(2)}, u32[]{:S(2)}) collective-permute-start(bf16[2,256,256]{2,1,0:T(8,128)(2,1)S(1)} %collective-permute-done.4), channel_id=1, source_target_pairs={{0,7},{1,0},{2,1},{3,2},{4,3},{5,4},{6,5},{7,6},{8,15},{9,8},{10,9... | collective-permute-start | bytes 786440 | tf_op jit(solution)/shard_map/while/body/eval_jaxpr/ppermute | solution.py:24
  100.8 5.2 %collective-permute-done.5 = bf16[2,256,256]{2,1,0:T(8,128)(2,1)S(1)} collective-permute-done((bf16[2,256,256]{2,1,0:T(8,128)(2,1)S(1)}, bf16[2,256,256]{2,1,0:T(8,128)(2,1)S(1)}, u32[]{:S(2)}, u32[]{:S(2)}) %collective-permute-start.5) | collective-permute-done | bytes 262176 | tf_op jit(solution)/shard_map/while/body/eval_jaxpr/ppermute | solution.py:24
  106.0 3.7 %collective-permute-start.6 = (bf16[2,256,256]{2,1,0:T(8,128)(2,1)S(1)}, bf16[2,256,256]{2,1,0:T(8,128)(2,1)S(1)}, u32[]{:S(2)}, u32[]{:S(2)}) collective-permute-start(bf16[2,256,256]{2,1,0:T(8,128)(2,1)S(1)} %collective-permute-done.5), channel_id=1, source_target_pairs={{0,7},{1,0},{2,1},{3,2},{4,3},{5,4},{6,5},{7,6},{8,15},{9,8},{10,9... | collective-permute-start | bytes 786440 | tf_op jit(solution)/shard_map/while/body/eval_jaxpr/ppermute | solution.py:24
  110.3 3.3 %collective-permute-done.6 = bf16[2,256,256]{2,1,0:T(8,128)(2,1)S(1)} collective-permute-done((bf16[2,256,256]{2,1,0:T(8,128)(2,1)S(1)}, bf16[2,256,256]{2,1,0:T(8,128)(2,1)S(1)}, u32[]{:S(2)}, u32[]{:S(2)}) %collective-permute-start.6) | collective-permute-done | bytes 262176 | tf_op jit(solution)/shard_map/while/body/eval_jaxpr/ppermute | solution.py:24
  113.6 3.8 %collective-permute-start.7 = (bf16[1,256,256]{2,1,0:T(8,128)(2,1)S(1)}, bf16[1,256,256]{2,1,0:T(8,128)(2,1)S(1)}, u32[]{:S(2)}, u32[]{:S(2)}) collective-permute-start(bf16[1,256,256]{2,1,0:T(8,128)(2,1)S(1)} %slice.162), channel_id=1, source_target_pairs={{0,7},{1,0},{2,1},{3,2},{4,3},{5,4},{6,5},{7,6},{8,15},{9,8},{10,9... | collective-permute-start | bytes 393224 | tf_op jit(solution)/shard_map/while/body/eval_jaxpr/ppermute | solution.py:33
  117.8 2.1 %collective-permute-done.7 = bf16[1,256,256]{2,1,0:T(8,128)(2,1)S(1)} collective-permute-done((bf16[1,256,256]{2,1,0:T(8,128)(2,1)S(1)}, bf16[1,256,256]{2,1,0:T(8,128)(2,1)S(1)}, u32[]{:S(2)}, u32[]{:S(2)}) %collective-permute-start.7) | collective-permute-done | bytes 131104 | tf_op jit(solution)/shard_map/while/body/eval_jaxpr/ppermute | solution.py:33
  119.9 3.8 %collective-permute-done.8 = bf16[1,256,256]{2,1,0:T(8,128)(2,1)S(1)} collective-permute-done((bf16[1,256,256]{2,1,0:T(8,128)(2,1)S(1)}, bf16[1,256,256]{2,1,0:T(8,128)(2,1)S(1)}, u32[]{:S(2)}, u32[]{:S(2)}) %collective-permute-start.8) | collective-permute-done | bytes 131104 | tf_op jit(solution)/shard_map/while/body/eval_jaxpr/ppermute | solution.py:32
  124.2 2.1 %collective-permute-start = (bf16[256,256]{1,0:T(8,128)(2,1)S(1)}, bf16[256,256]{1,0:T(8,128)(2,1)S(1)}, u32[]{:S(2)}, u32[]{:S(2)}) collective-permute-start(bf16[256,256]{1,0:T(8,128)(2,1)S(1)} %copy.26), channel_id=1, source_target_pairs={{0,8},{8,0},{1,9},{9,1},{2,10},{10,2},{3,11},{11,3},{4,12},{12,4},... | collective-permute-start | bytes 393224 | tf_op jit(solution)/shard_map/while/body/eval_jaxpr/ppermute | solution.py:29
  126.4 4.4 %collective-permute-done = bf16[256,256]{1,0:T(8,128)(2,1)S(1)} collective-permute-done((bf16[256,256]{1,0:T(8,128)(2,1)S(1)}, bf16[256,256]{1,0:T(8,128)(2,1)S(1)}, u32[]{:S(2)}, u32[]{:S(2)}) %collective-permute-start) | collective-permute-done | bytes 131104 | tf_op jit(solution)/shard_map/while/body/eval_jaxpr/ppermute | solution.py:29
  131.1 2.0 %collective-permute-start.1 = (bf16[2,256,256]{2,1,0:T(8,128)(2,1)S(1)}, bf16[2,256,256]{2,1,0:T(8,128)(2,1)S(1)}, u32[]{:S(2)}, u32[]{:S(2)}) collective-permute-start(bf16[2,256,256]{2,1,0:T(8,128)(2,1)S(1)} %fusion.122), channel_id=1, source_target_pairs={{0,1},{1,2},{2,3},{3,4},{4,5},{5,6},{6,7},{7,0},{8,9},{9,10},{10,1... | collective-permute-start | bytes 786440 | tf_op jit(solution)/shard_map/while/body/eval_jaxpr/ppermute | solution.py:23
  133.3 5.8 %collective-permute-done.4 = bf16[2,256,256]{2,1,0:T(8,128)(2,1)S(1)} collective-permute-done((bf16[2,256,256]{2,1,0:T(8,128)(2,1)S(1)}, bf16[2,256,256]{2,1,0:T(8,128)(2,1)S(1)}, u32[]{:S(2)}, u32[]{:S(2)}) %collective-permute-start.4) | collective-permute-done | bytes 262176 | tf_op jit(solution)/shard_map/while/body/eval_jaxpr/ppermute | solution.py:24
  142.4 3.1 %collective-permute-done.5 = bf16[2,256,256]{2,1,0:T(8,128)(2,1)S(1)} collective-permute-done((bf16[2,256,256]{2,1,0:T(8,128)(2,1)S(1)}, bf16[2,256,256]{2,1,0:T(8,128)(2,1)S(1)}, u32[]{:S(2)}, u32[]{:S(2)}) %collective-permute-start.5) | collective-permute-done | bytes 262176 | tf_op jit(solution)/shard_map/while/body/eval_jaxpr/ppermute | solution.py:24
  145.5 3.4 %collective-permute-start.6 = (bf16[2,256,256]{2,1,0:T(8,128)(2,1)S(1)}, bf16[2,256,256]{2,1,0:T(8,128)(2,1)S(1)}, u32[]{:S(2)}, u32[]{:S(2)}) collective-permute-start(bf16[2,256,256]{2,1,0:T(8,128)(2,1)S(1)} %collective-permute-done.5), channel_id=1, source_target_pairs={{0,7},{1,0},{2,1},{3,2},{4,3},{5,4},{6,5},{7,6},{8,15},{9,8},{10,9... | collective-permute-start | bytes 786440 | tf_op jit(solution)/shard_map/while/body/eval_jaxpr/ppermute | solution.py:24
  149.7 3.0 %collective-permute-done.6 = bf16[2,256,256]{2,1,0:T(8,128)(2,1)S(1)} collective-permute-done((bf16[2,256,256]{2,1,0:T(8,128)(2,1)S(1)}, bf16[2,256,256]{2,1,0:T(8,128)(2,1)S(1)}, u32[]{:S(2)}, u32[]{:S(2)}) %collective-permute-start.6) | collective-permute-done | bytes 262176 | tf_op jit(solution)/shard_map/while/body/eval_jaxpr/ppermute | solution.py:24
  152.8 3.8 %collective-permute-start.7 = (bf16[1,256,256]{2,1,0:T(8,128)(2,1)S(1)}, bf16[1,256,256]{2,1,0:T(8,128)(2,1)S(1)}, u32[]{:S(2)}, u32[]{:S(2)}) collective-permute-start(bf16[1,256,256]{2,1,0:T(8,128)(2,1)S(1)} %slice.162), channel_id=1, source_target_pairs={{0,7},{1,0},{2,1},{3,2},{4,3},{5,4},{6,5},{7,6},{8,15},{9,8},{10,9... | collective-permute-start | bytes 393224 | tf_op jit(solution)/shard_map/while/body/eval_jaxpr/ppermute | solution.py:33
  157.2 1.9 %collective-permute-done.7 = bf16[1,256,256]{2,1,0:T(8,128)(2,1)S(1)} collective-permute-done((bf16[1,256,256]{2,1,0:T(8,128)(2,1)S(1)}, bf16[1,256,256]{2,1,0:T(8,128)(2,1)S(1)}, u32[]{:S(2)}, u32[]{:S(2)}) %collective-permute-start.7) | collective-permute-done | bytes 131104 | tf_op jit(solution)/shard_map/while/body/eval_jaxpr/ppermute | solution.py:33
  159.1 4.0 %collective-permute-done.8 = bf16[1,256,256]{2,1,0:T(8,128)(2,1)S(1)} collective-permute-done((bf16[1,256,256]{2,1,0:T(8,128)(2,1)S(1)}, bf16[1,256,256]{2,1,0:T(8,128)(2,1)S(1)}, u32[]{:S(2)}, u32[]{:S(2)}) %collective-permute-start.8) | collective-permute-done | bytes 131104 | tf_op jit(solution)/shard_map/while/body/eval_jaxpr/ppermute | solution.py:32
  (121 shorter events, 37.6 us)
Async XLA Ops:
  0.9 6.7 %collective-permute-start.9 = (bf16[256,256]{1,0:T(8,128)(2,1)S(1)}, bf16[256,256]{1,0:T(8,128)(2,1)S(1)}, u32[]{:S(2)}, u32[]{:S(2)}) collective-permute-start(bf16[256,256]{1,0:T(8,128)(2,1)S(1)} %copy.31), channel_id=1, source_target_pairs={{0,8},{8,0},{1,9},{9,1},{2,10},{10,2},{3,11},{11,3},{4,12},{12,4},... | collective-permute-start | bytes 393224 | tf_op jit(solution)/shard_map/ppermute | solution.py:29
  6.8 11.2 %collective-permute-start.11 = (bf16[2,4,3,64,64]{3,4,2,1,0:T(8,128)(2,1)S(1)}, bf16[2,4,3,64,64]{3,4,2,1,0:T(8,128)(2,1)S(1)}, u32[]{:S(2)}, u32[]{:S(2)}) collective-permute-start(bf16[2,4,3,64,64]{3,4,2,1,0:T(8,128)(2,1)S(1)} %get-tuple-element.46), channel_id=1, source_target_pairs={{0,32},{32,0},{1,33},{33,1},{2,34},{34,2},{3,35},{35,3},{4,36},{36... | collective-permute-start | bytes 589832 | tf_op jit(solution)/shard_map/ppermute | solution.py:29
  7.8 13.8 %collective-permute-start.16 = (bf16[2,256,256]{2,1,0:T(8,128)(2,1)S(1)}, bf16[2,256,256]{2,1,0:T(8,128)(2,1)}, u32[]{:S(2)}, u32[]{:S(2)}) collective-permute-start(bf16[2,256,256]{2,1,0:T(8,128)(2,1)S(1)} %fusion.42), channel_id=1, source_target_pairs={{0,7},{1,0},{2,1},{3,2},{4,3},{5,4},{6,5},{7,6},{8,15},{9,8},{10,9... | collective-permute-start | bytes 786440 | tf_op jit(solution)/shard_map/ppermute | solution.py:24
  13.8 13.8 %collective-permute-start.19 = (bf16[2,256,256]{2,1,0:T(8,128)(2,1)S(1)}, bf16[2,256,256]{2,1,0:T(8,128)(2,1)S(1)}, u32[]{:S(2)}, u32[]{:S(2)}) collective-permute-start(bf16[2,256,256]{2,1,0:T(8,128)(2,1)S(1)} %fusion.42), channel_id=1, source_target_pairs={{0,1},{1,2},{2,3},{3,4},{4,5},{5,6},{6,7},{7,0},{8,9},{9,10},{10,1... | collective-permute-start | bytes 786440 | tf_op jit(solution)/shard_map/ppermute | solution.py:23
  19.4 18.9 %collective-permute-start.13 = (bf16[4,4,3,64,64]{4,3,2,1,0:T(8,128)(2,1)}, bf16[4,4,3,64,64]{4,3,2,1,0:T(8,128)(2,1)S(1)}, u32[]{:S(2)}, u32[]{:S(2)}) collective-permute-start(bf16[4,4,3,64,64]{4,3,2,1,0:T(8,128)(2,1)} %copy.18), channel_id=1, source_target_pairs={{0,64},{64,128},{128,192},{192,0},{1,65},{65,129},{129,193},{193,1... | collective-permute-start | bytes 1179656 | tf_op jit(solution)/shard_map/ppermute | solution.py:23
  20.9 19.1 %collective-permute-start.12 = (bf16[4,4,3,64,64]{4,3,2,1,0:T(8,128)(2,1)}, bf16[4,4,3,64,64]{4,3,2,1,0:T(8,128)(2,1)S(1)}, u32[]{:S(2)}, u32[]{:S(2)}) collective-permute-start(bf16[4,4,3,64,64]{4,3,2,1,0:T(8,128)(2,1)} %copy.18), channel_id=1, source_target_pairs={{0,192},{64,0},{128,64},{192,128},{1,193},{65,1},{129,65},{193,129... | collective-permute-start | bytes 1179656 | tf_op jit(solution)/shard_map/ppermute | solution.py:24
  21.7 22.7 %collective-permute-start.17 = (bf16[2,256,256]{2,1,0:T(8,128)(2,1)}, bf16[2,256,256]{2,1,0:T(8,128)(2,1)}, u32[]{:S(2)}, u32[]{:S(2)}) collective-permute-start(bf16[2,256,256]{2,1,0:T(8,128)(2,1)} %collective-permute-done.16), channel_id=1, source_target_pairs={{0,7},{1,0},{2,1},{3,2},{4,3},{5,4},{6,5},{7,6},{8,15},{9,8},{10,9... | collective-permute-start | bytes 786440 | tf_op jit(solution)/shard_map/ppermute | solution.py:24
  27.6 14.7 %collective-permute-start.20 = (bf16[2,256,256]{2,1,0:T(8,128)(2,1)S(1)}, bf16[2,256,256]{2,1,0:T(8,128)(2,1)}, u32[]{:S(2)}, u32[]{:S(2)}) collective-permute-start(bf16[2,256,256]{2,1,0:T(8,128)(2,1)S(1)} %collective-permute-done.19), channel_id=1, source_target_pairs={{0,1},{1,2},{2,3},{3,4},{4,5},{5,6},{6,7},{7,0},{8,9},{9,10},{10,1... | collective-permute-start | bytes 786440 | tf_op jit(solution)/shard_map/ppermute | solution.py:23
  38.4 10.2 %collective-permute-start.14 = (bf16[2,4,3,64,64]{4,3,2,1,0:T(8,128)(2,1)S(1)}, bf16[2,4,3,64,64]{4,3,2,1,0:T(8,128)(2,1)}, u32[]{:S(2)}, u32[]{:S(2)}) collective-permute-start(bf16[2,4,3,64,64]{4,3,2,1,0:T(8,128)(2,1)S(1)} %slice.92), channel_id=1, source_target_pairs={{0,64},{64,128},{128,192},{192,0},{1,65},{65,129},{129,193},{193,1... | collective-permute-start | bytes 589832 | tf_op jit(solution)/shard_map/ppermute | solution.py:32
  40.8 9.5 %collective-permute-start.15 = (bf16[2,4,3,64,64]{4,3,2,1,0:T(8,128)(2,1)}, bf16[2,4,3,64,64]{4,3,2,1,0:T(8,128)(2,1)}, u32[]{:S(2)}, u32[]{:S(2)}) collective-permute-start(bf16[2,4,3,64,64]{4,3,2,1,0:T(8,128)(2,1)} %slice.93), channel_id=1, source_target_pairs={{0,192},{64,0},{128,64},{192,128},{1,193},{65,1},{129,65},{193,129... | collective-permute-start | bytes 589832 | tf_op jit(solution)/shard_map/ppermute | solution.py:33
  42.3 22.8 %collective-permute-start.21 = (bf16[2,256,256]{2,1,0:T(8,128)(2,1)}, bf16[2,256,256]{2,1,0:T(8,128)(2,1)}, u32[]{:S(2)}, u32[]{:S(2)}) collective-permute-start(bf16[2,256,256]{2,1,0:T(8,128)(2,1)} %collective-permute-done.20), channel_id=1, source_target_pairs={{0,1},{1,2},{2,3},{3,4},{4,5},{5,6},{6,7},{7,0},{8,9},{9,10},{10,1... | collective-permute-start | bytes 786440 | tf_op jit(solution)/shard_map/ppermute | solution.py:23
  44.3 27.1 %collective-permute-start.18 = (bf16[2,256,256]{2,1,0:T(8,128)(2,1)}, bf16[2,256,256]{2,1,0:T(8,128)(2,1)}, u32[]{:S(2)}, u32[]{:S(2)}) collective-permute-start(bf16[2,256,256]{2,1,0:T(8,128)(2,1)} %collective-permute-done.17), channel_id=1, source_target_pairs={{0,7},{1,0},{2,1},{3,2},{4,3},{5,4},{6,5},{7,6},{8,15},{9,8},{10,9... | collective-permute-start | bytes 786440 | tf_op jit(solution)/shard_map/ppermute | solution.py:24
  66.0 11.5 %collective-permute-start.22 = (bf16[1,256,256]{2,1,0:T(8,128)(2,1)S(1)}, bf16[1,256,256]{2,1,0:T(8,128)(2,1)S(1)}, u32[]{:S(2)}, u32[]{:S(2)}) collective-permute-start(bf16[1,256,256]{2,1,0:T(8,128)(2,1)S(1)} %slice.98), channel_id=1, source_target_pairs={{0,1},{1,2},{2,3},{3,4},{4,5},{5,6},{6,7},{7,0},{8,9},{9,10},{10,1... | collective-permute-start | bytes 393224 | tf_op jit(solution)/shard_map/ppermute | solution.py:32
  72.3 5.8 %collective-permute-start.23 = (bf16[1,256,256]{2,1,0:T(8,128)(2,1)S(1)}, bf16[1,256,256]{2,1,0:T(8,128)(2,1)S(1)}, u32[]{:S(2)}, u32[]{:S(2)}) collective-permute-start(bf16[1,256,256]{2,1,0:T(8,128)(2,1)S(1)} %slice.99), channel_id=1, source_target_pairs={{0,7},{1,0},{2,1},{3,2},{4,3},{5,4},{6,5},{7,6},{8,15},{9,8},{10,9... | collective-permute-start | bytes 393224 | tf_op jit(solution)/shard_map/ppermute | solution.py:33
  79.6 6.6 %collective-permute-start = (bf16[256,256]{1,0:T(8,128)(2,1)S(1)}, bf16[256,256]{1,0:T(8,128)(2,1)S(1)}, u32[]{:S(2)}, u32[]{:S(2)}) collective-permute-start(bf16[256,256]{1,0:T(8,128)(2,1)S(1)} %copy.26), channel_id=1, source_target_pairs={{0,8},{8,0},{1,9},{9,1},{2,10},{10,2},{3,11},{11,3},{4,12},{12,4},... | collective-permute-start | bytes 393224 | tf_op jit(solution)/shard_map/while/body/eval_jaxpr/ppermute | solution.py:29
  86.3 10.0 %collective-permute-start.4 = (bf16[2,256,256]{2,1,0:T(8,128)(2,1)S(1)}, bf16[2,256,256]{2,1,0:T(8,128)(2,1)S(1)}, u32[]{:S(2)}, u32[]{:S(2)}) collective-permute-start(bf16[2,256,256]{2,1,0:T(8,128)(2,1)S(1)} %fusion.122), channel_id=1, source_target_pairs={{0,7},{1,0},{2,1},{3,2},{4,3},{5,4},{6,5},{7,6},{8,15},{9,8},{10,9... | collective-permute-start | bytes 786440 | tf_op jit(solution)/shard_map/while/body/eval_jaxpr/ppermute | solution.py:24
  90.1 10.2 %collective-permute-start.1 = (bf16[2,256,256]{2,1,0:T(8,128)(2,1)S(1)}, bf16[2,256,256]{2,1,0:T(8,128)(2,1)S(1)}, u32[]{:S(2)}, u32[]{:S(2)}) collective-permute-start(bf16[2,256,256]{2,1,0:T(8,128)(2,1)S(1)} %fusion.122), channel_id=1, source_target_pairs={{0,1},{1,2},{2,3},{3,4},{4,5},{5,6},{6,7},{7,0},{8,9},{9,10},{10,1... | collective-permute-start | bytes 786440 | tf_op jit(solution)/shard_map/while/body/eval_jaxpr/ppermute | solution.py:23
  96.3 9.7 %collective-permute-start.5 = (bf16[2,256,256]{2,1,0:T(8,128)(2,1)S(1)}, bf16[2,256,256]{2,1,0:T(8,128)(2,1)S(1)}, u32[]{:S(2)}, u32[]{:S(2)}) collective-permute-start(bf16[2,256,256]{2,1,0:T(8,128)(2,1)S(1)} %collective-permute-done.4), channel_id=1, source_target_pairs={{0,7},{1,0},{2,1},{3,2},{4,3},{5,4},{6,5},{7,6},{8,15},{9,8},{10,9... | collective-permute-start | bytes 786440 | tf_op jit(solution)/shard_map/while/body/eval_jaxpr/ppermute | solution.py:24
  100.3 9.5 %collective-permute-start.2 = (bf16[2,256,256]{2,1,0:T(8,128)(2,1)S(1)}, bf16[2,256,256]{2,1,0:T(8,128)(2,1)S(1)}, u32[]{:S(2)}, u32[]{:S(2)}) collective-permute-start(bf16[2,256,256]{2,1,0:T(8,128)(2,1)S(1)} %collective-permute-done.1), channel_id=1, source_target_pairs={{0,1},{1,2},{2,3},{3,4},{4,5},{5,6},{6,7},{7,0},{8,9},{9,10},{10,1... | collective-permute-start | bytes 786440 | tf_op jit(solution)/shard_map/while/body/eval_jaxpr/ppermute | solution.py:23
  106.0 7.6 %collective-permute-start.6 = (bf16[2,256,256]{2,1,0:T(8,128)(2,1)S(1)}, bf16[2,256,256]{2,1,0:T(8,128)(2,1)S(1)}, u32[]{:S(2)}, u32[]{:S(2)}) collective-permute-start(bf16[2,256,256]{2,1,0:T(8,128)(2,1)S(1)} %collective-permute-done.5), channel_id=1, source_target_pairs={{0,7},{1,0},{2,1},{3,2},{4,3},{5,4},{6,5},{7,6},{8,15},{9,8},{10,9... | collective-permute-start | bytes 786440 | tf_op jit(solution)/shard_map/while/body/eval_jaxpr/ppermute | solution.py:24
  109.8 7.6 %collective-permute-start.3 = (bf16[2,256,256]{2,1,0:T(8,128)(2,1)S(1)}, bf16[2,256,256]{2,1,0:T(8,128)(2,1)S(1)}, u32[]{:S(2)}, u32[]{:S(2)}) collective-permute-start(bf16[2,256,256]{2,1,0:T(8,128)(2,1)S(1)} %collective-permute-done.2), channel_id=1, source_target_pairs={{0,1},{1,2},{2,3},{3,4},{4,5},{5,6},{6,7},{7,0},{8,9},{9,10},{10,1... | collective-permute-start | bytes 786440 | tf_op jit(solution)/shard_map/while/body/eval_jaxpr/ppermute | solution.py:23
  113.6 6.3 %collective-permute-start.7 = (bf16[1,256,256]{2,1,0:T(8,128)(2,1)S(1)}, bf16[1,256,256]{2,1,0:T(8,128)(2,1)S(1)}, u32[]{:S(2)}, u32[]{:S(2)}) collective-permute-start(bf16[1,256,256]{2,1,0:T(8,128)(2,1)S(1)} %slice.162), channel_id=1, source_target_pairs={{0,7},{1,0},{2,1},{3,2},{4,3},{5,4},{6,5},{7,6},{8,15},{9,8},{10,9... | collective-permute-start | bytes 393224 | tf_op jit(solution)/shard_map/while/body/eval_jaxpr/ppermute | solution.py:33
  117.4 6.3 %collective-permute-start.8 = (bf16[1,256,256]{2,1,0:T(8,128)(2,1)S(1)}, bf16[1,256,256]{2,1,0:T(8,128)(2,1)S(1)}, u32[]{:S(2)}, u32[]{:S(2)}) collective-permute-start(bf16[1,256,256]{2,1,0:T(8,128)(2,1)S(1)} %slice.163), channel_id=1, source_target_pairs={{0,1},{1,2},{2,3},{3,4},{4,5},{5,6},{6,7},{7,0},{8,9},{9,10},{10,1... | collective-permute-start | bytes 393224 | tf_op jit(solution)/shard_map/while/body/eval_jaxpr/ppermute | solution.py:32
  124.2 6.6 %collective-permute-start = (bf16[256,256]{1,0:T(8,128)(2,1)S(1)}, bf16[256,256]{1,0:T(8,128)(2,1)S(1)}, u32[]{:S(2)}, u32[]{:S(2)}) collective-permute-start(bf16[256,256]{1,0:T(8,128)(2,1)S(1)} %copy.26), channel_id=1, source_target_pairs={{0,8},{8,0},{1,9},{9,1},{2,10},{10,2},{3,11},{11,3},{4,12},{12,4},... | collective-permute-start | bytes 393224 | tf_op jit(solution)/shard_map/while/body/eval_jaxpr/ppermute | solution.py:29
  131.0 8.1 %collective-permute-start.4 = (bf16[2,256,256]{2,1,0:T(8,128)(2,1)S(1)}, bf16[2,256,256]{2,1,0:T(8,128)(2,1)S(1)}, u32[]{:S(2)}, u32[]{:S(2)}) collective-permute-start(bf16[2,256,256]{2,1,0:T(8,128)(2,1)S(1)} %fusion.122), channel_id=1, source_target_pairs={{0,7},{1,0},{2,1},{3,2},{4,3},{5,4},{6,5},{7,6},{8,15},{9,8},{10,9... | collective-permute-start | bytes 786440 | tf_op jit(solution)/shard_map/while/body/eval_jaxpr/ppermute | solution.py:24
  131.1 9.2 %collective-permute-start.1 = (bf16[2,256,256]{2,1,0:T(8,128)(2,1)S(1)}, bf16[2,256,256]{2,1,0:T(8,128)(2,1)S(1)}, u32[]{:S(2)}, u32[]{:S(2)}) collective-permute-start(bf16[2,256,256]{2,1,0:T(8,128)(2,1)S(1)} %fusion.122), channel_id=1, source_target_pairs={{0,1},{1,2},{2,3},{3,4},{4,5},{5,6},{6,7},{7,0},{8,9},{9,10},{10,1... | collective-permute-start | bytes 786440 | tf_op jit(solution)/shard_map/while/body/eval_jaxpr/ppermute | solution.py:23
  139.1 6.4 %collective-permute-start.5 = (bf16[2,256,256]{2,1,0:T(8,128)(2,1)S(1)}, bf16[2,256,256]{2,1,0:T(8,128)(2,1)S(1)}, u32[]{:S(2)}, u32[]{:S(2)}) collective-permute-start(bf16[2,256,256]{2,1,0:T(8,128)(2,1)S(1)} %collective-permute-done.4), channel_id=1, source_target_pairs={{0,7},{1,0},{2,1},{3,2},{4,3},{5,4},{6,5},{7,6},{8,15},{9,8},{10,9... | collective-permute-start | bytes 786440 | tf_op jit(solution)/shard_map/while/body/eval_jaxpr/ppermute | solution.py:24
  140.3 9.0 %collective-permute-start.2 = (bf16[2,256,256]{2,1,0:T(8,128)(2,1)S(1)}, bf16[2,256,256]{2,1,0:T(8,128)(2,1)S(1)}, u32[]{:S(2)}, u32[]{:S(2)}) collective-permute-start(bf16[2,256,256]{2,1,0:T(8,128)(2,1)S(1)} %collective-permute-done.1), channel_id=1, source_target_pairs={{0,1},{1,2},{2,3},{3,4},{4,5},{5,6},{6,7},{7,0},{8,9},{9,10},{10,1... | collective-permute-start | bytes 786440 | tf_op jit(solution)/shard_map/while/body/eval_jaxpr/ppermute | solution.py:23
  145.5 7.3 %collective-permute-start.6 = (bf16[2,256,256]{2,1,0:T(8,128)(2,1)S(1)}, bf16[2,256,256]{2,1,0:T(8,128)(2,1)S(1)}, u32[]{:S(2)}, u32[]{:S(2)}) collective-permute-start(bf16[2,256,256]{2,1,0:T(8,128)(2,1)S(1)} %collective-permute-done.5), channel_id=1, source_target_pairs={{0,7},{1,0},{2,1},{3,2},{4,3},{5,4},{6,5},{7,6},{8,15},{9,8},{10,9... | collective-permute-start | bytes 786440 | tf_op jit(solution)/shard_map/while/body/eval_jaxpr/ppermute | solution.py:24
  149.3 7.6 %collective-permute-start.3 = (bf16[2,256,256]{2,1,0:T(8,128)(2,1)S(1)}, bf16[2,256,256]{2,1,0:T(8,128)(2,1)S(1)}, u32[]{:S(2)}, u32[]{:S(2)}) collective-permute-start(bf16[2,256,256]{2,1,0:T(8,128)(2,1)S(1)} %collective-permute-done.2), channel_id=1, source_target_pairs={{0,1},{1,2},{2,3},{3,4},{4,5},{5,6},{6,7},{7,0},{8,9},{9,10},{10,1... | collective-permute-start | bytes 786440 | tf_op jit(solution)/shard_map/while/body/eval_jaxpr/ppermute | solution.py:23
  152.8 6.3 %collective-permute-start.7 = (bf16[1,256,256]{2,1,0:T(8,128)(2,1)S(1)}, bf16[1,256,256]{2,1,0:T(8,128)(2,1)S(1)}, u32[]{:S(2)}, u32[]{:S(2)}) collective-permute-start(bf16[1,256,256]{2,1,0:T(8,128)(2,1)S(1)} %slice.162), channel_id=1, source_target_pairs={{0,7},{1,0},{2,1},{3,2},{4,3},{5,4},{6,5},{7,6},{8,15},{9,8},{10,9... | collective-permute-start | bytes 393224 | tf_op jit(solution)/shard_map/while/body/eval_jaxpr/ppermute | solution.py:33
  156.9 6.3 %collective-permute-start.8 = (bf16[1,256,256]{2,1,0:T(8,128)(2,1)S(1)}, bf16[1,256,256]{2,1,0:T(8,128)(2,1)S(1)}, u32[]{:S(2)}, u32[]{:S(2)}) collective-permute-start(bf16[1,256,256]{2,1,0:T(8,128)(2,1)S(1)} %slice.163), channel_id=1, source_target_pairs={{0,1},{1,2},{2,3},{3,4},{4,5},{5,6},{6,7},{7,0},{8,9},{9,10},{10,1... | collective-permute-start | bytes 393224 | tf_op jit(solution)/shard_map/while/body/eval_jaxpr/ppermute | solution.py:32
  (10 other events, 88.1 us)

commit v4 on v3

--- a/solution.py
+++ b/solution.py
@@ -112,12 +112,18 @@
     dense = dense.reshape(z_count, y_count, local_width, local_width)
 
     def apply_hamiltonian(field):
-        blocks = gather_col(field, y_count, z_count)
-        total = None
-        for d, chunk in enumerate(blocks):
-            part = jnp.einsum("ymj,yjo->mo", chunk, dense[d], preferred_element_type=jnp.float32)
-            total = part if total is None else total + part
-        return total
+        split = (field.shape[0] * 7 // 16) // 16 * 16
+        pairs_first = gather_col(field[:split], y_count, z_count)
+        ring_first = ring_blocks(field[split:], "z", z_count, 0)
+        pairs_later = [in_order(ring_blocks(block, "y_hi", y_count, 0), "y_hi") for block in ring_first]
+        total_first = None
+        total_later = None
+        for d in range(z_count):
+            part = jnp.einsum("ymj,yjo->mo", pairs_first[d], dense[d], preferred_element_type=jnp.float32)
+            total_first = part if total_first is None else total_first + part
+            part = jnp.einsum("ymj,yjo->mo", pairs_later[d], dense[d], preferred_element_type=jnp.float32)
+            total_later = part if total_later is None else total_later + part
+        return jnp.concatenate([total_first, total_later], axis=0)
 
     previous = coeffs
     current = apply_hamiltonian(coeffs).astype(jnp.bfloat16)

time: 166 us -> 243 us (1.46)
  starting transfers between devices: 65.6 us -> 131 us
  loops' own time: 0.24 us -> 13.9 us
  waiting for transfers between devices: 66.7 us -> 53.3 us
  Pallas kernels: 7.08 us -> 10.9 us
  matrix products: 10.3 us -> 14 us
    ppermute x5 -> x29, starting transfers between devices: 7.92 us -> 60.3 us  [ring_blocks(): blocks[1] = lax.ppermute(piece, axis, fwd)]
    ppermute x10 -> x19, starting transfers between devices: 32 us -> 47.3 us  [ring_blocks(): left = lax.ppermute(left, axis, bwd)]
    another operation x1, loops' own time: 0.24 us -> 13.9 us  [body(): lax.fori_loop(0, STEPS - 1, recurse, (previous, current))]
    ppermute x10 -> x19, waiting for transfers between devices: 26.5 us -> 14.8 us  [ring_blocks(): left = lax.ppermute(left, axis, bwd)]
    ppermute x10 -> x19, waiting for transfers between devices: 10.6 us -> 0.96 us  [ring_blocks(): right = lax.ppermute(right, axis, fwd)]
    ppermute x5 -> x29, waiting for transfers between devices: 14.6 us -> 22.4 us  [ring_blocks(): blocks[1] = lax.ppermute(piece, axis, fwd)]
    ppermute x4 -> x7, starting transfers between devices: 7.13 us -> 2.51 us  [ring_blocks(): lax.ppermute(lax.slice_in_dim(right, 0, split, axis=split_dim), axis, fwd)]
    pallas_call x1, Pallas kernels: 7.08 us -> 10.9 us  [place_tiles(): pl.pallas_call(kernel, out_shape=jax.ShapeDtypeStruct((rows * size, block...]
  transfers between devices with their start and end apart: 33 -> 81, of which waited for: 25 -> 25; matrix products, arithmetic and copies ran while one was open for 12% -> 10% of each run, Pallas kernels for 4% -> 5%
where the time goes in v4:
time: 243 us; the launch traced here: 239 us
  starting transfers between devices  131 us (54%)
  waiting for transfers between devices  53.3 us (22%)
  matrix products  14 us (6%)
  loops' own time  13.9 us (6%)
  Pallas kernels  10.9 us (4%)
  local copies, waits for them, and re-layouts  8.79 us (4%)
  other arithmetic  6.66 us (3%)
    ppermute x29, starting transfers between devices, ring_blocks(): blocks[1] = lax.ppermute(piece, axis, fwd)  60.3 us
    ppermute x19, starting transfers between devices, ring_blocks(): left = lax.ppermute(left, axis, bwd)  47.3 us
    ppermute x29, waiting for transfers between devices, ring_blocks(): blocks[1] = lax.ppermute(piece, axis, fwd)  22.4 us
    ppermute x19, waiting for transfers between devices, ring_blocks(): left = lax.ppermute(left, axis, bwd)  14.8 us
    ppermute x7, starting transfers between devices, ring_blocks(): lax.ppermute(lax.slice_in_dim(left, split, None, axis=split_dim), axis, bwd)  14.7 us
    another operation x1, loops' own time, body(): lax.fori_loop(0, STEPS - 1, recurse, (previous, current))  13.9 us
    ppermute x7, waiting for transfers between devices, ring_blocks(): lax.ppermute(lax.slice_in_dim(right, 0, split, axis=split_dim), axis, fwd)  11.7 us
    pallas_call x1, Pallas kernels, place_tiles(): pl.pallas_call(kernel, out_shape=jax.ShapeDtypeStruct((rows * size, block...  10.9 us
  transfers between devices with their start and end apart: 81, of which 25 were waited for; matrix products, arithmetic and copies ran while one was open for 10% of the time, Pallas kernels for 5%

profile of v4, /device:TPU:2, one launch (start us, length us, event | category | flops | bytes accessed | tf_op | source)
XLA Modules:
  0.0 239.3 jit_solution(14677153535844310600)
XLA Ops:
  2.9 4.0 %collective-permute-start.41 = (bf16[144,256]{1,0:T(8,128)(2,1)S(1)}, bf16[144,256]{1,0:T(8,128)(2,1)S(1)}, u32[]{:S(2)}, u32[]{:S(2)}) collective-permute-start(bf16[144,256]{1,0:T(8,128)(2,1)S(1)} %get-tuple-element.55), channel_id=1, source_target_pairs={{0,7},{1,0},{2,1},{3,2},{4,3},{5,4},{6,5},{7,6},{8,15},{9,8},{10,9... | collective-permute-start | bytes 221192 | tf_op jit(solution)/shard_map/ppermute | solution.py:24
  7.0 3.3 %collective-permute-start.25 = (bf16[112,256]{1,0:T(8,128)(2,1)S(1)}, bf16[112,256]{1,0:T(8,128)(2,1)S(1)}, u32[]{:S(2)}, u32[]{:S(2)}) collective-permute-start(bf16[112,256]{1,0:T(8,128)(2,1)S(1)} %get-tuple-element.52), channel_id=1, source_target_pairs={{0,8},{8,0},{1,9},{9,1},{2,10},{10,2},{3,11},{11,3},{4,12},{12,4},... | collective-permute-start | bytes 172040 | tf_op jit(solution)/shard_map/ppermute | solution.py:29
  13.7 3.3 %collective-permute-start.32 = (bf16[2,112,256]{2,1,0:T(8,128)(2,1)S(1)}, bf16[2,112,256]{2,1,0:T(8,128)(2,1)S(1)}, u32[]{:S(2)}, u32[]{:S(2)}) collective-permute-start(bf16[2,112,256]{2,1,0:T(8,128)(2,1)S(1)} %fusion.170), channel_id=1, source_target_pairs={{0,7},{1,0},{2,1},{3,2},{4,3},{5,4},{6,5},{7,6},{8,15},{9,8},{10,9... | collective-permute-start | bytes 344072 | tf_op jit(solution)/shard_map/ppermute | solution.py:24
  19.8 4.0 %collective-permute-done.27 = bf16[2,4,3,64,64]{3,4,2,1,0:T(8,128)(2,1)S(1)} collective-permute-done((bf16[2,4,3,64,64]{3,4,2,1,0:T(8,128)(2,1)S(1)}, bf16[2,4,3,64,64]{3,4,2,1,0:T(8,128)(2,1)S(1)}, u32[]{:S(2)}, u32[]{:S(2)}) %collective-permute-start.27) | collective-permute-done | bytes 196640 | tf_op jit(solution)/shard_map/ppermute | solution.py:29
  31.1 3.2 %collective-permute-start.33 = (bf16[2,112,256]{2,1,0:T(8,128)(2,1)S(1)}, bf16[2,112,256]{2,1,0:T(8,128)(2,1)S(1)}, u32[]{:S(2)}, u32[]{:S(2)}) collective-permute-start(bf16[2,112,256]{2,1,0:T(8,128)(2,1)S(1)} %collective-permute-done.32), channel_id=1, source_target_pairs={{0,7},{1,0},{2,1},{3,2},{4,3},{5,4},{6,5},{7,6},{8,15},{9,8},{10,9... | collective-permute-start | bytes 344072 | tf_op jit(solution)/shard_map/ppermute | solution.py:24
  35.2 10.2 %collective-permute-done.28 = bf16[4,4,3,64,64]{4,3,2,1,0:T(8,128)(2,1)S(1)} collective-permute-done((bf16[4,4,3,64,64]{4,3,2,1,0:T(8,128)(2,1)}, bf16[4,4,3,64,64]{4,3,2,1,0:T(8,128)(2,1)S(1)}, u32[]{:S(2)}, u32[]{:S(2)}) %collective-permute-start.28) | collective-permute-done | bytes 393248 | tf_op jit(solution)/shard_map/ppermute | solution.py:24
  47.6 3.2 %collective-permute-start.34 = (bf16[2,112,256]{2,1,0:T(8,128)(2,1)S(1)}, bf16[2,112,256]{2,1,0:T(8,128)(2,1)S(1)}, u32[]{:S(2)}, u32[]{:S(2)}) collective-permute-start(bf16[2,112,256]{2,1,0:T(8,128)(2,1)S(1)} %collective-permute-done.33), channel_id=1, source_target_pairs={{0,7},{1,0},{2,1},{3,2},{4,3},{5,4},{6,5},{7,6},{8,15},{9,8},{10,9... | collective-permute-start | bytes 344072 | tf_op jit(solution)/shard_map/ppermute | solution.py:24
  66.5 10.9 %shard_map.46 = bf16[4096,256]{1,0:T(8,128)(2,1)S(1)} custom-call(s32[192]{0:T(256)} %fusion.187.dest_ref, bf16[16,4,3,64,64]{4,3,2,1,0:T(8,128)(2,1)} %bitcast.378), custom_call_target="tpu_custom_call" | custom-call | tf_op jit(solution)/shard_map/pallas_call | solution.py:80
  79.5 3.6 %collective-permute-start.53 = (bf16[144,256]{1,0:T(8,128)(2,1)S(1)}, bf16[144,256]{1,0:T(8,128)(2,1)S(1)}, u32[]{:S(2)}, u32[]{:S(2)}) collective-permute-start(bf16[144,256]{1,0:T(8,128)(2,1)S(1)} %copy-done.13), channel_id=1, source_target_pairs={{0,8},{8,0},{1,9},{9,1},{2,10},{10,2},{3,11},{11,3},{4,12},{12,4},... | collective-permute-start | bytes 221192 | tf_op jit(solution)/shard_map/ppermute | solution.py:29
  86.5 3.4 %collective-permute-start.46 = (bf16[144,256]{1,0:T(8,128)(2,1)S(1)}, bf16[144,256]{1,0:T(8,128)(2,1)S(1)}, u32[]{:S(2)}, u32[]{:S(2)}) collective-permute-start(bf16[144,256]{1,0:T(8,128)(2,1)S(1)} %copy-done.15), channel_id=1, source_target_pairs={{0,8},{8,0},{1,9},{9,1},{2,10},{10,2},{3,11},{11,3},{4,12},{12,4},... | collective-permute-start | bytes 221192 | tf_op jit(solution)/shard_map/ppermute | solution.py:29
  98.6 139.8 %while.12 = (s32[]{:T(128)}, bf16[256,256]{1,0:T(8,128)(2,1)S(1)}, bf16[256,256]{1,0:T(8,128)(2,1)S(1)}, bf16[8,2,256,256]{3,2,1,0:T(8,128)(2,1)S(1)}, s32[]{:T(...) while((s32[]{:T(128)}, bf16[256,256]{1,0:T(8,128)(2,1)S(1)}, ...), condition=%wide.region_2.5_spmd, body=%wide.region_1.4_spmd.sunk | while | flops 539656192 | bytes 20284716 | solution.py:137
  111.9 3.4 %collective-permute-start.16 = (bf16[112,256]{1,0:T(8,128)(2,1)S(1)}, bf16[112,256]{1,0:T(8,128)(2,1)S(1)}, u32[]{:S(2)}, u32[]{:S(2)}) collective-permute-start(bf16[112,256]{1,0:T(8,128)(2,1)S(1)} %get-tuple-element.92), channel_id=1, source_target_pairs={{0,8},{8,0},{1,9},{9,1},{2,10},{10,2},{3,11},{11,3},{4,12},{12,4},... | collective-permute-start | bytes 172040 | tf_op jit(solution)/shard_map/while/body/eval_jaxpr/ppermute | solution.py:29
  115.4 3.2 %collective-permute-start.7 = (bf16[144,256]{1,0:T(8,128)(2,1)S(1)}, bf16[144,256]{1,0:T(8,128)(2,1)S(1)}, u32[]{:S(2)}, u32[]{:S(2)}) collective-permute-start(bf16[144,256]{1,0:T(8,128)(2,1)S(1)} %get-tuple-element.89), channel_id=1, source_target_pairs={{0,7},{1,0},{2,1},{3,2},{4,3},{5,4},{6,5},{7,6},{8,15},{9,8},{10,9... | collective-permute-start | bytes 221192 | tf_op jit(solution)/shard_map/while/body/eval_jaxpr/ppermute | solution.py:24
  119.0 3.2 %collective-permute-start.20 = (bf16[2,112,256]{2,1,0:T(8,128)(2,1)S(1)}, bf16[2,112,256]{2,1,0:T(8,128)(2,1)S(1)}, u32[]{:S(2)}, u32[]{:S(2)}) collective-permute-start(bf16[2,112,256]{2,1,0:T(8,128)(2,1)S(1)} %fusion.311), channel_id=1, source_target_pairs={{0,7},{1,0},{2,1},{3,2},{4,3},{5,4},{6,5},{7,6},{8,15},{9,8},{10,9... | collective-permute-start | bytes 344072 | tf_op jit(solution)/shard_map/while/body/eval_jaxpr/ppermute | solution.py:24
  122.2 3.3 %collective-permute-start.1 = (bf16[144,256]{1,0:T(8,128)(2,1)S(1)}, bf16[144,256]{1,0:T(8,128)(2,1)S(1)}, u32[]{:S(2)}, u32[]{:S(2)}) collective-permute-start(bf16[144,256]{1,0:T(8,128)(2,1)S(1)} %collective-permute-done), channel_id=1, source_target_pairs={{0,8},{8,0},{1,9},{9,1},{2,10},{10,2},{3,11},{11,3},{4,12},{12,4},... | collective-permute-start | bytes 221192 | tf_op jit(solution)/shard_map/while/body/eval_jaxpr/ppermute | solution.py:29
  128.1 4.0 %collective-permute-start.14 = (bf16[144,256]{1,0:T(8,128)(2,1)S(1)}, bf16[144,256]{1,0:T(8,128)(2,1)S(1)}, u32[]{:S(2)}, u32[]{:S(2)}) collective-permute-start(bf16[144,256]{1,0:T(8,128)(2,1)S(1)} %collective-permute-done.7), channel_id=1, source_target_pairs={{0,8},{8,0},{1,9},{9,1},{2,10},{10,2},{3,11},{11,3},{4,12},{12,4},... | collective-permute-start | bytes 221192 | tf_op jit(solution)/shard_map/while/body/eval_jaxpr/ppermute | solution.py:29
  135.3 3.1 %collective-permute-start.3 = (bf16[144,256]{1,0:T(8,128)(2,1)S(1)}, bf16[144,256]{1,0:T(8,128)(2,1)S(1)}, u32[]{:S(2)}, u32[]{:S(2)}) collective-permute-start(bf16[144,256]{1,0:T(8,128)(2,1)S(1)} %collective-permute-done.2), channel_id=1, source_target_pairs={{0,8},{8,0},{1,9},{9,1},{2,10},{10,2},{3,11},{11,3},{4,12},{12,4},... | collective-permute-start | bytes 221192 | tf_op jit(solution)/shard_map/while/body/eval_jaxpr/ppermute | solution.py:29
  142.8 3.2 %collective-permute-start.13 = (bf16[144,256]{1,0:T(8,128)(2,1)S(1)}, bf16[144,256]{1,0:T(8,128)(2,1)S(1)}, u32[]{:S(2)}, u32[]{:S(2)}) collective-permute-start(bf16[144,256]{1,0:T(8,128)(2,1)S(1)} %collective-permute-done.8), channel_id=1, source_target_pairs={{0,8},{8,0},{1,9},{9,1},{2,10},{10,2},{3,11},{11,3},{4,12},{12,4},... | collective-permute-start | bytes 221192 | tf_op jit(solution)/shard_map/while/body/eval_jaxpr/ppermute | solution.py:29
  146.6 3.3 %collective-permute-start.21 = (bf16[2,112,256]{2,1,0:T(8,128)(2,1)S(1)}, bf16[2,112,256]{2,1,0:T(8,128)(2,1)S(1)}, u32[]{:S(2)}, u32[]{:S(2)}) collective-permute-start(bf16[2,112,256]{2,1,0:T(8,128)(2,1)S(1)} %collective-permute-done.20), channel_id=1, source_target_pairs={{0,7},{1,0},{2,1},{3,2},{4,3},{5,4},{6,5},{7,6},{8,15},{9,8},{10,9... | collective-permute-start | bytes 344072 | tf_op jit(solution)/shard_map/while/body/eval_jaxpr/ppermute | solution.py:24
  149.9 3.2 %collective-permute-start.10 = (bf16[72,256]{1,0:T(8,128)(2,1)S(1)}, bf16[72,256]{1,0:T(8,128)(2,1)S(1)}, u32[]{:S(2)}, u32[]{:S(2)}) collective-permute-start(bf16[72,256]{1,0:T(8,128)(2,1)S(1)} %slice.273), channel_id=1, source_target_pairs={{0,7},{1,0},{2,1},{3,2},{4,3},{5,4},{6,5},{7,6},{8,15},{9,8},{10,9... | collective-permute-start | bytes 110600 | tf_op jit(solution)/shard_map/while/body/eval_jaxpr/ppermute | solution.py:33
  155.4 3.5 %collective-permute-start.12 = (bf16[144,256]{1,0:T(8,128)(2,1)S(1)}, bf16[144,256]{1,0:T(8,128)(2,1)S(1)}, u32[]{:S(2)}, u32[]{:S(2)}) collective-permute-start(bf16[144,256]{1,0:T(8,128)(2,1)S(1)} %collective-permute-done.9), channel_id=1, source_target_pairs={{0,8},{8,0},{1,9},{9,1},{2,10},{10,2},{3,11},{11,3},{4,12},{12,4},... | collective-permute-start | bytes 221192 | tf_op jit(solution)/shard_map/while/body/eval_jaxpr/ppermute | solution.py:29
  171.4 3.0 %collective-permute-done.24 = bf16[1,112,256]{2,1,0:T(8,128)(2,1)S(1)} collective-permute-done((bf16[1,112,256]{2,1,0:T(8,128)(2,1)S(1)}, bf16[1,112,256]{2,1,0:T(8,128)(2,1)S(1)}, u32[]{:S(2)}, u32[]{:S(2)}) %collective-permute-start.24) | collective-permute-done | bytes 57376 | tf_op jit(solution)/shard_map/while/body/eval_jaxpr/ppermute | solution.py:32
  174.9 4.3 %collective-permute-start.16 = (bf16[112,256]{1,0:T(8,128)(2,1)S(1)}, bf16[112,256]{1,0:T(8,128)(2,1)S(1)}, u32[]{:S(2)}, u32[]{:S(2)}) collective-permute-start(bf16[112,256]{1,0:T(8,128)(2,1)S(1)} %get-tuple-element.92), channel_id=1, source_target_pairs={{0,8},{8,0},{1,9},{9,1},{2,10},{10,2},{3,11},{11,3},{4,12},{12,4},... | collective-permute-start | bytes 172040 | tf_op jit(solution)/shard_map/while/body/eval_jaxpr/ppermute | solution.py:29
  179.3 3.2 %collective-permute-start.7 = (bf16[144,256]{1,0:T(8,128)(2,1)S(1)}, bf16[144,256]{1,0:T(8,128)(2,1)S(1)}, u32[]{:S(2)}, u32[]{:S(2)}) collective-permute-start(bf16[144,256]{1,0:T(8,128)(2,1)S(1)} %get-tuple-element.89), channel_id=1, source_target_pairs={{0,7},{1,0},{2,1},{3,2},{4,3},{5,4},{6,5},{7,6},{8,15},{9,8},{10,9... | collective-permute-start | bytes 221192 | tf_op jit(solution)/shard_map/while/body/eval_jaxpr/ppermute | solution.py:24
  182.7 3.2 %collective-permute-start.20 = (bf16[2,112,256]{2,1,0:T(8,128)(2,1)S(1)}, bf16[2,112,256]{2,1,0:T(8,128)(2,1)S(1)}, u32[]{:S(2)}, u32[]{:S(2)}) collective-permute-start(bf16[2,112,256]{2,1,0:T(8,128)(2,1)S(1)} %fusion.311), channel_id=1, source_target_pairs={{0,7},{1,0},{2,1},{3,2},{4,3},{5,4},{6,5},{7,6},{8,15},{9,8},{10,9... | collective-permute-start | bytes 344072 | tf_op jit(solution)/shard_map/while/body/eval_jaxpr/ppermute | solution.py:24
  186.0 3.5 %collective-permute-start.1 = (bf16[144,256]{1,0:T(8,128)(2,1)S(1)}, bf16[144,256]{1,0:T(8,128)(2,1)S(1)}, u32[]{:S(2)}, u32[]{:S(2)}) collective-permute-start(bf16[144,256]{1,0:T(8,128)(2,1)S(1)} %collective-permute-done), channel_id=1, source_target_pairs={{0,8},{8,0},{1,9},{9,1},{2,10},{10,2},{3,11},{11,3},{4,12},{12,4},... | collective-permute-start | bytes 221192 | tf_op jit(solution)/shard_map/while/body/eval_jaxpr/ppermute | solution.py:29
  191.8 3.5 %collective-permute-start.14 = (bf16[144,256]{1,0:T(8,128)(2,1)S(1)}, bf16[144,256]{1,0:T(8,128)(2,1)S(1)}, u32[]{:S(2)}, u32[]{:S(2)}) collective-permute-start(bf16[144,256]{1,0:T(8,128)(2,1)S(1)} %collective-permute-done.7), channel_id=1, source_target_pairs={{0,8},{8,0},{1,9},{9,1},{2,10},{10,2},{3,11},{11,3},{4,12},{12,4},... | collective-permute-start | bytes 221192 | tf_op jit(solution)/shard_map/while/body/eval_jaxpr/ppermute | solution.py:29
  195.6 2.8 %collective-permute-done.14 = bf16[144,256]{1,0:T(8,128)(2,1)S(1)} collective-permute-done((bf16[144,256]{1,0:T(8,128)(2,1)S(1)}, bf16[144,256]{1,0:T(8,128)(2,1)S(1)}, u32[]{:S(2)}, u32[]{:S(2)}) %collective-permute-start.14) | collective-permute-done | bytes 73760 | tf_op jit(solution)/shard_map/while/body/eval_jaxpr/ppermute | solution.py:29
  209.6 3.3 %collective-permute-start.21 = (bf16[2,112,256]{2,1,0:T(8,128)(2,1)S(1)}, bf16[2,112,256]{2,1,0:T(8,128)(2,1)S(1)}, u32[]{:S(2)}, u32[]{:S(2)}) collective-permute-start(bf16[2,112,256]{2,1,0:T(8,128)(2,1)S(1)} %collective-permute-done.20), channel_id=1, source_target_pairs={{0,7},{1,0},{2,1},{3,2},{4,3},{5,4},{6,5},{7,6},{8,15},{9,8},{10,9... | collective-permute-start | bytes 344072 | tf_op jit(solution)/shard_map/while/body/eval_jaxpr/ppermute | solution.py:24
  213.0 3.2 %collective-permute-start.10 = (bf16[72,256]{1,0:T(8,128)(2,1)S(1)}, bf16[72,256]{1,0:T(8,128)(2,1)S(1)}, u32[]{:S(2)}, u32[]{:S(2)}) collective-permute-start(bf16[72,256]{1,0:T(8,128)(2,1)S(1)} %slice.273), channel_id=1, source_target_pairs={{0,7},{1,0},{2,1},{3,2},{4,3},{5,4},{6,5},{7,6},{8,15},{9,8},{10,9... | collective-permute-start | bytes 110600 | tf_op jit(solution)/shard_map/while/body/eval_jaxpr/ppermute | solution.py:33
  228.8 3.6 %collective-permute-start.23 = (bf16[1,112,256]{2,1,0:T(8,128)(2,1)S(1)}, bf16[1,112,256]{2,1,0:T(8,128)(2,1)S(1)}, u32[]{:S(2)}, u32[]{:S(2)}) collective-permute-start(bf16[1,112,256]{2,1,0:T(8,128)(2,1)S(1)} %slice.274), channel_id=1, source_target_pairs={{0,7},{1,0},{2,1},{3,2},{4,3},{5,4},{6,5},{7,6},{8,15},{9,8},{10,9... | collective-permute-start | bytes 172040 | tf_op jit(solution)/shard_map/while/body/eval_jaxpr/ppermute | solution.py:33
  234.3 3.6 %collective-permute-done.24 = bf16[1,112,256]{2,1,0:T(8,128)(2,1)S(1)} collective-permute-done((bf16[1,112,256]{2,1,0:T(8,128)(2,1)S(1)}, bf16[1,112,256]{2,1,0:T(8,128)(2,1)S(1)}, u32[]{:S(2)}, u32[]{:S(2)}) %collective-permute-start.24) | collective-permute-done | bytes 57376 | tf_op jit(solution)/shard_map/while/body/eval_jaxpr/ppermute | solution.py:32
  (298 shorter events, 104.6 us)
Async XLA Ops:
  0.9 12.5 %collective-permute-start.47 = (bf16[144,256]{1,0:T(8,128)(2,1)S(1)}, bf16[144,256]{1,0:T(8,128)(2,1)S(1)}, u32[]{:S(2)}, u32[]{:S(2)}) collective-permute-start(bf16[144,256]{1,0:T(8,128)(2,1)S(1)} %get-tuple-element.55), channel_id=1, source_target_pairs={{0,1},{1,2},{2,3},{3,4},{4,5},{5,6},{6,7},{7,0},{8,9},{9,10},{10,1... | collective-permute-start | bytes 221192 | tf_op jit(solution)/shard_map/ppermute | solution.py:23
  2.9 14.0 %collective-permute-start.41 = (bf16[144,256]{1,0:T(8,128)(2,1)S(1)}, bf16[144,256]{1,0:T(8,128)(2,1)S(1)}, u32[]{:S(2)}, u32[]{:S(2)}) collective-permute-start(bf16[144,256]{1,0:T(8,128)(2,1)S(1)} %get-tuple-element.55), channel_id=1, source_target_pairs={{0,7},{1,0},{2,1},{3,2},{4,3},{5,4},{6,5},{7,6},{8,15},{9,8},{10,9... | collective-permute-start | bytes 221192 | tf_op jit(solution)/shard_map/ppermute | solution.py:24
  12.5 11.3 %collective-permute-start.27 = (bf16[2,4,3,64,64]{3,4,2,1,0:T(8,128)(2,1)S(1)}, bf16[2,4,3,64,64]{3,4,2,1,0:T(8,128)(2,1)S(1)}, u32[]{:S(2)}, u32[]{:S(2)}) collective-permute-start(bf16[2,4,3,64,64]{3,4,2,1,0:T(8,128)(2,1)S(1)} %get-tuple-element.51), channel_id=1, source_target_pairs={{0,32},{32,0},{1,33},{33,1},{2,34},{34,2},{3,35},{35,3},{4,36},{36... | collective-permute-start | bytes 589832 | tf_op jit(solution)/shard_map/ppermute | solution.py:29
  13.6 17.3 %collective-permute-start.35 = (bf16[2,112,256]{2,1,0:T(8,128)(2,1)S(1)}, bf16[2,112,256]{2,1,0:T(8,128)(2,1)S(1)}, u32[]{:S(2)}, u32[]{:S(2)}) collective-permute-start(bf16[2,112,256]{2,1,0:T(8,128)(2,1)S(1)} %fusion.170), channel_id=1, source_target_pairs={{0,1},{1,2},{2,3},{3,4},{4,5},{5,6},{6,7},{7,0},{8,9},{9,10},{10,1... | collective-permute-start | bytes 344072 | tf_op jit(solution)/shard_map/ppermute | solution.py:23
  13.7 17.4 %collective-permute-start.32 = (bf16[2,112,256]{2,1,0:T(8,128)(2,1)S(1)}, bf16[2,112,256]{2,1,0:T(8,128)(2,1)S(1)}, u32[]{:S(2)}, u32[]{:S(2)}) collective-permute-start(bf16[2,112,256]{2,1,0:T(8,128)(2,1)S(1)} %fusion.170), channel_id=1, source_target_pairs={{0,7},{1,0},{2,1},{3,2},{4,3},{5,4},{6,5},{7,6},{8,15},{9,8},{10,9... | collective-permute-start | bytes 344072 | tf_op jit(solution)/shard_map/ppermute | solution.py:24
  25.2 25.6 %collective-permute-start.29 = (bf16[4,4,3,64,64]{4,3,2,1,0:T(8,128)(2,1)}, bf16[4,4,3,64,64]{4,3,2,1,0:T(8,128)(2,1)S(1)}, u32[]{:S(2)}, u32[]{:S(2)}) collective-permute-start(bf16[4,4,3,64,64]{4,3,2,1,0:T(8,128)(2,1)} %copy.18), channel_id=1, source_target_pairs={{0,64},{64,128},{128,192},{192,0},{1,65},{65,129},{129,193},{193,1... | collective-permute-start | bytes 1179656 | tf_op jit(solution)/shard_map/ppermute | solution.py:23
  26.7 18.7 %collective-permute-start.28 = (bf16[4,4,3,64,64]{4,3,2,1,0:T(8,128)(2,1)}, bf16[4,4,3,64,64]{4,3,2,1,0:T(8,128)(2,1)S(1)}, u32[]{:S(2)}, u32[]{:S(2)}) collective-permute-start(bf16[4,4,3,64,64]{4,3,2,1,0:T(8,128)(2,1)} %copy.18), channel_id=1, source_target_pairs={{0,192},{64,0},{128,64},{192,128},{1,193},{65,1},{129,65},{193,129... | collective-permute-start | bytes 1179656 | tf_op jit(solution)/shard_map/ppermute | solution.py:24
  30.9 16.6 %collective-permute-start.36 = (bf16[2,112,256]{2,1,0:T(8,128)(2,1)S(1)}, bf16[2,112,256]{2,1,0:T(8,128)(2,1)}, u32[]{:S(2)}, u32[]{:S(2)}) collective-permute-start(bf16[2,112,256]{2,1,0:T(8,128)(2,1)S(1)} %collective-permute-done.35), channel_id=1, source_target_pairs={{0,1},{1,2},{2,3},{3,4},{4,5},{5,6},{6,7},{7,0},{8,9},{9,10},{10,1... | collective-permute-start | bytes 344072 | tf_op jit(solution)/shard_map/ppermute | solution.py:23
  31.1 16.5 %collective-permute-start.33 = (bf16[2,112,256]{2,1,0:T(8,128)(2,1)S(1)}, bf16[2,112,256]{2,1,0:T(8,128)(2,1)S(1)}, u32[]{:S(2)}, u32[]{:S(2)}) collective-permute-start(bf16[2,112,256]{2,1,0:T(8,128)(2,1)S(1)} %collective-permute-done.32), channel_id=1, source_target_pairs={{0,7},{1,0},{2,1},{3,2},{4,3},{5,4},{6,5},{7,6},{8,15},{9,8},{10,9... | collective-permute-start | bytes 344072 | tf_op jit(solution)/shard_map/ppermute | solution.py:24
  34.3 17.8 %collective-permute-start.50 = (bf16[72,256]{1,0:T(8,128)(2,1)S(1)}, bf16[72,256]{1,0:T(8,128)(2,1)S(1)}, u32[]{:S(2)}, u32[]{:S(2)}) collective-permute-start(bf16[72,256]{1,0:T(8,128)(2,1)S(1)} %slice.150), channel_id=1, source_target_pairs={{0,1},{1,2},{2,3},{3,4},{4,5},{5,6},{6,7},{7,0},{8,9},{9,10},{10,1... | collective-permute-start | bytes 110600 | tf_op jit(solution)/shard_map/ppermute | solution.py:32
  47.5 11.4 %collective-permute-start.37 = (bf16[2,112,256]{2,1,0:T(8,128)(2,1)}, bf16[2,112,256]{2,1,0:T(8,128)(2,1)S(1)}, u32[]{:S(2)}, u32[]{:S(2)}) collective-permute-start(bf16[2,112,256]{2,1,0:T(8,128)(2,1)} %collective-permute-done.36), channel_id=1, source_target_pairs={{0,1},{1,2},{2,3},{3,4},{4,5},{5,6},{6,7},{7,0},{8,9},{9,10},{10,1... | collective-permute-start | bytes 344072 | tf_op jit(solution)/shard_map/ppermute | solution.py:23
  52.1 10.9 %collective-permute-start.30 = (bf16[2,4,3,64,64]{4,3,2,1,0:T(8,128)(2,1)}, bf16[2,4,3,64,64]{4,3,2,1,0:T(8,128)(2,1)}, u32[]{:S(2)}, u32[]{:S(2)}) collective-permute-start(bf16[2,4,3,64,64]{4,3,2,1,0:T(8,128)(2,1)} %slice.138), channel_id=1, source_target_pairs={{0,64},{64,128},{128,192},{192,0},{1,65},{65,129},{129,193},{193,1... | collective-permute-start | bytes 589832 | tf_op jit(solution)/shard_map/ppermute | solution.py:32
  54.6 40.1 %collective-permute-start.40 = (bf16[144,256]{1,0:T(8,128)(2,1)}, bf16[144,256]{1,0:T(8,128)(2,1)S(1)}, u32[]{:S(2)}, u32[]{:S(2)}) collective-permute-start(bf16[144,256]{1,0:T(8,128)(2,1)} %copy-done.9), channel_id=1, source_target_pairs={{0,8},{8,0},{1,9},{9,1},{2,10},{10,2},{3,11},{11,3},{4,12},{12,4},... | collective-permute-start | bytes 221192 | tf_op jit(solution)/shard_map/ppermute | solution.py:29
  56.4 21.9 %collective-permute-start.55 = (bf16[144,256]{1,0:T(8,128)(2,1)}, bf16[144,256]{1,0:T(8,128)(2,1)}, u32[]{:S(2)}, u32[]{:S(2)}) collective-permute-start(bf16[144,256]{1,0:T(8,128)(2,1)} %copy-done.21), channel_id=1, source_target_pairs={{0,8},{8,0},{1,9},{9,1},{2,10},{10,2},{3,11},{11,3},{4,12},{12,4},... | collective-permute-start | bytes 221192 | tf_op jit(solution)/shard_map/ppermute | solution.py:29
  59.5 33.8 %collective-permute-start.42 = (bf16[144,256]{1,0:T(8,128)(2,1)}, bf16[144,256]{1,0:T(8,128)(2,1)}, u32[]{:S(2)}, u32[]{:S(2)}) collective-permute-start(bf16[144,256]{1,0:T(8,128)(2,1)} %copy-done.19), channel_id=1, source_target_pairs={{0,8},{8,0},{1,9},{9,1},{2,10},{10,2},{3,11},{11,3},{4,12},{12,4},... | collective-permute-start | bytes 221192 | tf_op jit(solution)/shard_map/ppermute | solution.py:29
  60.6 22.6 %collective-permute-start.54 = (bf16[144,256]{1,0:T(8,128)(2,1)}, bf16[144,256]{1,0:T(8,128)(2,1)}, u32[]{:S(2)}, u32[]{:S(2)}) collective-permute-start(bf16[144,256]{1,0:T(8,128)(2,1)} %copy-done.25), channel_id=1, source_target_pairs={{0,8},{8,0},{1,9},{9,1},{2,10},{10,2},{3,11},{11,3},{4,12},{12,4},... | collective-permute-start | bytes 221192 | tf_op jit(solution)/shard_map/ppermute | solution.py:29
  78.3 14.7 %collective-permute-start.44 = (bf16[144,256]{1,0:T(8,128)(2,1)S(1)}, bf16[144,256]{1,0:T(8,128)(2,1)S(1)}, u32[]{:S(2)}, u32[]{:S(2)}) collective-permute-start(bf16[144,256]{1,0:T(8,128)(2,1)S(1)} %copy-done.24), channel_id=1, source_target_pairs={{0,8},{8,0},{1,9},{9,1},{2,10},{10,2},{3,11},{11,3},{4,12},{12,4},... | collective-permute-start | bytes 221192 | tf_op jit(solution)/shard_map/ppermute | solution.py:29
  115.4 10.4 %collective-permute-start.7 = (bf16[144,256]{1,0:T(8,128)(2,1)S(1)}, bf16[144,256]{1,0:T(8,128)(2,1)S(1)}, u32[]{:S(2)}, u32[]{:S(2)}) collective-permute-start(bf16[144,256]{1,0:T(8,128)(2,1)S(1)} %get-tuple-element.89), channel_id=1, source_target_pairs={{0,7},{1,0},{2,1},{3,2},{4,3},{5,4},{6,5},{7,6},{8,15},{9,8},{10,9... | collective-permute-start | bytes 221192 | tf_op jit(solution)/shard_map/while/body/eval_jaxpr/ppermute | solution.py:24
  118.6 46.5 %collective-permute-start.15 = (bf16[144,256]{1,0:T(8,128)(2,1)S(1)}, bf16[144,256]{1,0:T(8,128)(2,1)S(1)}, u32[]{:S(2)}, u32[]{:S(2)}) collective-permute-start(bf16[144,256]{1,0:T(8,128)(2,1)S(1)} %get-tuple-element.89), channel_id=1, source_target_pairs={{0,8},{8,0},{1,9},{9,1},{2,10},{10,2},{3,11},{11,3},{4,12},{12,4},... | collective-permute-start | bytes 221192 | tf_op jit(solution)/shard_map/while/body/eval_jaxpr/ppermute | solution.py:29
  118.9 23.9 %collective-permute-start.17 = (bf16[2,112,256]{2,1,0:T(8,128)(2,1)S(1)}, bf16[2,112,256]{2,1,0:T(8,128)(2,1)S(1)}, u32[]{:S(2)}, u32[]{:S(2)}) collective-permute-start(bf16[2,112,256]{2,1,0:T(8,128)(2,1)S(1)} %fusion.311), channel_id=1, source_target_pairs={{0,1},{1,2},{2,3},{3,4},{4,5},{5,6},{6,7},{7,0},{8,9},{9,10},{10,1... | collective-permute-start | bytes 344072 | tf_op jit(solution)/shard_map/while/body/eval_jaxpr/ppermute | solution.py:23
  119.0 21.5 %collective-permute-start.20 = (bf16[2,112,256]{2,1,0:T(8,128)(2,1)S(1)}, bf16[2,112,256]{2,1,0:T(8,128)(2,1)S(1)}, u32[]{:S(2)}, u32[]{:S(2)}) collective-permute-start(bf16[2,112,256]{2,1,0:T(8,128)(2,1)S(1)} %fusion.311), channel_id=1, source_target_pairs={{0,7},{1,0},{2,1},{3,2},{4,3},{5,4},{6,5},{7,6},{8,15},{9,8},{10,9... | collective-permute-start | bytes 344072 | tf_op jit(solution)/shard_map/while/body/eval_jaxpr/ppermute | solution.py:24
  135.3 10.9 %collective-permute-start.3 = (bf16[144,256]{1,0:T(8,128)(2,1)S(1)}, bf16[144,256]{1,0:T(8,128)(2,1)S(1)}, u32[]{:S(2)}, u32[]{:S(2)}) collective-permute-start(bf16[144,256]{1,0:T(8,128)(2,1)S(1)} %collective-permute-done.2), channel_id=1, source_target_pairs={{0,8},{8,0},{1,9},{9,1},{2,10},{10,2},{3,11},{11,3},{4,12},{12,4},... | collective-permute-start | bytes 221192 | tf_op jit(solution)/shard_map/while/body/eval_jaxpr/ppermute | solution.py:29
  146.2 12.8 %collective-permute-start.18 = (bf16[2,112,256]{2,1,0:T(8,128)(2,1)S(1)}, bf16[2,112,256]{2,1,0:T(8,128)(2,1)S(1)}, u32[]{:S(2)}, u32[]{:S(2)}) collective-permute-start(bf16[2,112,256]{2,1,0:T(8,128)(2,1)S(1)} %collective-permute-done.17), channel_id=1, source_target_pairs={{0,1},{1,2},{2,3},{3,4},{4,5},{5,6},{6,7},{7,0},{8,9},{9,10},{10,1... | collective-permute-start | bytes 344072 | tf_op jit(solution)/shard_map/while/body/eval_jaxpr/ppermute | solution.py:23
  146.6 12.6 %collective-permute-start.21 = (bf16[2,112,256]{2,1,0:T(8,128)(2,1)S(1)}, bf16[2,112,256]{2,1,0:T(8,128)(2,1)S(1)}, u32[]{:S(2)}, u32[]{:S(2)}) collective-permute-start(bf16[2,112,256]{2,1,0:T(8,128)(2,1)S(1)} %collective-permute-done.20), channel_id=1, source_target_pairs={{0,7},{1,0},{2,1},{3,2},{4,3},{5,4},{6,5},{7,6},{8,15},{9,8},{10,9... | collective-permute-start | bytes 344072 | tf_op jit(solution)/shard_map/while/body/eval_jaxpr/ppermute | solution.py:24
  159.1 9.8 %collective-permute-start.19 = (bf16[2,112,256]{2,1,0:T(8,128)(2,1)S(1)}, bf16[2,112,256]{2,1,0:T(8,128)(2,1)S(1)}, u32[]{:S(2)}, u32[]{:S(2)}) collective-permute-start(bf16[2,112,256]{2,1,0:T(8,128)(2,1)S(1)} %collective-permute-done.18), channel_id=1, source_target_pairs={{0,1},{1,2},{2,3},{3,4},{4,5},{5,6},{6,7},{7,0},{8,9},{9,10},{10,1... | collective-permute-start | bytes 344072 | tf_op jit(solution)/shard_map/while/body/eval_jaxpr/ppermute | solution.py:23
  179.3 10.4 %collective-permute-start.7 = (bf16[144,256]{1,0:T(8,128)(2,1)S(1)}, bf16[144,256]{1,0:T(8,128)(2,1)S(1)}, u32[]{:S(2)}, u32[]{:S(2)}) collective-permute-start(bf16[144,256]{1,0:T(8,128)(2,1)S(1)} %get-tuple-element.89), channel_id=1, source_target_pairs={{0,7},{1,0},{2,1},{3,2},{4,3},{5,4},{6,5},{7,6},{8,15},{9,8},{10,9... | collective-permute-start | bytes 221192 | tf_op jit(solution)/shard_map/while/body/eval_jaxpr/ppermute | solution.py:24
  182.5 45.2 %collective-permute-start.15 = (bf16[144,256]{1,0:T(8,128)(2,1)S(1)}, bf16[144,256]{1,0:T(8,128)(2,1)S(1)}, u32[]{:S(2)}, u32[]{:S(2)}) collective-permute-start(bf16[144,256]{1,0:T(8,128)(2,1)S(1)} %get-tuple-element.89), channel_id=1, source_target_pairs={{0,8},{8,0},{1,9},{9,1},{2,10},{10,2},{3,11},{11,3},{4,12},{12,4},... | collective-permute-start | bytes 221192 | tf_op jit(solution)/shard_map/while/body/eval_jaxpr/ppermute | solution.py:29
  182.6 23.9 %collective-permute-start.17 = (bf16[2,112,256]{2,1,0:T(8,128)(2,1)S(1)}, bf16[2,112,256]{2,1,0:T(8,128)(2,1)S(1)}, u32[]{:S(2)}, u32[]{:S(2)}) collective-permute-start(bf16[2,112,256]{2,1,0:T(8,128)(2,1)S(1)} %fusion.311), channel_id=1, source_target_pairs={{0,1},{1,2},{2,3},{3,4},{4,5},{5,6},{6,7},{7,0},{8,9},{9,10},{10,1... | collective-permute-start | bytes 344072 | tf_op jit(solution)/shard_map/while/body/eval_jaxpr/ppermute | solution.py:23
  182.7 20.8 %collective-permute-start.20 = (bf16[2,112,256]{2,1,0:T(8,128)(2,1)S(1)}, bf16[2,112,256]{2,1,0:T(8,128)(2,1)S(1)}, u32[]{:S(2)}, u32[]{:S(2)}) collective-permute-start(bf16[2,112,256]{2,1,0:T(8,128)(2,1)S(1)} %fusion.311), channel_id=1, source_target_pairs={{0,7},{1,0},{2,1},{3,2},{4,3},{5,4},{6,5},{7,6},{8,15},{9,8},{10,9... | collective-permute-start | bytes 344072 | tf_op jit(solution)/shard_map/while/body/eval_jaxpr/ppermute | solution.py:24
  189.7 9.9 %collective-permute-start.2 = (bf16[144,256]{1,0:T(8,128)(2,1)S(1)}, bf16[144,256]{1,0:T(8,128)(2,1)S(1)}, u32[]{:S(2)}, u32[]{:S(2)}) collective-permute-start(bf16[144,256]{1,0:T(8,128)(2,1)S(1)} %collective-permute-done), channel_id=1, source_target_pairs={{0,1},{1,2},{2,3},{3,4},{4,5},{5,6},{6,7},{7,0},{8,9},{9,10},{10,1... | collective-permute-start | bytes 221192 | tf_op jit(solution)/shard_map/while/body/eval_jaxpr/ppermute | solution.py:23
  209.3 12.4 %collective-permute-start.18 = (bf16[2,112,256]{2,1,0:T(8,128)(2,1)S(1)}, bf16[2,112,256]{2,1,0:T(8,128)(2,1)S(1)}, u32[]{:S(2)}, u32[]{:S(2)}) collective-permute-start(bf16[2,112,256]{2,1,0:T(8,128)(2,1)S(1)} %collective-permute-done.17), channel_id=1, source_target_pairs={{0,1},{1,2},{2,3},{3,4},{4,5},{5,6},{6,7},{7,0},{8,9},{9,10},{10,1... | collective-permute-start | bytes 344072 | tf_op jit(solution)/shard_map/while/body/eval_jaxpr/ppermute | solution.py:23
  209.6 13.1 %collective-permute-start.21 = (bf16[2,112,256]{2,1,0:T(8,128)(2,1)S(1)}, bf16[2,112,256]{2,1,0:T(8,128)(2,1)S(1)}, u32[]{:S(2)}, u32[]{:S(2)}) collective-permute-start(bf16[2,112,256]{2,1,0:T(8,128)(2,1)S(1)} %collective-permute-done.20), channel_id=1, source_target_pairs={{0,7},{1,0},{2,1},{3,2},{4,3},{5,4},{6,5},{7,6},{8,15},{9,8},{10,9... | collective-permute-start | bytes 344072 | tf_op jit(solution)/shard_map/while/body/eval_jaxpr/ppermute | solution.py:24
  (76 other events, 566.3 us)

commit v5 on v3

--- a/solution.py
+++ b/solution.py
@@ -100,9 +100,9 @@
     live_counts = jnp.sum(jnp.where(region_match, density[None, :], 0), axis=1)
     live_mask = jnp.arange(slot_count, dtype=jnp.int32)[None, :] < live_counts[:, None]
 
-    tiles, slot_map = gather_slots(jnp.swapaxes(block_tiles, 2, 3))
-    ring_neighbours = neighbours[:, slot_map]
-    ring_live = live_mask[:, slot_map]
+    tiles = lax.all_gather(jnp.swapaxes(block_tiles, 2, 3), ROW_AXES, axis=1, tiled=True)[None]
+    ring_neighbours = neighbours
+    ring_live = live_mask
     per_col = block_rows
     owner = ring_neighbours // per_col
     offset = (owner % z_count - lax.axis_index("z")) % z_count

time: 166 us -> 153 us (0.922)
  between operations: 0.25 us -> 13.7 us
  starting transfers between devices: 65.6 us -> 52.5 us
  other arithmetic: 6.24 us -> 2.18 us
  matrix products: 10.3 us -> 6.49 us
  local copies, waits for them, and re-layouts: 8 us -> 4.72 us
  waiting for transfers between devices: 66.7 us -> 64.7 us
    ppermute x4 -> x3, starting transfers between devices: 7.13 us -> 0.25 us  [ring_blocks(): lax.ppermute(lax.slice_in_dim(right, 0, split, axis=split_dim), axis, fwd)]
    ppermute x10 -> x9, starting transfers between devices: 32 us -> 26.3 us  [ring_blocks(): left = lax.ppermute(left, axis, bwd)]
    another operation x4 -> x0, other arithmetic: 4.62 us -> none  [gather_slots(): jnp.stack(ring_blocks(stacked, axis, count, 0)).reshape(-1, *tiles.shape)]
    ppermute x5 -> x3, waiting for transfers between devices: 14.6 us -> 10.9 us  [ring_blocks(): blocks[1] = lax.ppermute(piece, axis, fwd)]
    dot_general x24, matrix products: 10.3 us -> 6.49 us  [apply_hamiltonian(): jnp.einsum('ymj,yjo->mo', chunk, dense[d], preferred_element_type=jnp.flo...]
    all_gather x0 -> x1, waiting for transfers between devices: none -> 3.3 us  [body(): lax.all_gather(jnp.swapaxes(block_tiles, 2, 3), ROW_AXES, axis=1, tiled=T...]
    ppermute x10 -> x9, starting transfers between devices: 7.15 us -> 4.03 us  [ring_blocks(): right = lax.ppermute(right, axis, fwd)]
    ppermute x5 -> x3, starting transfers between devices: 7.92 us -> 11 us  [ring_blocks(): blocks[1] = lax.ppermute(piece, axis, fwd)]
  transfers between devices with their start and end apart: 33 -> 28, of which waited for: 25 -> 17; matrix products, arithmetic and copies ran while one was open for 12% -> 4% of each run, Pallas kernels for 4% -> 5%
where the time goes in v5:
time: 153 us; the launch traced here: 152 us
  waiting for transfers between devices  64.7 us (42%)
  starting transfers between devices  52.5 us (34%)
  between operations  13.7 us (9%)
  Pallas kernels  7.34 us (5%)
  matrix products  6.49 us (4%)
  local copies, waits for them, and re-layouts  4.72 us (3%)
  other arithmetic  2.18 us (1%)
    ppermute x9, waiting for transfers between devices, ring_blocks(): left = lax.ppermute(left, axis, bwd)  26.6 us
    ppermute x9, starting transfers between devices, ring_blocks(): left = lax.ppermute(left, axis, bwd)  26.3 us
    ppermute x9, waiting for transfers between devices, ring_blocks(): right = lax.ppermute(right, axis, fwd)  12 us
    ppermute x3, starting transfers between devices, ring_blocks(): lax.ppermute(lax.slice_in_dim(left, split, None, axis=split_dim), axis, bwd)  11 us
    ppermute x3, starting transfers between devices, ring_blocks(): blocks[1] = lax.ppermute(piece, axis, fwd)  11 us
    ppermute x3, waiting for transfers between devices, ring_blocks(): blocks[1] = lax.ppermute(piece, axis, fwd)  10.9 us
    ppermute x3, waiting for transfers between devices, ring_blocks(): lax.ppermute(lax.slice_in_dim(right, 0, split, axis=split_dim), axis, fwd)  7.5 us
    pallas_call x1, Pallas kernels, place_tiles(): pl.pallas_call(kernel, out_shape=jax.ShapeDtypeStruct((rows * size, block...  7.34 us
  transfers between devices with their start and end apart: 28, of which 17 were waited for; matrix products, arithmetic and copies ran while one was open for 4% of the time, Pallas kernels for 5%

profile of v5, /device:TPU:2, one launch (start us, length us, event | category | flops | bytes accessed | tf_op | source)
XLA Modules:
  0.0 151.8 jit_solution(3410392804315594176)
XLA Ops:
  9.2 3.3 %collective-permute-start.9 = (bf16[256,256]{1,0:T(8,128)(2,1)S(1)}, bf16[256,256]{1,0:T(8,128)(2,1)S(1)}, u32[]{:S(2)}, u32[]{:S(2)}) collective-permute-start(bf16[256,256]{1,0:T(8,128)(2,1)S(1)} %copy.17), channel_id=1, source_target_pairs={{0,8},{8,0},{1,9},{9,1},{2,10},{10,2},{3,11},{11,3},{4,12},{12,4},... | collective-permute-start | bytes 393224 | tf_op jit(solution)/shard_map/ppermute | solution.py:29
  12.5 3.5 %collective-permute-done.9 = bf16[256,256]{1,0:T(8,128)(2,1)S(1)} collective-permute-done((bf16[256,256]{1,0:T(8,128)(2,1)S(1)}, bf16[256,256]{1,0:T(8,128)(2,1)S(1)}, u32[]{:S(2)}, u32[]{:S(2)}) %collective-permute-start.9) | collective-permute-done | bytes 131104 | tf_op jit(solution)/shard_map/ppermute | solution.py:29
  18.2 4.0 %collective-permute-start.10 = (bf16[2,256,256]{2,1,0:T(8,128)(2,1)S(1)}, bf16[2,256,256]{2,1,0:T(8,128)(2,1)S(1)}, u32[]{:S(2)}, u32[]{:S(2)}) collective-permute-start(bf16[2,256,256]{2,1,0:T(8,128)(2,1)S(1)} %fusion.42), channel_id=1, source_target_pairs={{0,7},{1,0},{2,1},{3,2},{4,3},{5,4},{6,5},{7,6},{8,15},{9,8},{10,9... | collective-permute-start | bytes 786440 | tf_op jit(solution)/shard_map/ppermute | solution.py:24
  22.2 5.4 %collective-permute-done.13 = bf16[2,256,256]{2,1,0:T(8,128)(2,1)S(1)} collective-permute-done((bf16[2,256,256]{2,1,0:T(8,128)(2,1)S(1)}, bf16[2,256,256]{2,1,0:T(8,128)(2,1)S(1)}, u32[]{:S(2)}, u32[]{:S(2)}) %collective-permute-start.13) | collective-permute-done | bytes 262176 | tf_op jit(solution)/shard_map/ppermute | solution.py:23
  27.6 3.2 %collective-permute-start.11 = (bf16[2,256,256]{2,1,0:T(8,128)(2,1)S(1)}, bf16[2,256,256]{2,1,0:T(8,128)(2,1)S(1)}, u32[]{:S(2)}, u32[]{:S(2)}) collective-permute-start(bf16[2,256,256]{2,1,0:T(8,128)(2,1)S(1)} %collective-permute-done.10), channel_id=1, source_target_pairs={{0,7},{1,0},{2,1},{3,2},{4,3},{5,4},{6,5},{7,6},{8,15},{9,8},{10,9... | collective-permute-start | bytes 786440 | tf_op jit(solution)/shard_map/ppermute | solution.py:24
  30.9 4.6 %collective-permute-done.14 = bf16[2,256,256]{2,1,0:T(8,128)(2,1)S(1)} collective-permute-done((bf16[2,256,256]{2,1,0:T(8,128)(2,1)S(1)}, bf16[2,256,256]{2,1,0:T(8,128)(2,1)S(1)}, u32[]{:S(2)}, u32[]{:S(2)}) %collective-permute-start.14) | collective-permute-done | bytes 262176 | tf_op jit(solution)/shard_map/ppermute | solution.py:23
  35.5 3.3 %collective-permute-start.12 = (bf16[2,256,256]{2,1,0:T(8,128)(2,1)S(1)}, bf16[2,256,256]{2,1,0:T(8,128)(2,1)S(1)}, u32[]{:S(2)}, u32[]{:S(2)}) collective-permute-start(bf16[2,256,256]{2,1,0:T(8,128)(2,1)S(1)} %collective-permute-done.11), channel_id=1, source_target_pairs={{0,7},{1,0},{2,1},{3,2},{4,3},{5,4},{6,5},{7,6},{8,15},{9,8},{10,9... | collective-permute-start | bytes 786440 | tf_op jit(solution)/shard_map/ppermute | solution.py:24
  43.2 3.5 %collective-permute-start.17 = (bf16[1,256,256]{2,1,0:T(8,128)(2,1)S(1)}, bf16[1,256,256]{2,1,0:T(8,128)(2,1)}, u32[]{:S(2)}, u32[]{:S(2)}) collective-permute-start(bf16[1,256,256]{2,1,0:T(8,128)(2,1)S(1)} %slice.85), channel_id=1, source_target_pairs={{0,7},{1,0},{2,1},{3,2},{4,3},{5,4},{6,5},{7,6},{8,15},{9,8},{10,9... | collective-permute-start | bytes 393224 | tf_op jit(solution)/shard_map/ppermute | solution.py:33
  46.6 3.3 %all-gather.2.cloned.1.call-done = bf16[4,48,64,64]{3,2,1,0:T(8,128)(2,1)} async-done(((bf16[4,3,64,64]{3,2,1,0:T(8,128)(2,1)}), bf16[4,48,64,64]{3,2,1,0:T(8,128)(2,1)}) %all-gather.2.cloned.1.call-update) | async-done | bytes 1572880 | tf_op jit(solution)/shard_map/all_gather | solution.py:103
  49.9 7.3 %shard_map.46 = bf16[4096,256]{1,0:T(8,128)(2,1)S(1)} custom-call(s32[192]{0:T(256)} %reshape.43.dest_ref, bf16[1,4,48,64,64]{4,3,2,1,0:T(8,128)(2,1)} %bitcast.183), custom_call_target="tpu_custom_call" | custom-call | tf_op jit(solution)/shard_map/pallas_call | solution.py:80
  60.9 83.4 %while.12 = (s32[]{:T(128)}, bf16[256,256]{1,0:T(8,128)(2,1)S(1)}, bf16[256,256]{1,0:T(8,128)(2,1)S(1)}, bf16[8,2,256,256]{3,2,1,0:T(8,128)(2,1)S(1)}, s32[]{:T(...) while((s32[]{:T(128)}, bf16[256,256]{1,0:T(8,128)(2,1)S(1)}, ...), condition=%wide.region_2.4_spmd, body=%wide.region_1.3_spmd.sunk | while | flops 538116096 | bytes 17564300 | solution.py:131
  61.0 4.5 %collective-permute-start = (bf16[256,256]{1,0:T(8,128)(2,1)S(1)}, bf16[256,256]{1,0:T(8,128)(2,1)S(1)}, u32[]{:S(2)}, u32[]{:S(2)}) collective-permute-start(bf16[256,256]{1,0:T(8,128)(2,1)S(1)} %copy.12), channel_id=1, source_target_pairs={{0,8},{8,0},{1,9},{9,1},{2,10},{10,2},{3,11},{11,3},{4,12},{12,4},... | collective-permute-start | bytes 393224 | tf_op jit(solution)/shard_map/while/body/eval_jaxpr/ppermute | solution.py:29
  65.5 3.9 %collective-permute-done = bf16[256,256]{1,0:T(8,128)(2,1)S(1)} collective-permute-done((bf16[256,256]{1,0:T(8,128)(2,1)S(1)}, bf16[256,256]{1,0:T(8,128)(2,1)S(1)}, u32[]{:S(2)}, u32[]{:S(2)}) %collective-permute-start) | collective-permute-done | bytes 131104 | tf_op jit(solution)/shard_map/while/body/eval_jaxpr/ppermute | solution.py:29
  69.6 2.9 %collective-permute-start.4 = (bf16[2,256,256]{2,1,0:T(8,128)(2,1)S(1)}, bf16[2,256,256]{2,1,0:T(8,128)(2,1)S(1)}, u32[]{:S(2)}, u32[]{:S(2)}) collective-permute-start(bf16[2,256,256]{2,1,0:T(8,128)(2,1)S(1)} %fusion.117), channel_id=1, source_target_pairs={{0,7},{1,0},{2,1},{3,2},{4,3},{5,4},{6,5},{7,6},{8,15},{9,8},{10,9... | collective-permute-start | bytes 786440 | tf_op jit(solution)/shard_map/while/body/eval_jaxpr/ppermute | solution.py:24
  72.8 5.6 %collective-permute-done.4 = bf16[2,256,256]{2,1,0:T(8,128)(2,1)S(1)} collective-permute-done((bf16[2,256,256]{2,1,0:T(8,128)(2,1)S(1)}, bf16[2,256,256]{2,1,0:T(8,128)(2,1)S(1)}, u32[]{:S(2)}, u32[]{:S(2)}) %collective-permute-start.4) | collective-permute-done | bytes 262176 | tf_op jit(solution)/shard_map/while/body/eval_jaxpr/ppermute | solution.py:24
  78.3 3.0 %collective-permute-start.5 = (bf16[2,256,256]{2,1,0:T(8,128)(2,1)S(1)}, bf16[2,256,256]{2,1,0:T(8,128)(2,1)S(1)}, u32[]{:S(2)}, u32[]{:S(2)}) collective-permute-start(bf16[2,256,256]{2,1,0:T(8,128)(2,1)S(1)} %collective-permute-done.4), channel_id=1, source_target_pairs={{0,7},{1,0},{2,1},{3,2},{4,3},{5,4},{6,5},{7,6},{8,15},{9,8},{10,9... | collective-permute-start | bytes 786440 | tf_op jit(solution)/shard_map/while/body/eval_jaxpr/ppermute | solution.py:24
  81.8 3.8 %collective-permute-done.5 = bf16[2,256,256]{2,1,0:T(8,128)(2,1)S(1)} collective-permute-done((bf16[2,256,256]{2,1,0:T(8,128)(2,1)S(1)}, bf16[2,256,256]{2,1,0:T(8,128)(2,1)S(1)}, u32[]{:S(2)}, u32[]{:S(2)}) %collective-permute-start.5) | collective-permute-done | bytes 262176 | tf_op jit(solution)/shard_map/while/body/eval_jaxpr/ppermute | solution.py:24
  85.6 3.6 %collective-permute-start.6 = (bf16[2,256,256]{2,1,0:T(8,128)(2,1)S(1)}, bf16[2,256,256]{2,1,0:T(8,128)(2,1)S(1)}, u32[]{:S(2)}, u32[]{:S(2)}) collective-permute-start(bf16[2,256,256]{2,1,0:T(8,128)(2,1)S(1)} %collective-permute-done.5), channel_id=1, source_target_pairs={{0,7},{1,0},{2,1},{3,2},{4,3},{5,4},{6,5},{7,6},{8,15},{9,8},{10,9... | collective-permute-start | bytes 786440 | tf_op jit(solution)/shard_map/while/body/eval_jaxpr/ppermute | solution.py:24
  89.7 3.4 %collective-permute-done.6 = bf16[2,256,256]{2,1,0:T(8,128)(2,1)S(1)} collective-permute-done((bf16[2,256,256]{2,1,0:T(8,128)(2,1)S(1)}, bf16[2,256,256]{2,1,0:T(8,128)(2,1)S(1)}, u32[]{:S(2)}, u32[]{:S(2)}) %collective-permute-start.6) | collective-permute-done | bytes 262176 | tf_op jit(solution)/shard_map/while/body/eval_jaxpr/ppermute | solution.py:24
  93.2 3.8 %collective-permute-start.7 = (bf16[1,256,256]{2,1,0:T(8,128)(2,1)S(1)}, bf16[1,256,256]{2,1,0:T(8,128)(2,1)S(1)}, u32[]{:S(2)}, u32[]{:S(2)}) collective-permute-start(bf16[1,256,256]{2,1,0:T(8,128)(2,1)S(1)} %slice.148), channel_id=1, source_target_pairs={{0,7},{1,0},{2,1},{3,2},{4,3},{5,4},{6,5},{7,6},{8,15},{9,8},{10,9... | collective-permute-start | bytes 393224 | tf_op jit(solution)/shard_map/while/body/eval_jaxpr/ppermute | solution.py:33
  97.3 2.2 %collective-permute-done.7 = bf16[1,256,256]{2,1,0:T(8,128)(2,1)S(1)} collective-permute-done((bf16[1,256,256]{2,1,0:T(8,128)(2,1)S(1)}, bf16[1,256,256]{2,1,0:T(8,128)(2,1)S(1)}, u32[]{:S(2)}, u32[]{:S(2)}) %collective-permute-start.7) | collective-permute-done | bytes 131104 | tf_op jit(solution)/shard_map/while/body/eval_jaxpr/ppermute | solution.py:33
  99.5 3.8 %collective-permute-done.8 = bf16[1,256,256]{2,1,0:T(8,128)(2,1)S(1)} collective-permute-done((bf16[1,256,256]{2,1,0:T(8,128)(2,1)S(1)}, bf16[1,256,256]{2,1,0:T(8,128)(2,1)S(1)}, u32[]{:S(2)}, u32[]{:S(2)}) %collective-permute-start.8) | collective-permute-done | bytes 131104 | tf_op jit(solution)/shard_map/while/body/eval_jaxpr/ppermute | solution.py:32
  103.7 3.1 %collective-permute-start = (bf16[256,256]{1,0:T(8,128)(2,1)S(1)}, bf16[256,256]{1,0:T(8,128)(2,1)S(1)}, u32[]{:S(2)}, u32[]{:S(2)}) collective-permute-start(bf16[256,256]{1,0:T(8,128)(2,1)S(1)} %copy.12), channel_id=1, source_target_pairs={{0,8},{8,0},{1,9},{9,1},{2,10},{10,2},{3,11},{11,3},{4,12},{12,4},... | collective-permute-start | bytes 393224 | tf_op jit(solution)/shard_map/while/body/eval_jaxpr/ppermute | solution.py:29
  106.9 3.4 %collective-permute-done = bf16[256,256]{1,0:T(8,128)(2,1)S(1)} collective-permute-done((bf16[256,256]{1,0:T(8,128)(2,1)S(1)}, bf16[256,256]{1,0:T(8,128)(2,1)S(1)}, u32[]{:S(2)}, u32[]{:S(2)}) %collective-permute-start) | collective-permute-done | bytes 131104 | tf_op jit(solution)/shard_map/while/body/eval_jaxpr/ppermute | solution.py:29
  112.8 5.4 %collective-permute-done.4 = bf16[2,256,256]{2,1,0:T(8,128)(2,1)S(1)} collective-permute-done((bf16[2,256,256]{2,1,0:T(8,128)(2,1)S(1)}, bf16[2,256,256]{2,1,0:T(8,128)(2,1)S(1)}, u32[]{:S(2)}, u32[]{:S(2)}) %collective-permute-start.4) | collective-permute-done | bytes 262176 | tf_op jit(solution)/shard_map/while/body/eval_jaxpr/ppermute | solution.py:24
  118.2 2.4 %collective-permute-start.5 = (bf16[2,256,256]{2,1,0:T(8,128)(2,1)S(1)}, bf16[2,256,256]{2,1,0:T(8,128)(2,1)S(1)}, u32[]{:S(2)}, u32[]{:S(2)}) collective-permute-start(bf16[2,256,256]{2,1,0:T(8,128)(2,1)S(1)} %collective-permute-done.4), channel_id=1, source_target_pairs={{0,7},{1,0},{2,1},{3,2},{4,3},{5,4},{6,5},{7,6},{8,15},{9,8},{10,9... | collective-permute-start | bytes 786440 | tf_op jit(solution)/shard_map/while/body/eval_jaxpr/ppermute | solution.py:24
  121.1 5.0 %collective-permute-done.5 = bf16[2,256,256]{2,1,0:T(8,128)(2,1)S(1)} collective-permute-done((bf16[2,256,256]{2,1,0:T(8,128)(2,1)S(1)}, bf16[2,256,256]{2,1,0:T(8,128)(2,1)S(1)}, u32[]{:S(2)}, u32[]{:S(2)}) %collective-permute-start.5) | collective-permute-done | bytes 262176 | tf_op jit(solution)/shard_map/while/body/eval_jaxpr/ppermute | solution.py:24
  126.2 3.7 %collective-permute-start.6 = (bf16[2,256,256]{2,1,0:T(8,128)(2,1)S(1)}, bf16[2,256,256]{2,1,0:T(8,128)(2,1)S(1)}, u32[]{:S(2)}, u32[]{:S(2)}) collective-permute-start(bf16[2,256,256]{2,1,0:T(8,128)(2,1)S(1)} %collective-permute-done.5), channel_id=1, source_target_pairs={{0,7},{1,0},{2,1},{3,2},{4,3},{5,4},{6,5},{7,6},{8,15},{9,8},{10,9... | collective-permute-start | bytes 786440 | tf_op jit(solution)/shard_map/while/body/eval_jaxpr/ppermute | solution.py:24
  130.3 3.4 %collective-permute-done.6 = bf16[2,256,256]{2,1,0:T(8,128)(2,1)S(1)} collective-permute-done((bf16[2,256,256]{2,1,0:T(8,128)(2,1)S(1)}, bf16[2,256,256]{2,1,0:T(8,128)(2,1)S(1)}, u32[]{:S(2)}, u32[]{:S(2)}) %collective-permute-start.6) | collective-permute-done | bytes 262176 | tf_op jit(solution)/shard_map/while/body/eval_jaxpr/ppermute | solution.py:24
  133.8 3.8 %collective-permute-start.7 = (bf16[1,256,256]{2,1,0:T(8,128)(2,1)S(1)}, bf16[1,256,256]{2,1,0:T(8,128)(2,1)S(1)}, u32[]{:S(2)}, u32[]{:S(2)}) collective-permute-start(bf16[1,256,256]{2,1,0:T(8,128)(2,1)S(1)} %slice.148), channel_id=1, source_target_pairs={{0,7},{1,0},{2,1},{3,2},{4,3},{5,4},{6,5},{7,6},{8,15},{9,8},{10,9... | collective-permute-start | bytes 393224 | tf_op jit(solution)/shard_map/while/body/eval_jaxpr/ppermute | solution.py:33
  137.9 2.2 %collective-permute-done.7 = bf16[1,256,256]{2,1,0:T(8,128)(2,1)S(1)} collective-permute-done((bf16[1,256,256]{2,1,0:T(8,128)(2,1)S(1)}, bf16[1,256,256]{2,1,0:T(8,128)(2,1)S(1)}, u32[]{:S(2)}, u32[]{:S(2)}) %collective-permute-start.7) | collective-permute-done | bytes 131104 | tf_op jit(solution)/shard_map/while/body/eval_jaxpr/ppermute | solution.py:33
  140.1 3.8 %collective-permute-done.8 = bf16[1,256,256]{2,1,0:T(8,128)(2,1)S(1)} collective-permute-done((bf16[1,256,256]{2,1,0:T(8,128)(2,1)S(1)}, bf16[1,256,256]{2,1,0:T(8,128)(2,1)S(1)}, u32[]{:S(2)}, u32[]{:S(2)}) %collective-permute-start.8) | collective-permute-done | bytes 131104 | tf_op jit(solution)/shard_map/while/body/eval_jaxpr/ppermute | solution.py:32
  (97 shorter events, 19.8 us)
Async XLA Ops:
  6.5 43.4 %all-gather.2.cloned.1.call-start = ((), (), s32[]{:S(2)}) async-start(), calls=%async_computation | async-start | bytes 3342336 | tf_op jit(solution)/shard_map/all_gather | solution.py:103
  9.2 6.8 %collective-permute-start.9 = (bf16[256,256]{1,0:T(8,128)(2,1)S(1)}, bf16[256,256]{1,0:T(8,128)(2,1)S(1)}, u32[]{:S(2)}, u32[]{:S(2)}) collective-permute-start(bf16[256,256]{1,0:T(8,128)(2,1)S(1)} %copy.17), channel_id=1, source_target_pairs={{0,8},{8,0},{1,9},{9,1},{2,10},{10,2},{3,11},{11,3},{4,12},{12,4},... | collective-permute-start | bytes 393224 | tf_op jit(solution)/shard_map/ppermute | solution.py:29
  16.2 11.4 %collective-permute-start.13 = (bf16[2,256,256]{2,1,0:T(8,128)(2,1)S(1)}, bf16[2,256,256]{2,1,0:T(8,128)(2,1)S(1)}, u32[]{:S(2)}, u32[]{:S(2)}) collective-permute-start(bf16[2,256,256]{2,1,0:T(8,128)(2,1)S(1)} %fusion.42), channel_id=1, source_target_pairs={{0,1},{1,2},{2,3},{3,4},{4,5},{5,6},{6,7},{7,0},{8,9},{9,10},{10,1... | collective-permute-start | bytes 786440 | tf_op jit(solution)/shard_map/ppermute | solution.py:23
  18.2 9.4 %collective-permute-start.10 = (bf16[2,256,256]{2,1,0:T(8,128)(2,1)S(1)}, bf16[2,256,256]{2,1,0:T(8,128)(2,1)S(1)}, u32[]{:S(2)}, u32[]{:S(2)}) collective-permute-start(bf16[2,256,256]{2,1,0:T(8,128)(2,1)S(1)} %fusion.42), channel_id=1, source_target_pairs={{0,7},{1,0},{2,1},{3,2},{4,3},{5,4},{6,5},{7,6},{8,15},{9,8},{10,9... | collective-permute-start | bytes 786440 | tf_op jit(solution)/shard_map/ppermute | solution.py:24
  27.6 7.8 %copy-start.5 = (bf16[2,256,256]{2,1,0:T(8,128)(2,1)}, bf16[2,256,256]{2,1,0:T(8,128)(2,1)S(1)}, u32[]{:S(2)}) copy-start(bf16[2,256,256]{2,1,0:T(8,128)(2,1)S(1)} %collective-permute-done.13) | copy-start | bytes 786436
  27.6 7.8 %collective-permute-start.14 = (bf16[2,256,256]{2,1,0:T(8,128)(2,1)S(1)}, bf16[2,256,256]{2,1,0:T(8,128)(2,1)S(1)}, u32[]{:S(2)}, u32[]{:S(2)}) collective-permute-start(bf16[2,256,256]{2,1,0:T(8,128)(2,1)S(1)} %collective-permute-done.13), channel_id=1, source_target_pairs={{0,1},{1,2},{2,3},{3,4},{4,5},{5,6},{6,7},{7,0},{8,9},{9,10},{10,1... | collective-permute-start | bytes 786440 | tf_op jit(solution)/shard_map/ppermute | solution.py:23
  27.6 22.3 %copy-start.9 = (bf16[2,256,256]{2,1,0:T(8,128)(2,1)}, bf16[2,256,256]{2,1,0:T(8,128)(2,1)S(1)}, u32[]{:S(2)}) copy-start(bf16[2,256,256]{2,1,0:T(8,128)(2,1)S(1)} %collective-permute-done.10) | copy-start | bytes 786436
  27.6 7.8 %collective-permute-start.11 = (bf16[2,256,256]{2,1,0:T(8,128)(2,1)S(1)}, bf16[2,256,256]{2,1,0:T(8,128)(2,1)S(1)}, u32[]{:S(2)}, u32[]{:S(2)}) collective-permute-start(bf16[2,256,256]{2,1,0:T(8,128)(2,1)S(1)} %collective-permute-done.10), channel_id=1, source_target_pairs={{0,7},{1,0},{2,1},{3,2},{4,3},{5,4},{6,5},{7,6},{8,15},{9,8},{10,9... | collective-permute-start | bytes 786440 | tf_op jit(solution)/shard_map/ppermute | solution.py:24
  35.4 14.5 %copy-start.7 = (bf16[2,256,256]{2,1,0:T(8,128)(2,1)}, bf16[2,256,256]{2,1,0:T(8,128)(2,1)S(1)}, u32[]{:S(2)}) copy-start(bf16[2,256,256]{2,1,0:T(8,128)(2,1)S(1)} %collective-permute-done.14) | copy-start | bytes 786436
  35.4 7.6 %collective-permute-start.15 = (bf16[2,256,256]{2,1,0:T(8,128)(2,1)S(1)}, bf16[2,256,256]{2,1,0:T(8,128)(2,1)S(1)}, u32[]{:S(2)}, u32[]{:S(2)}) collective-permute-start(bf16[2,256,256]{2,1,0:T(8,128)(2,1)S(1)} %collective-permute-done.14), channel_id=1, source_target_pairs={{0,1},{1,2},{2,3},{3,4},{4,5},{5,6},{6,7},{7,0},{8,9},{9,10},{10,1... | collective-permute-start | bytes 786440 | tf_op jit(solution)/shard_map/ppermute | solution.py:23
  35.4 14.5 %copy-start.11 = (bf16[2,256,256]{2,1,0:T(8,128)(2,1)}, bf16[2,256,256]{2,1,0:T(8,128)(2,1)S(1)}, u32[]{:S(2)}) copy-start(bf16[2,256,256]{2,1,0:T(8,128)(2,1)S(1)} %collective-permute-done.11) | copy-start | bytes 786436
  35.5 7.7 %collective-permute-start.12 = (bf16[2,256,256]{2,1,0:T(8,128)(2,1)S(1)}, bf16[2,256,256]{2,1,0:T(8,128)(2,1)S(1)}, u32[]{:S(2)}, u32[]{:S(2)}) collective-permute-start(bf16[2,256,256]{2,1,0:T(8,128)(2,1)S(1)} %collective-permute-done.11), channel_id=1, source_target_pairs={{0,7},{1,0},{2,1},{3,2},{4,3},{5,4},{6,5},{7,6},{8,15},{9,8},{10,9... | collective-permute-start | bytes 786440 | tf_op jit(solution)/shard_map/ppermute | solution.py:24
  43.0 16.4 %collective-permute-start.16 = (bf16[1,256,256]{2,1,0:T(8,128)(2,1)S(1)}, bf16[1,256,256]{2,1,0:T(8,128)(2,1)}, u32[]{:S(2)}, u32[]{:S(2)}) collective-permute-start(bf16[1,256,256]{2,1,0:T(8,128)(2,1)S(1)} %slice.84), channel_id=1, source_target_pairs={{0,1},{1,2},{2,3},{3,4},{4,5},{5,6},{6,7},{7,0},{8,9},{9,10},{10,1... | collective-permute-start | bytes 393224 | tf_op jit(solution)/shard_map/ppermute | solution.py:32
  43.2 16.3 %collective-permute-start.17 = (bf16[1,256,256]{2,1,0:T(8,128)(2,1)S(1)}, bf16[1,256,256]{2,1,0:T(8,128)(2,1)}, u32[]{:S(2)}, u32[]{:S(2)}) collective-permute-start(bf16[1,256,256]{2,1,0:T(8,128)(2,1)S(1)} %slice.85), channel_id=1, source_target_pairs={{0,7},{1,0},{2,1},{3,2},{4,3},{5,4},{6,5},{7,6},{8,15},{9,8},{10,9... | collective-permute-start | bytes 393224 | tf_op jit(solution)/shard_map/ppermute | solution.py:33
  61.0 8.4 %collective-permute-start = (bf16[256,256]{1,0:T(8,128)(2,1)S(1)}, bf16[256,256]{1,0:T(8,128)(2,1)S(1)}, u32[]{:S(2)}, u32[]{:S(2)}) collective-permute-start(bf16[256,256]{1,0:T(8,128)(2,1)S(1)} %copy.12), channel_id=1, source_target_pairs={{0,8},{8,0},{1,9},{9,1},{2,10},{10,2},{3,11},{11,3},{4,12},{12,4},... | collective-permute-start | bytes 393224 | tf_op jit(solution)/shard_map/while/body/eval_jaxpr/ppermute | solution.py:29
  69.6 8.7 %collective-permute-start.4 = (bf16[2,256,256]{2,1,0:T(8,128)(2,1)S(1)}, bf16[2,256,256]{2,1,0:T(8,128)(2,1)S(1)}, u32[]{:S(2)}, u32[]{:S(2)}) collective-permute-start(bf16[2,256,256]{2,1,0:T(8,128)(2,1)S(1)} %fusion.117), channel_id=1, source_target_pairs={{0,7},{1,0},{2,1},{3,2},{4,3},{5,4},{6,5},{7,6},{8,15},{9,8},{10,9... | collective-permute-start | bytes 786440 | tf_op jit(solution)/shard_map/while/body/eval_jaxpr/ppermute | solution.py:24
  72.5 8.8 %collective-permute-start.1 = (bf16[2,256,256]{2,1,0:T(8,128)(2,1)S(1)}, bf16[2,256,256]{2,1,0:T(8,128)(2,1)S(1)}, u32[]{:S(2)}, u32[]{:S(2)}) collective-permute-start(bf16[2,256,256]{2,1,0:T(8,128)(2,1)S(1)} %fusion.117), channel_id=1, source_target_pairs={{0,1},{1,2},{2,3},{3,4},{4,5},{5,6},{6,7},{7,0},{8,9},{9,10},{10,1... | collective-permute-start | bytes 786440 | tf_op jit(solution)/shard_map/while/body/eval_jaxpr/ppermute | solution.py:23
  78.3 7.3 %collective-permute-start.5 = (bf16[2,256,256]{2,1,0:T(8,128)(2,1)S(1)}, bf16[2,256,256]{2,1,0:T(8,128)(2,1)S(1)}, u32[]{:S(2)}, u32[]{:S(2)}) collective-permute-start(bf16[2,256,256]{2,1,0:T(8,128)(2,1)S(1)} %collective-permute-done.4), channel_id=1, source_target_pairs={{0,7},{1,0},{2,1},{3,2},{4,3},{5,4},{6,5},{7,6},{8,15},{9,8},{10,9... | collective-permute-start | bytes 786440 | tf_op jit(solution)/shard_map/while/body/eval_jaxpr/ppermute | solution.py:24
  81.3 7.9 %collective-permute-start.2 = (bf16[2,256,256]{2,1,0:T(8,128)(2,1)S(1)}, bf16[2,256,256]{2,1,0:T(8,128)(2,1)S(1)}, u32[]{:S(2)}, u32[]{:S(2)}) collective-permute-start(bf16[2,256,256]{2,1,0:T(8,128)(2,1)S(1)} %collective-permute-done.1), channel_id=1, source_target_pairs={{0,1},{1,2},{2,3},{3,4},{4,5},{5,6},{6,7},{7,0},{8,9},{9,10},{10,1... | collective-permute-start | bytes 786440 | tf_op jit(solution)/shard_map/while/body/eval_jaxpr/ppermute | solution.py:23
  85.6 7.5 %collective-permute-start.6 = (bf16[2,256,256]{2,1,0:T(8,128)(2,1)S(1)}, bf16[2,256,256]{2,1,0:T(8,128)(2,1)S(1)}, u32[]{:S(2)}, u32[]{:S(2)}) collective-permute-start(bf16[2,256,256]{2,1,0:T(8,128)(2,1)S(1)} %collective-permute-done.5), channel_id=1, source_target_pairs={{0,7},{1,0},{2,1},{3,2},{4,3},{5,4},{6,5},{7,6},{8,15},{9,8},{10,9... | collective-permute-start | bytes 786440 | tf_op jit(solution)/shard_map/while/body/eval_jaxpr/ppermute | solution.py:24
  89.3 7.7 %collective-permute-start.3 = (bf16[2,256,256]{2,1,0:T(8,128)(2,1)S(1)}, bf16[2,256,256]{2,1,0:T(8,128)(2,1)S(1)}, u32[]{:S(2)}, u32[]{:S(2)}) collective-permute-start(bf16[2,256,256]{2,1,0:T(8,128)(2,1)S(1)} %collective-permute-done.2), channel_id=1, source_target_pairs={{0,1},{1,2},{2,3},{3,4},{4,5},{5,6},{6,7},{7,0},{8,9},{9,10},{10,1... | collective-permute-start | bytes 786440 | tf_op jit(solution)/shard_map/while/body/eval_jaxpr/ppermute | solution.py:23
  93.2 6.3 %collective-permute-start.7 = (bf16[1,256,256]{2,1,0:T(8,128)(2,1)S(1)}, bf16[1,256,256]{2,1,0:T(8,128)(2,1)S(1)}, u32[]{:S(2)}, u32[]{:S(2)}) collective-permute-start(bf16[1,256,256]{2,1,0:T(8,128)(2,1)S(1)} %slice.148), channel_id=1, source_target_pairs={{0,7},{1,0},{2,1},{3,2},{4,3},{5,4},{6,5},{7,6},{8,15},{9,8},{10,9... | collective-permute-start | bytes 393224 | tf_op jit(solution)/shard_map/while/body/eval_jaxpr/ppermute | solution.py:33
  96.9 6.3 %collective-permute-start.8 = (bf16[1,256,256]{2,1,0:T(8,128)(2,1)S(1)}, bf16[1,256,256]{2,1,0:T(8,128)(2,1)S(1)}, u32[]{:S(2)}, u32[]{:S(2)}) collective-permute-start(bf16[1,256,256]{2,1,0:T(8,128)(2,1)S(1)} %slice.149), channel_id=1, source_target_pairs={{0,1},{1,2},{2,3},{3,4},{4,5},{5,6},{6,7},{7,0},{8,9},{9,10},{10,1... | collective-permute-start | bytes 393224 | tf_op jit(solution)/shard_map/while/body/eval_jaxpr/ppermute | solution.py:32
  103.7 6.6 %collective-permute-start = (bf16[256,256]{1,0:T(8,128)(2,1)S(1)}, bf16[256,256]{1,0:T(8,128)(2,1)S(1)}, u32[]{:S(2)}, u32[]{:S(2)}) collective-permute-start(bf16[256,256]{1,0:T(8,128)(2,1)S(1)} %copy.12), channel_id=1, source_target_pairs={{0,8},{8,0},{1,9},{9,1},{2,10},{10,2},{3,11},{11,3},{4,12},{12,4},... | collective-permute-start | bytes 393224 | tf_op jit(solution)/shard_map/while/body/eval_jaxpr/ppermute | solution.py:29
  110.5 7.7 %collective-permute-start.4 = (bf16[2,256,256]{2,1,0:T(8,128)(2,1)S(1)}, bf16[2,256,256]{2,1,0:T(8,128)(2,1)S(1)}, u32[]{:S(2)}, u32[]{:S(2)}) collective-permute-start(bf16[2,256,256]{2,1,0:T(8,128)(2,1)S(1)} %fusion.117), channel_id=1, source_target_pairs={{0,7},{1,0},{2,1},{3,2},{4,3},{5,4},{6,5},{7,6},{8,15},{9,8},{10,9... | collective-permute-start | bytes 786440 | tf_op jit(solution)/shard_map/while/body/eval_jaxpr/ppermute | solution.py:24
  110.6 10.1 %collective-permute-start.1 = (bf16[2,256,256]{2,1,0:T(8,128)(2,1)S(1)}, bf16[2,256,256]{2,1,0:T(8,128)(2,1)S(1)}, u32[]{:S(2)}, u32[]{:S(2)}) collective-permute-start(bf16[2,256,256]{2,1,0:T(8,128)(2,1)S(1)} %fusion.117), channel_id=1, source_target_pairs={{0,1},{1,2},{2,3},{3,4},{4,5},{5,6},{6,7},{7,0},{8,9},{9,10},{10,1... | collective-permute-start | bytes 786440 | tf_op jit(solution)/shard_map/while/body/eval_jaxpr/ppermute | solution.py:23
  118.2 7.9 %collective-permute-start.5 = (bf16[2,256,256]{2,1,0:T(8,128)(2,1)S(1)}, bf16[2,256,256]{2,1,0:T(8,128)(2,1)S(1)}, u32[]{:S(2)}, u32[]{:S(2)}) collective-permute-start(bf16[2,256,256]{2,1,0:T(8,128)(2,1)S(1)} %collective-permute-done.4), channel_id=1, source_target_pairs={{0,7},{1,0},{2,1},{3,2},{4,3},{5,4},{6,5},{7,6},{8,15},{9,8},{10,9... | collective-permute-start | bytes 786440 | tf_op jit(solution)/shard_map/while/body/eval_jaxpr/ppermute | solution.py:24
  120.7 9.2 %collective-permute-start.2 = (bf16[2,256,256]{2,1,0:T(8,128)(2,1)S(1)}, bf16[2,256,256]{2,1,0:T(8,128)(2,1)S(1)}, u32[]{:S(2)}, u32[]{:S(2)}) collective-permute-start(bf16[2,256,256]{2,1,0:T(8,128)(2,1)S(1)} %collective-permute-done.1), channel_id=1, source_target_pairs={{0,1},{1,2},{2,3},{3,4},{4,5},{5,6},{6,7},{7,0},{8,9},{9,10},{10,1... | collective-permute-start | bytes 786440 | tf_op jit(solution)/shard_map/while/body/eval_jaxpr/ppermute | solution.py:23
  126.2 7.6 %collective-permute-start.6 = (bf16[2,256,256]{2,1,0:T(8,128)(2,1)S(1)}, bf16[2,256,256]{2,1,0:T(8,128)(2,1)S(1)}, u32[]{:S(2)}, u32[]{:S(2)}) collective-permute-start(bf16[2,256,256]{2,1,0:T(8,128)(2,1)S(1)} %collective-permute-done.5), channel_id=1, source_target_pairs={{0,7},{1,0},{2,1},{3,2},{4,3},{5,4},{6,5},{7,6},{8,15},{9,8},{10,9... | collective-permute-start | bytes 786440 | tf_op jit(solution)/shard_map/while/body/eval_jaxpr/ppermute | solution.py:24
  129.9 7.7 %collective-permute-start.3 = (bf16[2,256,256]{2,1,0:T(8,128)(2,1)S(1)}, bf16[2,256,256]{2,1,0:T(8,128)(2,1)S(1)}, u32[]{:S(2)}, u32[]{:S(2)}) collective-permute-start(bf16[2,256,256]{2,1,0:T(8,128)(2,1)S(1)} %collective-permute-done.2), channel_id=1, source_target_pairs={{0,1},{1,2},{2,3},{3,4},{4,5},{5,6},{6,7},{7,0},{8,9},{9,10},{10,1... | collective-permute-start | bytes 786440 | tf_op jit(solution)/shard_map/while/body/eval_jaxpr/ppermute | solution.py:23
  133.8 6.3 %collective-permute-start.7 = (bf16[1,256,256]{2,1,0:T(8,128)(2,1)S(1)}, bf16[1,256,256]{2,1,0:T(8,128)(2,1)S(1)}, u32[]{:S(2)}, u32[]{:S(2)}) collective-permute-start(bf16[1,256,256]{2,1,0:T(8,128)(2,1)S(1)} %slice.148), channel_id=1, source_target_pairs={{0,7},{1,0},{2,1},{3,2},{4,3},{5,4},{6,5},{7,6},{8,15},{9,8},{10,9... | collective-permute-start | bytes 393224 | tf_op jit(solution)/shard_map/while/body/eval_jaxpr/ppermute | solution.py:33
  137.5 6.3 %collective-permute-start.8 = (bf16[1,256,256]{2,1,0:T(8,128)(2,1)S(1)}, bf16[1,256,256]{2,1,0:T(8,128)(2,1)S(1)}, u32[]{:S(2)}, u32[]{:S(2)}) collective-permute-start(bf16[1,256,256]{2,1,0:T(8,128)(2,1)S(1)} %slice.149), channel_id=1, source_target_pairs={{0,1},{1,2},{2,3},{3,4},{4,5},{5,6},{6,7},{7,0},{8,9},{9,10},{10,1... | collective-permute-start | bytes 393224 | tf_op jit(solution)/shard_map/while/body/eval_jaxpr/ppermute | solution.py:32
  (9 other events, 23.2 us)
Sparse Core Ops, SparseCore 0:
  9.3 40.5 all-gather.1

commit v6 on v5

--- a/solution.py
+++ b/solution.py
@@ -75,7 +75,7 @@
 
                 return carry
 
-            lax.fori_loop(0, slots, place, 0)
+            lax.fori_loop(0, slots, place, 0, unroll=True)
 
     return pl.pallas_call(
         kernel,

time: 153 us -> 153 us (level)
  waiting for transfers between devices: 64.7 us -> 68 us
  starting transfers between devices: 52.5 us -> 49.7 us
    ppermute x3, starting transfers between devices: 11 us -> 6.93 us  [ring_blocks(): blocks[1] = lax.ppermute(piece, axis, fwd)]
    ppermute x3, waiting for transfers between devices: 10.9 us -> 13.7 us  [ring_blocks(): blocks[1] = lax.ppermute(piece, axis, fwd)]
where the time goes in v6:
time: 153 us; the launch traced here: 152 us
  waiting for transfers between devices  68 us (44%)
  starting transfers between devices  49.7 us (32%)
  between operations  13.7 us (9%)
  Pallas kernels  7.21 us (5%)
  matrix products  6.48 us (4%)
  local copies, waits for them, and re-layouts  4.72 us (3%)
  other arithmetic  2.18 us (1%)
    ppermute x9, starting transfers between devices, ring_blocks(): left = lax.ppermute(left, axis, bwd)  27.7 us
    ppermute x9, waiting for transfers between devices, ring_blocks(): left = lax.ppermute(left, axis, bwd)  27 us
    ppermute x3, waiting for transfers between devices, ring_blocks(): blocks[1] = lax.ppermute(piece, axis, fwd)  13.7 us
    ppermute x9, waiting for transfers between devices, ring_blocks(): right = lax.ppermute(right, axis, fwd)  12 us
    ppermute x3, starting transfers between devices, ring_blocks(): lax.ppermute(lax.slice_in_dim(left, split, None, axis=split_dim), axis, bwd)  10.8 us
    ppermute x3, waiting for transfers between devices, ring_blocks(): lax.ppermute(lax.slice_in_dim(right, 0, split, axis=split_dim), axis, fwd)  7.5 us
    pallas_call x1, Pallas kernels, place_tiles(): pl.pallas_call(kernel, out_shape=jax.ShapeDtypeStruct((rows * size, block...  7.21 us
    ppermute x3, starting transfers between devices, ring_blocks(): blocks[1] = lax.ppermute(piece, axis, fwd)  6.93 us
  transfers between devices with their start and end apart: 28, of which 17 were waited for; matrix products, arithmetic and copies ran while one was open for 4% of the time, Pallas kernels for 5%

profile of v6, /device:TPU:2, one launch (start us, length us, event | category | flops | bytes accessed | tf_op | source)
XLA Modules:
  0.0 152.2 jit_solution(16104304760753376776)
XLA Ops:
  9.2 3.3 %collective-permute-start.9 = (bf16[256,256]{1,0:T(8,128)(2,1)S(1)}, bf16[256,256]{1,0:T(8,128)(2,1)S(1)}, u32[]{:S(2)}, u32[]{:S(2)}) collective-permute-start(bf16[256,256]{1,0:T(8,128)(2,1)S(1)} %copy.17), channel_id=1, source_target_pairs={{0,8},{8,0},{1,9},{9,1},{2,10},{10,2},{3,11},{11,3},{4,12},{12,4},... | collective-permute-start | bytes 393224 | tf_op jit(solution)/shard_map/ppermute | solution.py:29
  12.5 3.5 %collective-permute-done.9 = bf16[256,256]{1,0:T(8,128)(2,1)S(1)} collective-permute-done((bf16[256,256]{1,0:T(8,128)(2,1)S(1)}, bf16[256,256]{1,0:T(8,128)(2,1)S(1)}, u32[]{:S(2)}, u32[]{:S(2)}) %collective-permute-start.9) | collective-permute-done | bytes 131104 | tf_op jit(solution)/shard_map/ppermute | solution.py:29
  18.2 4.0 %collective-permute-start.10 = (bf16[2,256,256]{2,1,0:T(8,128)(2,1)S(1)}, bf16[2,256,256]{2,1,0:T(8,128)(2,1)S(1)}, u32[]{:S(2)}, u32[]{:S(2)}) collective-permute-start(bf16[2,256,256]{2,1,0:T(8,128)(2,1)S(1)} %fusion.42), channel_id=1, source_target_pairs={{0,7},{1,0},{2,1},{3,2},{4,3},{5,4},{6,5},{7,6},{8,15},{9,8},{10,9... | collective-permute-start | bytes 786440 | tf_op jit(solution)/shard_map/ppermute | solution.py:24
  22.2 5.4 %collective-permute-done.13 = bf16[2,256,256]{2,1,0:T(8,128)(2,1)S(1)} collective-permute-done((bf16[2,256,256]{2,1,0:T(8,128)(2,1)S(1)}, bf16[2,256,256]{2,1,0:T(8,128)(2,1)S(1)}, u32[]{:S(2)}, u32[]{:S(2)}) %collective-permute-start.13) | collective-permute-done | bytes 262176 | tf_op jit(solution)/shard_map/ppermute | solution.py:23
  27.6 3.2 %collective-permute-start.11 = (bf16[2,256,256]{2,1,0:T(8,128)(2,1)S(1)}, bf16[2,256,256]{2,1,0:T(8,128)(2,1)S(1)}, u32[]{:S(2)}, u32[]{:S(2)}) collective-permute-start(bf16[2,256,256]{2,1,0:T(8,128)(2,1)S(1)} %collective-permute-done.10), channel_id=1, source_target_pairs={{0,7},{1,0},{2,1},{3,2},{4,3},{5,4},{6,5},{7,6},{8,15},{9,8},{10,9... | collective-permute-start | bytes 786440 | tf_op jit(solution)/shard_map/ppermute | solution.py:24
  30.9 4.6 %collective-permute-done.14 = bf16[2,256,256]{2,1,0:T(8,128)(2,1)S(1)} collective-permute-done((bf16[2,256,256]{2,1,0:T(8,128)(2,1)S(1)}, bf16[2,256,256]{2,1,0:T(8,128)(2,1)S(1)}, u32[]{:S(2)}, u32[]{:S(2)}) %collective-permute-start.14) | collective-permute-done | bytes 262176 | tf_op jit(solution)/shard_map/ppermute | solution.py:23
  35.5 3.3 %collective-permute-start.12 = (bf16[2,256,256]{2,1,0:T(8,128)(2,1)S(1)}, bf16[2,256,256]{2,1,0:T(8,128)(2,1)S(1)}, u32[]{:S(2)}, u32[]{:S(2)}) collective-permute-start(bf16[2,256,256]{2,1,0:T(8,128)(2,1)S(1)} %collective-permute-done.11), channel_id=1, source_target_pairs={{0,7},{1,0},{2,1},{3,2},{4,3},{5,4},{6,5},{7,6},{8,15},{9,8},{10,9... | collective-permute-start | bytes 786440 | tf_op jit(solution)/shard_map/ppermute | solution.py:24
  41.0 2.0 %collective-permute-done.15 = bf16[2,256,256]{2,1,0:T(8,128)(2,1)S(1)} collective-permute-done((bf16[2,256,256]{2,1,0:T(8,128)(2,1)S(1)}, bf16[2,256,256]{2,1,0:T(8,128)(2,1)S(1)}, u32[]{:S(2)}, u32[]{:S(2)}) %collective-permute-start.15) | collective-permute-done | bytes 262176 | tf_op jit(solution)/shard_map/ppermute | solution.py:23
  43.2 3.3 %collective-permute-start.17 = (bf16[1,256,256]{2,1,0:T(8,128)(2,1)S(1)}, bf16[1,256,256]{2,1,0:T(8,128)(2,1)}, u32[]{:S(2)}, u32[]{:S(2)}) collective-permute-start(bf16[1,256,256]{2,1,0:T(8,128)(2,1)S(1)} %slice.85), channel_id=1, source_target_pairs={{0,7},{1,0},{2,1},{3,2},{4,3},{5,4},{6,5},{7,6},{8,15},{9,8},{10,9... | collective-permute-start | bytes 393224 | tf_op jit(solution)/shard_map/ppermute | solution.py:33
  46.4 3.5 %all-gather.2.cloned.1.call-done = bf16[4,48,64,64]{3,2,1,0:T(8,128)(2,1)} async-done(((bf16[4,3,64,64]{3,2,1,0:T(8,128)(2,1)}), bf16[4,48,64,64]{3,2,1,0:T(8,128)(2,1)}) %all-gather.2.cloned.1.call-update) | async-done | bytes 1572880 | tf_op jit(solution)/shard_map/all_gather | solution.py:103
  49.9 7.2 %shard_map.46 = bf16[4096,256]{1,0:T(8,128)(2,1)S(1)} custom-call(s32[192]{0:T(256)} %reshape.43.dest_ref, bf16[1,4,48,64,64]{4,3,2,1,0:T(8,128)(2,1)} %bitcast.183), custom_call_target="tpu_custom_call" | custom-call | tf_op jit(solution)/shard_map/pallas_call | solution.py:80
  60.8 83.9 %while.12 = (s32[]{:T(128)}, bf16[256,256]{1,0:T(8,128)(2,1)S(1)}, bf16[256,256]{1,0:T(8,128)(2,1)S(1)}, bf16[8,2,256,256]{3,2,1,0:T(8,128)(2,1)S(1)}, s32[]{:T(...) while((s32[]{:T(128)}, bf16[256,256]{1,0:T(8,128)(2,1)S(1)}, ...), condition=%wide.region_2.4_spmd, body=%wide.region_1.3_spmd.sunk | while | flops 538116096 | bytes 17564300 | solution.py:131
  61.7 6.3 %collective-permute-done = bf16[256,256]{1,0:T(8,128)(2,1)S(1)} collective-permute-done((bf16[256,256]{1,0:T(8,128)(2,1)S(1)}, bf16[256,256]{1,0:T(8,128)(2,1)S(1)}, u32[]{:S(2)}, u32[]{:S(2)}) %collective-permute-start) | collective-permute-done | bytes 131104 | tf_op jit(solution)/shard_map/while/body/eval_jaxpr/ppermute | solution.py:29
  68.3 3.6 %collective-permute-start.4 = (bf16[2,256,256]{2,1,0:T(8,128)(2,1)S(1)}, bf16[2,256,256]{2,1,0:T(8,128)(2,1)S(1)}, u32[]{:S(2)}, u32[]{:S(2)}) collective-permute-start(bf16[2,256,256]{2,1,0:T(8,128)(2,1)S(1)} %fusion.117), channel_id=1, source_target_pairs={{0,7},{1,0},{2,1},{3,2},{4,3},{5,4},{6,5},{7,6},{8,15},{9,8},{10,9... | collective-permute-start | bytes 786440 | tf_op jit(solution)/shard_map/while/body/eval_jaxpr/ppermute | solution.py:24
  72.1 5.1 %collective-permute-done.4 = bf16[2,256,256]{2,1,0:T(8,128)(2,1)S(1)} collective-permute-done((bf16[2,256,256]{2,1,0:T(8,128)(2,1)S(1)}, bf16[2,256,256]{2,1,0:T(8,128)(2,1)S(1)}, u32[]{:S(2)}, u32[]{:S(2)}) %collective-permute-start.4) | collective-permute-done | bytes 262176 | tf_op jit(solution)/shard_map/while/body/eval_jaxpr/ppermute | solution.py:24
  77.2 3.7 %collective-permute-start.5 = (bf16[2,256,256]{2,1,0:T(8,128)(2,1)S(1)}, bf16[2,256,256]{2,1,0:T(8,128)(2,1)S(1)}, u32[]{:S(2)}, u32[]{:S(2)}) collective-permute-start(bf16[2,256,256]{2,1,0:T(8,128)(2,1)S(1)} %collective-permute-done.4), channel_id=1, source_target_pairs={{0,7},{1,0},{2,1},{3,2},{4,3},{5,4},{6,5},{7,6},{8,15},{9,8},{10,9... | collective-permute-start | bytes 786440 | tf_op jit(solution)/shard_map/while/body/eval_jaxpr/ppermute | solution.py:24
  81.4 4.0 %collective-permute-done.5 = bf16[2,256,256]{2,1,0:T(8,128)(2,1)S(1)} collective-permute-done((bf16[2,256,256]{2,1,0:T(8,128)(2,1)S(1)}, bf16[2,256,256]{2,1,0:T(8,128)(2,1)S(1)}, u32[]{:S(2)}, u32[]{:S(2)}) %collective-permute-start.5) | collective-permute-done | bytes 262176 | tf_op jit(solution)/shard_map/while/body/eval_jaxpr/ppermute | solution.py:24
  85.4 3.7 %collective-permute-start.6 = (bf16[2,256,256]{2,1,0:T(8,128)(2,1)S(1)}, bf16[2,256,256]{2,1,0:T(8,128)(2,1)S(1)}, u32[]{:S(2)}, u32[]{:S(2)}) collective-permute-start(bf16[2,256,256]{2,1,0:T(8,128)(2,1)S(1)} %collective-permute-done.5), channel_id=1, source_target_pairs={{0,7},{1,0},{2,1},{3,2},{4,3},{5,4},{6,5},{7,6},{8,15},{9,8},{10,9... | collective-permute-start | bytes 786440 | tf_op jit(solution)/shard_map/while/body/eval_jaxpr/ppermute | solution.py:24
  89.6 3.4 %collective-permute-done.6 = bf16[2,256,256]{2,1,0:T(8,128)(2,1)S(1)} collective-permute-done((bf16[2,256,256]{2,1,0:T(8,128)(2,1)S(1)}, bf16[2,256,256]{2,1,0:T(8,128)(2,1)S(1)}, u32[]{:S(2)}, u32[]{:S(2)}) %collective-permute-start.6) | collective-permute-done | bytes 262176 | tf_op jit(solution)/shard_map/while/body/eval_jaxpr/ppermute | solution.py:24
  93.0 3.8 %collective-permute-start.7 = (bf16[1,256,256]{2,1,0:T(8,128)(2,1)S(1)}, bf16[1,256,256]{2,1,0:T(8,128)(2,1)S(1)}, u32[]{:S(2)}, u32[]{:S(2)}) collective-permute-start(bf16[1,256,256]{2,1,0:T(8,128)(2,1)S(1)} %slice.148), channel_id=1, source_target_pairs={{0,7},{1,0},{2,1},{3,2},{4,3},{5,4},{6,5},{7,6},{8,15},{9,8},{10,9... | collective-permute-start | bytes 393224 | tf_op jit(solution)/shard_map/while/body/eval_jaxpr/ppermute | solution.py:33
  97.1 2.2 %collective-permute-done.7 = bf16[1,256,256]{2,1,0:T(8,128)(2,1)S(1)} collective-permute-done((bf16[1,256,256]{2,1,0:T(8,128)(2,1)S(1)}, bf16[1,256,256]{2,1,0:T(8,128)(2,1)S(1)}, u32[]{:S(2)}, u32[]{:S(2)}) %collective-permute-start.7) | collective-permute-done | bytes 131104 | tf_op jit(solution)/shard_map/while/body/eval_jaxpr/ppermute | solution.py:33
  99.3 3.8 %collective-permute-done.8 = bf16[1,256,256]{2,1,0:T(8,128)(2,1)S(1)} collective-permute-done((bf16[1,256,256]{2,1,0:T(8,128)(2,1)S(1)}, bf16[1,256,256]{2,1,0:T(8,128)(2,1)S(1)}, u32[]{:S(2)}, u32[]{:S(2)}) %collective-permute-start.8) | collective-permute-done | bytes 131104 | tf_op jit(solution)/shard_map/while/body/eval_jaxpr/ppermute | solution.py:32
  103.6 2.8 %collective-permute-start = (bf16[256,256]{1,0:T(8,128)(2,1)S(1)}, bf16[256,256]{1,0:T(8,128)(2,1)S(1)}, u32[]{:S(2)}, u32[]{:S(2)}) collective-permute-start(bf16[256,256]{1,0:T(8,128)(2,1)S(1)} %copy.12), channel_id=1, source_target_pairs={{0,8},{8,0},{1,9},{9,1},{2,10},{10,2},{3,11},{11,3},{4,12},{12,4},... | collective-permute-start | bytes 393224 | tf_op jit(solution)/shard_map/while/body/eval_jaxpr/ppermute | solution.py:29
  106.4 3.8 %collective-permute-done = bf16[256,256]{1,0:T(8,128)(2,1)S(1)} collective-permute-done((bf16[256,256]{1,0:T(8,128)(2,1)S(1)}, bf16[256,256]{1,0:T(8,128)(2,1)S(1)}, u32[]{:S(2)}, u32[]{:S(2)}) %collective-permute-start) | collective-permute-done | bytes 131104 | tf_op jit(solution)/shard_map/while/body/eval_jaxpr/ppermute | solution.py:29
  112.7 5.7 %collective-permute-done.4 = bf16[2,256,256]{2,1,0:T(8,128)(2,1)S(1)} collective-permute-done((bf16[2,256,256]{2,1,0:T(8,128)(2,1)S(1)}, bf16[2,256,256]{2,1,0:T(8,128)(2,1)S(1)}, u32[]{:S(2)}, u32[]{:S(2)}) %collective-permute-start.4) | collective-permute-done | bytes 262176 | tf_op jit(solution)/shard_map/while/body/eval_jaxpr/ppermute | solution.py:24
  118.4 2.4 %collective-permute-start.5 = (bf16[2,256,256]{2,1,0:T(8,128)(2,1)S(1)}, bf16[2,256,256]{2,1,0:T(8,128)(2,1)S(1)}, u32[]{:S(2)}, u32[]{:S(2)}) collective-permute-start(bf16[2,256,256]{2,1,0:T(8,128)(2,1)S(1)} %collective-permute-done.4), channel_id=1, source_target_pairs={{0,7},{1,0},{2,1},{3,2},{4,3},{5,4},{6,5},{7,6},{8,15},{9,8},{10,9... | collective-permute-start | bytes 786440 | tf_op jit(solution)/shard_map/while/body/eval_jaxpr/ppermute | solution.py:24
  121.3 5.3 %collective-permute-done.5 = bf16[2,256,256]{2,1,0:T(8,128)(2,1)S(1)} collective-permute-done((bf16[2,256,256]{2,1,0:T(8,128)(2,1)S(1)}, bf16[2,256,256]{2,1,0:T(8,128)(2,1)S(1)}, u32[]{:S(2)}, u32[]{:S(2)}) %collective-permute-start.5) | collective-permute-done | bytes 262176 | tf_op jit(solution)/shard_map/while/body/eval_jaxpr/ppermute | solution.py:24
  126.6 3.7 %collective-permute-start.6 = (bf16[2,256,256]{2,1,0:T(8,128)(2,1)S(1)}, bf16[2,256,256]{2,1,0:T(8,128)(2,1)S(1)}, u32[]{:S(2)}, u32[]{:S(2)}) collective-permute-start(bf16[2,256,256]{2,1,0:T(8,128)(2,1)S(1)} %collective-permute-done.5), channel_id=1, source_target_pairs={{0,7},{1,0},{2,1},{3,2},{4,3},{5,4},{6,5},{7,6},{8,15},{9,8},{10,9... | collective-permute-start | bytes 786440 | tf_op jit(solution)/shard_map/while/body/eval_jaxpr/ppermute | solution.py:24
  130.7 3.4 %collective-permute-done.6 = bf16[2,256,256]{2,1,0:T(8,128)(2,1)S(1)} collective-permute-done((bf16[2,256,256]{2,1,0:T(8,128)(2,1)S(1)}, bf16[2,256,256]{2,1,0:T(8,128)(2,1)S(1)}, u32[]{:S(2)}, u32[]{:S(2)}) %collective-permute-start.6) | collective-permute-done | bytes 262176 | tf_op jit(solution)/shard_map/while/body/eval_jaxpr/ppermute | solution.py:24
  134.2 3.8 %collective-permute-start.7 = (bf16[1,256,256]{2,1,0:T(8,128)(2,1)S(1)}, bf16[1,256,256]{2,1,0:T(8,128)(2,1)S(1)}, u32[]{:S(2)}, u32[]{:S(2)}) collective-permute-start(bf16[1,256,256]{2,1,0:T(8,128)(2,1)S(1)} %slice.148), channel_id=1, source_target_pairs={{0,7},{1,0},{2,1},{3,2},{4,3},{5,4},{6,5},{7,6},{8,15},{9,8},{10,9... | collective-permute-start | bytes 393224 | tf_op jit(solution)/shard_map/while/body/eval_jaxpr/ppermute | solution.py:33
  138.3 2.2 %collective-permute-done.7 = bf16[1,256,256]{2,1,0:T(8,128)(2,1)S(1)} collective-permute-done((bf16[1,256,256]{2,1,0:T(8,128)(2,1)S(1)}, bf16[1,256,256]{2,1,0:T(8,128)(2,1)S(1)}, u32[]{:S(2)}, u32[]{:S(2)}) %collective-permute-start.7) | collective-permute-done | bytes 131104 | tf_op jit(solution)/shard_map/while/body/eval_jaxpr/ppermute | solution.py:33
  140.5 3.8 %collective-permute-done.8 = bf16[1,256,256]{2,1,0:T(8,128)(2,1)S(1)} collective-permute-done((bf16[1,256,256]{2,1,0:T(8,128)(2,1)S(1)}, bf16[1,256,256]{2,1,0:T(8,128)(2,1)S(1)}, u32[]{:S(2)}, u32[]{:S(2)}) %collective-permute-start.8) | collective-permute-done | bytes 131104 | tf_op jit(solution)/shard_map/while/body/eval_jaxpr/ppermute | solution.py:32
  (97 shorter events, 18.7 us)
Async XLA Ops:
  6.5 43.4 %all-gather.2.cloned.1.call-start = ((), (), s32[]{:S(2)}) async-start(), calls=%async_computation | async-start | bytes 3342336 | tf_op jit(solution)/shard_map/all_gather | solution.py:103
  9.2 6.8 %collective-permute-start.9 = (bf16[256,256]{1,0:T(8,128)(2,1)S(1)}, bf16[256,256]{1,0:T(8,128)(2,1)S(1)}, u32[]{:S(2)}, u32[]{:S(2)}) collective-permute-start(bf16[256,256]{1,0:T(8,128)(2,1)S(1)} %copy.17), channel_id=1, source_target_pairs={{0,8},{8,0},{1,9},{9,1},{2,10},{10,2},{3,11},{11,3},{4,12},{12,4},... | collective-permute-start | bytes 393224 | tf_op jit(solution)/shard_map/ppermute | solution.py:29
  16.2 11.4 %collective-permute-start.13 = (bf16[2,256,256]{2,1,0:T(8,128)(2,1)S(1)}, bf16[2,256,256]{2,1,0:T(8,128)(2,1)S(1)}, u32[]{:S(2)}, u32[]{:S(2)}) collective-permute-start(bf16[2,256,256]{2,1,0:T(8,128)(2,1)S(1)} %fusion.42), channel_id=1, source_target_pairs={{0,1},{1,2},{2,3},{3,4},{4,5},{5,6},{6,7},{7,0},{8,9},{9,10},{10,1... | collective-permute-start | bytes 786440 | tf_op jit(solution)/shard_map/ppermute | solution.py:23
  18.2 9.4 %collective-permute-start.10 = (bf16[2,256,256]{2,1,0:T(8,128)(2,1)S(1)}, bf16[2,256,256]{2,1,0:T(8,128)(2,1)S(1)}, u32[]{:S(2)}, u32[]{:S(2)}) collective-permute-start(bf16[2,256,256]{2,1,0:T(8,128)(2,1)S(1)} %fusion.42), channel_id=1, source_target_pairs={{0,7},{1,0},{2,1},{3,2},{4,3},{5,4},{6,5},{7,6},{8,15},{9,8},{10,9... | collective-permute-start | bytes 786440 | tf_op jit(solution)/shard_map/ppermute | solution.py:24
  27.6 7.8 %copy-start.5 = (bf16[2,256,256]{2,1,0:T(8,128)(2,1)}, bf16[2,256,256]{2,1,0:T(8,128)(2,1)S(1)}, u32[]{:S(2)}) copy-start(bf16[2,256,256]{2,1,0:T(8,128)(2,1)S(1)} %collective-permute-done.13) | copy-start | bytes 786436
  27.6 7.8 %collective-permute-start.14 = (bf16[2,256,256]{2,1,0:T(8,128)(2,1)S(1)}, bf16[2,256,256]{2,1,0:T(8,128)(2,1)S(1)}, u32[]{:S(2)}, u32[]{:S(2)}) collective-permute-start(bf16[2,256,256]{2,1,0:T(8,128)(2,1)S(1)} %collective-permute-done.13), channel_id=1, source_target_pairs={{0,1},{1,2},{2,3},{3,4},{4,5},{5,6},{6,7},{7,0},{8,9},{9,10},{10,1... | collective-permute-start | bytes 786440 | tf_op jit(solution)/shard_map/ppermute | solution.py:23
  27.6 22.3 %copy-start.9 = (bf16[2,256,256]{2,1,0:T(8,128)(2,1)}, bf16[2,256,256]{2,1,0:T(8,128)(2,1)S(1)}, u32[]{:S(2)}) copy-start(bf16[2,256,256]{2,1,0:T(8,128)(2,1)S(1)} %collective-permute-done.10) | copy-start | bytes 786436
  27.6 7.8 %collective-permute-start.11 = (bf16[2,256,256]{2,1,0:T(8,128)(2,1)S(1)}, bf16[2,256,256]{2,1,0:T(8,128)(2,1)S(1)}, u32[]{:S(2)}, u32[]{:S(2)}) collective-permute-start(bf16[2,256,256]{2,1,0:T(8,128)(2,1)S(1)} %collective-permute-done.10), channel_id=1, source_target_pairs={{0,7},{1,0},{2,1},{3,2},{4,3},{5,4},{6,5},{7,6},{8,15},{9,8},{10,9... | collective-permute-start | bytes 786440 | tf_op jit(solution)/shard_map/ppermute | solution.py:24
  35.4 14.5 %copy-start.7 = (bf16[2,256,256]{2,1,0:T(8,128)(2,1)}, bf16[2,256,256]{2,1,0:T(8,128)(2,1)S(1)}, u32[]{:S(2)}) copy-start(bf16[2,256,256]{2,1,0:T(8,128)(2,1)S(1)} %collective-permute-done.14) | copy-start | bytes 786436
  35.4 7.6 %collective-permute-start.15 = (bf16[2,256,256]{2,1,0:T(8,128)(2,1)S(1)}, bf16[2,256,256]{2,1,0:T(8,128)(2,1)S(1)}, u32[]{:S(2)}, u32[]{:S(2)}) collective-permute-start(bf16[2,256,256]{2,1,0:T(8,128)(2,1)S(1)} %collective-permute-done.14), channel_id=1, source_target_pairs={{0,1},{1,2},{2,3},{3,4},{4,5},{5,6},{6,7},{7,0},{8,9},{9,10},{10,1... | collective-permute-start | bytes 786440 | tf_op jit(solution)/shard_map/ppermute | solution.py:23
  35.4 14.5 %copy-start.11 = (bf16[2,256,256]{2,1,0:T(8,128)(2,1)}, bf16[2,256,256]{2,1,0:T(8,128)(2,1)S(1)}, u32[]{:S(2)}) copy-start(bf16[2,256,256]{2,1,0:T(8,128)(2,1)S(1)} %collective-permute-done.11) | copy-start | bytes 786436
  35.5 7.7 %collective-permute-start.12 = (bf16[2,256,256]{2,1,0:T(8,128)(2,1)S(1)}, bf16[2,256,256]{2,1,0:T(8,128)(2,1)S(1)}, u32[]{:S(2)}, u32[]{:S(2)}) collective-permute-start(bf16[2,256,256]{2,1,0:T(8,128)(2,1)S(1)} %collective-permute-done.11), channel_id=1, source_target_pairs={{0,7},{1,0},{2,1},{3,2},{4,3},{5,4},{6,5},{7,6},{8,15},{9,8},{10,9... | collective-permute-start | bytes 786440 | tf_op jit(solution)/shard_map/ppermute | solution.py:24
  43.0 16.3 %collective-permute-start.16 = (bf16[1,256,256]{2,1,0:T(8,128)(2,1)S(1)}, bf16[1,256,256]{2,1,0:T(8,128)(2,1)}, u32[]{:S(2)}, u32[]{:S(2)}) collective-permute-start(bf16[1,256,256]{2,1,0:T(8,128)(2,1)S(1)} %slice.84), channel_id=1, source_target_pairs={{0,1},{1,2},{2,3},{3,4},{4,5},{5,6},{6,7},{7,0},{8,9},{9,10},{10,1... | collective-permute-start | bytes 393224 | tf_op jit(solution)/shard_map/ppermute | solution.py:32
  43.2 16.2 %collective-permute-start.17 = (bf16[1,256,256]{2,1,0:T(8,128)(2,1)S(1)}, bf16[1,256,256]{2,1,0:T(8,128)(2,1)}, u32[]{:S(2)}, u32[]{:S(2)}) collective-permute-start(bf16[1,256,256]{2,1,0:T(8,128)(2,1)S(1)} %slice.85), channel_id=1, source_target_pairs={{0,7},{1,0},{2,1},{3,2},{4,3},{5,4},{6,5},{7,6},{8,15},{9,8},{10,9... | collective-permute-start | bytes 393224 | tf_op jit(solution)/shard_map/ppermute | solution.py:33
  60.8 7.2 %collective-permute-start = (bf16[256,256]{1,0:T(8,128)(2,1)S(1)}, bf16[256,256]{1,0:T(8,128)(2,1)S(1)}, u32[]{:S(2)}, u32[]{:S(2)}) collective-permute-start(bf16[256,256]{1,0:T(8,128)(2,1)S(1)} %copy.12), channel_id=1, source_target_pairs={{0,8},{8,0},{1,9},{9,1},{2,10},{10,2},{3,11},{11,3},{4,12},{12,4},... | collective-permute-start | bytes 393224 | tf_op jit(solution)/shard_map/while/body/eval_jaxpr/ppermute | solution.py:29
  68.3 9.0 %collective-permute-start.4 = (bf16[2,256,256]{2,1,0:T(8,128)(2,1)S(1)}, bf16[2,256,256]{2,1,0:T(8,128)(2,1)S(1)}, u32[]{:S(2)}, u32[]{:S(2)}) collective-permute-start(bf16[2,256,256]{2,1,0:T(8,128)(2,1)S(1)} %fusion.117), channel_id=1, source_target_pairs={{0,7},{1,0},{2,1},{3,2},{4,3},{5,4},{6,5},{7,6},{8,15},{9,8},{10,9... | collective-permute-start | bytes 786440 | tf_op jit(solution)/shard_map/while/body/eval_jaxpr/ppermute | solution.py:24
  71.8 9.1 %collective-permute-start.1 = (bf16[2,256,256]{2,1,0:T(8,128)(2,1)S(1)}, bf16[2,256,256]{2,1,0:T(8,128)(2,1)S(1)}, u32[]{:S(2)}, u32[]{:S(2)}) collective-permute-start(bf16[2,256,256]{2,1,0:T(8,128)(2,1)S(1)} %fusion.117), channel_id=1, source_target_pairs={{0,1},{1,2},{2,3},{3,4},{4,5},{5,6},{6,7},{7,0},{8,9},{9,10},{10,1... | collective-permute-start | bytes 786440 | tf_op jit(solution)/shard_map/while/body/eval_jaxpr/ppermute | solution.py:23
  77.2 8.2 %collective-permute-start.5 = (bf16[2,256,256]{2,1,0:T(8,128)(2,1)S(1)}, bf16[2,256,256]{2,1,0:T(8,128)(2,1)S(1)}, u32[]{:S(2)}, u32[]{:S(2)}) collective-permute-start(bf16[2,256,256]{2,1,0:T(8,128)(2,1)S(1)} %collective-permute-done.4), channel_id=1, source_target_pairs={{0,7},{1,0},{2,1},{3,2},{4,3},{5,4},{6,5},{7,6},{8,15},{9,8},{10,9... | collective-permute-start | bytes 786440 | tf_op jit(solution)/shard_map/while/body/eval_jaxpr/ppermute | solution.py:24
  80.9 8.2 %collective-permute-start.2 = (bf16[2,256,256]{2,1,0:T(8,128)(2,1)S(1)}, bf16[2,256,256]{2,1,0:T(8,128)(2,1)S(1)}, u32[]{:S(2)}, u32[]{:S(2)}) collective-permute-start(bf16[2,256,256]{2,1,0:T(8,128)(2,1)S(1)} %collective-permute-done.1), channel_id=1, source_target_pairs={{0,1},{1,2},{2,3},{3,4},{4,5},{5,6},{6,7},{7,0},{8,9},{9,10},{10,1... | collective-permute-start | bytes 786440 | tf_op jit(solution)/shard_map/while/body/eval_jaxpr/ppermute | solution.py:23
  85.4 7.6 %collective-permute-start.6 = (bf16[2,256,256]{2,1,0:T(8,128)(2,1)S(1)}, bf16[2,256,256]{2,1,0:T(8,128)(2,1)S(1)}, u32[]{:S(2)}, u32[]{:S(2)}) collective-permute-start(bf16[2,256,256]{2,1,0:T(8,128)(2,1)S(1)} %collective-permute-done.5), channel_id=1, source_target_pairs={{0,7},{1,0},{2,1},{3,2},{4,3},{5,4},{6,5},{7,6},{8,15},{9,8},{10,9... | collective-permute-start | bytes 786440 | tf_op jit(solution)/shard_map/while/body/eval_jaxpr/ppermute | solution.py:24
  89.1 7.7 %collective-permute-start.3 = (bf16[2,256,256]{2,1,0:T(8,128)(2,1)S(1)}, bf16[2,256,256]{2,1,0:T(8,128)(2,1)S(1)}, u32[]{:S(2)}, u32[]{:S(2)}) collective-permute-start(bf16[2,256,256]{2,1,0:T(8,128)(2,1)S(1)} %collective-permute-done.2), channel_id=1, source_target_pairs={{0,1},{1,2},{2,3},{3,4},{4,5},{5,6},{6,7},{7,0},{8,9},{9,10},{10,1... | collective-permute-start | bytes 786440 | tf_op jit(solution)/shard_map/while/body/eval_jaxpr/ppermute | solution.py:23
  93.0 6.3 %collective-permute-start.7 = (bf16[1,256,256]{2,1,0:T(8,128)(2,1)S(1)}, bf16[1,256,256]{2,1,0:T(8,128)(2,1)S(1)}, u32[]{:S(2)}, u32[]{:S(2)}) collective-permute-start(bf16[1,256,256]{2,1,0:T(8,128)(2,1)S(1)} %slice.148), channel_id=1, source_target_pairs={{0,7},{1,0},{2,1},{3,2},{4,3},{5,4},{6,5},{7,6},{8,15},{9,8},{10,9... | collective-permute-start | bytes 393224 | tf_op jit(solution)/shard_map/while/body/eval_jaxpr/ppermute | solution.py:33
  96.8 6.3 %collective-permute-start.8 = (bf16[1,256,256]{2,1,0:T(8,128)(2,1)S(1)}, bf16[1,256,256]{2,1,0:T(8,128)(2,1)S(1)}, u32[]{:S(2)}, u32[]{:S(2)}) collective-permute-start(bf16[1,256,256]{2,1,0:T(8,128)(2,1)S(1)} %slice.149), channel_id=1, source_target_pairs={{0,1},{1,2},{2,3},{3,4},{4,5},{5,6},{6,7},{7,0},{8,9},{9,10},{10,1... | collective-permute-start | bytes 393224 | tf_op jit(solution)/shard_map/while/body/eval_jaxpr/ppermute | solution.py:32
  103.6 6.6 %collective-permute-start = (bf16[256,256]{1,0:T(8,128)(2,1)S(1)}, bf16[256,256]{1,0:T(8,128)(2,1)S(1)}, u32[]{:S(2)}, u32[]{:S(2)}) collective-permute-start(bf16[256,256]{1,0:T(8,128)(2,1)S(1)} %copy.12), channel_id=1, source_target_pairs={{0,8},{8,0},{1,9},{9,1},{2,10},{10,2},{3,11},{11,3},{4,12},{12,4},... | collective-permute-start | bytes 393224 | tf_op jit(solution)/shard_map/while/body/eval_jaxpr/ppermute | solution.py:29
  110.4 8.0 %collective-permute-start.4 = (bf16[2,256,256]{2,1,0:T(8,128)(2,1)S(1)}, bf16[2,256,256]{2,1,0:T(8,128)(2,1)S(1)}, u32[]{:S(2)}, u32[]{:S(2)}) collective-permute-start(bf16[2,256,256]{2,1,0:T(8,128)(2,1)S(1)} %fusion.117), channel_id=1, source_target_pairs={{0,7},{1,0},{2,1},{3,2},{4,3},{5,4},{6,5},{7,6},{8,15},{9,8},{10,9... | collective-permute-start | bytes 786440 | tf_op jit(solution)/shard_map/while/body/eval_jaxpr/ppermute | solution.py:24
  110.5 10.3 %collective-permute-start.1 = (bf16[2,256,256]{2,1,0:T(8,128)(2,1)S(1)}, bf16[2,256,256]{2,1,0:T(8,128)(2,1)S(1)}, u32[]{:S(2)}, u32[]{:S(2)}) collective-permute-start(bf16[2,256,256]{2,1,0:T(8,128)(2,1)S(1)} %fusion.117), channel_id=1, source_target_pairs={{0,1},{1,2},{2,3},{3,4},{4,5},{5,6},{6,7},{7,0},{8,9},{9,10},{10,1... | collective-permute-start | bytes 786440 | tf_op jit(solution)/shard_map/while/body/eval_jaxpr/ppermute | solution.py:23
  118.4 8.2 %collective-permute-start.5 = (bf16[2,256,256]{2,1,0:T(8,128)(2,1)S(1)}, bf16[2,256,256]{2,1,0:T(8,128)(2,1)S(1)}, u32[]{:S(2)}, u32[]{:S(2)}) collective-permute-start(bf16[2,256,256]{2,1,0:T(8,128)(2,1)S(1)} %collective-permute-done.4), channel_id=1, source_target_pairs={{0,7},{1,0},{2,1},{3,2},{4,3},{5,4},{6,5},{7,6},{8,15},{9,8},{10,9... | collective-permute-start | bytes 786440 | tf_op jit(solution)/shard_map/while/body/eval_jaxpr/ppermute | solution.py:24
  120.8 9.5 %collective-permute-start.2 = (bf16[2,256,256]{2,1,0:T(8,128)(2,1)S(1)}, bf16[2,256,256]{2,1,0:T(8,128)(2,1)S(1)}, u32[]{:S(2)}, u32[]{:S(2)}) collective-permute-start(bf16[2,256,256]{2,1,0:T(8,128)(2,1)S(1)} %collective-permute-done.1), channel_id=1, source_target_pairs={{0,1},{1,2},{2,3},{3,4},{4,5},{5,6},{6,7},{7,0},{8,9},{9,10},{10,1... | collective-permute-start | bytes 786440 | tf_op jit(solution)/shard_map/while/body/eval_jaxpr/ppermute | solution.py:23
  126.6 7.6 %collective-permute-start.6 = (bf16[2,256,256]{2,1,0:T(8,128)(2,1)S(1)}, bf16[2,256,256]{2,1,0:T(8,128)(2,1)S(1)}, u32[]{:S(2)}, u32[]{:S(2)}) collective-permute-start(bf16[2,256,256]{2,1,0:T(8,128)(2,1)S(1)} %collective-permute-done.5), channel_id=1, source_target_pairs={{0,7},{1,0},{2,1},{3,2},{4,3},{5,4},{6,5},{7,6},{8,15},{9,8},{10,9... | collective-permute-start | bytes 786440 | tf_op jit(solution)/shard_map/while/body/eval_jaxpr/ppermute | solution.py:24
  130.3 7.7 %collective-permute-start.3 = (bf16[2,256,256]{2,1,0:T(8,128)(2,1)S(1)}, bf16[2,256,256]{2,1,0:T(8,128)(2,1)S(1)}, u32[]{:S(2)}, u32[]{:S(2)}) collective-permute-start(bf16[2,256,256]{2,1,0:T(8,128)(2,1)S(1)} %collective-permute-done.2), channel_id=1, source_target_pairs={{0,1},{1,2},{2,3},{3,4},{4,5},{5,6},{6,7},{7,0},{8,9},{9,10},{10,1... | collective-permute-start | bytes 786440 | tf_op jit(solution)/shard_map/while/body/eval_jaxpr/ppermute | solution.py:23
  134.2 6.3 %collective-permute-start.7 = (bf16[1,256,256]{2,1,0:T(8,128)(2,1)S(1)}, bf16[1,256,256]{2,1,0:T(8,128)(2,1)S(1)}, u32[]{:S(2)}, u32[]{:S(2)}) collective-permute-start(bf16[1,256,256]{2,1,0:T(8,128)(2,1)S(1)} %slice.148), channel_id=1, source_target_pairs={{0,7},{1,0},{2,1},{3,2},{4,3},{5,4},{6,5},{7,6},{8,15},{9,8},{10,9... | collective-permute-start | bytes 393224 | tf_op jit(solution)/shard_map/while/body/eval_jaxpr/ppermute | solution.py:33
  138.0 6.3 %collective-permute-start.8 = (bf16[1,256,256]{2,1,0:T(8,128)(2,1)S(1)}, bf16[1,256,256]{2,1,0:T(8,128)(2,1)S(1)}, u32[]{:S(2)}, u32[]{:S(2)}) collective-permute-start(bf16[1,256,256]{2,1,0:T(8,128)(2,1)S(1)} %slice.149), channel_id=1, source_target_pairs={{0,1},{1,2},{2,3},{3,4},{4,5},{5,6},{6,7},{7,0},{8,9},{9,10},{10,1... | collective-permute-start | bytes 393224 | tf_op jit(solution)/shard_map/while/body/eval_jaxpr/ppermute | solution.py:32
  (9 other events, 23.2 us)
Sparse Core Ops, SparseCore 0:
  9.3 40.5 all-gather.1

commit v7 on v5

--- a/solution.py
+++ b/solution.py
@@ -25,13 +25,7 @@
         blocks[(-k) % count] = right
         blocks[k] = left
     if count % 2 == 0 and count > 1:
-        if count == 2:
-            blocks[1] = lax.ppermute(piece, axis, fwd)
-        else:
-            split = piece.shape[split_dim] // 2
-            lo = lax.ppermute(lax.slice_in_dim(right, 0, split, axis=split_dim), axis, fwd)
-            hi = lax.ppermute(lax.slice_in_dim(left, split, None, axis=split_dim), axis, bwd)
-            blocks[count // 2] = jnp.concatenate([lo, hi], axis=split_dim)
+        blocks[count // 2] = lax.ppermute(right, axis, fwd)
     return blocks
 
 

time: 153 us -> 158 us (1.033)
  waiting for transfers between devices: 64.7 us -> 84.6 us
  starting transfers between devices: 52.5 us -> 33.6 us
  Pallas kernels: 7.34 us -> 10.3 us
  matrix products: 6.49 us -> 9.28 us
    ppermute x9 -> x6, starting transfers between devices: 22.2 us -> 5.2 us  [ring_blocks(): blocks[count // 2] = lax.ppermute(right, axis, fwd)]
    ppermute x9, waiting for transfers between devices: 12 us -> 27 us  [ring_blocks(): right = lax.ppermute(right, axis, fwd)]
    ppermute x9 -> x6, waiting for transfers between devices: 22.7 us -> 29.6 us  [ring_blocks(): blocks[count // 2] = lax.ppermute(right, axis, fwd)]
    ppermute x9, waiting for transfers between devices: 26.6 us -> 21.1 us  [ring_blocks(): left = lax.ppermute(left, axis, bwd)]
    all_gather x1, waiting for transfers between devices: 3.3 us -> 6.8 us  [body(): lax.all_gather(jnp.swapaxes(block_tiles, 2, 3), ROW_AXES, axis=1, tiled=T...]
    pallas_call x1, Pallas kernels: 7.34 us -> 10.3 us  [place_tiles(): pl.pallas_call(kernel, out_shape=jax.ShapeDtypeStruct((rows * size, block...]
    dot_general x24, matrix products: 6.49 us -> 9.28 us  [apply_hamiltonian(): jnp.einsum('ymj,yjo->mo', chunk, dense[d], preferred_element_type=jnp.flo...]
    ppermute x9, starting transfers between devices: 26.3 us -> 23.9 us  [ring_blocks(): left = lax.ppermute(left, axis, bwd)]
  transfers between devices with their start and end apart: 28 -> 25, of which waited for: 17 -> 17; matrix products, arithmetic and copies ran while one was open for 4% -> 6% of each run, Pallas kernels for 5% -> 7%
where the time goes in v7:
time: 158 us
  waiting for transfers between devices  84.6 us (54%)
  starting transfers between devices  33.6 us (21%)
  between operations  13.6 us (9%)
  Pallas kernels  10.3 us (7%)
  matrix products  9.28 us (6%)
  local copies, waits for them, and re-layouts  4.13 us (3%)
  other arithmetic  2.21 us (1%)
    ppermute x6, waiting for transfers between devices, ring_blocks(): blocks[count // 2] = lax.ppermute(right, axis, fwd)  29.6 us
    ppermute x9, waiting for transfers between devices, ring_blocks(): right = lax.ppermute(right, axis, fwd)  27 us
    ppermute x9, starting transfers between devices, ring_blocks(): left = lax.ppermute(left, axis, bwd)  23.9 us
    ppermute x9, waiting for transfers between devices, ring_blocks(): left = lax.ppermute(left, axis, bwd)  21.1 us
    pallas_call x1, Pallas kernels, place_tiles(): pl.pallas_call(kernel, out_shape=jax.ShapeDtypeStruct((rows * size, block...  10.3 us
    dot_general x24, matrix products, apply_hamiltonian(): jnp.einsum('ymj,yjo->mo', chunk, dense[d], preferred_element_type=jnp.flo...  9.28 us
    all_gather x1, waiting for transfers between devices, body(): lax.all_gather(jnp.swapaxes(block_tiles, 2, 3), ROW_AXES, axis=1, tiled=T...  6.8 us
    ppermute x6, starting transfers between devices, ring_blocks(): blocks[count // 2] = lax.ppermute(right, axis, fwd)  5.2 us
  transfers between devices with their start and end apart: 25, of which 17 were waited for; matrix products, arithmetic and copies ran while one was open for 6% of the time, Pallas kernels for 7%

profile of v7, /device:TPU:2, one launch (start us, length us, event | category | flops | bytes accessed | tf_op | source)
XLA Modules:
  0.0 157.9 jit_solution(14016629417695289520)
XLA Ops:
  7.4 1.7 %copy.6 = bf16[4,3,64,64]{2,3,1,0:T(8,128)(2,1)} copy(bf16[4,3,64,64]{3,2,1,0:T(8,128)(2,1)} %param.9) | data formatting | bytes 196608 | tf_op args[1]
  9.2 3.3 %collective-permute-start.8 = (bf16[256,256]{1,0:T(8,128)(2,1)S(1)}, bf16[256,256]{1,0:T(8,128)(2,1)S(1)}, u32[]{:S(2)}, u32[]{:S(2)}) collective-permute-start(bf16[256,256]{1,0:T(8,128)(2,1)S(1)} %copy.17), channel_id=1, source_target_pairs={{0,8},{8,0},{1,9},{9,1},{2,10},{10,2},{3,11},{11,3},{4,12},{12,4},... | collective-permute-start | bytes 393224 | tf_op jit(solution)/shard_map/ppermute | solution.py:28
  12.5 3.5 %collective-permute-done.8 = bf16[256,256]{1,0:T(8,128)(2,1)S(1)} collective-permute-done((bf16[256,256]{1,0:T(8,128)(2,1)S(1)}, bf16[256,256]{1,0:T(8,128)(2,1)S(1)}, u32[]{:S(2)}, u32[]{:S(2)}) %collective-permute-start.8) | collective-permute-done | bytes 131104 | tf_op jit(solution)/shard_map/ppermute | solution.py:28
  16.2 2.0 %collective-permute-start.12 = (bf16[2,256,256]{2,1,0:T(8,128)(2,1)S(1)}, bf16[2,256,256]{2,1,0:T(8,128)(2,1)S(1)}, u32[]{:S(2)}, u32[]{:S(2)}) collective-permute-start(bf16[2,256,256]{2,1,0:T(8,128)(2,1)S(1)} %fusion.38), channel_id=1, source_target_pairs={{0,1},{1,2},{2,3},{3,4},{4,5},{5,6},{6,7},{7,0},{8,9},{9,10},{10,1... | collective-permute-start | bytes 786440 | tf_op jit(solution)/shard_map/ppermute | solution.py:23
  18.2 4.0 %collective-permute-start.9 = (bf16[2,256,256]{2,1,0:T(8,128)(2,1)S(1)}, bf16[2,256,256]{2,1,0:T(8,128)(2,1)S(1)}, u32[]{:S(2)}, u32[]{:S(2)}) collective-permute-start(bf16[2,256,256]{2,1,0:T(8,128)(2,1)S(1)} %fusion.38), channel_id=1, source_target_pairs={{0,7},{1,0},{2,1},{3,2},{4,3},{5,4},{6,5},{7,6},{8,15},{9,8},{10,9... | collective-permute-start | bytes 786440 | tf_op jit(solution)/shard_map/ppermute | solution.py:24
  22.2 5.4 %collective-permute-done.12 = bf16[2,256,256]{2,1,0:T(8,128)(2,1)S(1)} collective-permute-done((bf16[2,256,256]{2,1,0:T(8,128)(2,1)S(1)}, bf16[2,256,256]{2,1,0:T(8,128)(2,1)S(1)}, u32[]{:S(2)}, u32[]{:S(2)}) %collective-permute-start.12) | collective-permute-done | bytes 262176 | tf_op jit(solution)/shard_map/ppermute | solution.py:23
  27.6 3.3 %collective-permute-start.10 = (bf16[2,256,256]{2,1,0:T(8,128)(2,1)S(1)}, bf16[2,256,256]{2,1,0:T(8,128)(2,1)}, u32[]{:S(2)}, u32[]{:S(2)}) collective-permute-start(bf16[2,256,256]{2,1,0:T(8,128)(2,1)S(1)} %collective-permute-done.9), channel_id=1, source_target_pairs={{0,7},{1,0},{2,1},{3,2},{4,3},{5,4},{6,5},{7,6},{8,15},{9,8},{10,9... | collective-permute-start | bytes 786440 | tf_op jit(solution)/shard_map/ppermute | solution.py:24
  30.9 4.5 %collective-permute-done.13 = bf16[2,256,256]{2,1,0:T(8,128)(2,1)S(1)} collective-permute-done((bf16[2,256,256]{2,1,0:T(8,128)(2,1)S(1)}, bf16[2,256,256]{2,1,0:T(8,128)(2,1)S(1)}, u32[]{:S(2)}, u32[]{:S(2)}) %collective-permute-start.13) | collective-permute-done | bytes 262176 | tf_op jit(solution)/shard_map/ppermute | solution.py:23
  37.7 3.2 %collective-permute-start.11 = (bf16[2,256,256]{2,1,0:T(8,128)(2,1)}, bf16[2,256,256]{2,1,0:T(8,128)(2,1)}, u32[]{:S(2)}, u32[]{:S(2)}) collective-permute-start(bf16[2,256,256]{2,1,0:T(8,128)(2,1)} %collective-permute-done.10), channel_id=1, source_target_pairs={{0,7},{1,0},{2,1},{3,2},{4,3},{5,4},{6,5},{7,6},{8,15},{9,8},{10,9... | collective-permute-start | bytes 786440 | tf_op jit(solution)/shard_map/ppermute | solution.py:24
  40.9 2.2 %collective-permute-done.14 = bf16[2,256,256]{2,1,0:T(8,128)(2,1)} collective-permute-done((bf16[2,256,256]{2,1,0:T(8,128)(2,1)S(1)}, bf16[2,256,256]{2,1,0:T(8,128)(2,1)}, u32[]{:S(2)}, u32[]{:S(2)}) %collective-permute-start.14) | collective-permute-done | bytes 262176 | tf_op jit(solution)/shard_map/ppermute | solution.py:23
  43.1 6.8 %all-gather.2.cloned.1.call-done = bf16[4,48,64,64]{3,2,1,0:T(8,128)(2,1)} async-done(((bf16[4,3,64,64]{3,2,1,0:T(8,128)(2,1)}), bf16[4,48,64,64]{3,2,1,0:T(8,128)(2,1)}) %all-gather.2.cloned.1.call-update) | async-done | bytes 1572880 | tf_op jit(solution)/shard_map/all_gather | solution.py:97
  49.9 10.3 %shard_map.46 = bf16[4096,256]{1,0:T(8,128)(2,1)S(1)} custom-call(s32[192]{0:T(256)} %reshape.43.dest_ref, bf16[1,4,48,64,64]{4,3,2,1,0:T(8,128)(2,1)} %bitcast.187), custom_call_target="tpu_custom_call" | custom-call | tf_op jit(solution)/shard_map/pallas_call | solution.py:74
  62.1 1.2 fusion.30
  65.0 1.2 fusion.36
  66.2 84.2 %while.12 = (s32[]{:T(128)}, bf16[256,256]{1,0:T(8,128)(2,1)S(1)}, bf16[256,256]{1,0:T(8,128)(2,1)S(1)}, bf16[8,2,256,256]{3,2,1,0:T(8,128)(2,1)S(1)}, s32[]{:T(...) while((s32[]{:T(128)}, bf16[256,256]{1,0:T(8,128)(2,1)S(1)}, ...), condition=%wide.region_2.4_spmd, body=%wide.region_1.3_spmd.sunk | while | flops 537985024 | bytes 17039972 | solution.py:125
  66.3 7.1 %collective-permute-done = bf16[256,256]{1,0:T(8,128)(2,1)S(1)} collective-permute-done((bf16[256,256]{1,0:T(8,128)(2,1)S(1)}, bf16[256,256]{1,0:T(8,128)(2,1)S(1)}, u32[]{:S(2)}, u32[]{:S(2)}) %collective-permute-start) | collective-permute-done | bytes 131104 | tf_op jit(solution)/shard_map/while/body/eval_jaxpr/ppermute | solution.py:28
  73.6 1.9 %collective-permute-start.4 = (bf16[2,256,256]{2,1,0:T(8,128)(2,1)S(1)}, bf16[2,256,256]{2,1,0:T(8,128)(2,1)S(1)}, u32[]{:S(2)}, u32[]{:S(2)}) collective-permute-start(bf16[2,256,256]{2,1,0:T(8,128)(2,1)S(1)} %fusion.112), channel_id=1, source_target_pairs={{0,7},{1,0},{2,1},{3,2},{4,3},{5,4},{6,5},{7,6},{8,15},{9,8},{10,9... | collective-permute-start | bytes 786440 | tf_op jit(solution)/shard_map/while/body/eval_jaxpr/ppermute | solution.py:24
  76.2 5.8 %collective-permute-done.4 = bf16[2,256,256]{2,1,0:T(8,128)(2,1)S(1)} collective-permute-done((bf16[2,256,256]{2,1,0:T(8,128)(2,1)S(1)}, bf16[2,256,256]{2,1,0:T(8,128)(2,1)S(1)}, u32[]{:S(2)}, u32[]{:S(2)}) %collective-permute-start.4) | collective-permute-done | bytes 262176 | tf_op jit(solution)/shard_map/while/body/eval_jaxpr/ppermute | solution.py:24
  81.9 2.3 %collective-permute-start.5 = (bf16[2,256,256]{2,1,0:T(8,128)(2,1)S(1)}, bf16[2,256,256]{2,1,0:T(8,128)(2,1)S(1)}, u32[]{:S(2)}, u32[]{:S(2)}) collective-permute-start(bf16[2,256,256]{2,1,0:T(8,128)(2,1)S(1)} %collective-permute-done.4), channel_id=1, source_target_pairs={{0,7},{1,0},{2,1},{3,2},{4,3},{5,4},{6,5},{7,6},{8,15},{9,8},{10,9... | collective-permute-start | bytes 786440 | tf_op jit(solution)/shard_map/while/body/eval_jaxpr/ppermute | solution.py:24
  84.9 4.3 %collective-permute-done.5 = bf16[2,256,256]{2,1,0:T(8,128)(2,1)S(1)} collective-permute-done((bf16[2,256,256]{2,1,0:T(8,128)(2,1)S(1)}, bf16[2,256,256]{2,1,0:T(8,128)(2,1)S(1)}, u32[]{:S(2)}, u32[]{:S(2)}) %collective-permute-start.5) | collective-permute-done | bytes 262176 | tf_op jit(solution)/shard_map/while/body/eval_jaxpr/ppermute | solution.py:24
  89.2 3.0 %collective-permute-start.6 = (bf16[2,256,256]{2,1,0:T(8,128)(2,1)S(1)}, bf16[2,256,256]{2,1,0:T(8,128)(2,1)S(1)}, u32[]{:S(2)}, u32[]{:S(2)}) collective-permute-start(bf16[2,256,256]{2,1,0:T(8,128)(2,1)S(1)} %collective-permute-done.5), channel_id=1, source_target_pairs={{0,7},{1,0},{2,1},{3,2},{4,3},{5,4},{6,5},{7,6},{8,15},{9,8},{10,9... | collective-permute-start | bytes 786440 | tf_op jit(solution)/shard_map/while/body/eval_jaxpr/ppermute | solution.py:24
  92.8 7.1 %collective-permute-done.3 = bf16[2,256,256]{2,1,0:T(8,128)(2,1)S(1)} collective-permute-done((bf16[2,256,256]{2,1,0:T(8,128)(2,1)S(1)}, bf16[2,256,256]{2,1,0:T(8,128)(2,1)S(1)}, u32[]{:S(2)}, u32[]{:S(2)}) %collective-permute-start.3) | collective-permute-done | bytes 262176 | tf_op jit(solution)/shard_map/while/body/eval_jaxpr/ppermute | solution.py:23
  100.4 7.1 %collective-permute-done.7 = bf16[2,256,256]{2,1,0:T(8,128)(2,1)S(1)} collective-permute-done((bf16[2,256,256]{2,1,0:T(8,128)(2,1)S(1)}, bf16[2,256,256]{2,1,0:T(8,128)(2,1)S(1)}, u32[]{:S(2)}, u32[]{:S(2)}) %collective-permute-start.7) | collective-permute-done | bytes 262176 | tf_op jit(solution)/shard_map/while/body/eval_jaxpr/ppermute | solution.py:28
  107.8 1.8 %collective-permute-start = (bf16[256,256]{1,0:T(8,128)(2,1)S(1)}, bf16[256,256]{1,0:T(8,128)(2,1)S(1)}, u32[]{:S(2)}, u32[]{:S(2)}) collective-permute-start(bf16[256,256]{1,0:T(8,128)(2,1)S(1)} %copy.12), channel_id=1, source_target_pairs={{0,8},{8,0},{1,9},{9,1},{2,10},{10,2},{3,11},{11,3},{4,12},{12,4},... | collective-permute-start | bytes 393224 | tf_op jit(solution)/shard_map/while/body/eval_jaxpr/ppermute | solution.py:28
  109.6 4.8 %collective-permute-done = bf16[256,256]{1,0:T(8,128)(2,1)S(1)} collective-permute-done((bf16[256,256]{1,0:T(8,128)(2,1)S(1)}, bf16[256,256]{1,0:T(8,128)(2,1)S(1)}, u32[]{:S(2)}, u32[]{:S(2)}) %collective-permute-start) | collective-permute-done | bytes 131104 | tf_op jit(solution)/shard_map/while/body/eval_jaxpr/ppermute | solution.py:28
  114.7 2.0 %collective-permute-start.1 = (bf16[2,256,256]{2,1,0:T(8,128)(2,1)S(1)}, bf16[2,256,256]{2,1,0:T(8,128)(2,1)S(1)}, u32[]{:S(2)}, u32[]{:S(2)}) collective-permute-start(bf16[2,256,256]{2,1,0:T(8,128)(2,1)S(1)} %fusion.112), channel_id=1, source_target_pairs={{0,1},{1,2},{2,3},{3,4},{4,5},{5,6},{6,7},{7,0},{8,9},{9,10},{10,1... | collective-permute-start | bytes 786440 | tf_op jit(solution)/shard_map/while/body/eval_jaxpr/ppermute | solution.py:23
  116.9 5.7 %collective-permute-done.4 = bf16[2,256,256]{2,1,0:T(8,128)(2,1)S(1)} collective-permute-done((bf16[2,256,256]{2,1,0:T(8,128)(2,1)S(1)}, bf16[2,256,256]{2,1,0:T(8,128)(2,1)S(1)}, u32[]{:S(2)}, u32[]{:S(2)}) %collective-permute-start.4) | collective-permute-done | bytes 262176 | tf_op jit(solution)/shard_map/while/body/eval_jaxpr/ppermute | solution.py:24
  122.6 2.4 %collective-permute-start.5 = (bf16[2,256,256]{2,1,0:T(8,128)(2,1)S(1)}, bf16[2,256,256]{2,1,0:T(8,128)(2,1)S(1)}, u32[]{:S(2)}, u32[]{:S(2)}) collective-permute-start(bf16[2,256,256]{2,1,0:T(8,128)(2,1)S(1)} %collective-permute-done.4), channel_id=1, source_target_pairs={{0,7},{1,0},{2,1},{3,2},{4,3},{5,4},{6,5},{7,6},{8,15},{9,8},{10,9... | collective-permute-start | bytes 786440 | tf_op jit(solution)/shard_map/while/body/eval_jaxpr/ppermute | solution.py:24
  125.5 5.3 %collective-permute-done.5 = bf16[2,256,256]{2,1,0:T(8,128)(2,1)S(1)} collective-permute-done((bf16[2,256,256]{2,1,0:T(8,128)(2,1)S(1)}, bf16[2,256,256]{2,1,0:T(8,128)(2,1)S(1)}, u32[]{:S(2)}, u32[]{:S(2)}) %collective-permute-start.5) | collective-permute-done | bytes 262176 | tf_op jit(solution)/shard_map/while/body/eval_jaxpr/ppermute | solution.py:24
  130.8 3.7 %collective-permute-start.6 = (bf16[2,256,256]{2,1,0:T(8,128)(2,1)S(1)}, bf16[2,256,256]{2,1,0:T(8,128)(2,1)S(1)}, u32[]{:S(2)}, u32[]{:S(2)}) collective-permute-start(bf16[2,256,256]{2,1,0:T(8,128)(2,1)S(1)} %collective-permute-done.5), channel_id=1, source_target_pairs={{0,7},{1,0},{2,1},{3,2},{4,3},{5,4},{6,5},{7,6},{8,15},{9,8},{10,9... | collective-permute-start | bytes 786440 | tf_op jit(solution)/shard_map/while/body/eval_jaxpr/ppermute | solution.py:24
  134.9 7.6 %collective-permute-done.3 = bf16[2,256,256]{2,1,0:T(8,128)(2,1)S(1)} collective-permute-done((bf16[2,256,256]{2,1,0:T(8,128)(2,1)S(1)}, bf16[2,256,256]{2,1,0:T(8,128)(2,1)S(1)}, u32[]{:S(2)}, u32[]{:S(2)}) %collective-permute-start.3) | collective-permute-done | bytes 262176 | tf_op jit(solution)/shard_map/while/body/eval_jaxpr/ppermute | solution.py:23
  143.0 7.1 %collective-permute-done.7 = bf16[2,256,256]{2,1,0:T(8,128)(2,1)S(1)} collective-permute-done((bf16[2,256,256]{2,1,0:T(8,128)(2,1)S(1)}, bf16[2,256,256]{2,1,0:T(8,128)(2,1)S(1)}, u32[]{:S(2)}, u32[]{:S(2)}) %collective-permute-start.7) | collective-permute-done | bytes 262176 | tf_op jit(solution)/shard_map/while/body/eval_jaxpr/ppermute | solution.py:28
  (73 shorter events, 12.5 us)
Async XLA Ops:
  6.5 43.4 %all-gather.2.cloned.1.call-start = ((), (), s32[]{:S(2)}) async-start(), calls=%async_computation | async-start | bytes 3342336 | tf_op jit(solution)/shard_map/all_gather | solution.py:97
  9.2 6.8 %collective-permute-start.8 = (bf16[256,256]{1,0:T(8,128)(2,1)S(1)}, bf16[256,256]{1,0:T(8,128)(2,1)S(1)}, u32[]{:S(2)}, u32[]{:S(2)}) collective-permute-start(bf16[256,256]{1,0:T(8,128)(2,1)S(1)} %copy.17), channel_id=1, source_target_pairs={{0,8},{8,0},{1,9},{9,1},{2,10},{10,2},{3,11},{11,3},{4,12},{12,4},... | collective-permute-start | bytes 393224 | tf_op jit(solution)/shard_map/ppermute | solution.py:28
  16.2 11.4 %collective-permute-start.12 = (bf16[2,256,256]{2,1,0:T(8,128)(2,1)S(1)}, bf16[2,256,256]{2,1,0:T(8,128)(2,1)S(1)}, u32[]{:S(2)}, u32[]{:S(2)}) collective-permute-start(bf16[2,256,256]{2,1,0:T(8,128)(2,1)S(1)} %fusion.38), channel_id=1, source_target_pairs={{0,1},{1,2},{2,3},{3,4},{4,5},{5,6},{6,7},{7,0},{8,9},{9,10},{10,1... | collective-permute-start | bytes 786440 | tf_op jit(solution)/shard_map/ppermute | solution.py:23
  18.2 9.4 %collective-permute-start.9 = (bf16[2,256,256]{2,1,0:T(8,128)(2,1)S(1)}, bf16[2,256,256]{2,1,0:T(8,128)(2,1)S(1)}, u32[]{:S(2)}, u32[]{:S(2)}) collective-permute-start(bf16[2,256,256]{2,1,0:T(8,128)(2,1)S(1)} %fusion.38), channel_id=1, source_target_pairs={{0,7},{1,0},{2,1},{3,2},{4,3},{5,4},{6,5},{7,6},{8,15},{9,8},{10,9... | collective-permute-start | bytes 786440 | tf_op jit(solution)/shard_map/ppermute | solution.py:24
  27.6 22.3 %copy-start.1 = (bf16[2,256,256]{2,1,0:T(8,128)(2,1)}, bf16[2,256,256]{2,1,0:T(8,128)(2,1)S(1)}, u32[]{:S(2)}) copy-start(bf16[2,256,256]{2,1,0:T(8,128)(2,1)S(1)} %collective-permute-done.12) | copy-start | bytes 786436
  27.6 7.8 %collective-permute-start.13 = (bf16[2,256,256]{2,1,0:T(8,128)(2,1)S(1)}, bf16[2,256,256]{2,1,0:T(8,128)(2,1)S(1)}, u32[]{:S(2)}, u32[]{:S(2)}) collective-permute-start(bf16[2,256,256]{2,1,0:T(8,128)(2,1)S(1)} %collective-permute-done.12), channel_id=1, source_target_pairs={{0,1},{1,2},{2,3},{3,4},{4,5},{5,6},{6,7},{7,0},{8,9},{9,10},{10,1... | collective-permute-start | bytes 786440 | tf_op jit(solution)/shard_map/ppermute | solution.py:23
  27.6 22.3 %copy-start.5 = (bf16[2,256,256]{2,1,0:T(8,128)(2,1)}, bf16[2,256,256]{2,1,0:T(8,128)(2,1)S(1)}, u32[]{:S(2)}) copy-start(bf16[2,256,256]{2,1,0:T(8,128)(2,1)S(1)} %collective-permute-done.9) | copy-start | bytes 786436
  27.6 10.1 %collective-permute-start.10 = (bf16[2,256,256]{2,1,0:T(8,128)(2,1)S(1)}, bf16[2,256,256]{2,1,0:T(8,128)(2,1)}, u32[]{:S(2)}, u32[]{:S(2)}) collective-permute-start(bf16[2,256,256]{2,1,0:T(8,128)(2,1)S(1)} %collective-permute-done.9), channel_id=1, source_target_pairs={{0,7},{1,0},{2,1},{3,2},{4,3},{5,4},{6,5},{7,6},{8,15},{9,8},{10,9... | collective-permute-start | bytes 786440 | tf_op jit(solution)/shard_map/ppermute | solution.py:24
  35.4 14.5 %copy-start.3 = (bf16[2,256,256]{2,1,0:T(8,128)(2,1)}, bf16[2,256,256]{2,1,0:T(8,128)(2,1)S(1)}, u32[]{:S(2)}) copy-start(bf16[2,256,256]{2,1,0:T(8,128)(2,1)S(1)} %collective-permute-done.13) | copy-start | bytes 786436
  35.4 7.7 %collective-permute-start.14 = (bf16[2,256,256]{2,1,0:T(8,128)(2,1)S(1)}, bf16[2,256,256]{2,1,0:T(8,128)(2,1)}, u32[]{:S(2)}, u32[]{:S(2)}) collective-permute-start(bf16[2,256,256]{2,1,0:T(8,128)(2,1)S(1)} %collective-permute-done.13), channel_id=1, source_target_pairs={{0,1},{1,2},{2,3},{3,4},{4,5},{5,6},{6,7},{7,0},{8,9},{9,10},{10,1... | collective-permute-start | bytes 786440 | tf_op jit(solution)/shard_map/ppermute | solution.py:23
  37.7 26.1 %collective-permute-start.11 = (bf16[2,256,256]{2,1,0:T(8,128)(2,1)}, bf16[2,256,256]{2,1,0:T(8,128)(2,1)}, u32[]{:S(2)}, u32[]{:S(2)}) collective-permute-start(bf16[2,256,256]{2,1,0:T(8,128)(2,1)} %collective-permute-done.10), channel_id=1, source_target_pairs={{0,7},{1,0},{2,1},{3,2},{4,3},{5,4},{6,5},{7,6},{8,15},{9,8},{10,9... | collective-permute-start | bytes 786440 | tf_op jit(solution)/shard_map/ppermute | solution.py:24
  43.1 21.9 %collective-permute-start.15 = (bf16[2,256,256]{2,1,0:T(8,128)(2,1)}, bf16[2,256,256]{2,1,0:T(8,128)(2,1)}, u32[]{:S(2)}, u32[]{:S(2)}) collective-permute-start(bf16[2,256,256]{2,1,0:T(8,128)(2,1)} %collective-permute-done.14), channel_id=1, source_target_pairs={{0,1},{1,2},{2,3},{3,4},{4,5},{5,6},{6,7},{7,0},{8,9},{9,10},{10,1... | collective-permute-start | bytes 786440 | tf_op jit(solution)/shard_map/ppermute | solution.py:28
  60.3 1.6 %copy-start.6 = (bf16[2,256,256]{2,1,0:T(8,128)(2,1)S(1)}, bf16[2,256,256]{2,1,0:T(8,128)(2,1)}, u32[]{:S(2)}) copy-start(bf16[2,256,256]{2,1,0:T(8,128)(2,1)} %copy-done.5) | copy-start | bytes 786436
  60.4 2.9 %copy-start.4 = (bf16[2,256,256]{2,1,0:T(8,128)(2,1)S(1)}, bf16[2,256,256]{2,1,0:T(8,128)(2,1)}, u32[]{:S(2)}) copy-start(bf16[2,256,256]{2,1,0:T(8,128)(2,1)} %copy-done.3) | copy-start | bytes 786436
  60.4 3.1 %copy-start.2 = (bf16[2,256,256]{2,1,0:T(8,128)(2,1)S(1)}, bf16[2,256,256]{2,1,0:T(8,128)(2,1)}, u32[]{:S(2)}) copy-start(bf16[2,256,256]{2,1,0:T(8,128)(2,1)} %copy-done.1) | copy-start | bytes 786436
  66.2 7.2 %collective-permute-start = (bf16[256,256]{1,0:T(8,128)(2,1)S(1)}, bf16[256,256]{1,0:T(8,128)(2,1)S(1)}, u32[]{:S(2)}, u32[]{:S(2)}) collective-permute-start(bf16[256,256]{1,0:T(8,128)(2,1)S(1)} %copy.12), channel_id=1, source_target_pairs={{0,8},{8,0},{1,9},{9,1},{2,10},{10,2},{3,11},{11,3},{4,12},{12,4},... | collective-permute-start | bytes 393224 | tf_op jit(solution)/shard_map/while/body/eval_jaxpr/ppermute | solution.py:28
  73.6 8.3 %collective-permute-start.4 = (bf16[2,256,256]{2,1,0:T(8,128)(2,1)S(1)}, bf16[2,256,256]{2,1,0:T(8,128)(2,1)S(1)}, u32[]{:S(2)}, u32[]{:S(2)}) collective-permute-start(bf16[2,256,256]{2,1,0:T(8,128)(2,1)S(1)} %fusion.112), channel_id=1, source_target_pairs={{0,7},{1,0},{2,1},{3,2},{4,3},{5,4},{6,5},{7,6},{8,15},{9,8},{10,9... | collective-permute-start | bytes 786440 | tf_op jit(solution)/shard_map/while/body/eval_jaxpr/ppermute | solution.py:24
  75.5 8.9 %collective-permute-start.1 = (bf16[2,256,256]{2,1,0:T(8,128)(2,1)S(1)}, bf16[2,256,256]{2,1,0:T(8,128)(2,1)S(1)}, u32[]{:S(2)}, u32[]{:S(2)}) collective-permute-start(bf16[2,256,256]{2,1,0:T(8,128)(2,1)S(1)} %fusion.112), channel_id=1, source_target_pairs={{0,1},{1,2},{2,3},{3,4},{4,5},{5,6},{6,7},{7,0},{8,9},{9,10},{10,1... | collective-permute-start | bytes 786440 | tf_op jit(solution)/shard_map/while/body/eval_jaxpr/ppermute | solution.py:23
  81.9 7.3 %collective-permute-start.5 = (bf16[2,256,256]{2,1,0:T(8,128)(2,1)S(1)}, bf16[2,256,256]{2,1,0:T(8,128)(2,1)S(1)}, u32[]{:S(2)}, u32[]{:S(2)}) collective-permute-start(bf16[2,256,256]{2,1,0:T(8,128)(2,1)S(1)} %collective-permute-done.4), channel_id=1, source_target_pairs={{0,7},{1,0},{2,1},{3,2},{4,3},{5,4},{6,5},{7,6},{8,15},{9,8},{10,9... | collective-permute-start | bytes 786440 | tf_op jit(solution)/shard_map/while/body/eval_jaxpr/ppermute | solution.py:24
  84.4 7.9 %collective-permute-start.2 = (bf16[2,256,256]{2,1,0:T(8,128)(2,1)S(1)}, bf16[2,256,256]{2,1,0:T(8,128)(2,1)S(1)}, u32[]{:S(2)}, u32[]{:S(2)}) collective-permute-start(bf16[2,256,256]{2,1,0:T(8,128)(2,1)S(1)} %collective-permute-done.1), channel_id=1, source_target_pairs={{0,1},{1,2},{2,3},{3,4},{4,5},{5,6},{6,7},{7,0},{8,9},{9,10},{10,1... | collective-permute-start | bytes 786440 | tf_op jit(solution)/shard_map/while/body/eval_jaxpr/ppermute | solution.py:23
  89.2 11.0 %collective-permute-start.6 = (bf16[2,256,256]{2,1,0:T(8,128)(2,1)S(1)}, bf16[2,256,256]{2,1,0:T(8,128)(2,1)S(1)}, u32[]{:S(2)}, u32[]{:S(2)}) collective-permute-start(bf16[2,256,256]{2,1,0:T(8,128)(2,1)S(1)} %collective-permute-done.5), channel_id=1, source_target_pairs={{0,7},{1,0},{2,1},{3,2},{4,3},{5,4},{6,5},{7,6},{8,15},{9,8},{10,9... | collective-permute-start | bytes 786440 | tf_op jit(solution)/shard_map/while/body/eval_jaxpr/ppermute | solution.py:24
  92.3 7.6 %collective-permute-start.3 = (bf16[2,256,256]{2,1,0:T(8,128)(2,1)S(1)}, bf16[2,256,256]{2,1,0:T(8,128)(2,1)S(1)}, u32[]{:S(2)}, u32[]{:S(2)}) collective-permute-start(bf16[2,256,256]{2,1,0:T(8,128)(2,1)S(1)} %collective-permute-done.2), channel_id=1, source_target_pairs={{0,1},{1,2},{2,3},{3,4},{4,5},{5,6},{6,7},{7,0},{8,9},{9,10},{10,1... | collective-permute-start | bytes 786440 | tf_op jit(solution)/shard_map/while/body/eval_jaxpr/ppermute | solution.py:23
  99.9 7.6 %collective-permute-start.7 = (bf16[2,256,256]{2,1,0:T(8,128)(2,1)S(1)}, bf16[2,256,256]{2,1,0:T(8,128)(2,1)S(1)}, u32[]{:S(2)}, u32[]{:S(2)}) collective-permute-start(bf16[2,256,256]{2,1,0:T(8,128)(2,1)S(1)} %collective-permute-done.3), channel_id=1, source_target_pairs={{0,1},{1,2},{2,3},{3,4},{4,5},{5,6},{6,7},{7,0},{8,9},{9,10},{10,1... | collective-permute-start | bytes 786440 | tf_op jit(solution)/shard_map/while/body/eval_jaxpr/ppermute | solution.py:28
  107.8 6.6 %collective-permute-start = (bf16[256,256]{1,0:T(8,128)(2,1)S(1)}, bf16[256,256]{1,0:T(8,128)(2,1)S(1)}, u32[]{:S(2)}, u32[]{:S(2)}) collective-permute-start(bf16[256,256]{1,0:T(8,128)(2,1)S(1)} %copy.12), channel_id=1, source_target_pairs={{0,8},{8,0},{1,9},{9,1},{2,10},{10,2},{3,11},{11,3},{4,12},{12,4},... | collective-permute-start | bytes 393224 | tf_op jit(solution)/shard_map/while/body/eval_jaxpr/ppermute | solution.py:28
  114.6 8.0 %collective-permute-start.4 = (bf16[2,256,256]{2,1,0:T(8,128)(2,1)S(1)}, bf16[2,256,256]{2,1,0:T(8,128)(2,1)S(1)}, u32[]{:S(2)}, u32[]{:S(2)}) collective-permute-start(bf16[2,256,256]{2,1,0:T(8,128)(2,1)S(1)} %fusion.112), channel_id=1, source_target_pairs={{0,7},{1,0},{2,1},{3,2},{4,3},{5,4},{6,5},{7,6},{8,15},{9,8},{10,9... | collective-permute-start | bytes 786440 | tf_op jit(solution)/shard_map/while/body/eval_jaxpr/ppermute | solution.py:24
  114.7 10.3 %collective-permute-start.1 = (bf16[2,256,256]{2,1,0:T(8,128)(2,1)S(1)}, bf16[2,256,256]{2,1,0:T(8,128)(2,1)S(1)}, u32[]{:S(2)}, u32[]{:S(2)}) collective-permute-start(bf16[2,256,256]{2,1,0:T(8,128)(2,1)S(1)} %fusion.112), channel_id=1, source_target_pairs={{0,1},{1,2},{2,3},{3,4},{4,5},{5,6},{6,7},{7,0},{8,9},{9,10},{10,1... | collective-permute-start | bytes 786440 | tf_op jit(solution)/shard_map/while/body/eval_jaxpr/ppermute | solution.py:23
  122.6 8.2 %collective-permute-start.5 = (bf16[2,256,256]{2,1,0:T(8,128)(2,1)S(1)}, bf16[2,256,256]{2,1,0:T(8,128)(2,1)S(1)}, u32[]{:S(2)}, u32[]{:S(2)}) collective-permute-start(bf16[2,256,256]{2,1,0:T(8,128)(2,1)S(1)} %collective-permute-done.4), channel_id=1, source_target_pairs={{0,7},{1,0},{2,1},{3,2},{4,3},{5,4},{6,5},{7,6},{8,15},{9,8},{10,9... | collective-permute-start | bytes 786440 | tf_op jit(solution)/shard_map/while/body/eval_jaxpr/ppermute | solution.py:24
  125.0 9.5 %collective-permute-start.2 = (bf16[2,256,256]{2,1,0:T(8,128)(2,1)S(1)}, bf16[2,256,256]{2,1,0:T(8,128)(2,1)S(1)}, u32[]{:S(2)}, u32[]{:S(2)}) collective-permute-start(bf16[2,256,256]{2,1,0:T(8,128)(2,1)S(1)} %collective-permute-done.1), channel_id=1, source_target_pairs={{0,1},{1,2},{2,3},{3,4},{4,5},{5,6},{6,7},{7,0},{8,9},{9,10},{10,1... | collective-permute-start | bytes 786440 | tf_op jit(solution)/shard_map/while/body/eval_jaxpr/ppermute | solution.py:23
  130.8 12.0 %collective-permute-start.6 = (bf16[2,256,256]{2,1,0:T(8,128)(2,1)S(1)}, bf16[2,256,256]{2,1,0:T(8,128)(2,1)S(1)}, u32[]{:S(2)}, u32[]{:S(2)}) collective-permute-start(bf16[2,256,256]{2,1,0:T(8,128)(2,1)S(1)} %collective-permute-done.5), channel_id=1, source_target_pairs={{0,7},{1,0},{2,1},{3,2},{4,3},{5,4},{6,5},{7,6},{8,15},{9,8},{10,9... | collective-permute-start | bytes 786440 | tf_op jit(solution)/shard_map/while/body/eval_jaxpr/ppermute | solution.py:24
  134.5 8.1 %collective-permute-start.3 = (bf16[2,256,256]{2,1,0:T(8,128)(2,1)S(1)}, bf16[2,256,256]{2,1,0:T(8,128)(2,1)S(1)}, u32[]{:S(2)}, u32[]{:S(2)}) collective-permute-start(bf16[2,256,256]{2,1,0:T(8,128)(2,1)S(1)} %collective-permute-done.2), channel_id=1, source_target_pairs={{0,1},{1,2},{2,3},{3,4},{4,5},{5,6},{6,7},{7,0},{8,9},{9,10},{10,1... | collective-permute-start | bytes 786440 | tf_op jit(solution)/shard_map/while/body/eval_jaxpr/ppermute | solution.py:23
  142.5 7.6 %collective-permute-start.7 = (bf16[2,256,256]{2,1,0:T(8,128)(2,1)S(1)}, bf16[2,256,256]{2,1,0:T(8,128)(2,1)S(1)}, u32[]{:S(2)}, u32[]{:S(2)}) collective-permute-start(bf16[2,256,256]{2,1,0:T(8,128)(2,1)S(1)} %collective-permute-done.3), channel_id=1, source_target_pairs={{0,1},{1,2},{2,3},{3,4},{4,5},{5,6},{6,7},{7,0},{8,9},{9,10},{10,1... | collective-permute-start | bytes 786440 | tf_op jit(solution)/shard_map/while/body/eval_jaxpr/ppermute | solution.py:28
  150.4 0.7 copy-start
Sparse Core Ops, SparseCore 0:
  9.3 40.5 all-gather.1

commit v8 on v5

--- a/solution.py
+++ b/solution.py
@@ -100,24 +100,29 @@
     live_counts = jnp.sum(jnp.where(region_match, density[None, :], 0), axis=1)
     live_mask = jnp.arange(slot_count, dtype=jnp.int32)[None, :] < live_counts[:, None]
 
-    tiles = lax.all_gather(jnp.swapaxes(block_tiles, 2, 3), ROW_AXES, axis=1, tiled=True)[None]
-    ring_neighbours = neighbours
-    ring_live = live_mask
+    tiles_t = jnp.swapaxes(block_tiles, 2, 3)
     per_col = block_rows
-    owner = ring_neighbours // per_col
+    owner = neighbours // per_col
     offset = (owner % z_count - lax.axis_index("z")) % z_count
-    target = (offset * y_count + owner // z_count) * per_col + ring_neighbours % per_col
-    dest = jnp.where(ring_live, target, -1)
-    dense = place_tiles(dest, tiles, total_blocks)
-    dense = dense.reshape(z_count, y_count, local_width, local_width)
+    target = (offset * y_count + owner // z_count) * per_col + neighbours % per_col
+    dest = jnp.where(live_mask, target, -1)
+    half = block_rows // 2
+    denses = []
+    for lo, hi in ((0, half), (half, block_rows)):
+        tiles = lax.all_gather(tiles_t[lo:hi], ROW_AXES, axis=1, tiled=True)[None]
+        dense = place_tiles(dest[lo:hi], tiles, total_blocks)
+        denses.append(dense.reshape(z_count, y_count, local_width, (hi - lo) * block_size))
 
     def apply_hamiltonian(field):
         blocks = gather_col(field, y_count, z_count)
-        total = None
-        for d, chunk in enumerate(blocks):
-            part = jnp.einsum("ymj,yjo->mo", chunk, dense[d], preferred_element_type=jnp.float32)
-            total = part if total is None else total + part
-        return total
+        totals = []
+        for dense in denses:
+            total = None
+            for d, chunk in enumerate(blocks):
+                part = jnp.einsum("ymj,yjo->mo", chunk, dense[d], preferred_element_type=jnp.float32)
+                total = part if total is None else total + part
+            totals.append(total)
+        return jnp.concatenate(totals, axis=1)
 
     previous = coeffs
     current = apply_hamiltonian(coeffs).astype(jnp.bfloat16)

time: 153 us -> 203 us (1.33)
  blocking collectives: 0 us -> 51.8 us
  between operations: 13.7 us -> 0.33 us
  waiting for transfers between devices: 64.7 us -> 57.1 us
  Pallas kernels: 7.34 us -> 13.8 us
  matrix products: 6.49 us -> 10.9 us
  local copies, waits for them, and re-layouts: 4.72 us -> 8.97 us
    all_gather x0 -> x2, blocking collectives: none -> 51.8 us  [body(): tiles = lax.all_gather(tiles_t[lo:hi], ROW_AXES, axis=1, tiled=True)[None]]
    ppermute x9, waiting for transfers between devices: 12 us -> 38.8 us  [ring_blocks(): right = lax.ppermute(right, axis, fwd)]
    ppermute x9, waiting for transfers between devices: 26.6 us -> 5.61 us  [ring_blocks(): left = lax.ppermute(left, axis, bwd)]
    pallas_call x1 -> x2, Pallas kernels: 7.34 us -> 13.8 us  [place_tiles(): pl.pallas_call(kernel, out_shape=jax.ShapeDtypeStruct((rows * size, block...]
    ppermute x3, waiting for transfers between devices: 10.9 us -> 5.91 us  [ring_blocks(): blocks[1] = lax.ppermute(piece, axis, fwd)]
    dot_general x24 -> x48, matrix products: 6.49 us -> 10.9 us  [apply_hamiltonian(): jnp.einsum('ymj,yjo->mo', chunk, dense[d], preferred_element_type=jnp.flo...]
    ppermute x3, waiting for transfers between devices: 4.36 us -> 0.01 us  [ring_blocks(): lax.ppermute(lax.slice_in_dim(left, split, None, axis=split_dim), axis, bwd)]
    ppermute x9, starting transfers between devices: 26.3 us -> 30.4 us  [ring_blocks(): left = lax.ppermute(left, axis, bwd)]
  transfers between devices with their start and end apart: 28 -> 27, of which waited for: 17 -> 14; matrix products, arithmetic and copies ran while one was open for 4% -> 8% of each run, Pallas kernels for 5% -> 7%
where the time goes in v8:
time: 203 us; the launch traced here: 200 us
  waiting for transfers between devices  57.1 us (28%)
  starting transfers between devices  53.4 us (26%)
  blocking collectives  51.8 us (26%)
  Pallas kernels  13.8 us (7%)
  matrix products  10.9 us (5%)
  local copies, waits for them, and re-layouts  8.97 us (4%)
  other arithmetic  3.33 us (2%)
    all_gather x2, blocking collectives, body(): tiles = lax.all_gather(tiles_t[lo:hi], ROW_AXES, axis=1, tiled=True)[None]  51.8 us
    ppermute x9, waiting for transfers between devices, ring_blocks(): right = lax.ppermute(right, axis, fwd)  38.8 us
    ppermute x9, starting transfers between devices, ring_blocks(): left = lax.ppermute(left, axis, bwd)  30.4 us
    pallas_call x2, Pallas kernels, place_tiles(): pl.pallas_call(kernel, out_shape=jax.ShapeDtypeStruct((rows * size, block...  13.8 us
    ppermute x3, starting transfers between devices, ring_blocks(): blocks[1] = lax.ppermute(piece, axis, fwd)  12.3 us
    dot_general x48, matrix products, apply_hamiltonian(): jnp.einsum('ymj,yjo->mo', chunk, dense[d], preferred_element_type=jnp.flo...  10.9 us
    ppermute x3, starting transfers between devices, ring_blocks(): lax.ppermute(lax.slice_in_dim(left, split, None, axis=split_dim), axis, bwd)  10.3 us
    ppermute x3, waiting for transfers between devices, ring_blocks(): lax.ppermute(lax.slice_in_dim(right, 0, split, axis=split_dim), axis, fwd)  6.73 us
  transfers between devices with their start and end apart: 27, of which 14 were waited for; matrix products, arithmetic and copies ran while one was open for 8% of the time, Pallas kernels for 7%

profile of v8, /device:TPU:2, one launch (start us, length us, event | category | flops | bytes accessed | tf_op | source)
XLA Modules:
  0.0 200.2 jit_solution(15115606397500694656)
XLA Ops:
  0.9 3.2 %collective-permute-start.9 = (bf16[256,256]{1,0:T(8,128)(2,1)S(1)}, bf16[256,256]{1,0:T(8,128)(2,1)}, u32[]{:S(2)}, u32[]{:S(2)}) collective-permute-start(bf16[256,256]{1,0:T(8,128)(2,1)S(1)} %copy.85), channel_id=1, source_target_pairs={{0,8},{8,0},{1,9},{9,1},{2,10},{10,2},{3,11},{11,3},{4,12},{12,4},... | collective-permute-start | bytes 393224 | tf_op jit(solution)/shard_map/ppermute | solution.py:29
  7.4 25.9 %all_gather.6 = bf16[2,48,64,64]{3,2,1,0:T(8,128)(2,1)} all-gather(bf16[2,3,64,64]{3,2,1,0:T(8,128)(2,1)S(1)} %get-tuple-element.80), channel_id=1, replica_groups=mesh['x'=4,'y_lo'=2,'core'=2,'y_hi'=2,'z'=8] {'x','y_lo','core'}, dimensions={1}, use_global_device_ids=true | all-gather | bytes 835584 | tf_op jit(solution)/shard_map/all_gather | solution.py:112
  33.3 6.4 %shard_map.46 = bf16[4096,128]{1,0:T(8,128)(2,1)} custom-call(s32[96]{0:T(128)} %reshape.65.dest_ref, bf16[1,2,48,64,64]{4,3,2,1,0:T(8,128)(2,1)} %bitcast.350), custom_call_target="tpu_custom_call" | custom-call | tf_op jit(solution)/shard_map/pallas_call | solution.py:80
  42.6 25.9 %all_gather.7 = bf16[2,48,64,64]{3,2,1,0:T(8,128)(2,1)} all-gather(bf16[2,3,64,64]{3,2,1,0:T(8,128)(2,1)S(1)} %get-tuple-element.81), channel_id=1, replica_groups=mesh['x'=4,'y_lo'=2,'core'=2,'y_hi'=2,'z'=8] {'x','y_lo','core'}, dimensions={1}, use_global_device_ids=true | all-gather | bytes 835584 | tf_op jit(solution)/shard_map/all_gather | solution.py:112
  69.1 7.4 %shard_map.47 = bf16[4096,128]{1,0:T(8,128)(2,1)} custom-call(s32[96]{0:T(128)} %reshape.66.dest_ref, bf16[1,2,48,64,64]{4,3,2,1,0:T(8,128)(2,1)} %bitcast.349), custom_call_target="tpu_custom_call" | custom-call | tf_op jit(solution)/shard_map/pallas_call | solution.py:80
  79.5 3.0 %collective-permute-start.10 = (bf16[2,256,256]{2,1,0:T(8,128)(2,1)S(1)}, bf16[2,256,256]{2,1,0:T(8,128)(2,1)S(1)}, u32[]{:S(2)}, u32[]{:S(2)}) collective-permute-start(bf16[2,256,256]{2,1,0:T(8,128)(2,1)S(1)} %fusion.68), channel_id=1, source_target_pairs={{0,7},{1,0},{2,1},{3,2},{4,3},{5,4},{6,5},{7,6},{8,15},{9,8},{10,9... | collective-permute-start | bytes 786440 | tf_op jit(solution)/shard_map/ppermute | solution.py:24
  82.9 5.6 %collective-permute-done.10 = bf16[2,256,256]{2,1,0:T(8,128)(2,1)S(1)} collective-permute-done((bf16[2,256,256]{2,1,0:T(8,128)(2,1)S(1)}, bf16[2,256,256]{2,1,0:T(8,128)(2,1)S(1)}, u32[]{:S(2)}, u32[]{:S(2)}) %collective-permute-start.10) | collective-permute-done | bytes 262176 | tf_op jit(solution)/shard_map/ppermute | solution.py:24
  88.5 3.7 %collective-permute-start.11 = (bf16[2,256,256]{2,1,0:T(8,128)(2,1)S(1)}, bf16[2,256,256]{2,1,0:T(8,128)(2,1)S(1)}, u32[]{:S(2)}, u32[]{:S(2)}) collective-permute-start(bf16[2,256,256]{2,1,0:T(8,128)(2,1)S(1)} %collective-permute-done.10), channel_id=1, source_target_pairs={{0,7},{1,0},{2,1},{3,2},{4,3},{5,4},{6,5},{7,6},{8,15},{9,8},{10,9... | collective-permute-start | bytes 786440 | tf_op jit(solution)/shard_map/ppermute | solution.py:24
  93.2 7.6 %collective-permute-done.14 = bf16[2,256,256]{2,1,0:T(8,128)(2,1)S(1)} collective-permute-done((bf16[2,256,256]{2,1,0:T(8,128)(2,1)S(1)}, bf16[2,256,256]{2,1,0:T(8,128)(2,1)S(1)}, u32[]{:S(2)}, u32[]{:S(2)}) %collective-permute-start.14) | collective-permute-done | bytes 262176 | tf_op jit(solution)/shard_map/ppermute | solution.py:23
  100.9 3.2 %collective-permute-start.12 = (bf16[2,256,256]{2,1,0:T(8,128)(2,1)S(1)}, bf16[2,256,256]{2,1,0:T(8,128)(2,1)S(1)}, u32[]{:S(2)}, u32[]{:S(2)}) collective-permute-start(bf16[2,256,256]{2,1,0:T(8,128)(2,1)S(1)} %collective-permute-done.11), channel_id=1, source_target_pairs={{0,7},{1,0},{2,1},{3,2},{4,3},{5,4},{6,5},{7,6},{8,15},{9,8},{10,9... | collective-permute-start | bytes 786440 | tf_op jit(solution)/shard_map/ppermute | solution.py:24
  105.1 3.6 %collective-permute-done.15 = bf16[2,256,256]{2,1,0:T(8,128)(2,1)S(1)} collective-permute-done((bf16[2,256,256]{2,1,0:T(8,128)(2,1)S(1)}, bf16[2,256,256]{2,1,0:T(8,128)(2,1)S(1)}, u32[]{:S(2)}, u32[]{:S(2)}) %collective-permute-start.15) | collective-permute-done | bytes 262176 | tf_op jit(solution)/shard_map/ppermute | solution.py:23
  108.8 3.5 %collective-permute-start.17 = (bf16[1,256,256]{2,1,0:T(8,128)(2,1)S(1)}, bf16[1,256,256]{2,1,0:T(8,128)(2,1)S(1)}, u32[]{:S(2)}, u32[]{:S(2)}) collective-permute-start(bf16[1,256,256]{2,1,0:T(8,128)(2,1)S(1)} %slice.166), channel_id=1, source_target_pairs={{0,7},{1,0},{2,1},{3,2},{4,3},{5,4},{6,5},{7,6},{8,15},{9,8},{10,9... | collective-permute-start | bytes 393224 | tf_op jit(solution)/shard_map/ppermute | solution.py:33
  116.0 83.5 %while.12 = (s32[]{:T(128)}, bf16[256,256]{1,0:T(8,128)(2,1)S(1)}, bf16[256,256]{0,1:T(8,128)(2,1)S(1)}, bf16[8,2,256,128]{2,3,1,0:T(8,128)(2,1)S(1)}, bf16[8,2,...) while((s32[]{:T(128)}, bf16[256,256]{1,0:T(8,128)(2,1)S(1)}, ...), condition=%wide.region_2.4_spmd, body=%wide.region_1.3_spmd.sunk | while | flops 538050560 | bytes 20972180 | solution.py:136
  116.1 5.8 %collective-permute-start = (bf16[256,256]{1,0:T(8,128)(2,1)S(1)}, bf16[256,256]{1,0:T(8,128)(2,1)S(1)}, u32[]{:S(2)}, u32[]{:S(2)}) collective-permute-start(bf16[256,256]{1,0:T(8,128)(2,1)S(1)} %copy.71), channel_id=1, source_target_pairs={{0,8},{8,0},{1,9},{9,1},{2,10},{10,2},{3,11},{11,3},{4,12},{12,4},... | collective-permute-start | bytes 393224 | tf_op jit(solution)/shard_map/while/body/eval_jaxpr/ppermute | solution.py:29
  122.0 2.8 %collective-permute-done = bf16[256,256]{1,0:T(8,128)(2,1)S(1)} collective-permute-done((bf16[256,256]{1,0:T(8,128)(2,1)S(1)}, bf16[256,256]{1,0:T(8,128)(2,1)S(1)}, u32[]{:S(2)}, u32[]{:S(2)}) %collective-permute-start) | collective-permute-done | bytes 131104 | tf_op jit(solution)/shard_map/while/body/eval_jaxpr/ppermute | solution.py:29
  125.1 3.6 %collective-permute-start.5 = (bf16[2,256,256]{2,1,0:T(8,128)(2,1)S(1)}, bf16[2,256,256]{2,1,0:T(8,128)(2,1)S(1)}, u32[]{:S(2)}, u32[]{:S(2)}) collective-permute-start(bf16[2,256,256]{2,1,0:T(8,128)(2,1)S(1)} %fusion.204), channel_id=1, source_target_pairs={{0,7},{1,0},{2,1},{3,2},{4,3},{5,4},{6,5},{7,6},{8,15},{9,8},{10,9... | collective-permute-start | bytes 786440 | tf_op jit(solution)/shard_map/while/body/eval_jaxpr/ppermute | solution.py:24
  129.1 5.7 %collective-permute-done.1 = bf16[2,256,256]{2,1,0:T(8,128)(2,1)S(1)} collective-permute-done((bf16[2,256,256]{2,1,0:T(8,128)(2,1)S(1)}, bf16[2,256,256]{2,1,0:T(8,128)(2,1)S(1)}, u32[]{:S(2)}, u32[]{:S(2)}) %collective-permute-start.1) | collective-permute-done | bytes 262176 | tf_op jit(solution)/shard_map/while/body/eval_jaxpr/ppermute | solution.py:23
  134.8 3.6 %collective-permute-start.6 = (bf16[2,256,256]{2,1,0:T(8,128)(2,1)S(1)}, bf16[2,256,256]{2,1,0:T(8,128)(2,1)S(1)}, u32[]{:S(2)}, u32[]{:S(2)}) collective-permute-start(bf16[2,256,256]{2,1,0:T(8,128)(2,1)S(1)} %collective-permute-done.5), channel_id=1, source_target_pairs={{0,7},{1,0},{2,1},{3,2},{4,3},{5,4},{6,5},{7,6},{8,15},{9,8},{10,9... | collective-permute-start | bytes 786440 | tf_op jit(solution)/shard_map/while/body/eval_jaxpr/ppermute | solution.py:24
  139.3 5.7 %collective-permute-done.2 = bf16[2,256,256]{2,1,0:T(8,128)(2,1)S(1)} collective-permute-done((bf16[2,256,256]{2,1,0:T(8,128)(2,1)S(1)}, bf16[2,256,256]{2,1,0:T(8,128)(2,1)S(1)}, u32[]{:S(2)}, u32[]{:S(2)}) %collective-permute-start.2) | collective-permute-done | bytes 262176 | tf_op jit(solution)/shard_map/while/body/eval_jaxpr/ppermute | solution.py:23
  145.2 3.3 %collective-permute-start.7 = (bf16[2,256,256]{2,1,0:T(8,128)(2,1)S(1)}, bf16[2,256,256]{2,1,0:T(8,128)(2,1)S(1)}, u32[]{:S(2)}, u32[]{:S(2)}) collective-permute-start(bf16[2,256,256]{2,1,0:T(8,128)(2,1)S(1)} %collective-permute-done.6), channel_id=1, source_target_pairs={{0,7},{1,0},{2,1},{3,2},{4,3},{5,4},{6,5},{7,6},{8,15},{9,8},{10,9... | collective-permute-start | bytes 786440 | tf_op jit(solution)/shard_map/while/body/eval_jaxpr/ppermute | solution.py:24
  149.2 3.8 %collective-permute-done.3 = bf16[2,256,256]{2,1,0:T(8,128)(2,1)S(1)} collective-permute-done((bf16[2,256,256]{2,1,0:T(8,128)(2,1)S(1)}, bf16[2,256,256]{2,1,0:T(8,128)(2,1)S(1)}, u32[]{:S(2)}, u32[]{:S(2)}) %collective-permute-start.3) | collective-permute-done | bytes 262176 | tf_op jit(solution)/shard_map/while/body/eval_jaxpr/ppermute | solution.py:23
  153.1 3.3 %collective-permute-start.8 = (bf16[1,256,256]{2,1,0:T(8,128)(2,1)S(1)}, bf16[1,256,256]{2,1,0:T(8,128)(2,1)S(1)}, u32[]{:S(2)}, u32[]{:S(2)}) collective-permute-start(bf16[1,256,256]{2,1,0:T(8,128)(2,1)S(1)} %slice.299), channel_id=1, source_target_pairs={{0,7},{1,0},{2,1},{3,2},{4,3},{5,4},{6,5},{7,6},{8,15},{9,8},{10,9... | collective-permute-start | bytes 393224 | tf_op jit(solution)/shard_map/while/body/eval_jaxpr/ppermute | solution.py:33
  156.9 2.4 %collective-permute-done.4 = bf16[1,256,256]{2,1,0:T(8,128)(2,1)S(1)} collective-permute-done((bf16[1,256,256]{2,1,0:T(8,128)(2,1)S(1)}, bf16[1,256,256]{2,1,0:T(8,128)(2,1)S(1)}, u32[]{:S(2)}, u32[]{:S(2)}) %collective-permute-start.4) | collective-permute-done | bytes 131104 | tf_op jit(solution)/shard_map/while/body/eval_jaxpr/ppermute | solution.py:32
  160.4 3.3 %collective-permute-start = (bf16[256,256]{1,0:T(8,128)(2,1)S(1)}, bf16[256,256]{1,0:T(8,128)(2,1)S(1)}, u32[]{:S(2)}, u32[]{:S(2)}) collective-permute-start(bf16[256,256]{1,0:T(8,128)(2,1)S(1)} %copy.71), channel_id=1, source_target_pairs={{0,8},{8,0},{1,9},{9,1},{2,10},{10,2},{3,11},{11,3},{4,12},{12,4},... | collective-permute-start | bytes 393224 | tf_op jit(solution)/shard_map/while/body/eval_jaxpr/ppermute | solution.py:29
  163.9 3.1 %collective-permute-done = bf16[256,256]{1,0:T(8,128)(2,1)S(1)} collective-permute-done((bf16[256,256]{1,0:T(8,128)(2,1)S(1)}, bf16[256,256]{1,0:T(8,128)(2,1)S(1)}, u32[]{:S(2)}, u32[]{:S(2)}) %collective-permute-start) | collective-permute-done | bytes 131104 | tf_op jit(solution)/shard_map/while/body/eval_jaxpr/ppermute | solution.py:29
  167.3 3.4 %collective-permute-start.5 = (bf16[2,256,256]{2,1,0:T(8,128)(2,1)S(1)}, bf16[2,256,256]{2,1,0:T(8,128)(2,1)S(1)}, u32[]{:S(2)}, u32[]{:S(2)}) collective-permute-start(bf16[2,256,256]{2,1,0:T(8,128)(2,1)S(1)} %fusion.204), channel_id=1, source_target_pairs={{0,7},{1,0},{2,1},{3,2},{4,3},{5,4},{6,5},{7,6},{8,15},{9,8},{10,9... | collective-permute-start | bytes 786440 | tf_op jit(solution)/shard_map/while/body/eval_jaxpr/ppermute | solution.py:24
  171.1 4.5 %collective-permute-done.1 = bf16[2,256,256]{2,1,0:T(8,128)(2,1)S(1)} collective-permute-done((bf16[2,256,256]{2,1,0:T(8,128)(2,1)S(1)}, bf16[2,256,256]{2,1,0:T(8,128)(2,1)S(1)}, u32[]{:S(2)}, u32[]{:S(2)}) %collective-permute-start.1) | collective-permute-done | bytes 262176 | tf_op jit(solution)/shard_map/while/body/eval_jaxpr/ppermute | solution.py:23
  175.6 3.4 %collective-permute-start.6 = (bf16[2,256,256]{2,1,0:T(8,128)(2,1)S(1)}, bf16[2,256,256]{2,1,0:T(8,128)(2,1)S(1)}, u32[]{:S(2)}, u32[]{:S(2)}) collective-permute-start(bf16[2,256,256]{2,1,0:T(8,128)(2,1)S(1)} %collective-permute-done.5), channel_id=1, source_target_pairs={{0,7},{1,0},{2,1},{3,2},{4,3},{5,4},{6,5},{7,6},{8,15},{9,8},{10,9... | collective-permute-start | bytes 786440 | tf_op jit(solution)/shard_map/while/body/eval_jaxpr/ppermute | solution.py:24
  179.9 4.7 %collective-permute-done.2 = bf16[2,256,256]{2,1,0:T(8,128)(2,1)S(1)} collective-permute-done((bf16[2,256,256]{2,1,0:T(8,128)(2,1)S(1)}, bf16[2,256,256]{2,1,0:T(8,128)(2,1)S(1)}, u32[]{:S(2)}, u32[]{:S(2)}) %collective-permute-start.2) | collective-permute-done | bytes 262176 | tf_op jit(solution)/shard_map/while/body/eval_jaxpr/ppermute | solution.py:23
  184.8 3.3 %collective-permute-start.7 = (bf16[2,256,256]{2,1,0:T(8,128)(2,1)S(1)}, bf16[2,256,256]{2,1,0:T(8,128)(2,1)S(1)}, u32[]{:S(2)}, u32[]{:S(2)}) collective-permute-start(bf16[2,256,256]{2,1,0:T(8,128)(2,1)S(1)} %collective-permute-done.6), channel_id=1, source_target_pairs={{0,7},{1,0},{2,1},{3,2},{4,3},{5,4},{6,5},{7,6},{8,15},{9,8},{10,9... | collective-permute-start | bytes 786440 | tf_op jit(solution)/shard_map/while/body/eval_jaxpr/ppermute | solution.py:24
  188.8 3.3 %collective-permute-done.3 = bf16[2,256,256]{2,1,0:T(8,128)(2,1)S(1)} collective-permute-done((bf16[2,256,256]{2,1,0:T(8,128)(2,1)S(1)}, bf16[2,256,256]{2,1,0:T(8,128)(2,1)S(1)}, u32[]{:S(2)}, u32[]{:S(2)}) %collective-permute-start.3) | collective-permute-done | bytes 262176 | tf_op jit(solution)/shard_map/while/body/eval_jaxpr/ppermute | solution.py:23
  192.3 3.5 %collective-permute-start.8 = (bf16[1,256,256]{2,1,0:T(8,128)(2,1)S(1)}, bf16[1,256,256]{2,1,0:T(8,128)(2,1)S(1)}, u32[]{:S(2)}, u32[]{:S(2)}) collective-permute-start(bf16[1,256,256]{2,1,0:T(8,128)(2,1)S(1)} %slice.299), channel_id=1, source_target_pairs={{0,7},{1,0},{2,1},{3,2},{4,3},{5,4},{6,5},{7,6},{8,15},{9,8},{10,9... | collective-permute-start | bytes 393224 | tf_op jit(solution)/shard_map/while/body/eval_jaxpr/ppermute | solution.py:33
  (129 shorter events, 28.0 us)
Async XLA Ops:
  0.9 77.3 %collective-permute-start.9 = (bf16[256,256]{1,0:T(8,128)(2,1)S(1)}, bf16[256,256]{1,0:T(8,128)(2,1)}, u32[]{:S(2)}, u32[]{:S(2)}) collective-permute-start(bf16[256,256]{1,0:T(8,128)(2,1)S(1)} %copy.85), channel_id=1, source_target_pairs={{0,8},{8,0},{1,9},{9,1},{2,10},{10,2},{3,11},{11,3},{4,12},{12,4},... | collective-permute-start | bytes 393224 | tf_op jit(solution)/shard_map/ppermute | solution.py:29
  39.7 28.8 %copy-start = (bf16[4096,128]{1,0:T(8,128)(2,1)S(1)}, bf16[4096,128]{1,0:T(8,128)(2,1)}, u32[]{:S(2)}) copy-start(bf16[4096,128]{1,0:T(8,128)(2,1)} %shard_map.46) | copy-start | bytes 3145732
  78.1 14.1 %copy-start.6 = (bf16[512,128]{1,0:T(8,128)(2,1)S(1)}, bf16[512,128]{1,0:T(8,128)(2,1)}, u32[]{:S(2)}) copy-start(bf16[512,128]{1,0:T(8,128)(2,1)} %get-tuple-element.65) | copy-start | bytes 393220
  78.2 14.3 %copy-start.2 = (bf16[512,128]{1,0:T(8,128)(2,1)S(1)}, bf16[512,128]{1,0:T(8,128)(2,1)}, u32[]{:S(2)}) copy-start(bf16[512,128]{1,0:T(8,128)(2,1)} %get-tuple-element.70) | copy-start | bytes 393220
  79.5 9.0 %collective-permute-start.10 = (bf16[2,256,256]{2,1,0:T(8,128)(2,1)S(1)}, bf16[2,256,256]{2,1,0:T(8,128)(2,1)S(1)}, u32[]{:S(2)}, u32[]{:S(2)}) collective-permute-start(bf16[2,256,256]{2,1,0:T(8,128)(2,1)S(1)} %fusion.68), channel_id=1, source_target_pairs={{0,7},{1,0},{2,1},{3,2},{4,3},{5,4},{6,5},{7,6},{8,15},{9,8},{10,9... | collective-permute-start | bytes 786440 | tf_op jit(solution)/shard_map/ppermute | solution.py:24
  82.4 9.8 %collective-permute-start.13 = (bf16[2,256,256]{2,1,0:T(8,128)(2,1)S(1)}, bf16[2,256,256]{2,1,0:T(8,128)(2,1)S(1)}, u32[]{:S(2)}, u32[]{:S(2)}) collective-permute-start(bf16[2,256,256]{2,1,0:T(8,128)(2,1)S(1)} %fusion.68), channel_id=1, source_target_pairs={{0,1},{1,2},{2,3},{3,4},{4,5},{5,6},{6,7},{7,0},{8,9},{9,10},{10,1... | collective-permute-start | bytes 786440 | tf_op jit(solution)/shard_map/ppermute | solution.py:23
  82.7 21.4 %copy-start.5 = (bf16[512,128]{1,0:T(8,128)(2,1)S(1)}, bf16[512,128]{1,0:T(8,128)(2,1)}, u32[]{:S(2)}) copy-start(bf16[512,128]{1,0:T(8,128)(2,1)} %get-tuple-element.66) | copy-start | bytes 393220
  88.5 12.3 %collective-permute-start.11 = (bf16[2,256,256]{2,1,0:T(8,128)(2,1)S(1)}, bf16[2,256,256]{2,1,0:T(8,128)(2,1)S(1)}, u32[]{:S(2)}, u32[]{:S(2)}) collective-permute-start(bf16[2,256,256]{2,1,0:T(8,128)(2,1)S(1)} %collective-permute-done.10), channel_id=1, source_target_pairs={{0,7},{1,0},{2,1},{3,2},{4,3},{5,4},{6,5},{7,6},{8,15},{9,8},{10,9... | collective-permute-start | bytes 786440 | tf_op jit(solution)/shard_map/ppermute | solution.py:24
  92.2 8.6 %collective-permute-start.14 = (bf16[2,256,256]{2,1,0:T(8,128)(2,1)S(1)}, bf16[2,256,256]{2,1,0:T(8,128)(2,1)S(1)}, u32[]{:S(2)}, u32[]{:S(2)}) collective-permute-start(bf16[2,256,256]{2,1,0:T(8,128)(2,1)S(1)} %collective-permute-done.13), channel_id=1, source_target_pairs={{0,1},{1,2},{2,3},{3,4},{4,5},{5,6},{6,7},{7,0},{8,9},{9,10},{10,1... | collective-permute-start | bytes 786440 | tf_op jit(solution)/shard_map/ppermute | solution.py:23
  93.2 19.0 %copy-start.4 = (bf16[512,128]{1,0:T(8,128)(2,1)S(1)}, bf16[512,128]{1,0:T(8,128)(2,1)}, u32[]{:S(2)}) copy-start(bf16[512,128]{1,0:T(8,128)(2,1)} %get-tuple-element.67) | copy-start | bytes 393220
  100.9 7.8 %collective-permute-start.15 = (bf16[2,256,256]{2,1,0:T(8,128)(2,1)S(1)}, bf16[2,256,256]{2,1,0:T(8,128)(2,1)S(1)}, u32[]{:S(2)}, u32[]{:S(2)}) collective-permute-start(bf16[2,256,256]{2,1,0:T(8,128)(2,1)S(1)} %collective-permute-done.14), channel_id=1, source_target_pairs={{0,1},{1,2},{2,3},{3,4},{4,5},{5,6},{6,7},{7,0},{8,9},{9,10},{10,1... | collective-permute-start | bytes 786440 | tf_op jit(solution)/shard_map/ppermute | solution.py:23
  100.9 7.9 %collective-permute-start.12 = (bf16[2,256,256]{2,1,0:T(8,128)(2,1)S(1)}, bf16[2,256,256]{2,1,0:T(8,128)(2,1)S(1)}, u32[]{:S(2)}, u32[]{:S(2)}) collective-permute-start(bf16[2,256,256]{2,1,0:T(8,128)(2,1)S(1)} %collective-permute-done.11), channel_id=1, source_target_pairs={{0,7},{1,0},{2,1},{3,2},{4,3},{5,4},{6,5},{7,6},{8,15},{9,8},{10,9... | collective-permute-start | bytes 786440 | tf_op jit(solution)/shard_map/ppermute | solution.py:24
  108.7 6.3 %collective-permute-start.16 = (bf16[1,256,256]{2,1,0:T(8,128)(2,1)S(1)}, bf16[1,256,256]{2,1,0:T(8,128)(2,1)S(1)}, u32[]{:S(2)}, u32[]{:S(2)}) collective-permute-start(bf16[1,256,256]{2,1,0:T(8,128)(2,1)S(1)} %slice.165), channel_id=1, source_target_pairs={{0,1},{1,2},{2,3},{3,4},{4,5},{5,6},{6,7},{7,0},{8,9},{9,10},{10,1... | collective-permute-start | bytes 393224 | tf_op jit(solution)/shard_map/ppermute | solution.py:32
  108.8 6.2 %collective-permute-start.17 = (bf16[1,256,256]{2,1,0:T(8,128)(2,1)S(1)}, bf16[1,256,256]{2,1,0:T(8,128)(2,1)S(1)}, u32[]{:S(2)}, u32[]{:S(2)}) collective-permute-start(bf16[1,256,256]{2,1,0:T(8,128)(2,1)S(1)} %slice.166), channel_id=1, source_target_pairs={{0,7},{1,0},{2,1},{3,2},{4,3},{5,4},{6,5},{7,6},{8,15},{9,8},{10,9... | collective-permute-start | bytes 393224 | tf_op jit(solution)/shard_map/ppermute | solution.py:33
  116.1 8.7 %collective-permute-start = (bf16[256,256]{1,0:T(8,128)(2,1)S(1)}, bf16[256,256]{1,0:T(8,128)(2,1)S(1)}, u32[]{:S(2)}, u32[]{:S(2)}) collective-permute-start(bf16[256,256]{1,0:T(8,128)(2,1)S(1)} %copy.71), channel_id=1, source_target_pairs={{0,8},{8,0},{1,9},{9,1},{2,10},{10,2},{3,11},{11,3},{4,12},{12,4},... | collective-permute-start | bytes 393224 | tf_op jit(solution)/shard_map/while/body/eval_jaxpr/ppermute | solution.py:29
  125.0 9.8 %collective-permute-start.1 = (bf16[2,256,256]{2,1,0:T(8,128)(2,1)S(1)}, bf16[2,256,256]{2,1,0:T(8,128)(2,1)S(1)}, u32[]{:S(2)}, u32[]{:S(2)}) collective-permute-start(bf16[2,256,256]{2,1,0:T(8,128)(2,1)S(1)} %fusion.204), channel_id=1, source_target_pairs={{0,1},{1,2},{2,3},{3,4},{4,5},{5,6},{6,7},{7,0},{8,9},{9,10},{10,1... | collective-permute-start | bytes 786440 | tf_op jit(solution)/shard_map/while/body/eval_jaxpr/ppermute | solution.py:23
  125.1 9.7 %collective-permute-start.5 = (bf16[2,256,256]{2,1,0:T(8,128)(2,1)S(1)}, bf16[2,256,256]{2,1,0:T(8,128)(2,1)S(1)}, u32[]{:S(2)}, u32[]{:S(2)}) collective-permute-start(bf16[2,256,256]{2,1,0:T(8,128)(2,1)S(1)} %fusion.204), channel_id=1, source_target_pairs={{0,7},{1,0},{2,1},{3,2},{4,3},{5,4},{6,5},{7,6},{8,15},{9,8},{10,9... | collective-permute-start | bytes 786440 | tf_op jit(solution)/shard_map/while/body/eval_jaxpr/ppermute | solution.py:24
  134.8 10.2 %collective-permute-start.2 = (bf16[2,256,256]{2,1,0:T(8,128)(2,1)S(1)}, bf16[2,256,256]{2,1,0:T(8,128)(2,1)S(1)}, u32[]{:S(2)}, u32[]{:S(2)}) collective-permute-start(bf16[2,256,256]{2,1,0:T(8,128)(2,1)S(1)} %collective-permute-done.1), channel_id=1, source_target_pairs={{0,1},{1,2},{2,3},{3,4},{4,5},{5,6},{6,7},{7,0},{8,9},{9,10},{10,1... | collective-permute-start | bytes 786440 | tf_op jit(solution)/shard_map/while/body/eval_jaxpr/ppermute | solution.py:23
  134.8 10.4 %collective-permute-start.6 = (bf16[2,256,256]{2,1,0:T(8,128)(2,1)S(1)}, bf16[2,256,256]{2,1,0:T(8,128)(2,1)S(1)}, u32[]{:S(2)}, u32[]{:S(2)}) collective-permute-start(bf16[2,256,256]{2,1,0:T(8,128)(2,1)S(1)} %collective-permute-done.5), channel_id=1, source_target_pairs={{0,7},{1,0},{2,1},{3,2},{4,3},{5,4},{6,5},{7,6},{8,15},{9,8},{10,9... | collective-permute-start | bytes 786440 | tf_op jit(solution)/shard_map/while/body/eval_jaxpr/ppermute | solution.py:24
  145.0 8.0 %collective-permute-start.3 = (bf16[2,256,256]{2,1,0:T(8,128)(2,1)S(1)}, bf16[2,256,256]{2,1,0:T(8,128)(2,1)S(1)}, u32[]{:S(2)}, u32[]{:S(2)}) collective-permute-start(bf16[2,256,256]{2,1,0:T(8,128)(2,1)S(1)} %collective-permute-done.2), channel_id=1, source_target_pairs={{0,1},{1,2},{2,3},{3,4},{4,5},{5,6},{6,7},{7,0},{8,9},{9,10},{10,1... | collective-permute-start | bytes 786440 | tf_op jit(solution)/shard_map/while/body/eval_jaxpr/ppermute | solution.py:23
  145.2 7.9 %collective-permute-start.7 = (bf16[2,256,256]{2,1,0:T(8,128)(2,1)S(1)}, bf16[2,256,256]{2,1,0:T(8,128)(2,1)S(1)}, u32[]{:S(2)}, u32[]{:S(2)}) collective-permute-start(bf16[2,256,256]{2,1,0:T(8,128)(2,1)S(1)} %collective-permute-done.6), channel_id=1, source_target_pairs={{0,7},{1,0},{2,1},{3,2},{4,3},{5,4},{6,5},{7,6},{8,15},{9,8},{10,9... | collective-permute-start | bytes 786440 | tf_op jit(solution)/shard_map/while/body/eval_jaxpr/ppermute | solution.py:24
  153.0 6.3 %collective-permute-start.4 = (bf16[1,256,256]{2,1,0:T(8,128)(2,1)S(1)}, bf16[1,256,256]{2,1,0:T(8,128)(2,1)S(1)}, u32[]{:S(2)}, u32[]{:S(2)}) collective-permute-start(bf16[1,256,256]{2,1,0:T(8,128)(2,1)S(1)} %slice.298), channel_id=1, source_target_pairs={{0,1},{1,2},{2,3},{3,4},{4,5},{5,6},{6,7},{7,0},{8,9},{9,10},{10,1... | collective-permute-start | bytes 393224 | tf_op jit(solution)/shard_map/while/body/eval_jaxpr/ppermute | solution.py:32
  153.1 6.2 %collective-permute-start.8 = (bf16[1,256,256]{2,1,0:T(8,128)(2,1)S(1)}, bf16[1,256,256]{2,1,0:T(8,128)(2,1)S(1)}, u32[]{:S(2)}, u32[]{:S(2)}) collective-permute-start(bf16[1,256,256]{2,1,0:T(8,128)(2,1)S(1)} %slice.299), channel_id=1, source_target_pairs={{0,7},{1,0},{2,1},{3,2},{4,3},{5,4},{6,5},{7,6},{8,15},{9,8},{10,9... | collective-permute-start | bytes 393224 | tf_op jit(solution)/shard_map/while/body/eval_jaxpr/ppermute | solution.py:33
  160.4 6.6 %collective-permute-start = (bf16[256,256]{1,0:T(8,128)(2,1)S(1)}, bf16[256,256]{1,0:T(8,128)(2,1)S(1)}, u32[]{:S(2)}, u32[]{:S(2)}) collective-permute-start(bf16[256,256]{1,0:T(8,128)(2,1)S(1)} %copy.71), channel_id=1, source_target_pairs={{0,8},{8,0},{1,9},{9,1},{2,10},{10,2},{3,11},{11,3},{4,12},{12,4},... | collective-permute-start | bytes 393224 | tf_op jit(solution)/shard_map/while/body/eval_jaxpr/ppermute | solution.py:29
  167.2 8.4 %collective-permute-start.1 = (bf16[2,256,256]{2,1,0:T(8,128)(2,1)S(1)}, bf16[2,256,256]{2,1,0:T(8,128)(2,1)S(1)}, u32[]{:S(2)}, u32[]{:S(2)}) collective-permute-start(bf16[2,256,256]{2,1,0:T(8,128)(2,1)S(1)} %fusion.204), channel_id=1, source_target_pairs={{0,1},{1,2},{2,3},{3,4},{4,5},{5,6},{6,7},{7,0},{8,9},{9,10},{10,1... | collective-permute-start | bytes 786440 | tf_op jit(solution)/shard_map/while/body/eval_jaxpr/ppermute | solution.py:23
  167.3 8.3 %collective-permute-start.5 = (bf16[2,256,256]{2,1,0:T(8,128)(2,1)S(1)}, bf16[2,256,256]{2,1,0:T(8,128)(2,1)S(1)}, u32[]{:S(2)}, u32[]{:S(2)}) collective-permute-start(bf16[2,256,256]{2,1,0:T(8,128)(2,1)S(1)} %fusion.204), channel_id=1, source_target_pairs={{0,7},{1,0},{2,1},{3,2},{4,3},{5,4},{6,5},{7,6},{8,15},{9,8},{10,9... | collective-permute-start | bytes 786440 | tf_op jit(solution)/shard_map/while/body/eval_jaxpr/ppermute | solution.py:24
  175.6 9.0 %collective-permute-start.2 = (bf16[2,256,256]{2,1,0:T(8,128)(2,1)S(1)}, bf16[2,256,256]{2,1,0:T(8,128)(2,1)S(1)}, u32[]{:S(2)}, u32[]{:S(2)}) collective-permute-start(bf16[2,256,256]{2,1,0:T(8,128)(2,1)S(1)} %collective-permute-done.1), channel_id=1, source_target_pairs={{0,1},{1,2},{2,3},{3,4},{4,5},{5,6},{6,7},{7,0},{8,9},{9,10},{10,1... | collective-permute-start | bytes 786440 | tf_op jit(solution)/shard_map/while/body/eval_jaxpr/ppermute | solution.py:23
  175.6 9.2 %collective-permute-start.6 = (bf16[2,256,256]{2,1,0:T(8,128)(2,1)S(1)}, bf16[2,256,256]{2,1,0:T(8,128)(2,1)S(1)}, u32[]{:S(2)}, u32[]{:S(2)}) collective-permute-start(bf16[2,256,256]{2,1,0:T(8,128)(2,1)S(1)} %collective-permute-done.5), channel_id=1, source_target_pairs={{0,7},{1,0},{2,1},{3,2},{4,3},{5,4},{6,5},{7,6},{8,15},{9,8},{10,9... | collective-permute-start | bytes 786440 | tf_op jit(solution)/shard_map/while/body/eval_jaxpr/ppermute | solution.py:24
  184.6 7.6 %collective-permute-start.3 = (bf16[2,256,256]{2,1,0:T(8,128)(2,1)S(1)}, bf16[2,256,256]{2,1,0:T(8,128)(2,1)S(1)}, u32[]{:S(2)}, u32[]{:S(2)}) collective-permute-start(bf16[2,256,256]{2,1,0:T(8,128)(2,1)S(1)} %collective-permute-done.2), channel_id=1, source_target_pairs={{0,1},{1,2},{2,3},{3,4},{4,5},{5,6},{6,7},{7,0},{8,9},{9,10},{10,1... | collective-permute-start | bytes 786440 | tf_op jit(solution)/shard_map/while/body/eval_jaxpr/ppermute | solution.py:23
  184.8 7.4 %collective-permute-start.7 = (bf16[2,256,256]{2,1,0:T(8,128)(2,1)S(1)}, bf16[2,256,256]{2,1,0:T(8,128)(2,1)S(1)}, u32[]{:S(2)}, u32[]{:S(2)}) collective-permute-start(bf16[2,256,256]{2,1,0:T(8,128)(2,1)S(1)} %collective-permute-done.6), channel_id=1, source_target_pairs={{0,7},{1,0},{2,1},{3,2},{4,3},{5,4},{6,5},{7,6},{8,15},{9,8},{10,9... | collective-permute-start | bytes 786440 | tf_op jit(solution)/shard_map/while/body/eval_jaxpr/ppermute | solution.py:24
  192.1 6.3 %collective-permute-start.4 = (bf16[1,256,256]{2,1,0:T(8,128)(2,1)S(1)}, bf16[1,256,256]{2,1,0:T(8,128)(2,1)S(1)}, u32[]{:S(2)}, u32[]{:S(2)}) collective-permute-start(bf16[1,256,256]{2,1,0:T(8,128)(2,1)S(1)} %slice.298), channel_id=1, source_target_pairs={{0,1},{1,2},{2,3},{3,4},{4,5},{5,6},{6,7},{7,0},{8,9},{9,10},{10,1... | collective-permute-start | bytes 393224 | tf_op jit(solution)/shard_map/while/body/eval_jaxpr/ppermute | solution.py:32
  192.3 6.2 %collective-permute-start.8 = (bf16[1,256,256]{2,1,0:T(8,128)(2,1)S(1)}, bf16[1,256,256]{2,1,0:T(8,128)(2,1)S(1)}, u32[]{:S(2)}, u32[]{:S(2)}) collective-permute-start(bf16[1,256,256]{2,1,0:T(8,128)(2,1)S(1)} %slice.299), channel_id=1, source_target_pairs={{0,7},{1,0},{2,1},{3,2},{4,3},{5,4},{6,5},{7,6},{8,15},{9,8},{10,9... | collective-permute-start | bytes 393224 | tf_op jit(solution)/shard_map/while/body/eval_jaxpr/ppermute | solution.py:33
  (3 other events, 16.3 us)

commit v9 on v5

--- a/solution.py
+++ b/solution.py
@@ -61,12 +61,14 @@
 def place_tiles(dest, tiles, rows):
     positions, block_rows, local_slots, size, _ = tiles.shape
     slots = positions * local_slots
+    group = max(1, 128 // size)
 
     def kernel(dest_ref, tiles_ref, out_ref):
+        first = pl.program_id(0) * group
         out_ref[...] = jnp.zeros(out_ref.shape, out_ref.dtype)
-        for b in range(block_rows):
+        for b in range(group):
             def place(p, carry):
-                target = dest_ref[b * slots + p]
+                target = dest_ref[(first + b) * slots + p]
 
                 @pl.when(target >= 0)
                 def _():
@@ -79,9 +81,13 @@
 
     return pl.pallas_call(
         kernel,
+        grid=(block_rows // group,),
         out_shape=jax.ShapeDtypeStruct((rows * size, block_rows * size), tiles.dtype),
-        in_specs=[pl.BlockSpec(memory_space=pltpu.SMEM), pl.BlockSpec(memory_space=pltpu.VMEM)],
-        out_specs=pl.BlockSpec(memory_space=pltpu.VMEM),
+        in_specs=[
+            pl.BlockSpec(memory_space=pltpu.SMEM),
+            pl.BlockSpec((positions, group, local_slots, size, size), lambda g: (0, g, 0, 0, 0)),
+        ],
+        out_specs=pl.BlockSpec((rows * size, group * size), lambda g: (0, g)),
     )(dest.reshape(-1), tiles)
 
 

time: 153 us -> 156 us (1.020)
  starting transfers between devices: 52.5 us -> 54.9 us
    ppermute x9, starting transfers between devices: 26.3 us -> 29.2 us  [ring_blocks(): left = lax.ppermute(left, axis, bwd)]
where the time goes in v9:
time: 156 us; the launch traced here: 155 us
  waiting for transfers between devices  65.3 us (42%)
  starting transfers between devices  54.9 us (35%)
  between operations  13.7 us (9%)
  Pallas kernels  7.68 us (5%)
  matrix products  6.47 us (4%)
  local copies, waits for them, and re-layouts  4.73 us (3%)
  other arithmetic  2.18 us (1%)
    ppermute x9, starting transfers between devices, ring_blocks(): left = lax.ppermute(left, axis, bwd)  29.2 us
    ppermute x9, waiting for transfers between devices, ring_blocks(): left = lax.ppermute(left, axis, bwd)  27 us
    ppermute x9, waiting for transfers between devices, ring_blocks(): right = lax.ppermute(right, axis, fwd)  12 us
    ppermute x3, waiting for transfers between devices, ring_blocks(): blocks[1] = lax.ppermute(piece, axis, fwd)  11.2 us
    ppermute x3, starting transfers between devices, ring_blocks(): lax.ppermute(lax.slice_in_dim(left, split, None, axis=split_dim), axis, bwd)  11 us
    ppermute x3, starting transfers between devices, ring_blocks(): blocks[1] = lax.ppermute(piece, axis, fwd)  10.4 us
    pallas_call x1, Pallas kernels, place_tiles(): pl.pallas_call(kernel, grid=(block_rows // group,), out_shape=jax.ShapeDt...  7.68 us
    ppermute x3, waiting for transfers between devices, ring_blocks(): lax.ppermute(lax.slice_in_dim(right, 0, split, axis=split_dim), axis, fwd)  7.5 us
  transfers between devices with their start and end apart: 28, of which 17 were waited for; matrix products, arithmetic and copies ran while one was open for 4% of the time, Pallas kernels for 5%

profile of v9, /device:TPU:2, one launch (start us, length us, event | category | flops | bytes accessed | tf_op | source)
XLA Modules:
  0.0 155.2 jit_solution(5393918216446776862)
XLA Ops:
  9.2 3.3 %collective-permute-start.9 = (bf16[256,256]{1,0:T(8,128)(2,1)S(1)}, bf16[256,256]{1,0:T(8,128)(2,1)S(1)}, u32[]{:S(2)}, u32[]{:S(2)}) collective-permute-start(bf16[256,256]{1,0:T(8,128)(2,1)S(1)} %copy.17), channel_id=1, source_target_pairs={{0,8},{8,0},{1,9},{9,1},{2,10},{10,2},{3,11},{11,3},{4,12},{12,4},... | collective-permute-start | bytes 393224 | tf_op jit(solution)/shard_map/ppermute | solution.py:29
  12.5 3.5 %collective-permute-done.9 = bf16[256,256]{1,0:T(8,128)(2,1)S(1)} collective-permute-done((bf16[256,256]{1,0:T(8,128)(2,1)S(1)}, bf16[256,256]{1,0:T(8,128)(2,1)S(1)}, u32[]{:S(2)}, u32[]{:S(2)}) %collective-permute-start.9) | collective-permute-done | bytes 131104 | tf_op jit(solution)/shard_map/ppermute | solution.py:29
  18.2 4.0 %collective-permute-start.10 = (bf16[2,256,256]{2,1,0:T(8,128)(2,1)S(1)}, bf16[2,256,256]{2,1,0:T(8,128)(2,1)S(1)}, u32[]{:S(2)}, u32[]{:S(2)}) collective-permute-start(bf16[2,256,256]{2,1,0:T(8,128)(2,1)S(1)} %fusion.42), channel_id=1, source_target_pairs={{0,7},{1,0},{2,1},{3,2},{4,3},{5,4},{6,5},{7,6},{8,15},{9,8},{10,9... | collective-permute-start | bytes 786440 | tf_op jit(solution)/shard_map/ppermute | solution.py:24
  22.2 5.4 %collective-permute-done.13 = bf16[2,256,256]{2,1,0:T(8,128)(2,1)S(1)} collective-permute-done((bf16[2,256,256]{2,1,0:T(8,128)(2,1)S(1)}, bf16[2,256,256]{2,1,0:T(8,128)(2,1)S(1)}, u32[]{:S(2)}, u32[]{:S(2)}) %collective-permute-start.13) | collective-permute-done | bytes 262176 | tf_op jit(solution)/shard_map/ppermute | solution.py:23
  27.6 3.2 %collective-permute-start.11 = (bf16[2,256,256]{2,1,0:T(8,128)(2,1)S(1)}, bf16[2,256,256]{2,1,0:T(8,128)(2,1)S(1)}, u32[]{:S(2)}, u32[]{:S(2)}) collective-permute-start(bf16[2,256,256]{2,1,0:T(8,128)(2,1)S(1)} %collective-permute-done.10), channel_id=1, source_target_pairs={{0,7},{1,0},{2,1},{3,2},{4,3},{5,4},{6,5},{7,6},{8,15},{9,8},{10,9... | collective-permute-start | bytes 786440 | tf_op jit(solution)/shard_map/ppermute | solution.py:24
  30.9 4.6 %collective-permute-done.14 = bf16[2,256,256]{2,1,0:T(8,128)(2,1)S(1)} collective-permute-done((bf16[2,256,256]{2,1,0:T(8,128)(2,1)S(1)}, bf16[2,256,256]{2,1,0:T(8,128)(2,1)S(1)}, u32[]{:S(2)}, u32[]{:S(2)}) %collective-permute-start.14) | collective-permute-done | bytes 262176 | tf_op jit(solution)/shard_map/ppermute | solution.py:23
  35.5 3.3 %collective-permute-start.12 = (bf16[2,256,256]{2,1,0:T(8,128)(2,1)S(1)}, bf16[2,256,256]{2,1,0:T(8,128)(2,1)S(1)}, u32[]{:S(2)}, u32[]{:S(2)}) collective-permute-start(bf16[2,256,256]{2,1,0:T(8,128)(2,1)S(1)} %collective-permute-done.11), channel_id=1, source_target_pairs={{0,7},{1,0},{2,1},{3,2},{4,3},{5,4},{6,5},{7,6},{8,15},{9,8},{10,9... | collective-permute-start | bytes 786440 | tf_op jit(solution)/shard_map/ppermute | solution.py:24
  43.2 3.5 %collective-permute-start.17 = (bf16[1,256,256]{2,1,0:T(8,128)(2,1)S(1)}, bf16[1,256,256]{2,1,0:T(8,128)(2,1)}, u32[]{:S(2)}, u32[]{:S(2)}) collective-permute-start(bf16[1,256,256]{2,1,0:T(8,128)(2,1)S(1)} %slice.85), channel_id=1, source_target_pairs={{0,7},{1,0},{2,1},{3,2},{4,3},{5,4},{6,5},{7,6},{8,15},{9,8},{10,9... | collective-permute-start | bytes 393224 | tf_op jit(solution)/shard_map/ppermute | solution.py:33
  46.6 3.3 %all-gather.2.cloned.1.call-done = bf16[4,48,64,64]{3,2,1,0:T(8,128)(2,1)} async-done(((bf16[4,3,64,64]{3,2,1,0:T(8,128)(2,1)}), bf16[4,48,64,64]{3,2,1,0:T(8,128)(2,1)}) %all-gather.2.cloned.1.call-update) | async-done | bytes 1572880 | tf_op jit(solution)/shard_map/all_gather | solution.py:109
  49.9 7.7 %shard_map.46 = bf16[4096,256]{1,0:T(8,128)(2,1)S(1)} custom-call(s32[192]{0:T(256)} %reshape.43.dest_ref, bf16[1,4,48,64,64]{4,3,2,1,0:T(8,128)(2,1)} %bitcast.183), custom_call_target="tpu_custom_call" | custom-call | tf_op jit(solution)/shard_map/pallas_call | solution.py:82
  61.3 86.4 %while.12 = (s32[]{:T(128)}, bf16[256,256]{1,0:T(8,128)(2,1)S(1)}, bf16[256,256]{1,0:T(8,128)(2,1)S(1)}, bf16[8,2,256,256]{3,2,1,0:T(8,128)(2,1)S(1)}, s32[]{:T(...) while((s32[]{:T(128)}, bf16[256,256]{1,0:T(8,128)(2,1)S(1)}, ...), condition=%wide.region_2.4_spmd, body=%wide.region_1.3_spmd.sunk | while | flops 538116096 | bytes 17564300 | solution.py:137
  61.3 4.4 %collective-permute-start = (bf16[256,256]{1,0:T(8,128)(2,1)S(1)}, bf16[256,256]{1,0:T(8,128)(2,1)S(1)}, u32[]{:S(2)}, u32[]{:S(2)}) collective-permute-start(bf16[256,256]{1,0:T(8,128)(2,1)S(1)} %copy.12), channel_id=1, source_target_pairs={{0,8},{8,0},{1,9},{9,1},{2,10},{10,2},{3,11},{11,3},{4,12},{12,4},... | collective-permute-start | bytes 393224 | tf_op jit(solution)/shard_map/while/body/eval_jaxpr/ppermute | solution.py:29
  65.7 3.9 %collective-permute-done = bf16[256,256]{1,0:T(8,128)(2,1)S(1)} collective-permute-done((bf16[256,256]{1,0:T(8,128)(2,1)S(1)}, bf16[256,256]{1,0:T(8,128)(2,1)S(1)}, u32[]{:S(2)}, u32[]{:S(2)}) %collective-permute-start) | collective-permute-done | bytes 131104 | tf_op jit(solution)/shard_map/while/body/eval_jaxpr/ppermute | solution.py:29
  69.8 5.1 %collective-permute-start.4 = (bf16[2,256,256]{2,1,0:T(8,128)(2,1)S(1)}, bf16[2,256,256]{2,1,0:T(8,128)(2,1)S(1)}, u32[]{:S(2)}, u32[]{:S(2)}) collective-permute-start(bf16[2,256,256]{2,1,0:T(8,128)(2,1)S(1)} %fusion.117), channel_id=1, source_target_pairs={{0,7},{1,0},{2,1},{3,2},{4,3},{5,4},{6,5},{7,6},{8,15},{9,8},{10,9... | collective-permute-start | bytes 786440 | tf_op jit(solution)/shard_map/while/body/eval_jaxpr/ppermute | solution.py:24
  75.1 5.1 %collective-permute-done.4 = bf16[2,256,256]{2,1,0:T(8,128)(2,1)S(1)} collective-permute-done((bf16[2,256,256]{2,1,0:T(8,128)(2,1)S(1)}, bf16[2,256,256]{2,1,0:T(8,128)(2,1)S(1)}, u32[]{:S(2)}, u32[]{:S(2)}) %collective-permute-start.4) | collective-permute-done | bytes 262176 | tf_op jit(solution)/shard_map/while/body/eval_jaxpr/ppermute | solution.py:24
  80.2 3.7 %collective-permute-start.5 = (bf16[2,256,256]{2,1,0:T(8,128)(2,1)S(1)}, bf16[2,256,256]{2,1,0:T(8,128)(2,1)S(1)}, u32[]{:S(2)}, u32[]{:S(2)}) collective-permute-start(bf16[2,256,256]{2,1,0:T(8,128)(2,1)S(1)} %collective-permute-done.4), channel_id=1, source_target_pairs={{0,7},{1,0},{2,1},{3,2},{4,3},{5,4},{6,5},{7,6},{8,15},{9,8},{10,9... | collective-permute-start | bytes 786440 | tf_op jit(solution)/shard_map/while/body/eval_jaxpr/ppermute | solution.py:24
  84.4 4.0 %collective-permute-done.5 = bf16[2,256,256]{2,1,0:T(8,128)(2,1)S(1)} collective-permute-done((bf16[2,256,256]{2,1,0:T(8,128)(2,1)S(1)}, bf16[2,256,256]{2,1,0:T(8,128)(2,1)S(1)}, u32[]{:S(2)}, u32[]{:S(2)}) %collective-permute-start.5) | collective-permute-done | bytes 262176 | tf_op jit(solution)/shard_map/while/body/eval_jaxpr/ppermute | solution.py:24
  88.4 3.7 %collective-permute-start.6 = (bf16[2,256,256]{2,1,0:T(8,128)(2,1)S(1)}, bf16[2,256,256]{2,1,0:T(8,128)(2,1)S(1)}, u32[]{:S(2)}, u32[]{:S(2)}) collective-permute-start(bf16[2,256,256]{2,1,0:T(8,128)(2,1)S(1)} %collective-permute-done.5), channel_id=1, source_target_pairs={{0,7},{1,0},{2,1},{3,2},{4,3},{5,4},{6,5},{7,6},{8,15},{9,8},{10,9... | collective-permute-start | bytes 786440 | tf_op jit(solution)/shard_map/while/body/eval_jaxpr/ppermute | solution.py:24
  92.6 3.4 %collective-permute-done.6 = bf16[2,256,256]{2,1,0:T(8,128)(2,1)S(1)} collective-permute-done((bf16[2,256,256]{2,1,0:T(8,128)(2,1)S(1)}, bf16[2,256,256]{2,1,0:T(8,128)(2,1)S(1)}, u32[]{:S(2)}, u32[]{:S(2)}) %collective-permute-start.6) | collective-permute-done | bytes 262176 | tf_op jit(solution)/shard_map/while/body/eval_jaxpr/ppermute | solution.py:24
  96.0 3.8 %collective-permute-start.7 = (bf16[1,256,256]{2,1,0:T(8,128)(2,1)S(1)}, bf16[1,256,256]{2,1,0:T(8,128)(2,1)S(1)}, u32[]{:S(2)}, u32[]{:S(2)}) collective-permute-start(bf16[1,256,256]{2,1,0:T(8,128)(2,1)S(1)} %slice.148), channel_id=1, source_target_pairs={{0,7},{1,0},{2,1},{3,2},{4,3},{5,4},{6,5},{7,6},{8,15},{9,8},{10,9... | collective-permute-start | bytes 393224 | tf_op jit(solution)/shard_map/while/body/eval_jaxpr/ppermute | solution.py:33
  100.1 2.2 %collective-permute-done.7 = bf16[1,256,256]{2,1,0:T(8,128)(2,1)S(1)} collective-permute-done((bf16[1,256,256]{2,1,0:T(8,128)(2,1)S(1)}, bf16[1,256,256]{2,1,0:T(8,128)(2,1)S(1)}, u32[]{:S(2)}, u32[]{:S(2)}) %collective-permute-start.7) | collective-permute-done | bytes 131104 | tf_op jit(solution)/shard_map/while/body/eval_jaxpr/ppermute | solution.py:33
  102.3 3.8 %collective-permute-done.8 = bf16[1,256,256]{2,1,0:T(8,128)(2,1)S(1)} collective-permute-done((bf16[1,256,256]{2,1,0:T(8,128)(2,1)S(1)}, bf16[1,256,256]{2,1,0:T(8,128)(2,1)S(1)}, u32[]{:S(2)}, u32[]{:S(2)}) %collective-permute-start.8) | collective-permute-done | bytes 131104 | tf_op jit(solution)/shard_map/while/body/eval_jaxpr/ppermute | solution.py:32
  106.6 2.8 %collective-permute-start = (bf16[256,256]{1,0:T(8,128)(2,1)S(1)}, bf16[256,256]{1,0:T(8,128)(2,1)S(1)}, u32[]{:S(2)}, u32[]{:S(2)}) collective-permute-start(bf16[256,256]{1,0:T(8,128)(2,1)S(1)} %copy.12), channel_id=1, source_target_pairs={{0,8},{8,0},{1,9},{9,1},{2,10},{10,2},{3,11},{11,3},{4,12},{12,4},... | collective-permute-start | bytes 393224 | tf_op jit(solution)/shard_map/while/body/eval_jaxpr/ppermute | solution.py:29
  109.4 3.8 %collective-permute-done = bf16[256,256]{1,0:T(8,128)(2,1)S(1)} collective-permute-done((bf16[256,256]{1,0:T(8,128)(2,1)S(1)}, bf16[256,256]{1,0:T(8,128)(2,1)S(1)}, u32[]{:S(2)}, u32[]{:S(2)}) %collective-permute-start) | collective-permute-done | bytes 131104 | tf_op jit(solution)/shard_map/while/body/eval_jaxpr/ppermute | solution.py:29
  115.7 5.7 %collective-permute-done.4 = bf16[2,256,256]{2,1,0:T(8,128)(2,1)S(1)} collective-permute-done((bf16[2,256,256]{2,1,0:T(8,128)(2,1)S(1)}, bf16[2,256,256]{2,1,0:T(8,128)(2,1)S(1)}, u32[]{:S(2)}, u32[]{:S(2)}) %collective-permute-start.4) | collective-permute-done | bytes 262176 | tf_op jit(solution)/shard_map/while/body/eval_jaxpr/ppermute | solution.py:24
  121.4 2.4 %collective-permute-start.5 = (bf16[2,256,256]{2,1,0:T(8,128)(2,1)S(1)}, bf16[2,256,256]{2,1,0:T(8,128)(2,1)S(1)}, u32[]{:S(2)}, u32[]{:S(2)}) collective-permute-start(bf16[2,256,256]{2,1,0:T(8,128)(2,1)S(1)} %collective-permute-done.4), channel_id=1, source_target_pairs={{0,7},{1,0},{2,1},{3,2},{4,3},{5,4},{6,5},{7,6},{8,15},{9,8},{10,9... | collective-permute-start | bytes 786440 | tf_op jit(solution)/shard_map/while/body/eval_jaxpr/ppermute | solution.py:24
  124.3 5.3 %collective-permute-done.5 = bf16[2,256,256]{2,1,0:T(8,128)(2,1)S(1)} collective-permute-done((bf16[2,256,256]{2,1,0:T(8,128)(2,1)S(1)}, bf16[2,256,256]{2,1,0:T(8,128)(2,1)S(1)}, u32[]{:S(2)}, u32[]{:S(2)}) %collective-permute-start.5) | collective-permute-done | bytes 262176 | tf_op jit(solution)/shard_map/while/body/eval_jaxpr/ppermute | solution.py:24
  129.6 3.7 %collective-permute-start.6 = (bf16[2,256,256]{2,1,0:T(8,128)(2,1)S(1)}, bf16[2,256,256]{2,1,0:T(8,128)(2,1)S(1)}, u32[]{:S(2)}, u32[]{:S(2)}) collective-permute-start(bf16[2,256,256]{2,1,0:T(8,128)(2,1)S(1)} %collective-permute-done.5), channel_id=1, source_target_pairs={{0,7},{1,0},{2,1},{3,2},{4,3},{5,4},{6,5},{7,6},{8,15},{9,8},{10,9... | collective-permute-start | bytes 786440 | tf_op jit(solution)/shard_map/while/body/eval_jaxpr/ppermute | solution.py:24
  133.7 3.4 %collective-permute-done.6 = bf16[2,256,256]{2,1,0:T(8,128)(2,1)S(1)} collective-permute-done((bf16[2,256,256]{2,1,0:T(8,128)(2,1)S(1)}, bf16[2,256,256]{2,1,0:T(8,128)(2,1)S(1)}, u32[]{:S(2)}, u32[]{:S(2)}) %collective-permute-start.6) | collective-permute-done | bytes 262176 | tf_op jit(solution)/shard_map/while/body/eval_jaxpr/ppermute | solution.py:24
  137.2 3.8 %collective-permute-start.7 = (bf16[1,256,256]{2,1,0:T(8,128)(2,1)S(1)}, bf16[1,256,256]{2,1,0:T(8,128)(2,1)S(1)}, u32[]{:S(2)}, u32[]{:S(2)}) collective-permute-start(bf16[1,256,256]{2,1,0:T(8,128)(2,1)S(1)} %slice.148), channel_id=1, source_target_pairs={{0,7},{1,0},{2,1},{3,2},{4,3},{5,4},{6,5},{7,6},{8,15},{9,8},{10,9... | collective-permute-start | bytes 393224 | tf_op jit(solution)/shard_map/while/body/eval_jaxpr/ppermute | solution.py:33
  141.3 2.2 %collective-permute-done.7 = bf16[1,256,256]{2,1,0:T(8,128)(2,1)S(1)} collective-permute-done((bf16[1,256,256]{2,1,0:T(8,128)(2,1)S(1)}, bf16[1,256,256]{2,1,0:T(8,128)(2,1)S(1)}, u32[]{:S(2)}, u32[]{:S(2)}) %collective-permute-start.7) | collective-permute-done | bytes 131104 | tf_op jit(solution)/shard_map/while/body/eval_jaxpr/ppermute | solution.py:33
  143.5 3.8 %collective-permute-done.8 = bf16[1,256,256]{2,1,0:T(8,128)(2,1)S(1)} collective-permute-done((bf16[1,256,256]{2,1,0:T(8,128)(2,1)S(1)}, bf16[1,256,256]{2,1,0:T(8,128)(2,1)S(1)}, u32[]{:S(2)}, u32[]{:S(2)}) %collective-permute-start.8) | collective-permute-done | bytes 131104 | tf_op jit(solution)/shard_map/while/body/eval_jaxpr/ppermute | solution.py:32
  (97 shorter events, 19.8 us)
Async XLA Ops:
  6.5 43.4 %all-gather.2.cloned.1.call-start = ((), (), s32[]{:S(2)}) async-start(), calls=%async_computation | async-start | bytes 3342336 | tf_op jit(solution)/shard_map/all_gather | solution.py:109
  9.2 6.8 %collective-permute-start.9 = (bf16[256,256]{1,0:T(8,128)(2,1)S(1)}, bf16[256,256]{1,0:T(8,128)(2,1)S(1)}, u32[]{:S(2)}, u32[]{:S(2)}) collective-permute-start(bf16[256,256]{1,0:T(8,128)(2,1)S(1)} %copy.17), channel_id=1, source_target_pairs={{0,8},{8,0},{1,9},{9,1},{2,10},{10,2},{3,11},{11,3},{4,12},{12,4},... | collective-permute-start | bytes 393224 | tf_op jit(solution)/shard_map/ppermute | solution.py:29
  16.2 11.4 %collective-permute-start.13 = (bf16[2,256,256]{2,1,0:T(8,128)(2,1)S(1)}, bf16[2,256,256]{2,1,0:T(8,128)(2,1)S(1)}, u32[]{:S(2)}, u32[]{:S(2)}) collective-permute-start(bf16[2,256,256]{2,1,0:T(8,128)(2,1)S(1)} %fusion.42), channel_id=1, source_target_pairs={{0,1},{1,2},{2,3},{3,4},{4,5},{5,6},{6,7},{7,0},{8,9},{9,10},{10,1... | collective-permute-start | bytes 786440 | tf_op jit(solution)/shard_map/ppermute | solution.py:23
  18.2 9.4 %collective-permute-start.10 = (bf16[2,256,256]{2,1,0:T(8,128)(2,1)S(1)}, bf16[2,256,256]{2,1,0:T(8,128)(2,1)S(1)}, u32[]{:S(2)}, u32[]{:S(2)}) collective-permute-start(bf16[2,256,256]{2,1,0:T(8,128)(2,1)S(1)} %fusion.42), channel_id=1, source_target_pairs={{0,7},{1,0},{2,1},{3,2},{4,3},{5,4},{6,5},{7,6},{8,15},{9,8},{10,9... | collective-permute-start | bytes 786440 | tf_op jit(solution)/shard_map/ppermute | solution.py:24
  27.6 7.8 %copy-start.5 = (bf16[2,256,256]{2,1,0:T(8,128)(2,1)}, bf16[2,256,256]{2,1,0:T(8,128)(2,1)S(1)}, u32[]{:S(2)}) copy-start(bf16[2,256,256]{2,1,0:T(8,128)(2,1)S(1)} %collective-permute-done.13) | copy-start | bytes 786436
  27.6 7.8 %collective-permute-start.14 = (bf16[2,256,256]{2,1,0:T(8,128)(2,1)S(1)}, bf16[2,256,256]{2,1,0:T(8,128)(2,1)S(1)}, u32[]{:S(2)}, u32[]{:S(2)}) collective-permute-start(bf16[2,256,256]{2,1,0:T(8,128)(2,1)S(1)} %collective-permute-done.13), channel_id=1, source_target_pairs={{0,1},{1,2},{2,3},{3,4},{4,5},{5,6},{6,7},{7,0},{8,9},{9,10},{10,1... | collective-permute-start | bytes 786440 | tf_op jit(solution)/shard_map/ppermute | solution.py:23
  27.6 22.3 %copy-start.9 = (bf16[2,256,256]{2,1,0:T(8,128)(2,1)}, bf16[2,256,256]{2,1,0:T(8,128)(2,1)S(1)}, u32[]{:S(2)}) copy-start(bf16[2,256,256]{2,1,0:T(8,128)(2,1)S(1)} %collective-permute-done.10) | copy-start | bytes 786436
  27.6 7.8 %collective-permute-start.11 = (bf16[2,256,256]{2,1,0:T(8,128)(2,1)S(1)}, bf16[2,256,256]{2,1,0:T(8,128)(2,1)S(1)}, u32[]{:S(2)}, u32[]{:S(2)}) collective-permute-start(bf16[2,256,256]{2,1,0:T(8,128)(2,1)S(1)} %collective-permute-done.10), channel_id=1, source_target_pairs={{0,7},{1,0},{2,1},{3,2},{4,3},{5,4},{6,5},{7,6},{8,15},{9,8},{10,9... | collective-permute-start | bytes 786440 | tf_op jit(solution)/shard_map/ppermute | solution.py:24
  35.4 14.5 %copy-start.7 = (bf16[2,256,256]{2,1,0:T(8,128)(2,1)}, bf16[2,256,256]{2,1,0:T(8,128)(2,1)S(1)}, u32[]{:S(2)}) copy-start(bf16[2,256,256]{2,1,0:T(8,128)(2,1)S(1)} %collective-permute-done.14) | copy-start | bytes 786436
  35.4 7.6 %collective-permute-start.15 = (bf16[2,256,256]{2,1,0:T(8,128)(2,1)S(1)}, bf16[2,256,256]{2,1,0:T(8,128)(2,1)S(1)}, u32[]{:S(2)}, u32[]{:S(2)}) collective-permute-start(bf16[2,256,256]{2,1,0:T(8,128)(2,1)S(1)} %collective-permute-done.14), channel_id=1, source_target_pairs={{0,1},{1,2},{2,3},{3,4},{4,5},{5,6},{6,7},{7,0},{8,9},{9,10},{10,1... | collective-permute-start | bytes 786440 | tf_op jit(solution)/shard_map/ppermute | solution.py:23
  35.4 14.5 %copy-start.11 = (bf16[2,256,256]{2,1,0:T(8,128)(2,1)}, bf16[2,256,256]{2,1,0:T(8,128)(2,1)S(1)}, u32[]{:S(2)}) copy-start(bf16[2,256,256]{2,1,0:T(8,128)(2,1)S(1)} %collective-permute-done.11) | copy-start | bytes 786436
  35.5 7.7 %collective-permute-start.12 = (bf16[2,256,256]{2,1,0:T(8,128)(2,1)S(1)}, bf16[2,256,256]{2,1,0:T(8,128)(2,1)S(1)}, u32[]{:S(2)}, u32[]{:S(2)}) collective-permute-start(bf16[2,256,256]{2,1,0:T(8,128)(2,1)S(1)} %collective-permute-done.11), channel_id=1, source_target_pairs={{0,7},{1,0},{2,1},{3,2},{4,3},{5,4},{6,5},{7,6},{8,15},{9,8},{10,9... | collective-permute-start | bytes 786440 | tf_op jit(solution)/shard_map/ppermute | solution.py:24
  43.0 16.8 %collective-permute-start.16 = (bf16[1,256,256]{2,1,0:T(8,128)(2,1)S(1)}, bf16[1,256,256]{2,1,0:T(8,128)(2,1)}, u32[]{:S(2)}, u32[]{:S(2)}) collective-permute-start(bf16[1,256,256]{2,1,0:T(8,128)(2,1)S(1)} %slice.84), channel_id=1, source_target_pairs={{0,1},{1,2},{2,3},{3,4},{4,5},{5,6},{6,7},{7,0},{8,9},{9,10},{10,1... | collective-permute-start | bytes 393224 | tf_op jit(solution)/shard_map/ppermute | solution.py:32
  43.2 16.7 %collective-permute-start.17 = (bf16[1,256,256]{2,1,0:T(8,128)(2,1)S(1)}, bf16[1,256,256]{2,1,0:T(8,128)(2,1)}, u32[]{:S(2)}, u32[]{:S(2)}) collective-permute-start(bf16[1,256,256]{2,1,0:T(8,128)(2,1)S(1)} %slice.85), channel_id=1, source_target_pairs={{0,7},{1,0},{2,1},{3,2},{4,3},{5,4},{6,5},{7,6},{8,15},{9,8},{10,9... | collective-permute-start | bytes 393224 | tf_op jit(solution)/shard_map/ppermute | solution.py:33
  61.3 8.3 %collective-permute-start = (bf16[256,256]{1,0:T(8,128)(2,1)S(1)}, bf16[256,256]{1,0:T(8,128)(2,1)S(1)}, u32[]{:S(2)}, u32[]{:S(2)}) collective-permute-start(bf16[256,256]{1,0:T(8,128)(2,1)S(1)} %copy.12), channel_id=1, source_target_pairs={{0,8},{8,0},{1,9},{9,1},{2,10},{10,2},{3,11},{11,3},{4,12},{12,4},... | collective-permute-start | bytes 393224 | tf_op jit(solution)/shard_map/while/body/eval_jaxpr/ppermute | solution.py:29
  69.8 10.5 %collective-permute-start.4 = (bf16[2,256,256]{2,1,0:T(8,128)(2,1)S(1)}, bf16[2,256,256]{2,1,0:T(8,128)(2,1)S(1)}, u32[]{:S(2)}, u32[]{:S(2)}) collective-permute-start(bf16[2,256,256]{2,1,0:T(8,128)(2,1)S(1)} %fusion.117), channel_id=1, source_target_pairs={{0,7},{1,0},{2,1},{3,2},{4,3},{5,4},{6,5},{7,6},{8,15},{9,8},{10,9... | collective-permute-start | bytes 786440 | tf_op jit(solution)/shard_map/while/body/eval_jaxpr/ppermute | solution.py:24
  74.9 9.1 %collective-permute-start.1 = (bf16[2,256,256]{2,1,0:T(8,128)(2,1)S(1)}, bf16[2,256,256]{2,1,0:T(8,128)(2,1)S(1)}, u32[]{:S(2)}, u32[]{:S(2)}) collective-permute-start(bf16[2,256,256]{2,1,0:T(8,128)(2,1)S(1)} %fusion.117), channel_id=1, source_target_pairs={{0,1},{1,2},{2,3},{3,4},{4,5},{5,6},{6,7},{7,0},{8,9},{9,10},{10,1... | collective-permute-start | bytes 786440 | tf_op jit(solution)/shard_map/while/body/eval_jaxpr/ppermute | solution.py:23
  80.2 8.2 %collective-permute-start.5 = (bf16[2,256,256]{2,1,0:T(8,128)(2,1)S(1)}, bf16[2,256,256]{2,1,0:T(8,128)(2,1)S(1)}, u32[]{:S(2)}, u32[]{:S(2)}) collective-permute-start(bf16[2,256,256]{2,1,0:T(8,128)(2,1)S(1)} %collective-permute-done.4), channel_id=1, source_target_pairs={{0,7},{1,0},{2,1},{3,2},{4,3},{5,4},{6,5},{7,6},{8,15},{9,8},{10,9... | collective-permute-start | bytes 786440 | tf_op jit(solution)/shard_map/while/body/eval_jaxpr/ppermute | solution.py:24
  83.9 8.2 %collective-permute-start.2 = (bf16[2,256,256]{2,1,0:T(8,128)(2,1)S(1)}, bf16[2,256,256]{2,1,0:T(8,128)(2,1)S(1)}, u32[]{:S(2)}, u32[]{:S(2)}) collective-permute-start(bf16[2,256,256]{2,1,0:T(8,128)(2,1)S(1)} %collective-permute-done.1), channel_id=1, source_target_pairs={{0,1},{1,2},{2,3},{3,4},{4,5},{5,6},{6,7},{7,0},{8,9},{9,10},{10,1... | collective-permute-start | bytes 786440 | tf_op jit(solution)/shard_map/while/body/eval_jaxpr/ppermute | solution.py:23
  88.4 7.6 %collective-permute-start.6 = (bf16[2,256,256]{2,1,0:T(8,128)(2,1)S(1)}, bf16[2,256,256]{2,1,0:T(8,128)(2,1)S(1)}, u32[]{:S(2)}, u32[]{:S(2)}) collective-permute-start(bf16[2,256,256]{2,1,0:T(8,128)(2,1)S(1)} %collective-permute-done.5), channel_id=1, source_target_pairs={{0,7},{1,0},{2,1},{3,2},{4,3},{5,4},{6,5},{7,6},{8,15},{9,8},{10,9... | collective-permute-start | bytes 786440 | tf_op jit(solution)/shard_map/while/body/eval_jaxpr/ppermute | solution.py:24
  92.1 7.7 %collective-permute-start.3 = (bf16[2,256,256]{2,1,0:T(8,128)(2,1)S(1)}, bf16[2,256,256]{2,1,0:T(8,128)(2,1)S(1)}, u32[]{:S(2)}, u32[]{:S(2)}) collective-permute-start(bf16[2,256,256]{2,1,0:T(8,128)(2,1)S(1)} %collective-permute-done.2), channel_id=1, source_target_pairs={{0,1},{1,2},{2,3},{3,4},{4,5},{5,6},{6,7},{7,0},{8,9},{9,10},{10,1... | collective-permute-start | bytes 786440 | tf_op jit(solution)/shard_map/while/body/eval_jaxpr/ppermute | solution.py:23
  96.0 6.3 %collective-permute-start.7 = (bf16[1,256,256]{2,1,0:T(8,128)(2,1)S(1)}, bf16[1,256,256]{2,1,0:T(8,128)(2,1)S(1)}, u32[]{:S(2)}, u32[]{:S(2)}) collective-permute-start(bf16[1,256,256]{2,1,0:T(8,128)(2,1)S(1)} %slice.148), channel_id=1, source_target_pairs={{0,7},{1,0},{2,1},{3,2},{4,3},{5,4},{6,5},{7,6},{8,15},{9,8},{10,9... | collective-permute-start | bytes 393224 | tf_op jit(solution)/shard_map/while/body/eval_jaxpr/ppermute | solution.py:33
  99.8 6.3 %collective-permute-start.8 = (bf16[1,256,256]{2,1,0:T(8,128)(2,1)S(1)}, bf16[1,256,256]{2,1,0:T(8,128)(2,1)S(1)}, u32[]{:S(2)}, u32[]{:S(2)}) collective-permute-start(bf16[1,256,256]{2,1,0:T(8,128)(2,1)S(1)} %slice.149), channel_id=1, source_target_pairs={{0,1},{1,2},{2,3},{3,4},{4,5},{5,6},{6,7},{7,0},{8,9},{9,10},{10,1... | collective-permute-start | bytes 393224 | tf_op jit(solution)/shard_map/while/body/eval_jaxpr/ppermute | solution.py:32
  106.6 6.6 %collective-permute-start = (bf16[256,256]{1,0:T(8,128)(2,1)S(1)}, bf16[256,256]{1,0:T(8,128)(2,1)S(1)}, u32[]{:S(2)}, u32[]{:S(2)}) collective-permute-start(bf16[256,256]{1,0:T(8,128)(2,1)S(1)} %copy.12), channel_id=1, source_target_pairs={{0,8},{8,0},{1,9},{9,1},{2,10},{10,2},{3,11},{11,3},{4,12},{12,4},... | collective-permute-start | bytes 393224 | tf_op jit(solution)/shard_map/while/body/eval_jaxpr/ppermute | solution.py:29
  113.4 8.0 %collective-permute-start.4 = (bf16[2,256,256]{2,1,0:T(8,128)(2,1)S(1)}, bf16[2,256,256]{2,1,0:T(8,128)(2,1)S(1)}, u32[]{:S(2)}, u32[]{:S(2)}) collective-permute-start(bf16[2,256,256]{2,1,0:T(8,128)(2,1)S(1)} %fusion.117), channel_id=1, source_target_pairs={{0,7},{1,0},{2,1},{3,2},{4,3},{5,4},{6,5},{7,6},{8,15},{9,8},{10,9... | collective-permute-start | bytes 786440 | tf_op jit(solution)/shard_map/while/body/eval_jaxpr/ppermute | solution.py:24
  113.5 10.3 %collective-permute-start.1 = (bf16[2,256,256]{2,1,0:T(8,128)(2,1)S(1)}, bf16[2,256,256]{2,1,0:T(8,128)(2,1)S(1)}, u32[]{:S(2)}, u32[]{:S(2)}) collective-permute-start(bf16[2,256,256]{2,1,0:T(8,128)(2,1)S(1)} %fusion.117), channel_id=1, source_target_pairs={{0,1},{1,2},{2,3},{3,4},{4,5},{5,6},{6,7},{7,0},{8,9},{9,10},{10,1... | collective-permute-start | bytes 786440 | tf_op jit(solution)/shard_map/while/body/eval_jaxpr/ppermute | solution.py:23
  121.4 8.2 %collective-permute-start.5 = (bf16[2,256,256]{2,1,0:T(8,128)(2,1)S(1)}, bf16[2,256,256]{2,1,0:T(8,128)(2,1)S(1)}, u32[]{:S(2)}, u32[]{:S(2)}) collective-permute-start(bf16[2,256,256]{2,1,0:T(8,128)(2,1)S(1)} %collective-permute-done.4), channel_id=1, source_target_pairs={{0,7},{1,0},{2,1},{3,2},{4,3},{5,4},{6,5},{7,6},{8,15},{9,8},{10,9... | collective-permute-start | bytes 786440 | tf_op jit(solution)/shard_map/while/body/eval_jaxpr/ppermute | solution.py:24
  123.8 9.5 %collective-permute-start.2 = (bf16[2,256,256]{2,1,0:T(8,128)(2,1)S(1)}, bf16[2,256,256]{2,1,0:T(8,128)(2,1)S(1)}, u32[]{:S(2)}, u32[]{:S(2)}) collective-permute-start(bf16[2,256,256]{2,1,0:T(8,128)(2,1)S(1)} %collective-permute-done.1), channel_id=1, source_target_pairs={{0,1},{1,2},{2,3},{3,4},{4,5},{5,6},{6,7},{7,0},{8,9},{9,10},{10,1... | collective-permute-start | bytes 786440 | tf_op jit(solution)/shard_map/while/body/eval_jaxpr/ppermute | solution.py:23
  129.6 7.6 %collective-permute-start.6 = (bf16[2,256,256]{2,1,0:T(8,128)(2,1)S(1)}, bf16[2,256,256]{2,1,0:T(8,128)(2,1)S(1)}, u32[]{:S(2)}, u32[]{:S(2)}) collective-permute-start(bf16[2,256,256]{2,1,0:T(8,128)(2,1)S(1)} %collective-permute-done.5), channel_id=1, source_target_pairs={{0,7},{1,0},{2,1},{3,2},{4,3},{5,4},{6,5},{7,6},{8,15},{9,8},{10,9... | collective-permute-start | bytes 786440 | tf_op jit(solution)/shard_map/while/body/eval_jaxpr/ppermute | solution.py:24
  133.3 7.7 %collective-permute-start.3 = (bf16[2,256,256]{2,1,0:T(8,128)(2,1)S(1)}, bf16[2,256,256]{2,1,0:T(8,128)(2,1)S(1)}, u32[]{:S(2)}, u32[]{:S(2)}) collective-permute-start(bf16[2,256,256]{2,1,0:T(8,128)(2,1)S(1)} %collective-permute-done.2), channel_id=1, source_target_pairs={{0,1},{1,2},{2,3},{3,4},{4,5},{5,6},{6,7},{7,0},{8,9},{9,10},{10,1... | collective-permute-start | bytes 786440 | tf_op jit(solution)/shard_map/while/body/eval_jaxpr/ppermute | solution.py:23
  137.2 6.3 %collective-permute-start.7 = (bf16[1,256,256]{2,1,0:T(8,128)(2,1)S(1)}, bf16[1,256,256]{2,1,0:T(8,128)(2,1)S(1)}, u32[]{:S(2)}, u32[]{:S(2)}) collective-permute-start(bf16[1,256,256]{2,1,0:T(8,128)(2,1)S(1)} %slice.148), channel_id=1, source_target_pairs={{0,7},{1,0},{2,1},{3,2},{4,3},{5,4},{6,5},{7,6},{8,15},{9,8},{10,9... | collective-permute-start | bytes 393224 | tf_op jit(solution)/shard_map/while/body/eval_jaxpr/ppermute | solution.py:33
  141.0 6.3 %collective-permute-start.8 = (bf16[1,256,256]{2,1,0:T(8,128)(2,1)S(1)}, bf16[1,256,256]{2,1,0:T(8,128)(2,1)S(1)}, u32[]{:S(2)}, u32[]{:S(2)}) collective-permute-start(bf16[1,256,256]{2,1,0:T(8,128)(2,1)S(1)} %slice.149), channel_id=1, source_target_pairs={{0,1},{1,2},{2,3},{3,4},{4,5},{5,6},{6,7},{7,0},{8,9},{9,10},{10,1... | collective-permute-start | bytes 393224 | tf_op jit(solution)/shard_map/while/body/eval_jaxpr/ppermute | solution.py:32
  (9 other events, 23.2 us)
Sparse Core Ops, SparseCore 0:
  9.3 40.5 all-gather.1

commit v10 on v5

--- a/solution.py
+++ b/solution.py
@@ -111,25 +111,33 @@
     dense = place_tiles(dest, tiles, total_blocks)
     dense = dense.reshape(z_count, y_count, local_width, local_width)
 
-    def apply_hamiltonian(field):
-        blocks = gather_col(field, y_count, z_count)
-        total = None
-        for d, chunk in enumerate(blocks):
-            part = jnp.einsum("ymj,yjo->mo", chunk, dense[d], preferred_element_type=jnp.float32)
-            total = part if total is None else total + part
-        return total
+    def products(pairs, operators):
+        totals = []
+        for operator in operators:
+            total = None
+            for d, chunk in enumerate(ring_blocks(pairs, "z", z_count, 0)):
+                part = jnp.einsum("ymj,yjo->mo", chunk, operator[d], preferred_element_type=jnp.float32)
+                total = part if total is None else total + part
+            totals.append(total)
+        return totals
 
+    y = lax.axis_index("y_hi")
+    swap = [(i, (i + 1) % y_count) for i in range(y_count)]
+
+    def order(own, other):
+        return jnp.where(y == 0, jnp.stack([own, other]), jnp.stack([other, own]))
+
+    partner_dense = lax.ppermute(dense, "y_hi", swap)
     previous = coeffs
-    current = apply_hamiltonian(coeffs).astype(jnp.bfloat16)
-
-    def recurse(repeat, carry):
-        previous, current = carry
-        product = apply_hamiltonian(current)
-        following = (2.0 * product - previous.astype(jnp.float32)).astype(jnp.bfloat16)
-        return current, following
-
-    previous, current = lax.fori_loop(0, STEPS - 1, recurse, (previous, current))
-    return current
+    partner_previous = lax.ppermute(coeffs, "y_hi", swap)
+    (product,) = products(order(coeffs, partner_previous), (dense,))
+    current = product.astype(jnp.bfloat16)
+    partner_current = lax.ppermute(current, "y_hi", swap)
+    own_product, partner_product = products(order(current, partner_current), (dense, partner_dense))
+    following = (2.0 * own_product - previous.astype(jnp.float32)).astype(jnp.bfloat16)
+    partner_following = (2.0 * partner_product - partner_previous.astype(jnp.float32)).astype(jnp.bfloat16)
+    (product,) = products(order(following, partner_following), (dense,))
+    return (2.0 * product - current.astype(jnp.float32)).astype(jnp.bfloat16)
 
 
 def solution(mesh):

time: 153 us -> 161 us (1.052)
  waiting for transfers between devices: 64.7 us -> 70.7 us
  Pallas kernels: 7.34 us -> 11.5 us
  starting transfers between devices: 52.5 us -> 50 us
    ppermute x9, waiting for transfers between devices: 26.6 us -> 5.09 us  [ring_blocks(): left = lax.ppermute(left, axis, bwd)]
    ppermute x9, waiting for transfers between devices: 12 us -> 31.8 us  [ring_blocks(): right = lax.ppermute(right, axis, fwd)]
    ppermute x3, waiting for transfers between devices: 10.9 us -> 22.1 us  [the longest x1 14 us: body(): partner_dense = lax.ppermute(dense, 'y_hi', swap)]
    ppermute x3, starting transfers between devices: 11 us -> 6.71 us  [the longest x1 3.28 us: body(): partner_previous = lax.ppermute(coeffs, 'y_hi', swap)]
    pallas_call x1, Pallas kernels: 7.34 us -> 11.5 us  [place_tiles(): pl.pallas_call(kernel, out_shape=jax.ShapeDtypeStruct((rows * size, block...]
    ppermute x9, starting transfers between devices: 26.3 us -> 29.4 us  [ring_blocks(): left = lax.ppermute(left, axis, bwd)]
    ppermute x3, waiting for transfers between devices: 4.36 us -> 2.19 us  [ring_blocks(): lax.ppermute(lax.slice_in_dim(left, split, None, axis=split_dim), axis, bwd)]
    unnamed x28 -> x6, local copies, waits for them, and re-layouts: 3.83 us -> 1.93 us
  transfers between devices with their start and end apart: 28 -> 28, of which waited for: 17 -> 16; matrix products, arithmetic and copies ran while one was open for 4% -> 6% of each run, Pallas kernels for 5% -> 7%
where the time goes in v10:
time: 161 us
  waiting for transfers between devices  70.7 us (44%)
  starting transfers between devices  50 us (31%)
  between operations  13.8 us (9%)
  Pallas kernels  11.5 us (7%)
  matrix products  8.03 us (5%)
  local copies, waits for them, and re-layouts  4.29 us (3%)
  other arithmetic  2.67 us (2%)
    ppermute x9, waiting for transfers between devices, ring_blocks(): right = lax.ppermute(right, axis, fwd)  31.8 us
    ppermute x9, starting transfers between devices, ring_blocks(): left = lax.ppermute(left, axis, bwd)  29.4 us
    ppermute x1, waiting for transfers between devices, body(): partner_dense = lax.ppermute(dense, 'y_hi', swap)  14 us
    pallas_call x1, Pallas kernels, place_tiles(): pl.pallas_call(kernel, out_shape=jax.ShapeDtypeStruct((rows * size, block...  11.5 us
    ppermute x3, starting transfers between devices, ring_blocks(): lax.ppermute(lax.slice_in_dim(left, split, None, axis=split_dim), axis, bwd)  10.9 us
    dot_general x32, matrix products, products(): jnp.einsum('ymj,yjo->mo', chunk, operator[d], preferred_element_type=jnp....  8.03 us
    ppermute x3, waiting for transfers between devices, ring_blocks(): lax.ppermute(lax.slice_in_dim(right, 0, split, axis=split_dim), axis, fwd)  6.27 us
    ppermute x9, waiting for transfers between devices, ring_blocks(): left = lax.ppermute(left, axis, bwd)  5.09 us
  transfers between devices with their start and end apart: 28, of which 16 were waited for; matrix products, arithmetic and copies ran while one was open for 6% of the time, Pallas kernels for 7%

profile of v10, /device:TPU:2, one launch (start us, length us, event | category | flops | bytes accessed | tf_op | source)
XLA Modules:
  0.0 160.9 jit_solution(13417103855626658867)
XLA Ops:
  6.5 1.7 %copy.6 = bf16[4,3,64,64]{2,3,1,0:T(8,128)(2,1)} copy(bf16[4,3,64,64]{3,2,1,0:T(8,128)(2,1)} %param.5) | data formatting | bytes 196608 | tf_op args[1]
  8.3 3.3 %collective-permute-start = (bf16[256,256]{1,0:T(8,128)(2,1)}, bf16[256,256]{1,0:T(8,128)(2,1)S(1)}, u32[]{:S(2)}, u32[]{:S(2)}) collective-permute-start(bf16[256,256]{1,0:T(8,128)(2,1)} %param.4), channel_id=1, source_target_pairs={{0,8},{8,0},{1,9},{9,1},{2,10},{10,2},{3,11},{11,3},{4,12},{12,4},... | collective-permute-start | bytes 393224 | tf_op jit(solution)/shard_map/ppermute | solution.py:132
  11.6 3.8 %collective-permute-done = bf16[256,256]{1,0:T(8,128)(2,1)S(1)} collective-permute-done((bf16[256,256]{1,0:T(8,128)(2,1)}, bf16[256,256]{1,0:T(8,128)(2,1)S(1)}, u32[]{:S(2)}, u32[]{:S(2)}) %collective-permute-start) | collective-permute-done | bytes 131104 | tf_op jit(solution)/shard_map/ppermute | solution.py:132
  16.3 2.0 %collective-permute-start.4 = (bf16[2,256,256]{2,1,0:T(8,128)(2,1)S(1)}, bf16[2,256,256]{2,1,0:T(8,128)(2,1)S(1)}, u32[]{:S(2)}, u32[]{:S(2)}) collective-permute-start(bf16[2,256,256]{2,1,0:T(8,128)(2,1)S(1)} %maximum_select_fusion), channel_id=1, source_target_pairs={{0,1},{1,2},{2,3},{3,4},{4,5},{5,6},{6,7},{7,0},{8,9},{9,10},{10,1... | collective-permute-start | bytes 786440 | tf_op jit(solution)/shard_map/ppermute | solution.py:23
  18.3 4.0 %collective-permute-start.1 = (bf16[2,256,256]{2,1,0:T(8,128)(2,1)S(1)}, bf16[2,256,256]{2,1,0:T(8,128)(2,1)S(1)}, u32[]{:S(2)}, u32[]{:S(2)}) collective-permute-start(bf16[2,256,256]{2,1,0:T(8,128)(2,1)S(1)} %maximum_select_fusion), channel_id=1, source_target_pairs={{0,7},{1,0},{2,1},{3,2},{4,3},{5,4},{6,5},{7,6},{8,15},{9,8},{10,9... | collective-permute-start | bytes 786440 | tf_op jit(solution)/shard_map/ppermute | solution.py:24
  22.4 5.4 %collective-permute-done.4 = bf16[2,256,256]{2,1,0:T(8,128)(2,1)S(1)} collective-permute-done((bf16[2,256,256]{2,1,0:T(8,128)(2,1)S(1)}, bf16[2,256,256]{2,1,0:T(8,128)(2,1)S(1)}, u32[]{:S(2)}, u32[]{:S(2)}) %collective-permute-start.4) | collective-permute-done | bytes 262176 | tf_op jit(solution)/shard_map/ppermute | solution.py:23
  27.7 3.2 %collective-permute-start.2 = (bf16[2,256,256]{2,1,0:T(8,128)(2,1)S(1)}, bf16[2,256,256]{2,1,0:T(8,128)(2,1)S(1)}, u32[]{:S(2)}, u32[]{:S(2)}) collective-permute-start(bf16[2,256,256]{2,1,0:T(8,128)(2,1)S(1)} %collective-permute-done.1), channel_id=1, source_target_pairs={{0,7},{1,0},{2,1},{3,2},{4,3},{5,4},{6,5},{7,6},{8,15},{9,8},{10,9... | collective-permute-start | bytes 786440 | tf_op jit(solution)/shard_map/ppermute | solution.py:24
  31.0 4.6 %collective-permute-done.5 = bf16[2,256,256]{2,1,0:T(8,128)(2,1)S(1)} collective-permute-done((bf16[2,256,256]{2,1,0:T(8,128)(2,1)S(1)}, bf16[2,256,256]{2,1,0:T(8,128)(2,1)S(1)}, u32[]{:S(2)}, u32[]{:S(2)}) %collective-permute-start.5) | collective-permute-done | bytes 262176 | tf_op jit(solution)/shard_map/ppermute | solution.py:23
  35.6 3.2 %collective-permute-start.3 = (bf16[2,256,256]{2,1,0:T(8,128)(2,1)S(1)}, bf16[2,256,256]{2,1,0:T(8,128)(2,1)S(1)}, u32[]{:S(2)}, u32[]{:S(2)}) collective-permute-start(bf16[2,256,256]{2,1,0:T(8,128)(2,1)S(1)} %collective-permute-done.2), channel_id=1, source_target_pairs={{0,7},{1,0},{2,1},{3,2},{4,3},{5,4},{6,5},{7,6},{8,15},{9,8},{10,9... | collective-permute-start | bytes 786440 | tf_op jit(solution)/shard_map/ppermute | solution.py:24
  42.7 3.8 %collective-permute-start.8 = (bf16[1,256,256]{2,1,0:T(8,128)(2,1)S(1)}, bf16[1,256,256]{2,1,0:T(8,128)(2,1)S(1)}, u32[]{:S(2)}, u32[]{:S(2)}) collective-permute-start(bf16[1,256,256]{2,1,0:T(8,128)(2,1)S(1)} %slice.119), channel_id=1, source_target_pairs={{0,7},{1,0},{2,1},{3,2},{4,3},{5,4},{6,5},{7,6},{8,15},{9,8},{10,9... | collective-permute-start | bytes 393224 | tf_op jit(solution)/shard_map/ppermute | solution.py:33
  46.6 3.2 %all-gather.2.cloned.1.call-done = bf16[4,48,64,64]{3,2,1,0:T(8,128)(2,1)} async-done(((bf16[4,3,64,64]{3,2,1,0:T(8,128)(2,1)}), bf16[4,48,64,64]{3,2,1,0:T(8,128)(2,1)}) %all-gather.2.cloned.1.call-update) | async-done | bytes 1572880 | tf_op jit(solution)/shard_map/all_gather | solution.py:103
  49.7 11.5 %shard_map.46 = bf16[4096,256]{1,0:T(8,128)(2,1)} custom-call(s32[192]{0:T(256)} %reshape.43.dest_ref, bf16[1,4,48,64,64]{4,3,2,1,0:T(8,128)(2,1)} %bitcast.266), custom_call_target="tpu_custom_call" | custom-call | tf_op jit(solution)/shard_map/pallas_call | solution.py:80
  65.4 3.0 %collective-permute-start.18 = (bf16[8,2,256,256]{3,2,1,0:T(8,128)(2,1)S(1)}, bf16[8,2,256,256]{3,2,1,0:T(8,128)(2,1)S(1)}, u32[]{:S(2)}, u32[]{:S(2)}) collective-permute-start(bf16[8,2,256,256]{3,2,1,0:T(8,128)(2,1)S(1)} %bitcast.241), channel_id=1, source_target_pairs={{0,8},{8,0},{1,9},{9,1},{2,10},{10,2},{3,11},{11,3},{4,12},{12,4},... | collective-permute-start | bytes 6291464 | tf_op jit(solution)/shard_map/ppermute | solution.py:130
  68.4 4.3 %collective-permute-done.9 = bf16[256,256]{1,0:T(8,128)(2,1)S(1)} collective-permute-done((bf16[256,256]{1,0:T(8,128)(2,1)S(1)}, bf16[256,256]{1,0:T(8,128)(2,1)S(1)}, u32[]{:S(2)}, u32[]{:S(2)}) %collective-permute-start.9) | collective-permute-done | bytes 131104 | tf_op jit(solution)/shard_map/ppermute | solution.py:135
  72.9 3.2 %collective-permute-start.10 = (bf16[2,256,256]{2,1,0:T(8,128)(2,1)S(1)}, bf16[2,256,256]{2,1,0:T(8,128)(2,1)S(1)}, u32[]{:S(2)}, u32[]{:S(2)}) collective-permute-start(bf16[2,256,256]{2,1,0:T(8,128)(2,1)S(1)} %maximum_select_fusion.1), channel_id=1, source_target_pairs={{0,7},{1,0},{2,1},{3,2},{4,3},{5,4},{6,5},{7,6},{8,15},{9,8},{10,9... | collective-permute-start | bytes 786440 | tf_op jit(solution)/shard_map/ppermute | solution.py:24
  76.1 4.8 %collective-permute-done.13 = bf16[2,256,256]{2,1,0:T(8,128)(2,1)S(1)} collective-permute-done((bf16[2,256,256]{2,1,0:T(8,128)(2,1)S(1)}, bf16[2,256,256]{2,1,0:T(8,128)(2,1)S(1)}, u32[]{:S(2)}, u32[]{:S(2)}) %collective-permute-start.13) | collective-permute-done | bytes 262176 | tf_op jit(solution)/shard_map/ppermute | solution.py:23
  80.9 3.2 %collective-permute-start.11 = (bf16[2,256,256]{2,1,0:T(8,128)(2,1)S(1)}, bf16[2,256,256]{2,1,0:T(8,128)(2,1)S(1)}, u32[]{:S(2)}, u32[]{:S(2)}) collective-permute-start(bf16[2,256,256]{2,1,0:T(8,128)(2,1)S(1)} %collective-permute-done.10), channel_id=1, source_target_pairs={{0,7},{1,0},{2,1},{3,2},{4,3},{5,4},{6,5},{7,6},{8,15},{9,8},{10,9... | collective-permute-start | bytes 786440 | tf_op jit(solution)/shard_map/ppermute | solution.py:24
  84.9 3.6 %collective-permute-done.14 = bf16[2,256,256]{2,1,0:T(8,128)(2,1)S(1)} collective-permute-done((bf16[2,256,256]{2,1,0:T(8,128)(2,1)S(1)}, bf16[2,256,256]{2,1,0:T(8,128)(2,1)S(1)}, u32[]{:S(2)}, u32[]{:S(2)}) %collective-permute-start.14) | collective-permute-done | bytes 262176 | tf_op jit(solution)/shard_map/ppermute | solution.py:23
  88.5 3.2 %collective-permute-start.12 = (bf16[2,256,256]{2,1,0:T(8,128)(2,1)S(1)}, bf16[2,256,256]{2,1,0:T(8,128)(2,1)S(1)}, u32[]{:S(2)}, u32[]{:S(2)}) collective-permute-start(bf16[2,256,256]{2,1,0:T(8,128)(2,1)S(1)} %collective-permute-done.11), channel_id=1, source_target_pairs={{0,7},{1,0},{2,1},{3,2},{4,3},{5,4},{6,5},{7,6},{8,15},{9,8},{10,9... | collective-permute-start | bytes 786440 | tf_op jit(solution)/shard_map/ppermute | solution.py:24
  92.2 3.9 %collective-permute-done.15 = bf16[2,256,256]{2,1,0:T(8,128)(2,1)S(1)} collective-permute-done((bf16[2,256,256]{2,1,0:T(8,128)(2,1)S(1)}, bf16[2,256,256]{2,1,0:T(8,128)(2,1)S(1)}, u32[]{:S(2)}, u32[]{:S(2)}) %collective-permute-start.15) | collective-permute-done | bytes 262176 | tf_op jit(solution)/shard_map/ppermute | solution.py:23
  96.3 3.4 %collective-permute-start.17 = (bf16[1,256,256]{2,1,0:T(8,128)(2,1)S(1)}, bf16[1,256,256]{2,1,0:T(8,128)(2,1)S(1)}, u32[]{:S(2)}, u32[]{:S(2)}) collective-permute-start(bf16[1,256,256]{2,1,0:T(8,128)(2,1)S(1)} %slice.125), channel_id=1, source_target_pairs={{0,7},{1,0},{2,1},{3,2},{4,3},{5,4},{6,5},{7,6},{8,15},{9,8},{10,9... | collective-permute-start | bytes 393224 | tf_op jit(solution)/shard_map/ppermute | solution.py:33
  99.9 2.5 %collective-permute-done.16 = bf16[1,256,256]{2,1,0:T(8,128)(2,1)S(1)} collective-permute-done((bf16[1,256,256]{2,1,0:T(8,128)(2,1)S(1)}, bf16[1,256,256]{2,1,0:T(8,128)(2,1)S(1)}, u32[]{:S(2)}, u32[]{:S(2)}) %collective-permute-start.16) | collective-permute-done | bytes 131104 | tf_op jit(solution)/shard_map/ppermute | solution.py:32
  102.9 14.0 %collective-permute-done.18 = bf16[8,2,256,256]{3,2,1,0:T(8,128)(2,1)S(1)} collective-permute-done((bf16[8,2,256,256]{3,2,1,0:T(8,128)(2,1)S(1)}, bf16[8,2,256,256]{3,2,1,0:T(8,128)(2,1)S(1)}, u32[]{:S(2)}, u32[]{:S(2)}) %collective-permute-start.18) | collective-permute-done | bytes 2097184 | tf_op jit(solution)/shard_map/ppermute | solution.py:130
  119.5 2.7 %collective-permute-start.19 = (bf16[2,256,256]{2,1,0:T(8,128)(2,1)S(1)}, bf16[2,256,256]{2,1,0:T(8,128)(2,1)S(1)}, u32[]{:S(2)}, u32[]{:S(2)}) collective-permute-start(bf16[2,256,256]{2,1,0:T(8,128)(2,1)S(1)} %maximum_select_fusion.2), channel_id=1, source_target_pairs={{0,7},{1,0},{2,1},{3,2},{4,3},{5,4},{6,5},{7,6},{8,15},{9,8},{10,9... | collective-permute-start | bytes 786440 | tf_op jit(solution)/shard_map/ppermute | solution.py:24
  122.4 5.3 %collective-permute-done.22 = bf16[2,256,256]{2,1,0:T(8,128)(2,1)S(1)} collective-permute-done((bf16[2,256,256]{2,1,0:T(8,128)(2,1)S(1)}, bf16[2,256,256]{2,1,0:T(8,128)(2,1)S(1)}, u32[]{:S(2)}, u32[]{:S(2)}) %collective-permute-start.22) | collective-permute-done | bytes 262176 | tf_op jit(solution)/shard_map/ppermute | solution.py:23
  127.8 3.2 %collective-permute-start.20 = (bf16[2,256,256]{2,1,0:T(8,128)(2,1)S(1)}, bf16[2,256,256]{2,1,0:T(8,128)(2,1)S(1)}, u32[]{:S(2)}, u32[]{:S(2)}) collective-permute-start(bf16[2,256,256]{2,1,0:T(8,128)(2,1)S(1)} %collective-permute-done.19), channel_id=1, source_target_pairs={{0,7},{1,0},{2,1},{3,2},{4,3},{5,4},{6,5},{7,6},{8,15},{9,8},{10,9... | collective-permute-start | bytes 786440 | tf_op jit(solution)/shard_map/ppermute | solution.py:24
  131.5 4.2 %collective-permute-done.23 = bf16[2,256,256]{2,1,0:T(8,128)(2,1)S(1)} collective-permute-done((bf16[2,256,256]{2,1,0:T(8,128)(2,1)S(1)}, bf16[2,256,256]{2,1,0:T(8,128)(2,1)S(1)}, u32[]{:S(2)}, u32[]{:S(2)}) %collective-permute-start.23) | collective-permute-done | bytes 262176 | tf_op jit(solution)/shard_map/ppermute | solution.py:23
  135.7 3.2 %collective-permute-start.21 = (bf16[2,256,256]{2,1,0:T(8,128)(2,1)S(1)}, bf16[2,256,256]{2,1,0:T(8,128)(2,1)S(1)}, u32[]{:S(2)}, u32[]{:S(2)}) collective-permute-start(bf16[2,256,256]{2,1,0:T(8,128)(2,1)S(1)} %collective-permute-done.20), channel_id=1, source_target_pairs={{0,7},{1,0},{2,1},{3,2},{4,3},{5,4},{6,5},{7,6},{8,15},{9,8},{10,9... | collective-permute-start | bytes 786440 | tf_op jit(solution)/shard_map/ppermute | solution.py:24
  139.4 3.4 %collective-permute-done.21 = bf16[2,256,256]{2,1,0:T(8,128)(2,1)S(1)} collective-permute-done((bf16[2,256,256]{2,1,0:T(8,128)(2,1)S(1)}, bf16[2,256,256]{2,1,0:T(8,128)(2,1)S(1)}, u32[]{:S(2)}, u32[]{:S(2)}) %collective-permute-start.21) | collective-permute-done | bytes 262176 | tf_op jit(solution)/shard_map/ppermute | solution.py:24
  142.8 3.8 %collective-permute-start.26 = (bf16[1,256,256]{2,1,0:T(8,128)(2,1)S(1)}, bf16[1,256,256]{2,1,0:T(8,128)(2,1)S(1)}, u32[]{:S(2)}, u32[]{:S(2)}) collective-permute-start(bf16[1,256,256]{2,1,0:T(8,128)(2,1)S(1)} %slice.135), channel_id=1, source_target_pairs={{0,7},{1,0},{2,1},{3,2},{4,3},{5,4},{6,5},{7,6},{8,15},{9,8},{10,9... | collective-permute-start | bytes 393224 | tf_op jit(solution)/shard_map/ppermute | solution.py:33
  146.9 2.2 %collective-permute-done.26 = bf16[1,256,256]{2,1,0:T(8,128)(2,1)S(1)} collective-permute-done((bf16[1,256,256]{2,1,0:T(8,128)(2,1)S(1)}, bf16[1,256,256]{2,1,0:T(8,128)(2,1)S(1)}, u32[]{:S(2)}, u32[]{:S(2)}) %collective-permute-start.26) | collective-permute-done | bytes 131104 | tf_op jit(solution)/shard_map/ppermute | solution.py:33
  149.1 3.8 %collective-permute-done.25 = bf16[1,256,256]{2,1,0:T(8,128)(2,1)S(1)} collective-permute-done((bf16[1,256,256]{2,1,0:T(8,128)(2,1)S(1)}, bf16[1,256,256]{2,1,0:T(8,128)(2,1)S(1)}, u32[]{:S(2)}, u32[]{:S(2)}) %collective-permute-start.25) | collective-permute-done | bytes 131104 | tf_op jit(solution)/shard_map/ppermute | solution.py:32
  (79 shorter events, 16.3 us)
Async XLA Ops:
  6.5 43.2 %all-gather.2.cloned.1.call-start = ((), (), s32[]{:S(2)}) async-start(), calls=%async_computation | async-start | bytes 3342336 | tf_op jit(solution)/shard_map/all_gather | solution.py:103
  8.3 7.0 %collective-permute-start = (bf16[256,256]{1,0:T(8,128)(2,1)}, bf16[256,256]{1,0:T(8,128)(2,1)S(1)}, u32[]{:S(2)}, u32[]{:S(2)}) collective-permute-start(bf16[256,256]{1,0:T(8,128)(2,1)} %param.4), channel_id=1, source_target_pairs={{0,8},{8,0},{1,9},{9,1},{2,10},{10,2},{3,11},{11,3},{4,12},{12,4},... | collective-permute-start | bytes 393224 | tf_op jit(solution)/shard_map/ppermute | solution.py:132
  16.3 11.4 %collective-permute-start.4 = (bf16[2,256,256]{2,1,0:T(8,128)(2,1)S(1)}, bf16[2,256,256]{2,1,0:T(8,128)(2,1)S(1)}, u32[]{:S(2)}, u32[]{:S(2)}) collective-permute-start(bf16[2,256,256]{2,1,0:T(8,128)(2,1)S(1)} %maximum_select_fusion), channel_id=1, source_target_pairs={{0,1},{1,2},{2,3},{3,4},{4,5},{5,6},{6,7},{7,0},{8,9},{9,10},{10,1... | collective-permute-start | bytes 786440 | tf_op jit(solution)/shard_map/ppermute | solution.py:23
  18.3 9.4 %collective-permute-start.1 = (bf16[2,256,256]{2,1,0:T(8,128)(2,1)S(1)}, bf16[2,256,256]{2,1,0:T(8,128)(2,1)S(1)}, u32[]{:S(2)}, u32[]{:S(2)}) collective-permute-start(bf16[2,256,256]{2,1,0:T(8,128)(2,1)S(1)} %maximum_select_fusion), channel_id=1, source_target_pairs={{0,7},{1,0},{2,1},{3,2},{4,3},{5,4},{6,5},{7,6},{8,15},{9,8},{10,9... | collective-permute-start | bytes 786440 | tf_op jit(solution)/shard_map/ppermute | solution.py:24
  27.7 7.8 %collective-permute-start.5 = (bf16[2,256,256]{2,1,0:T(8,128)(2,1)S(1)}, bf16[2,256,256]{2,1,0:T(8,128)(2,1)S(1)}, u32[]{:S(2)}, u32[]{:S(2)}) collective-permute-start(bf16[2,256,256]{2,1,0:T(8,128)(2,1)S(1)} %collective-permute-done.4), channel_id=1, source_target_pairs={{0,1},{1,2},{2,3},{3,4},{4,5},{5,6},{6,7},{7,0},{8,9},{9,10},{10,1... | collective-permute-start | bytes 786440 | tf_op jit(solution)/shard_map/ppermute | solution.py:23
  27.7 7.8 %collective-permute-start.2 = (bf16[2,256,256]{2,1,0:T(8,128)(2,1)S(1)}, bf16[2,256,256]{2,1,0:T(8,128)(2,1)S(1)}, u32[]{:S(2)}, u32[]{:S(2)}) collective-permute-start(bf16[2,256,256]{2,1,0:T(8,128)(2,1)S(1)} %collective-permute-done.1), channel_id=1, source_target_pairs={{0,7},{1,0},{2,1},{3,2},{4,3},{5,4},{6,5},{7,6},{8,15},{9,8},{10,9... | collective-permute-start | bytes 786440 | tf_op jit(solution)/shard_map/ppermute | solution.py:24
  35.6 10.9 %collective-permute-start.6 = (bf16[2,256,256]{2,1,0:T(8,128)(2,1)S(1)}, bf16[2,256,256]{2,1,0:T(8,128)(2,1)S(1)}, u32[]{:S(2)}, u32[]{:S(2)}) collective-permute-start(bf16[2,256,256]{2,1,0:T(8,128)(2,1)S(1)} %collective-permute-done.5), channel_id=1, source_target_pairs={{0,1},{1,2},{2,3},{3,4},{4,5},{5,6},{6,7},{7,0},{8,9},{9,10},{10,1... | collective-permute-start | bytes 786440 | tf_op jit(solution)/shard_map/ppermute | solution.py:23
  35.6 7.1 %collective-permute-start.3 = (bf16[2,256,256]{2,1,0:T(8,128)(2,1)S(1)}, bf16[2,256,256]{2,1,0:T(8,128)(2,1)S(1)}, u32[]{:S(2)}, u32[]{:S(2)}) collective-permute-start(bf16[2,256,256]{2,1,0:T(8,128)(2,1)S(1)} %collective-permute-done.2), channel_id=1, source_target_pairs={{0,7},{1,0},{2,1},{3,2},{4,3},{5,4},{6,5},{7,6},{8,15},{9,8},{10,9... | collective-permute-start | bytes 786440 | tf_op jit(solution)/shard_map/ppermute | solution.py:24
  42.7 21.6 %collective-permute-start.8 = (bf16[1,256,256]{2,1,0:T(8,128)(2,1)S(1)}, bf16[1,256,256]{2,1,0:T(8,128)(2,1)S(1)}, u32[]{:S(2)}, u32[]{:S(2)}) collective-permute-start(bf16[1,256,256]{2,1,0:T(8,128)(2,1)S(1)} %slice.119), channel_id=1, source_target_pairs={{0,7},{1,0},{2,1},{3,2},{4,3},{5,4},{6,5},{7,6},{8,15},{9,8},{10,9... | collective-permute-start | bytes 393224 | tf_op jit(solution)/shard_map/ppermute | solution.py:33
  46.5 17.8 %collective-permute-start.7 = (bf16[1,256,256]{2,1,0:T(8,128)(2,1)S(1)}, bf16[1,256,256]{2,1,0:T(8,128)(2,1)S(1)}, u32[]{:S(2)}, u32[]{:S(2)}) collective-permute-start(bf16[1,256,256]{2,1,0:T(8,128)(2,1)S(1)} %slice.118), channel_id=1, source_target_pairs={{0,1},{1,2},{2,3},{3,4},{4,5},{5,6},{6,7},{7,0},{8,9},{9,10},{10,1... | collective-permute-start | bytes 393224 | tf_op jit(solution)/shard_map/ppermute | solution.py:32
  63.8 1.6 copy-start
  64.8 8.0 %collective-permute-start.9 = (bf16[256,256]{1,0:T(8,128)(2,1)S(1)}, bf16[256,256]{1,0:T(8,128)(2,1)S(1)}, u32[]{:S(2)}, u32[]{:S(2)}) collective-permute-start(bf16[256,256]{1,0:T(8,128)(2,1)S(1)} %fusion.37), channel_id=1, source_target_pairs={{0,8},{8,0},{1,9},{9,1},{2,10},{10,2},{3,11},{11,3},{4,12},{12,4},... | collective-permute-start | bytes 393224 | tf_op jit(solution)/shard_map/ppermute | solution.py:135
  65.4 51.5 %collective-permute-start.18 = (bf16[8,2,256,256]{3,2,1,0:T(8,128)(2,1)S(1)}, bf16[8,2,256,256]{3,2,1,0:T(8,128)(2,1)S(1)}, u32[]{:S(2)}, u32[]{:S(2)}) collective-permute-start(bf16[8,2,256,256]{3,2,1,0:T(8,128)(2,1)S(1)} %bitcast.241), channel_id=1, source_target_pairs={{0,8},{8,0},{1,9},{9,1},{2,10},{10,2},{3,11},{11,3},{4,12},{12,4},... | collective-permute-start | bytes 6291464 | tf_op jit(solution)/shard_map/ppermute | solution.py:130
  72.8 8.1 %collective-permute-start.13 = (bf16[2,256,256]{2,1,0:T(8,128)(2,1)S(1)}, bf16[2,256,256]{2,1,0:T(8,128)(2,1)S(1)}, u32[]{:S(2)}, u32[]{:S(2)}) collective-permute-start(bf16[2,256,256]{2,1,0:T(8,128)(2,1)S(1)} %maximum_select_fusion.1), channel_id=1, source_target_pairs={{0,1},{1,2},{2,3},{3,4},{4,5},{5,6},{6,7},{7,0},{8,9},{9,10},{10,1... | collective-permute-start | bytes 786440 | tf_op jit(solution)/shard_map/ppermute | solution.py:23
  72.9 8.0 %collective-permute-start.10 = (bf16[2,256,256]{2,1,0:T(8,128)(2,1)S(1)}, bf16[2,256,256]{2,1,0:T(8,128)(2,1)S(1)}, u32[]{:S(2)}, u32[]{:S(2)}) collective-permute-start(bf16[2,256,256]{2,1,0:T(8,128)(2,1)S(1)} %maximum_select_fusion.1), channel_id=1, source_target_pairs={{0,7},{1,0},{2,1},{3,2},{4,3},{5,4},{6,5},{7,6},{8,15},{9,8},{10,9... | collective-permute-start | bytes 786440 | tf_op jit(solution)/shard_map/ppermute | solution.py:24
  80.9 7.6 %collective-permute-start.14 = (bf16[2,256,256]{2,1,0:T(8,128)(2,1)S(1)}, bf16[2,256,256]{2,1,0:T(8,128)(2,1)S(1)}, u32[]{:S(2)}, u32[]{:S(2)}) collective-permute-start(bf16[2,256,256]{2,1,0:T(8,128)(2,1)S(1)} %collective-permute-done.13), channel_id=1, source_target_pairs={{0,1},{1,2},{2,3},{3,4},{4,5},{5,6},{6,7},{7,0},{8,9},{9,10},{10,1... | collective-permute-start | bytes 786440 | tf_op jit(solution)/shard_map/ppermute | solution.py:23
  80.9 7.6 %collective-permute-start.11 = (bf16[2,256,256]{2,1,0:T(8,128)(2,1)S(1)}, bf16[2,256,256]{2,1,0:T(8,128)(2,1)S(1)}, u32[]{:S(2)}, u32[]{:S(2)}) collective-permute-start(bf16[2,256,256]{2,1,0:T(8,128)(2,1)S(1)} %collective-permute-done.10), channel_id=1, source_target_pairs={{0,7},{1,0},{2,1},{3,2},{4,3},{5,4},{6,5},{7,6},{8,15},{9,8},{10,9... | collective-permute-start | bytes 786440 | tf_op jit(solution)/shard_map/ppermute | solution.py:24
  84.9 17.8 %copy-start.1 = (bf16[256,256]{1,0:T(8,128)(2,1)S(1)}, bf16[256,256]{1,0:T(8,128)(2,1)}, u32[]{:S(2)}) copy-start(bf16[256,256]{1,0:T(8,128)(2,1)} %param.4) | copy-start | bytes 393220
  88.5 7.6 %collective-permute-start.15 = (bf16[2,256,256]{2,1,0:T(8,128)(2,1)S(1)}, bf16[2,256,256]{2,1,0:T(8,128)(2,1)S(1)}, u32[]{:S(2)}, u32[]{:S(2)}) collective-permute-start(bf16[2,256,256]{2,1,0:T(8,128)(2,1)S(1)} %collective-permute-done.14), channel_id=1, source_target_pairs={{0,1},{1,2},{2,3},{3,4},{4,5},{5,6},{6,7},{7,0},{8,9},{9,10},{10,1... | collective-permute-start | bytes 786440 | tf_op jit(solution)/shard_map/ppermute | solution.py:23
  88.5 7.7 %collective-permute-start.12 = (bf16[2,256,256]{2,1,0:T(8,128)(2,1)S(1)}, bf16[2,256,256]{2,1,0:T(8,128)(2,1)S(1)}, u32[]{:S(2)}, u32[]{:S(2)}) collective-permute-start(bf16[2,256,256]{2,1,0:T(8,128)(2,1)S(1)} %collective-permute-done.11), channel_id=1, source_target_pairs={{0,7},{1,0},{2,1},{3,2},{4,3},{5,4},{6,5},{7,6},{8,15},{9,8},{10,9... | collective-permute-start | bytes 786440 | tf_op jit(solution)/shard_map/ppermute | solution.py:24
  96.1 6.3 %collective-permute-start.16 = (bf16[1,256,256]{2,1,0:T(8,128)(2,1)S(1)}, bf16[1,256,256]{2,1,0:T(8,128)(2,1)S(1)}, u32[]{:S(2)}, u32[]{:S(2)}) collective-permute-start(bf16[1,256,256]{2,1,0:T(8,128)(2,1)S(1)} %slice.124), channel_id=1, source_target_pairs={{0,1},{1,2},{2,3},{3,4},{4,5},{5,6},{6,7},{7,0},{8,9},{9,10},{10,1... | collective-permute-start | bytes 393224 | tf_op jit(solution)/shard_map/ppermute | solution.py:32
  96.3 6.2 %collective-permute-start.17 = (bf16[1,256,256]{2,1,0:T(8,128)(2,1)S(1)}, bf16[1,256,256]{2,1,0:T(8,128)(2,1)S(1)}, u32[]{:S(2)}, u32[]{:S(2)}) collective-permute-start(bf16[1,256,256]{2,1,0:T(8,128)(2,1)S(1)} %slice.125), channel_id=1, source_target_pairs={{0,7},{1,0},{2,1},{3,2},{4,3},{5,4},{6,5},{7,6},{8,15},{9,8},{10,9... | collective-permute-start | bytes 393224 | tf_op jit(solution)/shard_map/ppermute | solution.py:33
  118.9 8.9 %collective-permute-start.22 = (bf16[2,256,256]{2,1,0:T(8,128)(2,1)S(1)}, bf16[2,256,256]{2,1,0:T(8,128)(2,1)S(1)}, u32[]{:S(2)}, u32[]{:S(2)}) collective-permute-start(bf16[2,256,256]{2,1,0:T(8,128)(2,1)S(1)} %maximum_select_fusion.2), channel_id=1, source_target_pairs={{0,1},{1,2},{2,3},{3,4},{4,5},{5,6},{6,7},{7,0},{8,9},{9,10},{10,1... | collective-permute-start | bytes 786440 | tf_op jit(solution)/shard_map/ppermute | solution.py:23
  119.5 8.3 %collective-permute-start.19 = (bf16[2,256,256]{2,1,0:T(8,128)(2,1)S(1)}, bf16[2,256,256]{2,1,0:T(8,128)(2,1)S(1)}, u32[]{:S(2)}, u32[]{:S(2)}) collective-permute-start(bf16[2,256,256]{2,1,0:T(8,128)(2,1)S(1)} %maximum_select_fusion.2), channel_id=1, source_target_pairs={{0,7},{1,0},{2,1},{3,2},{4,3},{5,4},{6,5},{7,6},{8,15},{9,8},{10,9... | collective-permute-start | bytes 786440 | tf_op jit(solution)/shard_map/ppermute | solution.py:24
  127.8 7.9 %collective-permute-start.23 = (bf16[2,256,256]{2,1,0:T(8,128)(2,1)S(1)}, bf16[2,256,256]{2,1,0:T(8,128)(2,1)S(1)}, u32[]{:S(2)}, u32[]{:S(2)}) collective-permute-start(bf16[2,256,256]{2,1,0:T(8,128)(2,1)S(1)} %collective-permute-done.22), channel_id=1, source_target_pairs={{0,1},{1,2},{2,3},{3,4},{4,5},{5,6},{6,7},{7,0},{8,9},{9,10},{10,1... | collective-permute-start | bytes 786440 | tf_op jit(solution)/shard_map/ppermute | solution.py:23
  127.8 7.9 %collective-permute-start.20 = (bf16[2,256,256]{2,1,0:T(8,128)(2,1)S(1)}, bf16[2,256,256]{2,1,0:T(8,128)(2,1)S(1)}, u32[]{:S(2)}, u32[]{:S(2)}) collective-permute-start(bf16[2,256,256]{2,1,0:T(8,128)(2,1)S(1)} %collective-permute-done.19), channel_id=1, source_target_pairs={{0,7},{1,0},{2,1},{3,2},{4,3},{5,4},{6,5},{7,6},{8,15},{9,8},{10,9... | collective-permute-start | bytes 786440 | tf_op jit(solution)/shard_map/ppermute | solution.py:24
  135.7 10.9 %collective-permute-start.24 = (bf16[2,256,256]{2,1,0:T(8,128)(2,1)S(1)}, bf16[2,256,256]{2,1,0:T(8,128)(2,1)S(1)}, u32[]{:S(2)}, u32[]{:S(2)}) collective-permute-start(bf16[2,256,256]{2,1,0:T(8,128)(2,1)S(1)} %collective-permute-done.23), channel_id=1, source_target_pairs={{0,1},{1,2},{2,3},{3,4},{4,5},{5,6},{6,7},{7,0},{8,9},{9,10},{10,1... | collective-permute-start | bytes 786440 | tf_op jit(solution)/shard_map/ppermute | solution.py:23
  135.7 7.1 %collective-permute-start.21 = (bf16[2,256,256]{2,1,0:T(8,128)(2,1)S(1)}, bf16[2,256,256]{2,1,0:T(8,128)(2,1)S(1)}, u32[]{:S(2)}, u32[]{:S(2)}) collective-permute-start(bf16[2,256,256]{2,1,0:T(8,128)(2,1)S(1)} %collective-permute-done.20), channel_id=1, source_target_pairs={{0,7},{1,0},{2,1},{3,2},{4,3},{5,4},{6,5},{7,6},{8,15},{9,8},{10,9... | collective-permute-start | bytes 786440 | tf_op jit(solution)/shard_map/ppermute | solution.py:24
  142.8 6.3 %collective-permute-start.26 = (bf16[1,256,256]{2,1,0:T(8,128)(2,1)S(1)}, bf16[1,256,256]{2,1,0:T(8,128)(2,1)S(1)}, u32[]{:S(2)}, u32[]{:S(2)}) collective-permute-start(bf16[1,256,256]{2,1,0:T(8,128)(2,1)S(1)} %slice.135), channel_id=1, source_target_pairs={{0,7},{1,0},{2,1},{3,2},{4,3},{5,4},{6,5},{7,6},{8,15},{9,8},{10,9... | collective-permute-start | bytes 393224 | tf_op jit(solution)/shard_map/ppermute | solution.py:33
  146.6 6.3 %collective-permute-start.25 = (bf16[1,256,256]{2,1,0:T(8,128)(2,1)S(1)}, bf16[1,256,256]{2,1,0:T(8,128)(2,1)S(1)}, u32[]{:S(2)}, u32[]{:S(2)}) collective-permute-start(bf16[1,256,256]{2,1,0:T(8,128)(2,1)S(1)} %slice.134), channel_id=1, source_target_pairs={{0,1},{1,2},{2,3},{3,4},{4,5},{5,6},{6,7},{7,0},{8,9},{9,10},{10,1... | collective-permute-start | bytes 393224 | tf_op jit(solution)/shard_map/ppermute | solution.py:32
Sparse Core Ops, SparseCore 0:
  9.1 40.5 all-gather.1

commit v11 on v5

--- a/solution.py
+++ b/solution.py
@@ -71,7 +71,8 @@
                 @pl.when(target >= 0)
                 def _():
                     start = pl.multiple_of(target * size, size)
-                    out_ref[pl.ds(start, size), b * size:(b + 1) * size] = tiles_ref[p // local_slots, b, p % local_slots]
+                    tile = tiles_ref[p // local_slots, b, p % local_slots].astype(jnp.float32)
+                    out_ref[pl.ds(start, size), b * size:(b + 1) * size] = tile.T.astype(out_ref.dtype)
 
                 return carry
 
@@ -100,7 +101,7 @@
     live_counts = jnp.sum(jnp.where(region_match, density[None, :], 0), axis=1)
     live_mask = jnp.arange(slot_count, dtype=jnp.int32)[None, :] < live_counts[:, None]
 
-    tiles = lax.all_gather(jnp.swapaxes(block_tiles, 2, 3), ROW_AXES, axis=1, tiled=True)[None]
+    tiles = lax.all_gather(block_tiles, ROW_AXES, axis=1, tiled=True)[None]
     ring_neighbours = neighbours
     ring_live = live_mask
     per_col = block_rows

time: 153 us -> 163 us (1.065)
  Pallas kernels: 7.34 us -> 20.7 us
  starting transfers between devices: 52.5 us -> 43.1 us
  waiting for transfers between devices: 64.7 us -> 73.8 us
  local copies, waits for them, and re-layouts: 4.72 us -> 3.01 us
    pallas_call x1, Pallas kernels: 7.34 us -> 20.7 us  [place_tiles(): pl.pallas_call(kernel, out_shape=jax.ShapeDtypeStruct((rows * size, block...]
    ppermute x9, starting transfers between devices: 26.3 us -> 16.8 us  [ring_blocks(): left = lax.ppermute(left, axis, bwd)]
    ppermute x9, starting transfers between devices: 4.03 us -> 9.89 us  [ring_blocks(): right = lax.ppermute(right, axis, fwd)]
    ppermute x3, starting transfers between devices: 11 us -> 5.89 us  [ring_blocks(): blocks[1] = lax.ppermute(piece, axis, fwd)]
    ppermute x3, waiting for transfers between devices: 10.9 us -> 14.7 us  [ring_blocks(): blocks[1] = lax.ppermute(piece, axis, fwd)]
    ppermute x9, waiting for transfers between devices: 26.6 us -> 29.5 us  [ring_blocks(): left = lax.ppermute(left, axis, bwd)]
    unnamed x28 -> x27, local copies, waits for them, and re-layouts: 3.83 us -> 2.11 us
  transfers between devices with their start and end apart: 28 -> 28, of which waited for: 17 -> 20; matrix products, arithmetic and copies ran while one was open for 4% -> 4% of each run, Pallas kernels for 5% -> 13%
where the time goes in v11:
time: 163 us
  waiting for transfers between devices  73.8 us (45%)
  starting transfers between devices  43.1 us (26%)
  Pallas kernels  20.7 us (13%)
  between operations  13.7 us (8%)
  matrix products  6.45 us (4%)
  local copies, waits for them, and re-layouts  3.01 us (2%)
  other arithmetic  2.18 us (1%)
    ppermute x9, waiting for transfers between devices, ring_blocks(): left = lax.ppermute(left, axis, bwd)  29.5 us
    pallas_call x1, Pallas kernels, place_tiles(): pl.pallas_call(kernel, out_shape=jax.ShapeDtypeStruct((rows * size, block...  20.7 us
    ppermute x9, starting transfers between devices, ring_blocks(): left = lax.ppermute(left, axis, bwd)  16.8 us
    ppermute x3, waiting for transfers between devices, ring_blocks(): blocks[1] = lax.ppermute(piece, axis, fwd)  14.7 us
    ppermute x9, waiting for transfers between devices, ring_blocks(): right = lax.ppermute(right, axis, fwd)  12.8 us
    ppermute x3, starting transfers between devices, ring_blocks(): lax.ppermute(lax.slice_in_dim(left, split, None, axis=split_dim), axis, bwd)  10.3 us
    ppermute x9, starting transfers between devices, ring_blocks(): right = lax.ppermute(right, axis, fwd)  9.89 us
    ppermute x3, waiting for transfers between devices, ring_blocks(): lax.ppermute(lax.slice_in_dim(right, 0, split, axis=split_dim), axis, fwd)  7.5 us
  transfers between devices with their start and end apart: 28, of which 20 were waited for; matrix products, arithmetic and copies ran while one was open for 4% of the time, Pallas kernels for 13%

profile of v11, /device:TPU:2, one launch (start us, length us, event | category | flops | bytes accessed | tf_op | source)
XLA Modules:
  0.0 163.2 jit_solution(18187645635304868186)
XLA Ops:
  7.5 3.3 %collective-permute-start.9 = (bf16[256,256]{1,0:T(8,128)(2,1)S(1)}, bf16[256,256]{1,0:T(8,128)(2,1)S(1)}, u32[]{:S(2)}, u32[]{:S(2)}) collective-permute-start(bf16[256,256]{1,0:T(8,128)(2,1)S(1)} %copy.15), channel_id=1, source_target_pairs={{0,8},{8,0},{1,9},{9,1},{2,10},{10,2},{3,11},{11,3},{4,12},{12,4},... | collective-permute-start | bytes 393224 | tf_op jit(solution)/shard_map/ppermute | solution.py:29
  10.7 3.5 %collective-permute-done.9 = bf16[256,256]{1,0:T(8,128)(2,1)S(1)} collective-permute-done((bf16[256,256]{1,0:T(8,128)(2,1)S(1)}, bf16[256,256]{1,0:T(8,128)(2,1)S(1)}, u32[]{:S(2)}, u32[]{:S(2)}) %collective-permute-start.9) | collective-permute-done | bytes 131104 | tf_op jit(solution)/shard_map/ppermute | solution.py:29
  14.5 2.0 %collective-permute-start.13 = (bf16[2,256,256]{2,1,0:T(8,128)(2,1)S(1)}, bf16[2,256,256]{2,1,0:T(8,128)(2,1)S(1)}, u32[]{:S(2)}, u32[]{:S(2)}) collective-permute-start(bf16[2,256,256]{2,1,0:T(8,128)(2,1)S(1)} %fusion.42), channel_id=1, source_target_pairs={{0,1},{1,2},{2,3},{3,4},{4,5},{5,6},{6,7},{7,0},{8,9},{9,10},{10,1... | collective-permute-start | bytes 786440 | tf_op jit(solution)/shard_map/ppermute | solution.py:23
  16.5 4.0 %collective-permute-start.10 = (bf16[2,256,256]{2,1,0:T(8,128)(2,1)S(1)}, bf16[2,256,256]{2,1,0:T(8,128)(2,1)S(1)}, u32[]{:S(2)}, u32[]{:S(2)}) collective-permute-start(bf16[2,256,256]{2,1,0:T(8,128)(2,1)S(1)} %fusion.42), channel_id=1, source_target_pairs={{0,7},{1,0},{2,1},{3,2},{4,3},{5,4},{6,5},{7,6},{8,15},{9,8},{10,9... | collective-permute-start | bytes 786440 | tf_op jit(solution)/shard_map/ppermute | solution.py:24
  20.5 5.4 %collective-permute-done.13 = bf16[2,256,256]{2,1,0:T(8,128)(2,1)S(1)} collective-permute-done((bf16[2,256,256]{2,1,0:T(8,128)(2,1)S(1)}, bf16[2,256,256]{2,1,0:T(8,128)(2,1)S(1)}, u32[]{:S(2)}, u32[]{:S(2)}) %collective-permute-start.13) | collective-permute-done | bytes 262176 | tf_op jit(solution)/shard_map/ppermute | solution.py:23
  25.9 3.2 %collective-permute-start.11 = (bf16[2,256,256]{2,1,0:T(8,128)(2,1)S(1)}, bf16[2,256,256]{2,1,0:T(8,128)(2,1)S(1)}, u32[]{:S(2)}, u32[]{:S(2)}) collective-permute-start(bf16[2,256,256]{2,1,0:T(8,128)(2,1)S(1)} %collective-permute-done.10), channel_id=1, source_target_pairs={{0,7},{1,0},{2,1},{3,2},{4,3},{5,4},{6,5},{7,6},{8,15},{9,8},{10,9... | collective-permute-start | bytes 786440 | tf_op jit(solution)/shard_map/ppermute | solution.py:24
  29.1 4.6 %collective-permute-done.14 = bf16[2,256,256]{2,1,0:T(8,128)(2,1)S(1)} collective-permute-done((bf16[2,256,256]{2,1,0:T(8,128)(2,1)S(1)}, bf16[2,256,256]{2,1,0:T(8,128)(2,1)S(1)}, u32[]{:S(2)}, u32[]{:S(2)}) %collective-permute-start.14) | collective-permute-done | bytes 262176 | tf_op jit(solution)/shard_map/ppermute | solution.py:23
  33.7 3.3 %collective-permute-start.12 = (bf16[2,256,256]{2,1,0:T(8,128)(2,1)S(1)}, bf16[2,256,256]{2,1,0:T(8,128)(2,1)S(1)}, u32[]{:S(2)}, u32[]{:S(2)}) collective-permute-start(bf16[2,256,256]{2,1,0:T(8,128)(2,1)S(1)} %collective-permute-done.11), channel_id=1, source_target_pairs={{0,7},{1,0},{2,1},{3,2},{4,3},{5,4},{6,5},{7,6},{8,15},{9,8},{10,9... | collective-permute-start | bytes 786440 | tf_op jit(solution)/shard_map/ppermute | solution.py:24
  39.3 2.0 %collective-permute-done.15 = bf16[2,256,256]{2,1,0:T(8,128)(2,1)S(1)} collective-permute-done((bf16[2,256,256]{2,1,0:T(8,128)(2,1)S(1)}, bf16[2,256,256]{2,1,0:T(8,128)(2,1)S(1)}, u32[]{:S(2)}, u32[]{:S(2)}) %collective-permute-start.15) | collective-permute-done | bytes 262176 | tf_op jit(solution)/shard_map/ppermute | solution.py:23
  41.4 3.5 %collective-permute-start.17 = (bf16[1,256,256]{2,1,0:T(8,128)(2,1)S(1)}, bf16[1,256,256]{2,1,0:T(8,128)(2,1)}, u32[]{:S(2)}, u32[]{:S(2)}) collective-permute-start(bf16[1,256,256]{2,1,0:T(8,128)(2,1)S(1)} %slice.85), channel_id=1, source_target_pairs={{0,7},{1,0},{2,1},{3,2},{4,3},{5,4},{6,5},{7,6},{8,15},{9,8},{10,9... | collective-permute-start | bytes 393224 | tf_op jit(solution)/shard_map/ppermute | solution.py:33
  44.9 4.9 %all-gather.2.cloned.1.call-done = bf16[4,48,64,64]{3,2,1,0:T(8,128)(2,1)} async-done(((bf16[4,3,64,64]{3,2,1,0:T(8,128)(2,1)}), bf16[4,48,64,64]{3,2,1,0:T(8,128)(2,1)}) %all-gather.2.cloned.1.call-update) | async-done | bytes 1572880 | tf_op jit(solution)/shard_map/all_gather | solution.py:104
  49.8 20.7 %shard_map.46 = bf16[4096,256]{1,0:T(8,128)(2,1)S(1)} custom-call(s32[192]{0:T(256)} %reshape.43.dest_ref, bf16[1,4,48,64,64]{4,3,2,1,0:T(8,128)(2,1)} %bitcast.182), custom_call_target="tpu_custom_call" | custom-call | tf_op jit(solution)/shard_map/pallas_call | solution.py:81
  74.2 81.5 %while.12 = (s32[]{:T(128)}, bf16[256,256]{1,0:T(8,128)(2,1)S(1)}, bf16[256,256]{1,0:T(8,128)(2,1)S(1)}, bf16[8,2,256,256]{3,2,1,0:T(8,128)(2,1)S(1)}, s32[]{:T(...) while((s32[]{:T(128)}, bf16[256,256]{1,0:T(8,128)(2,1)S(1)}, ...), condition=%wide.region_2.4_spmd, body=%wide.region_1.3_spmd.sunk | while | flops 538116096 | bytes 17564300 | solution.py:132
  74.4 7.1 %collective-permute-done = bf16[256,256]{1,0:T(8,128)(2,1)S(1)} collective-permute-done((bf16[256,256]{1,0:T(8,128)(2,1)S(1)}, bf16[256,256]{1,0:T(8,128)(2,1)S(1)}, u32[]{:S(2)}, u32[]{:S(2)}) %collective-permute-start) | collective-permute-done | bytes 131104 | tf_op jit(solution)/shard_map/while/body/eval_jaxpr/ppermute | solution.py:29
  81.8 3.1 %collective-permute-start.1 = (bf16[2,256,256]{2,1,0:T(8,128)(2,1)S(1)}, bf16[2,256,256]{2,1,0:T(8,128)(2,1)S(1)}, u32[]{:S(2)}, u32[]{:S(2)}) collective-permute-start(bf16[2,256,256]{2,1,0:T(8,128)(2,1)S(1)} %fusion.117), channel_id=1, source_target_pairs={{0,1},{1,2},{2,3},{3,4},{4,5},{5,6},{6,7},{7,0},{8,9},{9,10},{10,1... | collective-permute-start | bytes 786440 | tf_op jit(solution)/shard_map/while/body/eval_jaxpr/ppermute | solution.py:23
  85.1 5.8 %collective-permute-done.4 = bf16[2,256,256]{2,1,0:T(8,128)(2,1)S(1)} collective-permute-done((bf16[2,256,256]{2,1,0:T(8,128)(2,1)S(1)}, bf16[2,256,256]{2,1,0:T(8,128)(2,1)S(1)}, u32[]{:S(2)}, u32[]{:S(2)}) %collective-permute-start.4) | collective-permute-done | bytes 262176 | tf_op jit(solution)/shard_map/while/body/eval_jaxpr/ppermute | solution.py:24
  91.2 1.7 %collective-permute-start.2 = (bf16[2,256,256]{2,1,0:T(8,128)(2,1)S(1)}, bf16[2,256,256]{2,1,0:T(8,128)(2,1)S(1)}, u32[]{:S(2)}, u32[]{:S(2)}) collective-permute-start(bf16[2,256,256]{2,1,0:T(8,128)(2,1)S(1)} %collective-permute-done.1), channel_id=1, source_target_pairs={{0,1},{1,2},{2,3},{3,4},{4,5},{5,6},{6,7},{7,0},{8,9},{9,10},{10,1... | collective-permute-start | bytes 786440 | tf_op jit(solution)/shard_map/while/body/eval_jaxpr/ppermute | solution.py:23
  93.4 4.8 %collective-permute-done.5 = bf16[2,256,256]{2,1,0:T(8,128)(2,1)S(1)} collective-permute-done((bf16[2,256,256]{2,1,0:T(8,128)(2,1)S(1)}, bf16[2,256,256]{2,1,0:T(8,128)(2,1)S(1)}, u32[]{:S(2)}, u32[]{:S(2)}) %collective-permute-start.5) | collective-permute-done | bytes 262176 | tf_op jit(solution)/shard_map/while/body/eval_jaxpr/ppermute | solution.py:24
  100.7 3.9 %collective-permute-done.6 = bf16[2,256,256]{2,1,0:T(8,128)(2,1)S(1)} collective-permute-done((bf16[2,256,256]{2,1,0:T(8,128)(2,1)S(1)}, bf16[2,256,256]{2,1,0:T(8,128)(2,1)S(1)}, u32[]{:S(2)}, u32[]{:S(2)}) %collective-permute-start.6) | collective-permute-done | bytes 262176 | tf_op jit(solution)/shard_map/while/body/eval_jaxpr/ppermute | solution.py:24
  104.6 3.1 %collective-permute-start.7 = (bf16[1,256,256]{2,1,0:T(8,128)(2,1)S(1)}, bf16[1,256,256]{2,1,0:T(8,128)(2,1)S(1)}, u32[]{:S(2)}, u32[]{:S(2)}) collective-permute-start(bf16[1,256,256]{2,1,0:T(8,128)(2,1)S(1)} %slice.148), channel_id=1, source_target_pairs={{0,7},{1,0},{2,1},{3,2},{4,3},{5,4},{6,5},{7,6},{8,15},{9,8},{10,9... | collective-permute-start | bytes 393224 | tf_op jit(solution)/shard_map/while/body/eval_jaxpr/ppermute | solution.py:33
  108.0 2.2 %collective-permute-done.7 = bf16[1,256,256]{2,1,0:T(8,128)(2,1)S(1)} collective-permute-done((bf16[1,256,256]{2,1,0:T(8,128)(2,1)S(1)}, bf16[1,256,256]{2,1,0:T(8,128)(2,1)S(1)}, u32[]{:S(2)}, u32[]{:S(2)}) %collective-permute-start.7) | collective-permute-done | bytes 131104 | tf_op jit(solution)/shard_map/while/body/eval_jaxpr/ppermute | solution.py:33
  110.2 3.8 %collective-permute-done.8 = bf16[1,256,256]{2,1,0:T(8,128)(2,1)S(1)} collective-permute-done((bf16[1,256,256]{2,1,0:T(8,128)(2,1)S(1)}, bf16[1,256,256]{2,1,0:T(8,128)(2,1)S(1)}, u32[]{:S(2)}, u32[]{:S(2)}) %collective-permute-start.8) | collective-permute-done | bytes 131104 | tf_op jit(solution)/shard_map/while/body/eval_jaxpr/ppermute | solution.py:32
  114.5 2.5 %collective-permute-start = (bf16[256,256]{1,0:T(8,128)(2,1)S(1)}, bf16[256,256]{1,0:T(8,128)(2,1)S(1)}, u32[]{:S(2)}, u32[]{:S(2)}) collective-permute-start(bf16[256,256]{1,0:T(8,128)(2,1)S(1)} %copy.10), channel_id=1, source_target_pairs={{0,8},{8,0},{1,9},{9,1},{2,10},{10,2},{3,11},{11,3},{4,12},{12,4},... | collective-permute-start | bytes 393224 | tf_op jit(solution)/shard_map/while/body/eval_jaxpr/ppermute | solution.py:29
  117.0 4.1 %collective-permute-done = bf16[256,256]{1,0:T(8,128)(2,1)S(1)} collective-permute-done((bf16[256,256]{1,0:T(8,128)(2,1)S(1)}, bf16[256,256]{1,0:T(8,128)(2,1)S(1)}, u32[]{:S(2)}, u32[]{:S(2)}) %collective-permute-start) | collective-permute-done | bytes 131104 | tf_op jit(solution)/shard_map/while/body/eval_jaxpr/ppermute | solution.py:29
  121.3 2.0 %collective-permute-start.1 = (bf16[2,256,256]{2,1,0:T(8,128)(2,1)S(1)}, bf16[2,256,256]{2,1,0:T(8,128)(2,1)S(1)}, u32[]{:S(2)}, u32[]{:S(2)}) collective-permute-start(bf16[2,256,256]{2,1,0:T(8,128)(2,1)S(1)} %fusion.117), channel_id=1, source_target_pairs={{0,1},{1,2},{2,3},{3,4},{4,5},{5,6},{6,7},{7,0},{8,9},{9,10},{10,1... | collective-permute-start | bytes 786440 | tf_op jit(solution)/shard_map/while/body/eval_jaxpr/ppermute | solution.py:23
  123.6 6.2 %collective-permute-done.4 = bf16[2,256,256]{2,1,0:T(8,128)(2,1)S(1)} collective-permute-done((bf16[2,256,256]{2,1,0:T(8,128)(2,1)S(1)}, bf16[2,256,256]{2,1,0:T(8,128)(2,1)S(1)}, u32[]{:S(2)}, u32[]{:S(2)}) %collective-permute-start.4) | collective-permute-done | bytes 262176 | tf_op jit(solution)/shard_map/while/body/eval_jaxpr/ppermute | solution.py:24
  132.3 5.1 %collective-permute-done.5 = bf16[2,256,256]{2,1,0:T(8,128)(2,1)S(1)} collective-permute-done((bf16[2,256,256]{2,1,0:T(8,128)(2,1)S(1)}, bf16[2,256,256]{2,1,0:T(8,128)(2,1)S(1)}, u32[]{:S(2)}, u32[]{:S(2)}) %collective-permute-start.5) | collective-permute-done | bytes 262176 | tf_op jit(solution)/shard_map/while/body/eval_jaxpr/ppermute | solution.py:24
  137.4 3.5 %collective-permute-start.6 = (bf16[2,256,256]{2,1,0:T(8,128)(2,1)S(1)}, bf16[2,256,256]{2,1,0:T(8,128)(2,1)S(1)}, u32[]{:S(2)}, u32[]{:S(2)}) collective-permute-start(bf16[2,256,256]{2,1,0:T(8,128)(2,1)S(1)} %collective-permute-done.5), channel_id=1, source_target_pairs={{0,7},{1,0},{2,1},{3,2},{4,3},{5,4},{6,5},{7,6},{8,15},{9,8},{10,9... | collective-permute-start | bytes 786440 | tf_op jit(solution)/shard_map/while/body/eval_jaxpr/ppermute | solution.py:24
  141.5 3.6 %collective-permute-done.6 = bf16[2,256,256]{2,1,0:T(8,128)(2,1)S(1)} collective-permute-done((bf16[2,256,256]{2,1,0:T(8,128)(2,1)S(1)}, bf16[2,256,256]{2,1,0:T(8,128)(2,1)S(1)}, u32[]{:S(2)}, u32[]{:S(2)}) %collective-permute-start.6) | collective-permute-done | bytes 262176 | tf_op jit(solution)/shard_map/while/body/eval_jaxpr/ppermute | solution.py:24
  145.1 3.8 %collective-permute-start.7 = (bf16[1,256,256]{2,1,0:T(8,128)(2,1)S(1)}, bf16[1,256,256]{2,1,0:T(8,128)(2,1)S(1)}, u32[]{:S(2)}, u32[]{:S(2)}) collective-permute-start(bf16[1,256,256]{2,1,0:T(8,128)(2,1)S(1)} %slice.148), channel_id=1, source_target_pairs={{0,7},{1,0},{2,1},{3,2},{4,3},{5,4},{6,5},{7,6},{8,15},{9,8},{10,9... | collective-permute-start | bytes 393224 | tf_op jit(solution)/shard_map/while/body/eval_jaxpr/ppermute | solution.py:33
  149.2 2.2 %collective-permute-done.7 = bf16[1,256,256]{2,1,0:T(8,128)(2,1)S(1)} collective-permute-done((bf16[1,256,256]{2,1,0:T(8,128)(2,1)S(1)}, bf16[1,256,256]{2,1,0:T(8,128)(2,1)S(1)}, u32[]{:S(2)}, u32[]{:S(2)}) %collective-permute-start.7) | collective-permute-done | bytes 131104 | tf_op jit(solution)/shard_map/while/body/eval_jaxpr/ppermute | solution.py:33
  151.4 3.8 %collective-permute-done.8 = bf16[1,256,256]{2,1,0:T(8,128)(2,1)S(1)} collective-permute-done((bf16[1,256,256]{2,1,0:T(8,128)(2,1)S(1)}, bf16[1,256,256]{2,1,0:T(8,128)(2,1)S(1)}, u32[]{:S(2)}, u32[]{:S(2)}) %collective-permute-start.8) | collective-permute-done | bytes 131104 | tf_op jit(solution)/shard_map/while/body/eval_jaxpr/ppermute | solution.py:32
  (96 shorter events, 16.7 us)
Async XLA Ops:
  6.5 43.3 %all-gather.2.cloned.1.call-start = ((), (), s32[]{:S(2)}) async-start(), calls=%async_computation | async-start | bytes 3342336 | tf_op jit(solution)/shard_map/all_gather | solution.py:104
  7.5 6.8 %collective-permute-start.9 = (bf16[256,256]{1,0:T(8,128)(2,1)S(1)}, bf16[256,256]{1,0:T(8,128)(2,1)S(1)}, u32[]{:S(2)}, u32[]{:S(2)}) collective-permute-start(bf16[256,256]{1,0:T(8,128)(2,1)S(1)} %copy.15), channel_id=1, source_target_pairs={{0,8},{8,0},{1,9},{9,1},{2,10},{10,2},{3,11},{11,3},{4,12},{12,4},... | collective-permute-start | bytes 393224 | tf_op jit(solution)/shard_map/ppermute | solution.py:29
  14.5 11.4 %collective-permute-start.13 = (bf16[2,256,256]{2,1,0:T(8,128)(2,1)S(1)}, bf16[2,256,256]{2,1,0:T(8,128)(2,1)S(1)}, u32[]{:S(2)}, u32[]{:S(2)}) collective-permute-start(bf16[2,256,256]{2,1,0:T(8,128)(2,1)S(1)} %fusion.42), channel_id=1, source_target_pairs={{0,1},{1,2},{2,3},{3,4},{4,5},{5,6},{6,7},{7,0},{8,9},{9,10},{10,1... | collective-permute-start | bytes 786440 | tf_op jit(solution)/shard_map/ppermute | solution.py:23
  16.5 9.4 %collective-permute-start.10 = (bf16[2,256,256]{2,1,0:T(8,128)(2,1)S(1)}, bf16[2,256,256]{2,1,0:T(8,128)(2,1)S(1)}, u32[]{:S(2)}, u32[]{:S(2)}) collective-permute-start(bf16[2,256,256]{2,1,0:T(8,128)(2,1)S(1)} %fusion.42), channel_id=1, source_target_pairs={{0,7},{1,0},{2,1},{3,2},{4,3},{5,4},{6,5},{7,6},{8,15},{9,8},{10,9... | collective-permute-start | bytes 786440 | tf_op jit(solution)/shard_map/ppermute | solution.py:24
  25.9 7.8 %collective-permute-start.14 = (bf16[2,256,256]{2,1,0:T(8,128)(2,1)S(1)}, bf16[2,256,256]{2,1,0:T(8,128)(2,1)S(1)}, u32[]{:S(2)}, u32[]{:S(2)}) collective-permute-start(bf16[2,256,256]{2,1,0:T(8,128)(2,1)S(1)} %collective-permute-done.13), channel_id=1, source_target_pairs={{0,1},{1,2},{2,3},{3,4},{4,5},{5,6},{6,7},{7,0},{8,9},{9,10},{10,1... | collective-permute-start | bytes 786440 | tf_op jit(solution)/shard_map/ppermute | solution.py:23
  25.9 23.9 %copy-start.9 = (bf16[2,256,256]{2,1,0:T(8,128)(2,1)}, bf16[2,256,256]{2,1,0:T(8,128)(2,1)S(1)}, u32[]{:S(2)}) copy-start(bf16[2,256,256]{2,1,0:T(8,128)(2,1)S(1)} %collective-permute-done.10) | copy-start | bytes 786436
  25.9 7.8 %collective-permute-start.11 = (bf16[2,256,256]{2,1,0:T(8,128)(2,1)S(1)}, bf16[2,256,256]{2,1,0:T(8,128)(2,1)S(1)}, u32[]{:S(2)}, u32[]{:S(2)}) collective-permute-start(bf16[2,256,256]{2,1,0:T(8,128)(2,1)S(1)} %collective-permute-done.10), channel_id=1, source_target_pairs={{0,7},{1,0},{2,1},{3,2},{4,3},{5,4},{6,5},{7,6},{8,15},{9,8},{10,9... | collective-permute-start | bytes 786440 | tf_op jit(solution)/shard_map/ppermute | solution.py:24
  33.7 16.1 %copy-start.7 = (bf16[2,256,256]{2,1,0:T(8,128)(2,1)}, bf16[2,256,256]{2,1,0:T(8,128)(2,1)S(1)}, u32[]{:S(2)}) copy-start(bf16[2,256,256]{2,1,0:T(8,128)(2,1)S(1)} %collective-permute-done.14) | copy-start | bytes 786436
  33.7 7.6 %collective-permute-start.15 = (bf16[2,256,256]{2,1,0:T(8,128)(2,1)S(1)}, bf16[2,256,256]{2,1,0:T(8,128)(2,1)S(1)}, u32[]{:S(2)}, u32[]{:S(2)}) collective-permute-start(bf16[2,256,256]{2,1,0:T(8,128)(2,1)S(1)} %collective-permute-done.14), channel_id=1, source_target_pairs={{0,1},{1,2},{2,3},{3,4},{4,5},{5,6},{6,7},{7,0},{8,9},{9,10},{10,1... | collective-permute-start | bytes 786440 | tf_op jit(solution)/shard_map/ppermute | solution.py:23
  33.7 16.1 %copy-start.11 = (bf16[2,256,256]{2,1,0:T(8,128)(2,1)}, bf16[2,256,256]{2,1,0:T(8,128)(2,1)S(1)}, u32[]{:S(2)}) copy-start(bf16[2,256,256]{2,1,0:T(8,128)(2,1)S(1)} %collective-permute-done.11) | copy-start | bytes 786436
  33.7 7.7 %collective-permute-start.12 = (bf16[2,256,256]{2,1,0:T(8,128)(2,1)S(1)}, bf16[2,256,256]{2,1,0:T(8,128)(2,1)S(1)}, u32[]{:S(2)}, u32[]{:S(2)}) collective-permute-start(bf16[2,256,256]{2,1,0:T(8,128)(2,1)S(1)} %collective-permute-done.11), channel_id=1, source_target_pairs={{0,7},{1,0},{2,1},{3,2},{4,3},{5,4},{6,5},{7,6},{8,15},{9,8},{10,9... | collective-permute-start | bytes 786440 | tf_op jit(solution)/shard_map/ppermute | solution.py:24
  41.3 8.5 %copy-start.3 = (bf16[2,256,256]{2,1,0:T(8,128)(2,1)}, bf16[2,256,256]{2,1,0:T(8,128)(2,1)S(1)}, u32[]{:S(2)}) copy-start(bf16[2,256,256]{2,1,0:T(8,128)(2,1)S(1)} %collective-permute-done.15) | copy-start | bytes 786436
  41.3 31.4 %collective-permute-start.16 = (bf16[1,256,256]{2,1,0:T(8,128)(2,1)S(1)}, bf16[1,256,256]{2,1,0:T(8,128)(2,1)}, u32[]{:S(2)}, u32[]{:S(2)}) collective-permute-start(bf16[1,256,256]{2,1,0:T(8,128)(2,1)S(1)} %slice.84), channel_id=1, source_target_pairs={{0,1},{1,2},{2,3},{3,4},{4,5},{5,6},{6,7},{7,0},{8,9},{9,10},{10,1... | collective-permute-start | bytes 393224 | tf_op jit(solution)/shard_map/ppermute | solution.py:32
  41.4 31.3 %collective-permute-start.17 = (bf16[1,256,256]{2,1,0:T(8,128)(2,1)S(1)}, bf16[1,256,256]{2,1,0:T(8,128)(2,1)}, u32[]{:S(2)}, u32[]{:S(2)}) collective-permute-start(bf16[1,256,256]{2,1,0:T(8,128)(2,1)S(1)} %slice.85), channel_id=1, source_target_pairs={{0,7},{1,0},{2,1},{3,2},{4,3},{5,4},{6,5},{7,6},{8,15},{9,8},{10,9... | collective-permute-start | bytes 393224 | tf_op jit(solution)/shard_map/ppermute | solution.py:33
  74.3 7.2 %collective-permute-start = (bf16[256,256]{1,0:T(8,128)(2,1)S(1)}, bf16[256,256]{1,0:T(8,128)(2,1)S(1)}, u32[]{:S(2)}, u32[]{:S(2)}) collective-permute-start(bf16[256,256]{1,0:T(8,128)(2,1)S(1)} %copy.10), channel_id=1, source_target_pairs={{0,8},{8,0},{1,9},{9,1},{2,10},{10,2},{3,11},{11,3},{4,12},{12,4},... | collective-permute-start | bytes 393224 | tf_op jit(solution)/shard_map/while/body/eval_jaxpr/ppermute | solution.py:29
  81.7 9.2 %collective-permute-start.4 = (bf16[2,256,256]{2,1,0:T(8,128)(2,1)S(1)}, bf16[2,256,256]{2,1,0:T(8,128)(2,1)S(1)}, u32[]{:S(2)}, u32[]{:S(2)}) collective-permute-start(bf16[2,256,256]{2,1,0:T(8,128)(2,1)S(1)} %fusion.117), channel_id=1, source_target_pairs={{0,7},{1,0},{2,1},{3,2},{4,3},{5,4},{6,5},{7,6},{8,15},{9,8},{10,9... | collective-permute-start | bytes 786440 | tf_op jit(solution)/shard_map/while/body/eval_jaxpr/ppermute | solution.py:24
  81.8 9.5 %collective-permute-start.1 = (bf16[2,256,256]{2,1,0:T(8,128)(2,1)S(1)}, bf16[2,256,256]{2,1,0:T(8,128)(2,1)S(1)}, u32[]{:S(2)}, u32[]{:S(2)}) collective-permute-start(bf16[2,256,256]{2,1,0:T(8,128)(2,1)S(1)} %fusion.117), channel_id=1, source_target_pairs={{0,1},{1,2},{2,3},{3,4},{4,5},{5,6},{6,7},{7,0},{8,9},{9,10},{10,1... | collective-permute-start | bytes 786440 | tf_op jit(solution)/shard_map/while/body/eval_jaxpr/ppermute | solution.py:23
  90.9 7.3 %collective-permute-start.5 = (bf16[2,256,256]{2,1,0:T(8,128)(2,1)S(1)}, bf16[2,256,256]{2,1,0:T(8,128)(2,1)S(1)}, u32[]{:S(2)}, u32[]{:S(2)}) collective-permute-start(bf16[2,256,256]{2,1,0:T(8,128)(2,1)S(1)} %collective-permute-done.4), channel_id=1, source_target_pairs={{0,7},{1,0},{2,1},{3,2},{4,3},{5,4},{6,5},{7,6},{8,15},{9,8},{10,9... | collective-permute-start | bytes 786440 | tf_op jit(solution)/shard_map/while/body/eval_jaxpr/ppermute | solution.py:24
  91.2 8.4 %collective-permute-start.2 = (bf16[2,256,256]{2,1,0:T(8,128)(2,1)S(1)}, bf16[2,256,256]{2,1,0:T(8,128)(2,1)S(1)}, u32[]{:S(2)}, u32[]{:S(2)}) collective-permute-start(bf16[2,256,256]{2,1,0:T(8,128)(2,1)S(1)} %collective-permute-done.1), channel_id=1, source_target_pairs={{0,1},{1,2},{2,3},{3,4},{4,5},{5,6},{6,7},{7,0},{8,9},{9,10},{10,1... | collective-permute-start | bytes 786440 | tf_op jit(solution)/shard_map/while/body/eval_jaxpr/ppermute | solution.py:23
  98.2 6.4 %collective-permute-start.6 = (bf16[2,256,256]{2,1,0:T(8,128)(2,1)S(1)}, bf16[2,256,256]{2,1,0:T(8,128)(2,1)S(1)}, u32[]{:S(2)}, u32[]{:S(2)}) collective-permute-start(bf16[2,256,256]{2,1,0:T(8,128)(2,1)S(1)} %collective-permute-done.5), channel_id=1, source_target_pairs={{0,7},{1,0},{2,1},{3,2},{4,3},{5,4},{6,5},{7,6},{8,15},{9,8},{10,9... | collective-permute-start | bytes 786440 | tf_op jit(solution)/shard_map/while/body/eval_jaxpr/ppermute | solution.py:24
  99.7 8.0 %collective-permute-start.3 = (bf16[2,256,256]{2,1,0:T(8,128)(2,1)S(1)}, bf16[2,256,256]{2,1,0:T(8,128)(2,1)S(1)}, u32[]{:S(2)}, u32[]{:S(2)}) collective-permute-start(bf16[2,256,256]{2,1,0:T(8,128)(2,1)S(1)} %collective-permute-done.2), channel_id=1, source_target_pairs={{0,1},{1,2},{2,3},{3,4},{4,5},{5,6},{6,7},{7,0},{8,9},{9,10},{10,1... | collective-permute-start | bytes 786440 | tf_op jit(solution)/shard_map/while/body/eval_jaxpr/ppermute | solution.py:23
  104.6 5.6 %collective-permute-start.7 = (bf16[1,256,256]{2,1,0:T(8,128)(2,1)S(1)}, bf16[1,256,256]{2,1,0:T(8,128)(2,1)S(1)}, u32[]{:S(2)}, u32[]{:S(2)}) collective-permute-start(bf16[1,256,256]{2,1,0:T(8,128)(2,1)S(1)} %slice.148), channel_id=1, source_target_pairs={{0,7},{1,0},{2,1},{3,2},{4,3},{5,4},{6,5},{7,6},{8,15},{9,8},{10,9... | collective-permute-start | bytes 393224 | tf_op jit(solution)/shard_map/while/body/eval_jaxpr/ppermute | solution.py:33
  107.7 6.3 %collective-permute-start.8 = (bf16[1,256,256]{2,1,0:T(8,128)(2,1)S(1)}, bf16[1,256,256]{2,1,0:T(8,128)(2,1)S(1)}, u32[]{:S(2)}, u32[]{:S(2)}) collective-permute-start(bf16[1,256,256]{2,1,0:T(8,128)(2,1)S(1)} %slice.149), channel_id=1, source_target_pairs={{0,1},{1,2},{2,3},{3,4},{4,5},{5,6},{6,7},{7,0},{8,9},{9,10},{10,1... | collective-permute-start | bytes 393224 | tf_op jit(solution)/shard_map/while/body/eval_jaxpr/ppermute | solution.py:32
  114.5 6.6 %collective-permute-start = (bf16[256,256]{1,0:T(8,128)(2,1)S(1)}, bf16[256,256]{1,0:T(8,128)(2,1)S(1)}, u32[]{:S(2)}, u32[]{:S(2)}) collective-permute-start(bf16[256,256]{1,0:T(8,128)(2,1)S(1)} %copy.10), channel_id=1, source_target_pairs={{0,8},{8,0},{1,9},{9,1},{2,10},{10,2},{3,11},{11,3},{4,12},{12,4},... | collective-permute-start | bytes 393224 | tf_op jit(solution)/shard_map/while/body/eval_jaxpr/ppermute | solution.py:29
  121.2 8.6 %collective-permute-start.4 = (bf16[2,256,256]{2,1,0:T(8,128)(2,1)S(1)}, bf16[2,256,256]{2,1,0:T(8,128)(2,1)S(1)}, u32[]{:S(2)}, u32[]{:S(2)}) collective-permute-start(bf16[2,256,256]{2,1,0:T(8,128)(2,1)S(1)} %fusion.117), channel_id=1, source_target_pairs={{0,7},{1,0},{2,1},{3,2},{4,3},{5,4},{6,5},{7,6},{8,15},{9,8},{10,9... | collective-permute-start | bytes 786440 | tf_op jit(solution)/shard_map/while/body/eval_jaxpr/ppermute | solution.py:24
  121.3 9.9 %collective-permute-start.1 = (bf16[2,256,256]{2,1,0:T(8,128)(2,1)S(1)}, bf16[2,256,256]{2,1,0:T(8,128)(2,1)S(1)}, u32[]{:S(2)}, u32[]{:S(2)}) collective-permute-start(bf16[2,256,256]{2,1,0:T(8,128)(2,1)S(1)} %fusion.117), channel_id=1, source_target_pairs={{0,1},{1,2},{2,3},{3,4},{4,5},{5,6},{6,7},{7,0},{8,9},{9,10},{10,1... | collective-permute-start | bytes 786440 | tf_op jit(solution)/shard_map/while/body/eval_jaxpr/ppermute | solution.py:23
  129.8 7.6 %collective-permute-start.5 = (bf16[2,256,256]{2,1,0:T(8,128)(2,1)S(1)}, bf16[2,256,256]{2,1,0:T(8,128)(2,1)S(1)}, u32[]{:S(2)}, u32[]{:S(2)}) collective-permute-start(bf16[2,256,256]{2,1,0:T(8,128)(2,1)S(1)} %collective-permute-done.4), channel_id=1, source_target_pairs={{0,7},{1,0},{2,1},{3,2},{4,3},{5,4},{6,5},{7,6},{8,15},{9,8},{10,9... | collective-permute-start | bytes 786440 | tf_op jit(solution)/shard_map/while/body/eval_jaxpr/ppermute | solution.py:24
  131.3 9.8 %collective-permute-start.2 = (bf16[2,256,256]{2,1,0:T(8,128)(2,1)S(1)}, bf16[2,256,256]{2,1,0:T(8,128)(2,1)S(1)}, u32[]{:S(2)}, u32[]{:S(2)}) collective-permute-start(bf16[2,256,256]{2,1,0:T(8,128)(2,1)S(1)} %collective-permute-done.1), channel_id=1, source_target_pairs={{0,1},{1,2},{2,3},{3,4},{4,5},{5,6},{6,7},{7,0},{8,9},{9,10},{10,1... | collective-permute-start | bytes 786440 | tf_op jit(solution)/shard_map/while/body/eval_jaxpr/ppermute | solution.py:23
  137.4 7.7 %collective-permute-start.6 = (bf16[2,256,256]{2,1,0:T(8,128)(2,1)S(1)}, bf16[2,256,256]{2,1,0:T(8,128)(2,1)S(1)}, u32[]{:S(2)}, u32[]{:S(2)}) collective-permute-start(bf16[2,256,256]{2,1,0:T(8,128)(2,1)S(1)} %collective-permute-done.5), channel_id=1, source_target_pairs={{0,7},{1,0},{2,1},{3,2},{4,3},{5,4},{6,5},{7,6},{8,15},{9,8},{10,9... | collective-permute-start | bytes 786440 | tf_op jit(solution)/shard_map/while/body/eval_jaxpr/ppermute | solution.py:24
  141.0 7.9 %collective-permute-start.3 = (bf16[2,256,256]{2,1,0:T(8,128)(2,1)S(1)}, bf16[2,256,256]{2,1,0:T(8,128)(2,1)S(1)}, u32[]{:S(2)}, u32[]{:S(2)}) collective-permute-start(bf16[2,256,256]{2,1,0:T(8,128)(2,1)S(1)} %collective-permute-done.2), channel_id=1, source_target_pairs={{0,1},{1,2},{2,3},{3,4},{4,5},{5,6},{6,7},{7,0},{8,9},{9,10},{10,1... | collective-permute-start | bytes 786440 | tf_op jit(solution)/shard_map/while/body/eval_jaxpr/ppermute | solution.py:23
  145.1 6.3 %collective-permute-start.7 = (bf16[1,256,256]{2,1,0:T(8,128)(2,1)S(1)}, bf16[1,256,256]{2,1,0:T(8,128)(2,1)S(1)}, u32[]{:S(2)}, u32[]{:S(2)}) collective-permute-start(bf16[1,256,256]{2,1,0:T(8,128)(2,1)S(1)} %slice.148), channel_id=1, source_target_pairs={{0,7},{1,0},{2,1},{3,2},{4,3},{5,4},{6,5},{7,6},{8,15},{9,8},{10,9... | collective-permute-start | bytes 393224 | tf_op jit(solution)/shard_map/while/body/eval_jaxpr/ppermute | solution.py:33
  148.9 6.3 %collective-permute-start.8 = (bf16[1,256,256]{2,1,0:T(8,128)(2,1)S(1)}, bf16[1,256,256]{2,1,0:T(8,128)(2,1)S(1)}, u32[]{:S(2)}, u32[]{:S(2)}) collective-permute-start(bf16[1,256,256]{2,1,0:T(8,128)(2,1)S(1)} %slice.149), channel_id=1, source_target_pairs={{0,1},{1,2},{2,3},{3,4},{4,5},{5,6},{6,7},{7,0},{8,9},{9,10},{10,1... | collective-permute-start | bytes 393224 | tf_op jit(solution)/shard_map/while/body/eval_jaxpr/ppermute | solution.py:32
  (9 other events, 25.7 us)
Sparse Core Ops, SparseCore 0:
  9.1 40.6 all-gather.1

commit v12 on v5

--- a/solution.py
+++ b/solution.py
@@ -100,7 +100,9 @@
     live_counts = jnp.sum(jnp.where(region_match, density[None, :], 0), axis=1)
     live_mask = jnp.arange(slot_count, dtype=jnp.int32)[None, :] < live_counts[:, None]
 
-    tiles = lax.all_gather(jnp.swapaxes(block_tiles, 2, 3), ROW_AXES, axis=1, tiled=True)[None]
+    dense_rows = jnp.swapaxes(block_tiles, 2, 3).reshape(block_tiles.shape[0], block_tiles.shape[1], -1, 128)
+    tiles = lax.all_gather(dense_rows, ROW_AXES, axis=1, tiled=True)
+    tiles = tiles.reshape(tiles.shape[0], tiles.shape[1], block_tiles.shape[3], block_tiles.shape[2])[None]
     ring_neighbours = neighbours
     ring_live = live_mask
     per_col = block_rows

time: 153 us -> 158 us (1.033)
  local copies, waits for them, and re-layouts: 4.72 us -> 11 us
    another operation x2 -> x3, local copies, waits for them, and re-layouts: 0.02 us -> 5.13 us  [the longest x1 5.11 us: body(): tiles.reshape(tiles.shape[0], tiles.shape[1], block_tiles.shape[3], block...]
    ppermute x3, starting transfers between devices: 11 us -> 7.06 us  [ring_blocks(): blocks[1] = lax.ppermute(piece, axis, fwd)]
    all_gather x1, waiting for transfers between devices: 3.3 us -> 0.01 us  [body(): tiles = lax.all_gather(dense_rows, ROW_AXES, axis=1, tiled=True)]
    ppermute x9, starting transfers between devices: 26.3 us -> 29.2 us  [ring_blocks(): left = lax.ppermute(left, axis, bwd)]
    ppermute x3, waiting for transfers between devices: 10.9 us -> 13.4 us  [ring_blocks(): blocks[1] = lax.ppermute(piece, axis, fwd)]
    unnamed x28 -> x11, local copies, waits for them, and re-layouts: 3.83 us -> 1.79 us
  transfers between devices with their start and end apart: 28 -> 28, of which waited for: 17 -> 16; matrix products, arithmetic and copies ran while one was open for 4% -> 8% of each run, Pallas kernels for 5% -> 6%
where the time goes in v12:
time: 158 us
  waiting for transfers between devices  64.3 us (41%)
  starting transfers between devices  51.3 us (32%)
  between operations  13.6 us (9%)
  local copies, waits for them, and re-layouts  11 us (7%)
  Pallas kernels  8.74 us (6%)
  matrix products  6.48 us (4%)
  other arithmetic  2.18 us (1%)
    ppermute x9, starting transfers between devices, ring_blocks(): left = lax.ppermute(left, axis, bwd)  29.2 us
    ppermute x9, waiting for transfers between devices, ring_blocks(): left = lax.ppermute(left, axis, bwd)  27 us
    ppermute x3, waiting for transfers between devices, ring_blocks(): blocks[1] = lax.ppermute(piece, axis, fwd)  13.4 us
    ppermute x9, waiting for transfers between devices, ring_blocks(): right = lax.ppermute(right, axis, fwd)  11.9 us
    ppermute x3, starting transfers between devices, ring_blocks(): lax.ppermute(lax.slice_in_dim(left, split, None, axis=split_dim), axis, bwd)  10.8 us
    pallas_call x1, Pallas kernels, place_tiles(): pl.pallas_call(kernel, out_shape=jax.ShapeDtypeStruct((rows * size, block...  8.74 us
    ppermute x3, waiting for transfers between devices, ring_blocks(): lax.ppermute(lax.slice_in_dim(right, 0, split, axis=split_dim), axis, fwd)  7.5 us
    ppermute x3, starting transfers between devices, ring_blocks(): blocks[1] = lax.ppermute(piece, axis, fwd)  7.06 us
  transfers between devices with their start and end apart: 28, of which 16 were waited for; matrix products, arithmetic and copies ran while one was open for 8% of the time, Pallas kernels for 6%

profile of v12, /device:TPU:2, one launch (start us, length us, event | category | flops | bytes accessed | tf_op | source)
XLA Modules:
  0.0 157.7 jit_solution(10450586103361785019)
XLA Ops:
  9.3 3.3 %collective-permute-start.9 = (bf16[256,256]{1,0:T(8,128)(2,1)S(1)}, bf16[256,256]{1,0:T(8,128)(2,1)S(1)}, u32[]{:S(2)}, u32[]{:S(2)}) collective-permute-start(bf16[256,256]{1,0:T(8,128)(2,1)S(1)} %copy.17), channel_id=1, source_target_pairs={{0,8},{8,0},{1,9},{9,1},{2,10},{10,2},{3,11},{11,3},{4,12},{12,4},... | collective-permute-start | bytes 393224 | tf_op jit(solution)/shard_map/ppermute | solution.py:29
  12.6 3.5 %collective-permute-done.9 = bf16[256,256]{1,0:T(8,128)(2,1)S(1)} collective-permute-done((bf16[256,256]{1,0:T(8,128)(2,1)S(1)}, bf16[256,256]{1,0:T(8,128)(2,1)S(1)}, u32[]{:S(2)}, u32[]{:S(2)}) %collective-permute-start.9) | collective-permute-done | bytes 131104 | tf_op jit(solution)/shard_map/ppermute | solution.py:29
  18.3 4.0 %collective-permute-start.10 = (bf16[2,256,256]{2,1,0:T(8,128)(2,1)S(1)}, bf16[2,256,256]{2,1,0:T(8,128)(2,1)S(1)}, u32[]{:S(2)}, u32[]{:S(2)}) collective-permute-start(bf16[2,256,256]{2,1,0:T(8,128)(2,1)S(1)} %fusion.42), channel_id=1, source_target_pairs={{0,7},{1,0},{2,1},{3,2},{4,3},{5,4},{6,5},{7,6},{8,15},{9,8},{10,9... | collective-permute-start | bytes 786440 | tf_op jit(solution)/shard_map/ppermute | solution.py:24
  22.4 5.4 %collective-permute-done.13 = bf16[2,256,256]{2,1,0:T(8,128)(2,1)S(1)} collective-permute-done((bf16[2,256,256]{2,1,0:T(8,128)(2,1)S(1)}, bf16[2,256,256]{2,1,0:T(8,128)(2,1)S(1)}, u32[]{:S(2)}, u32[]{:S(2)}) %collective-permute-start.13) | collective-permute-done | bytes 262176 | tf_op jit(solution)/shard_map/ppermute | solution.py:23
  27.7 3.2 %collective-permute-start.11 = (bf16[2,256,256]{2,1,0:T(8,128)(2,1)S(1)}, bf16[2,256,256]{2,1,0:T(8,128)(2,1)S(1)}, u32[]{:S(2)}, u32[]{:S(2)}) collective-permute-start(bf16[2,256,256]{2,1,0:T(8,128)(2,1)S(1)} %collective-permute-done.10), channel_id=1, source_target_pairs={{0,7},{1,0},{2,1},{3,2},{4,3},{5,4},{6,5},{7,6},{8,15},{9,8},{10,9... | collective-permute-start | bytes 786440 | tf_op jit(solution)/shard_map/ppermute | solution.py:24
  31.0 4.6 %collective-permute-done.14 = bf16[2,256,256]{2,1,0:T(8,128)(2,1)S(1)} collective-permute-done((bf16[2,256,256]{2,1,0:T(8,128)(2,1)S(1)}, bf16[2,256,256]{2,1,0:T(8,128)(2,1)S(1)}, u32[]{:S(2)}, u32[]{:S(2)}) %collective-permute-start.14) | collective-permute-done | bytes 262176 | tf_op jit(solution)/shard_map/ppermute | solution.py:23
  35.6 3.3 %collective-permute-start.12 = (bf16[2,256,256]{2,1,0:T(8,128)(2,1)S(1)}, bf16[2,256,256]{2,1,0:T(8,128)(2,1)S(1)}, u32[]{:S(2)}, u32[]{:S(2)}) collective-permute-start(bf16[2,256,256]{2,1,0:T(8,128)(2,1)S(1)} %collective-permute-done.11), channel_id=1, source_target_pairs={{0,7},{1,0},{2,1},{3,2},{4,3},{5,4},{6,5},{7,6},{8,15},{9,8},{10,9... | collective-permute-start | bytes 786440 | tf_op jit(solution)/shard_map/ppermute | solution.py:24
  44.5 3.2 %collective-permute-start.17 = (bf16[1,256,256]{2,1,0:T(8,128)(2,1)}, bf16[1,256,256]{2,1,0:T(8,128)(2,1)}, u32[]{:S(2)}, u32[]{:S(2)}) collective-permute-start(bf16[1,256,256]{2,1,0:T(8,128)(2,1)} %slice.85), channel_id=1, source_target_pairs={{0,7},{1,0},{2,1},{3,2},{4,3},{5,4},{6,5},{7,6},{8,15},{9,8},{10,9... | collective-permute-start | bytes 393224 | tf_op jit(solution)/shard_map/ppermute | solution.py:33
  47.7 5.1 %broadcast_in_dim_reshape.3.tiles_ref = bf16[1,4,48,64,64]{4,3,2,1,0:T(8,128)(2,1)} reshape(bf16[4,48,32,128]{3,2,1,0:T(8,128)(2,1)} %all-gather.2.cloned.1.call-done) | data formatting | bytes 3145728 | tf_op jit(solution)/shard_map/broadcast_in_dim;reshape | solution.py:105
  52.8 8.7 %shard_map.46 = bf16[4096,256]{1,0:T(8,128)(2,1)S(1)} custom-call(s32[192]{0:T(256)} %reshape.46.dest_ref, bf16[1,4,48,64,64]{4,3,2,1,0:T(8,128)(2,1)} %broadcast_in_dim_reshape.3.tiles_ref), custom_call_target="tpu_custom_call" | custom-call | tf_op jit(solution)/shard_map/pallas_call | solution.py:80
  64.9 85.3 %while.12 = (s32[]{:T(128)}, bf16[256,256]{1,0:T(8,128)(2,1)S(1)}, bf16[256,256]{1,0:T(8,128)(2,1)S(1)}, bf16[8,2,256,256]{3,2,1,0:T(8,128)(2,1)S(1)}, s32[]{:T(...) while((s32[]{:T(128)}, bf16[256,256]{1,0:T(8,128)(2,1)S(1)}, ...), condition=%wide.region_2.4_spmd, body=%wide.region_1.3_spmd.sunk | while | flops 538116096 | bytes 17564300 | solution.py:133
  65.9 6.1 %collective-permute-done = bf16[256,256]{1,0:T(8,128)(2,1)S(1)} collective-permute-done((bf16[256,256]{1,0:T(8,128)(2,1)S(1)}, bf16[256,256]{1,0:T(8,128)(2,1)S(1)}, u32[]{:S(2)}, u32[]{:S(2)}) %collective-permute-start) | collective-permute-done | bytes 131104 | tf_op jit(solution)/shard_map/while/body/eval_jaxpr/ppermute | solution.py:29
  72.2 5.1 %collective-permute-start.4 = (bf16[2,256,256]{2,1,0:T(8,128)(2,1)S(1)}, bf16[2,256,256]{2,1,0:T(8,128)(2,1)S(1)}, u32[]{:S(2)}, u32[]{:S(2)}) collective-permute-start(bf16[2,256,256]{2,1,0:T(8,128)(2,1)S(1)} %fusion.117), channel_id=1, source_target_pairs={{0,7},{1,0},{2,1},{3,2},{4,3},{5,4},{6,5},{7,6},{8,15},{9,8},{10,9... | collective-permute-start | bytes 786440 | tf_op jit(solution)/shard_map/while/body/eval_jaxpr/ppermute | solution.py:24
  77.6 5.1 %collective-permute-done.4 = bf16[2,256,256]{2,1,0:T(8,128)(2,1)S(1)} collective-permute-done((bf16[2,256,256]{2,1,0:T(8,128)(2,1)S(1)}, bf16[2,256,256]{2,1,0:T(8,128)(2,1)S(1)}, u32[]{:S(2)}, u32[]{:S(2)}) %collective-permute-start.4) | collective-permute-done | bytes 262176 | tf_op jit(solution)/shard_map/while/body/eval_jaxpr/ppermute | solution.py:24
  82.7 3.7 %collective-permute-start.5 = (bf16[2,256,256]{2,1,0:T(8,128)(2,1)S(1)}, bf16[2,256,256]{2,1,0:T(8,128)(2,1)S(1)}, u32[]{:S(2)}, u32[]{:S(2)}) collective-permute-start(bf16[2,256,256]{2,1,0:T(8,128)(2,1)S(1)} %collective-permute-done.4), channel_id=1, source_target_pairs={{0,7},{1,0},{2,1},{3,2},{4,3},{5,4},{6,5},{7,6},{8,15},{9,8},{10,9... | collective-permute-start | bytes 786440 | tf_op jit(solution)/shard_map/while/body/eval_jaxpr/ppermute | solution.py:24
  86.9 4.0 %collective-permute-done.5 = bf16[2,256,256]{2,1,0:T(8,128)(2,1)S(1)} collective-permute-done((bf16[2,256,256]{2,1,0:T(8,128)(2,1)S(1)}, bf16[2,256,256]{2,1,0:T(8,128)(2,1)S(1)}, u32[]{:S(2)}, u32[]{:S(2)}) %collective-permute-start.5) | collective-permute-done | bytes 262176 | tf_op jit(solution)/shard_map/while/body/eval_jaxpr/ppermute | solution.py:24
  90.9 3.7 %collective-permute-start.6 = (bf16[2,256,256]{2,1,0:T(8,128)(2,1)S(1)}, bf16[2,256,256]{2,1,0:T(8,128)(2,1)S(1)}, u32[]{:S(2)}, u32[]{:S(2)}) collective-permute-start(bf16[2,256,256]{2,1,0:T(8,128)(2,1)S(1)} %collective-permute-done.5), channel_id=1, source_target_pairs={{0,7},{1,0},{2,1},{3,2},{4,3},{5,4},{6,5},{7,6},{8,15},{9,8},{10,9... | collective-permute-start | bytes 786440 | tf_op jit(solution)/shard_map/while/body/eval_jaxpr/ppermute | solution.py:24
  95.1 3.4 %collective-permute-done.6 = bf16[2,256,256]{2,1,0:T(8,128)(2,1)S(1)} collective-permute-done((bf16[2,256,256]{2,1,0:T(8,128)(2,1)S(1)}, bf16[2,256,256]{2,1,0:T(8,128)(2,1)S(1)}, u32[]{:S(2)}, u32[]{:S(2)}) %collective-permute-start.6) | collective-permute-done | bytes 262176 | tf_op jit(solution)/shard_map/while/body/eval_jaxpr/ppermute | solution.py:24
  98.5 3.8 %collective-permute-start.7 = (bf16[1,256,256]{2,1,0:T(8,128)(2,1)S(1)}, bf16[1,256,256]{2,1,0:T(8,128)(2,1)S(1)}, u32[]{:S(2)}, u32[]{:S(2)}) collective-permute-start(bf16[1,256,256]{2,1,0:T(8,128)(2,1)S(1)} %slice.148), channel_id=1, source_target_pairs={{0,7},{1,0},{2,1},{3,2},{4,3},{5,4},{6,5},{7,6},{8,15},{9,8},{10,9... | collective-permute-start | bytes 393224 | tf_op jit(solution)/shard_map/while/body/eval_jaxpr/ppermute | solution.py:33
  102.6 2.2 %collective-permute-done.7 = bf16[1,256,256]{2,1,0:T(8,128)(2,1)S(1)} collective-permute-done((bf16[1,256,256]{2,1,0:T(8,128)(2,1)S(1)}, bf16[1,256,256]{2,1,0:T(8,128)(2,1)S(1)}, u32[]{:S(2)}, u32[]{:S(2)}) %collective-permute-start.7) | collective-permute-done | bytes 131104 | tf_op jit(solution)/shard_map/while/body/eval_jaxpr/ppermute | solution.py:33
  104.8 3.8 %collective-permute-done.8 = bf16[1,256,256]{2,1,0:T(8,128)(2,1)S(1)} collective-permute-done((bf16[1,256,256]{2,1,0:T(8,128)(2,1)S(1)}, bf16[1,256,256]{2,1,0:T(8,128)(2,1)S(1)}, u32[]{:S(2)}, u32[]{:S(2)}) %collective-permute-start.8) | collective-permute-done | bytes 131104 | tf_op jit(solution)/shard_map/while/body/eval_jaxpr/ppermute | solution.py:32
  109.1 2.8 %collective-permute-start = (bf16[256,256]{1,0:T(8,128)(2,1)S(1)}, bf16[256,256]{1,0:T(8,128)(2,1)S(1)}, u32[]{:S(2)}, u32[]{:S(2)}) collective-permute-start(bf16[256,256]{1,0:T(8,128)(2,1)S(1)} %copy.12), channel_id=1, source_target_pairs={{0,8},{8,0},{1,9},{9,1},{2,10},{10,2},{3,11},{11,3},{4,12},{12,4},... | collective-permute-start | bytes 393224 | tf_op jit(solution)/shard_map/while/body/eval_jaxpr/ppermute | solution.py:29
  111.9 3.8 %collective-permute-done = bf16[256,256]{1,0:T(8,128)(2,1)S(1)} collective-permute-done((bf16[256,256]{1,0:T(8,128)(2,1)S(1)}, bf16[256,256]{1,0:T(8,128)(2,1)S(1)}, u32[]{:S(2)}, u32[]{:S(2)}) %collective-permute-start) | collective-permute-done | bytes 131104 | tf_op jit(solution)/shard_map/while/body/eval_jaxpr/ppermute | solution.py:29
  115.9 2.0 %collective-permute-start.1 = (bf16[2,256,256]{2,1,0:T(8,128)(2,1)S(1)}, bf16[2,256,256]{2,1,0:T(8,128)(2,1)S(1)}, u32[]{:S(2)}, u32[]{:S(2)}) collective-permute-start(bf16[2,256,256]{2,1,0:T(8,128)(2,1)S(1)} %fusion.117), channel_id=1, source_target_pairs={{0,1},{1,2},{2,3},{3,4},{4,5},{5,6},{6,7},{7,0},{8,9},{9,10},{10,1... | collective-permute-start | bytes 786440 | tf_op jit(solution)/shard_map/while/body/eval_jaxpr/ppermute | solution.py:23
  118.2 5.7 %collective-permute-done.4 = bf16[2,256,256]{2,1,0:T(8,128)(2,1)S(1)} collective-permute-done((bf16[2,256,256]{2,1,0:T(8,128)(2,1)S(1)}, bf16[2,256,256]{2,1,0:T(8,128)(2,1)S(1)}, u32[]{:S(2)}, u32[]{:S(2)}) %collective-permute-start.4) | collective-permute-done | bytes 262176 | tf_op jit(solution)/shard_map/while/body/eval_jaxpr/ppermute | solution.py:24
  123.9 2.4 %collective-permute-start.5 = (bf16[2,256,256]{2,1,0:T(8,128)(2,1)S(1)}, bf16[2,256,256]{2,1,0:T(8,128)(2,1)S(1)}, u32[]{:S(2)}, u32[]{:S(2)}) collective-permute-start(bf16[2,256,256]{2,1,0:T(8,128)(2,1)S(1)} %collective-permute-done.4), channel_id=1, source_target_pairs={{0,7},{1,0},{2,1},{3,2},{4,3},{5,4},{6,5},{7,6},{8,15},{9,8},{10,9... | collective-permute-start | bytes 786440 | tf_op jit(solution)/shard_map/while/body/eval_jaxpr/ppermute | solution.py:24
  126.8 5.3 %collective-permute-done.5 = bf16[2,256,256]{2,1,0:T(8,128)(2,1)S(1)} collective-permute-done((bf16[2,256,256]{2,1,0:T(8,128)(2,1)S(1)}, bf16[2,256,256]{2,1,0:T(8,128)(2,1)S(1)}, u32[]{:S(2)}, u32[]{:S(2)}) %collective-permute-start.5) | collective-permute-done | bytes 262176 | tf_op jit(solution)/shard_map/while/body/eval_jaxpr/ppermute | solution.py:24
  132.1 3.7 %collective-permute-start.6 = (bf16[2,256,256]{2,1,0:T(8,128)(2,1)S(1)}, bf16[2,256,256]{2,1,0:T(8,128)(2,1)S(1)}, u32[]{:S(2)}, u32[]{:S(2)}) collective-permute-start(bf16[2,256,256]{2,1,0:T(8,128)(2,1)S(1)} %collective-permute-done.5), channel_id=1, source_target_pairs={{0,7},{1,0},{2,1},{3,2},{4,3},{5,4},{6,5},{7,6},{8,15},{9,8},{10,9... | collective-permute-start | bytes 786440 | tf_op jit(solution)/shard_map/while/body/eval_jaxpr/ppermute | solution.py:24
  136.2 3.4 %collective-permute-done.6 = bf16[2,256,256]{2,1,0:T(8,128)(2,1)S(1)} collective-permute-done((bf16[2,256,256]{2,1,0:T(8,128)(2,1)S(1)}, bf16[2,256,256]{2,1,0:T(8,128)(2,1)S(1)}, u32[]{:S(2)}, u32[]{:S(2)}) %collective-permute-start.6) | collective-permute-done | bytes 262176 | tf_op jit(solution)/shard_map/while/body/eval_jaxpr/ppermute | solution.py:24
  139.7 3.8 %collective-permute-start.7 = (bf16[1,256,256]{2,1,0:T(8,128)(2,1)S(1)}, bf16[1,256,256]{2,1,0:T(8,128)(2,1)S(1)}, u32[]{:S(2)}, u32[]{:S(2)}) collective-permute-start(bf16[1,256,256]{2,1,0:T(8,128)(2,1)S(1)} %slice.148), channel_id=1, source_target_pairs={{0,7},{1,0},{2,1},{3,2},{4,3},{5,4},{6,5},{7,6},{8,15},{9,8},{10,9... | collective-permute-start | bytes 393224 | tf_op jit(solution)/shard_map/while/body/eval_jaxpr/ppermute | solution.py:33
  143.8 2.2 %collective-permute-done.7 = bf16[1,256,256]{2,1,0:T(8,128)(2,1)S(1)} collective-permute-done((bf16[1,256,256]{2,1,0:T(8,128)(2,1)S(1)}, bf16[1,256,256]{2,1,0:T(8,128)(2,1)S(1)}, u32[]{:S(2)}, u32[]{:S(2)}) %collective-permute-start.7) | collective-permute-done | bytes 131104 | tf_op jit(solution)/shard_map/while/body/eval_jaxpr/ppermute | solution.py:33
  146.0 3.8 %collective-permute-done.8 = bf16[1,256,256]{2,1,0:T(8,128)(2,1)S(1)} collective-permute-done((bf16[1,256,256]{2,1,0:T(8,128)(2,1)S(1)}, bf16[1,256,256]{2,1,0:T(8,128)(2,1)S(1)}, u32[]{:S(2)}, u32[]{:S(2)}) %collective-permute-start.8) | collective-permute-done | bytes 131104 | tf_op jit(solution)/shard_map/while/body/eval_jaxpr/ppermute | solution.py:32
  (83 shorter events, 19.9 us)
Async XLA Ops:
  6.5 41.2 %all-gather.2.cloned.1.call-start = ((), (), s32[]{:S(2)}) async-start(), calls=%async_computation | async-start | bytes 1671168 | tf_op jit(solution)/shard_map/all_gather | solution.py:104
  9.3 6.8 %collective-permute-start.9 = (bf16[256,256]{1,0:T(8,128)(2,1)S(1)}, bf16[256,256]{1,0:T(8,128)(2,1)S(1)}, u32[]{:S(2)}, u32[]{:S(2)}) collective-permute-start(bf16[256,256]{1,0:T(8,128)(2,1)S(1)} %copy.17), channel_id=1, source_target_pairs={{0,8},{8,0},{1,9},{9,1},{2,10},{10,2},{3,11},{11,3},{4,12},{12,4},... | collective-permute-start | bytes 393224 | tf_op jit(solution)/shard_map/ppermute | solution.py:29
  16.3 11.4 %collective-permute-start.13 = (bf16[2,256,256]{2,1,0:T(8,128)(2,1)S(1)}, bf16[2,256,256]{2,1,0:T(8,128)(2,1)S(1)}, u32[]{:S(2)}, u32[]{:S(2)}) collective-permute-start(bf16[2,256,256]{2,1,0:T(8,128)(2,1)S(1)} %fusion.42), channel_id=1, source_target_pairs={{0,1},{1,2},{2,3},{3,4},{4,5},{5,6},{6,7},{7,0},{8,9},{9,10},{10,1... | collective-permute-start | bytes 786440 | tf_op jit(solution)/shard_map/ppermute | solution.py:23
  18.3 9.4 %collective-permute-start.10 = (bf16[2,256,256]{2,1,0:T(8,128)(2,1)S(1)}, bf16[2,256,256]{2,1,0:T(8,128)(2,1)S(1)}, u32[]{:S(2)}, u32[]{:S(2)}) collective-permute-start(bf16[2,256,256]{2,1,0:T(8,128)(2,1)S(1)} %fusion.42), channel_id=1, source_target_pairs={{0,7},{1,0},{2,1},{3,2},{4,3},{5,4},{6,5},{7,6},{8,15},{9,8},{10,9... | collective-permute-start | bytes 786440 | tf_op jit(solution)/shard_map/ppermute | solution.py:24
  27.7 7.8 %collective-permute-start.14 = (bf16[2,256,256]{2,1,0:T(8,128)(2,1)S(1)}, bf16[2,256,256]{2,1,0:T(8,128)(2,1)S(1)}, u32[]{:S(2)}, u32[]{:S(2)}) collective-permute-start(bf16[2,256,256]{2,1,0:T(8,128)(2,1)S(1)} %collective-permute-done.13), channel_id=1, source_target_pairs={{0,1},{1,2},{2,3},{3,4},{4,5},{5,6},{6,7},{7,0},{8,9},{9,10},{10,1... | collective-permute-start | bytes 786440 | tf_op jit(solution)/shard_map/ppermute | solution.py:23
  27.7 7.8 %copy-start.1 = (bf16[2,256,256]{2,1,0:T(8,128)(2,1)}, bf16[2,256,256]{2,1,0:T(8,128)(2,1)S(1)}, u32[]{:S(2)}) copy-start(bf16[2,256,256]{2,1,0:T(8,128)(2,1)S(1)} %collective-permute-done.10) | copy-start | bytes 786436
  27.7 7.8 %collective-permute-start.11 = (bf16[2,256,256]{2,1,0:T(8,128)(2,1)S(1)}, bf16[2,256,256]{2,1,0:T(8,128)(2,1)S(1)}, u32[]{:S(2)}, u32[]{:S(2)}) collective-permute-start(bf16[2,256,256]{2,1,0:T(8,128)(2,1)S(1)} %collective-permute-done.10), channel_id=1, source_target_pairs={{0,7},{1,0},{2,1},{3,2},{4,3},{5,4},{6,5},{7,6},{8,15},{9,8},{10,9... | collective-permute-start | bytes 786440 | tf_op jit(solution)/shard_map/ppermute | solution.py:24
  35.5 7.6 %collective-permute-start.15 = (bf16[2,256,256]{2,1,0:T(8,128)(2,1)S(1)}, bf16[2,256,256]{2,1,0:T(8,128)(2,1)S(1)}, u32[]{:S(2)}, u32[]{:S(2)}) collective-permute-start(bf16[2,256,256]{2,1,0:T(8,128)(2,1)S(1)} %collective-permute-done.14), channel_id=1, source_target_pairs={{0,1},{1,2},{2,3},{3,4},{4,5},{5,6},{6,7},{7,0},{8,9},{9,10},{10,1... | collective-permute-start | bytes 786440 | tf_op jit(solution)/shard_map/ppermute | solution.py:23
  35.6 12.1 %copy-start.3 = (bf16[2,256,256]{2,1,0:T(8,128)(2,1)}, bf16[2,256,256]{2,1,0:T(8,128)(2,1)S(1)}, u32[]{:S(2)}) copy-start(bf16[2,256,256]{2,1,0:T(8,128)(2,1)S(1)} %collective-permute-done.11) | copy-start | bytes 786436
  35.6 8.2 %collective-permute-start.12 = (bf16[2,256,256]{2,1,0:T(8,128)(2,1)S(1)}, bf16[2,256,256]{2,1,0:T(8,128)(2,1)S(1)}, u32[]{:S(2)}, u32[]{:S(2)}) collective-permute-start(bf16[2,256,256]{2,1,0:T(8,128)(2,1)S(1)} %collective-permute-done.11), channel_id=1, source_target_pairs={{0,7},{1,0},{2,1},{3,2},{4,3},{5,4},{6,5},{7,6},{8,15},{9,8},{10,9... | collective-permute-start | bytes 786440 | tf_op jit(solution)/shard_map/ppermute | solution.py:24
  43.8 19.6 %collective-permute-start.16 = (bf16[1,256,256]{2,1,0:T(8,128)(2,1)}, bf16[1,256,256]{2,1,0:T(8,128)(2,1)}, u32[]{:S(2)}, u32[]{:S(2)}) collective-permute-start(bf16[1,256,256]{2,1,0:T(8,128)(2,1)} %slice.84), channel_id=1, source_target_pairs={{0,1},{1,2},{2,3},{3,4},{4,5},{5,6},{6,7},{7,0},{8,9},{9,10},{10,1... | collective-permute-start | bytes 393224 | tf_op jit(solution)/shard_map/ppermute | solution.py:32
  44.5 19.0 %collective-permute-start.17 = (bf16[1,256,256]{2,1,0:T(8,128)(2,1)}, bf16[1,256,256]{2,1,0:T(8,128)(2,1)}, u32[]{:S(2)}, u32[]{:S(2)}) collective-permute-start(bf16[1,256,256]{2,1,0:T(8,128)(2,1)} %slice.85), channel_id=1, source_target_pairs={{0,7},{1,0},{2,1},{3,2},{4,3},{5,4},{6,5},{7,6},{8,15},{9,8},{10,9... | collective-permute-start | bytes 393224 | tf_op jit(solution)/shard_map/ppermute | solution.py:33
  61.8 1.0 copy-start.2
  61.8 1.2 copy-start.4
  64.9 7.1 %collective-permute-start = (bf16[256,256]{1,0:T(8,128)(2,1)S(1)}, bf16[256,256]{1,0:T(8,128)(2,1)S(1)}, u32[]{:S(2)}, u32[]{:S(2)}) collective-permute-start(bf16[256,256]{1,0:T(8,128)(2,1)S(1)} %copy.12), channel_id=1, source_target_pairs={{0,8},{8,0},{1,9},{9,1},{2,10},{10,2},{3,11},{11,3},{4,12},{12,4},... | collective-permute-start | bytes 393224 | tf_op jit(solution)/shard_map/while/body/eval_jaxpr/ppermute | solution.py:29
  72.2 10.5 %collective-permute-start.4 = (bf16[2,256,256]{2,1,0:T(8,128)(2,1)S(1)}, bf16[2,256,256]{2,1,0:T(8,128)(2,1)S(1)}, u32[]{:S(2)}, u32[]{:S(2)}) collective-permute-start(bf16[2,256,256]{2,1,0:T(8,128)(2,1)S(1)} %fusion.117), channel_id=1, source_target_pairs={{0,7},{1,0},{2,1},{3,2},{4,3},{5,4},{6,5},{7,6},{8,15},{9,8},{10,9... | collective-permute-start | bytes 786440 | tf_op jit(solution)/shard_map/while/body/eval_jaxpr/ppermute | solution.py:24
  77.3 9.1 %collective-permute-start.1 = (bf16[2,256,256]{2,1,0:T(8,128)(2,1)S(1)}, bf16[2,256,256]{2,1,0:T(8,128)(2,1)S(1)}, u32[]{:S(2)}, u32[]{:S(2)}) collective-permute-start(bf16[2,256,256]{2,1,0:T(8,128)(2,1)S(1)} %fusion.117), channel_id=1, source_target_pairs={{0,1},{1,2},{2,3},{3,4},{4,5},{5,6},{6,7},{7,0},{8,9},{9,10},{10,1... | collective-permute-start | bytes 786440 | tf_op jit(solution)/shard_map/while/body/eval_jaxpr/ppermute | solution.py:23
  82.7 8.2 %collective-permute-start.5 = (bf16[2,256,256]{2,1,0:T(8,128)(2,1)S(1)}, bf16[2,256,256]{2,1,0:T(8,128)(2,1)S(1)}, u32[]{:S(2)}, u32[]{:S(2)}) collective-permute-start(bf16[2,256,256]{2,1,0:T(8,128)(2,1)S(1)} %collective-permute-done.4), channel_id=1, source_target_pairs={{0,7},{1,0},{2,1},{3,2},{4,3},{5,4},{6,5},{7,6},{8,15},{9,8},{10,9... | collective-permute-start | bytes 786440 | tf_op jit(solution)/shard_map/while/body/eval_jaxpr/ppermute | solution.py:24
  86.4 8.2 %collective-permute-start.2 = (bf16[2,256,256]{2,1,0:T(8,128)(2,1)S(1)}, bf16[2,256,256]{2,1,0:T(8,128)(2,1)S(1)}, u32[]{:S(2)}, u32[]{:S(2)}) collective-permute-start(bf16[2,256,256]{2,1,0:T(8,128)(2,1)S(1)} %collective-permute-done.1), channel_id=1, source_target_pairs={{0,1},{1,2},{2,3},{3,4},{4,5},{5,6},{6,7},{7,0},{8,9},{9,10},{10,1... | collective-permute-start | bytes 786440 | tf_op jit(solution)/shard_map/while/body/eval_jaxpr/ppermute | solution.py:23
  90.9 7.6 %collective-permute-start.6 = (bf16[2,256,256]{2,1,0:T(8,128)(2,1)S(1)}, bf16[2,256,256]{2,1,0:T(8,128)(2,1)S(1)}, u32[]{:S(2)}, u32[]{:S(2)}) collective-permute-start(bf16[2,256,256]{2,1,0:T(8,128)(2,1)S(1)} %collective-permute-done.5), channel_id=1, source_target_pairs={{0,7},{1,0},{2,1},{3,2},{4,3},{5,4},{6,5},{7,6},{8,15},{9,8},{10,9... | collective-permute-start | bytes 786440 | tf_op jit(solution)/shard_map/while/body/eval_jaxpr/ppermute | solution.py:24
  94.6 7.7 %collective-permute-start.3 = (bf16[2,256,256]{2,1,0:T(8,128)(2,1)S(1)}, bf16[2,256,256]{2,1,0:T(8,128)(2,1)S(1)}, u32[]{:S(2)}, u32[]{:S(2)}) collective-permute-start(bf16[2,256,256]{2,1,0:T(8,128)(2,1)S(1)} %collective-permute-done.2), channel_id=1, source_target_pairs={{0,1},{1,2},{2,3},{3,4},{4,5},{5,6},{6,7},{7,0},{8,9},{9,10},{10,1... | collective-permute-start | bytes 786440 | tf_op jit(solution)/shard_map/while/body/eval_jaxpr/ppermute | solution.py:23
  98.5 6.3 %collective-permute-start.7 = (bf16[1,256,256]{2,1,0:T(8,128)(2,1)S(1)}, bf16[1,256,256]{2,1,0:T(8,128)(2,1)S(1)}, u32[]{:S(2)}, u32[]{:S(2)}) collective-permute-start(bf16[1,256,256]{2,1,0:T(8,128)(2,1)S(1)} %slice.148), channel_id=1, source_target_pairs={{0,7},{1,0},{2,1},{3,2},{4,3},{5,4},{6,5},{7,6},{8,15},{9,8},{10,9... | collective-permute-start | bytes 393224 | tf_op jit(solution)/shard_map/while/body/eval_jaxpr/ppermute | solution.py:33
  102.3 6.3 %collective-permute-start.8 = (bf16[1,256,256]{2,1,0:T(8,128)(2,1)S(1)}, bf16[1,256,256]{2,1,0:T(8,128)(2,1)S(1)}, u32[]{:S(2)}, u32[]{:S(2)}) collective-permute-start(bf16[1,256,256]{2,1,0:T(8,128)(2,1)S(1)} %slice.149), channel_id=1, source_target_pairs={{0,1},{1,2},{2,3},{3,4},{4,5},{5,6},{6,7},{7,0},{8,9},{9,10},{10,1... | collective-permute-start | bytes 393224 | tf_op jit(solution)/shard_map/while/body/eval_jaxpr/ppermute | solution.py:32
  109.1 6.6 %collective-permute-start = (bf16[256,256]{1,0:T(8,128)(2,1)S(1)}, bf16[256,256]{1,0:T(8,128)(2,1)S(1)}, u32[]{:S(2)}, u32[]{:S(2)}) collective-permute-start(bf16[256,256]{1,0:T(8,128)(2,1)S(1)} %copy.12), channel_id=1, source_target_pairs={{0,8},{8,0},{1,9},{9,1},{2,10},{10,2},{3,11},{11,3},{4,12},{12,4},... | collective-permute-start | bytes 393224 | tf_op jit(solution)/shard_map/while/body/eval_jaxpr/ppermute | solution.py:29
  115.9 8.0 %collective-permute-start.4 = (bf16[2,256,256]{2,1,0:T(8,128)(2,1)S(1)}, bf16[2,256,256]{2,1,0:T(8,128)(2,1)S(1)}, u32[]{:S(2)}, u32[]{:S(2)}) collective-permute-start(bf16[2,256,256]{2,1,0:T(8,128)(2,1)S(1)} %fusion.117), channel_id=1, source_target_pairs={{0,7},{1,0},{2,1},{3,2},{4,3},{5,4},{6,5},{7,6},{8,15},{9,8},{10,9... | collective-permute-start | bytes 786440 | tf_op jit(solution)/shard_map/while/body/eval_jaxpr/ppermute | solution.py:24
  115.9 10.3 %collective-permute-start.1 = (bf16[2,256,256]{2,1,0:T(8,128)(2,1)S(1)}, bf16[2,256,256]{2,1,0:T(8,128)(2,1)S(1)}, u32[]{:S(2)}, u32[]{:S(2)}) collective-permute-start(bf16[2,256,256]{2,1,0:T(8,128)(2,1)S(1)} %fusion.117), channel_id=1, source_target_pairs={{0,1},{1,2},{2,3},{3,4},{4,5},{5,6},{6,7},{7,0},{8,9},{9,10},{10,1... | collective-permute-start | bytes 786440 | tf_op jit(solution)/shard_map/while/body/eval_jaxpr/ppermute | solution.py:23
  123.9 8.2 %collective-permute-start.5 = (bf16[2,256,256]{2,1,0:T(8,128)(2,1)S(1)}, bf16[2,256,256]{2,1,0:T(8,128)(2,1)S(1)}, u32[]{:S(2)}, u32[]{:S(2)}) collective-permute-start(bf16[2,256,256]{2,1,0:T(8,128)(2,1)S(1)} %collective-permute-done.4), channel_id=1, source_target_pairs={{0,7},{1,0},{2,1},{3,2},{4,3},{5,4},{6,5},{7,6},{8,15},{9,8},{10,9... | collective-permute-start | bytes 786440 | tf_op jit(solution)/shard_map/while/body/eval_jaxpr/ppermute | solution.py:24
  126.3 9.5 %collective-permute-start.2 = (bf16[2,256,256]{2,1,0:T(8,128)(2,1)S(1)}, bf16[2,256,256]{2,1,0:T(8,128)(2,1)S(1)}, u32[]{:S(2)}, u32[]{:S(2)}) collective-permute-start(bf16[2,256,256]{2,1,0:T(8,128)(2,1)S(1)} %collective-permute-done.1), channel_id=1, source_target_pairs={{0,1},{1,2},{2,3},{3,4},{4,5},{5,6},{6,7},{7,0},{8,9},{9,10},{10,1... | collective-permute-start | bytes 786440 | tf_op jit(solution)/shard_map/while/body/eval_jaxpr/ppermute | solution.py:23
  132.1 7.6 %collective-permute-start.6 = (bf16[2,256,256]{2,1,0:T(8,128)(2,1)S(1)}, bf16[2,256,256]{2,1,0:T(8,128)(2,1)S(1)}, u32[]{:S(2)}, u32[]{:S(2)}) collective-permute-start(bf16[2,256,256]{2,1,0:T(8,128)(2,1)S(1)} %collective-permute-done.5), channel_id=1, source_target_pairs={{0,7},{1,0},{2,1},{3,2},{4,3},{5,4},{6,5},{7,6},{8,15},{9,8},{10,9... | collective-permute-start | bytes 786440 | tf_op jit(solution)/shard_map/while/body/eval_jaxpr/ppermute | solution.py:24
  135.8 7.7 %collective-permute-start.3 = (bf16[2,256,256]{2,1,0:T(8,128)(2,1)S(1)}, bf16[2,256,256]{2,1,0:T(8,128)(2,1)S(1)}, u32[]{:S(2)}, u32[]{:S(2)}) collective-permute-start(bf16[2,256,256]{2,1,0:T(8,128)(2,1)S(1)} %collective-permute-done.2), channel_id=1, source_target_pairs={{0,1},{1,2},{2,3},{3,4},{4,5},{5,6},{6,7},{7,0},{8,9},{9,10},{10,1... | collective-permute-start | bytes 786440 | tf_op jit(solution)/shard_map/while/body/eval_jaxpr/ppermute | solution.py:23
  139.7 6.3 %collective-permute-start.7 = (bf16[1,256,256]{2,1,0:T(8,128)(2,1)S(1)}, bf16[1,256,256]{2,1,0:T(8,128)(2,1)S(1)}, u32[]{:S(2)}, u32[]{:S(2)}) collective-permute-start(bf16[1,256,256]{2,1,0:T(8,128)(2,1)S(1)} %slice.148), channel_id=1, source_target_pairs={{0,7},{1,0},{2,1},{3,2},{4,3},{5,4},{6,5},{7,6},{8,15},{9,8},{10,9... | collective-permute-start | bytes 393224 | tf_op jit(solution)/shard_map/while/body/eval_jaxpr/ppermute | solution.py:33
  143.4 6.3 %collective-permute-start.8 = (bf16[1,256,256]{2,1,0:T(8,128)(2,1)S(1)}, bf16[1,256,256]{2,1,0:T(8,128)(2,1)S(1)}, u32[]{:S(2)}, u32[]{:S(2)}) collective-permute-start(bf16[1,256,256]{2,1,0:T(8,128)(2,1)S(1)} %slice.149), channel_id=1, source_target_pairs={{0,1},{1,2},{2,3},{3,4},{4,5},{5,6},{6,7},{7,0},{8,9},{9,10},{10,1... | collective-permute-start | bytes 393224 | tf_op jit(solution)/shard_map/while/body/eval_jaxpr/ppermute | solution.py:32
  (1 other events, 0.7 us)
Sparse Core Ops, SparseCore 0:
  9.4 38.1 all-gather.1

commit v13 on v6

--- a/solution.py
+++ b/solution.py
@@ -67,19 +67,16 @@
         for b in range(block_rows):
             def place(p, carry):
                 target = dest_ref[b * slots + p]
-
-                @pl.when(target >= 0)
-                def _():
-                    start = pl.multiple_of(target * size, size)
-                    out_ref[pl.ds(start, size), b * size:(b + 1) * size] = tiles_ref[p // local_slots, b, p % local_slots]
-
+                target = jnp.where(target >= 0, target, rows)
+                start = pl.multiple_of(target * size, size)
+                out_ref[pl.ds(start, size), b * size:(b + 1) * size] = tiles_ref[p // local_slots, b, p % local_slots]
                 return carry
 
             lax.fori_loop(0, slots, place, 0, unroll=True)
 
     return pl.pallas_call(
         kernel,
-        out_shape=jax.ShapeDtypeStruct((rows * size, block_rows * size), tiles.dtype),
+        out_shape=jax.ShapeDtypeStruct(((rows + 1) * size, block_rows * size), tiles.dtype),
         in_specs=[pl.BlockSpec(memory_space=pltpu.SMEM), pl.BlockSpec(memory_space=pltpu.VMEM)],
         out_specs=pl.BlockSpec(memory_space=pltpu.VMEM),
     )(dest.reshape(-1), tiles)
@@ -109,7 +106,7 @@
     target = (offset * y_count + owner // z_count) * per_col + ring_neighbours % per_col
     dest = jnp.where(ring_live, target, -1)
     dense = place_tiles(dest, tiles, total_blocks)
-    dense = dense.reshape(z_count, y_count, local_width, local_width)
+    dense = dense[: total_blocks * block_size].reshape(z_count, y_count, local_width, local_width)
 
     def apply_hamiltonian(field):
         blocks = gather_col(field, y_count, z_count)

time: 153 us -> 149 us (0.974)
  waiting for transfers between devices: 68 us -> 64.7 us
  Pallas kernels: 7.21 us -> 4.49 us
  starting transfers between devices: 49.7 us -> 51.8 us
    pallas_call x1, Pallas kernels: 7.21 us -> 4.49 us  [place_tiles(): pl.pallas_call(kernel, out_shape=jax.ShapeDtypeStruct(((rows + 1) * size,...]
    ppermute x3, waiting for transfers between devices: 13.7 us -> 11.6 us  [ring_blocks(): blocks[1] = lax.ppermute(piece, axis, fwd)]
    ppermute x3, starting transfers between devices: 6.93 us -> 9.02 us  [ring_blocks(): blocks[1] = lax.ppermute(piece, axis, fwd)]
    unnamed x28 -> x12, local copies, waits for them, and re-layouts: 3.83 us -> 3.28 us
  transfers between devices with their start and end apart: 28 -> 28, of which waited for: 17 -> 17; matrix products, arithmetic and copies ran while one was open for 4% -> 6% of each run, Pallas kernels for 5% -> 3%
where the time goes in v13:
time: 149 us
  waiting for transfers between devices  64.7 us (43%)
  starting transfers between devices  51.8 us (35%)
  between operations  13.6 us (9%)
  matrix products  6.6 us (4%)
  local copies, waits for them, and re-layouts  5.67 us (4%)
  Pallas kernels  4.49 us (3%)
  other arithmetic  2.18 us (1%)
    ppermute x9, starting transfers between devices, ring_blocks(): left = lax.ppermute(left, axis, bwd)  27.4 us
    ppermute x9, waiting for transfers between devices, ring_blocks(): left = lax.ppermute(left, axis, bwd)  25.9 us
    ppermute x9, waiting for transfers between devices, ring_blocks(): right = lax.ppermute(right, axis, fwd)  12.1 us
    ppermute x3, waiting for transfers between devices, ring_blocks(): blocks[1] = lax.ppermute(piece, axis, fwd)  11.6 us
    ppermute x3, starting transfers between devices, ring_blocks(): lax.ppermute(lax.slice_in_dim(left, split, None, axis=split_dim), axis, bwd)  11 us
    ppermute x3, starting transfers between devices, ring_blocks(): blocks[1] = lax.ppermute(piece, axis, fwd)  9.02 us
    ppermute x3, waiting for transfers between devices, ring_blocks(): lax.ppermute(lax.slice_in_dim(right, 0, split, axis=split_dim), axis, fwd)  7.5 us
    dot_general x24, matrix products, apply_hamiltonian(): jnp.einsum('ymj,yjo->mo', chunk, dense[d], preferred_element_type=jnp.flo...  6.6 us
  transfers between devices with their start and end apart: 28, of which 17 were waited for; matrix products, arithmetic and copies ran while one was open for 6% of the time, Pallas kernels for 3%

profile of v13, /device:TPU:2, one launch (start us, length us, event | category | flops | bytes accessed | tf_op | source)
XLA Modules:
  0.0 149.2 jit_solution(16625909115386319185)
XLA Ops:
  9.2 3.3 %collective-permute-start.9 = (bf16[256,256]{1,0:T(8,128)(2,1)S(1)}, bf16[256,256]{1,0:T(8,128)(2,1)S(1)}, u32[]{:S(2)}, u32[]{:S(2)}) collective-permute-start(bf16[256,256]{1,0:T(8,128)(2,1)S(1)} %copy.17), channel_id=1, source_target_pairs={{0,8},{8,0},{1,9},{9,1},{2,10},{10,2},{3,11},{11,3},{4,12},{12,4},... | collective-permute-start | bytes 393224 | tf_op jit(solution)/shard_map/ppermute | solution.py:29
  12.5 3.5 %collective-permute-done.9 = bf16[256,256]{1,0:T(8,128)(2,1)S(1)} collective-permute-done((bf16[256,256]{1,0:T(8,128)(2,1)S(1)}, bf16[256,256]{1,0:T(8,128)(2,1)S(1)}, u32[]{:S(2)}, u32[]{:S(2)}) %collective-permute-start.9) | collective-permute-done | bytes 131104 | tf_op jit(solution)/shard_map/ppermute | solution.py:29
  18.2 4.0 %collective-permute-start.10 = (bf16[2,256,256]{2,1,0:T(8,128)(2,1)S(1)}, bf16[2,256,256]{2,1,0:T(8,128)(2,1)S(1)}, u32[]{:S(2)}, u32[]{:S(2)}) collective-permute-start(bf16[2,256,256]{2,1,0:T(8,128)(2,1)S(1)} %fusion.42), channel_id=1, source_target_pairs={{0,7},{1,0},{2,1},{3,2},{4,3},{5,4},{6,5},{7,6},{8,15},{9,8},{10,9... | collective-permute-start | bytes 786440 | tf_op jit(solution)/shard_map/ppermute | solution.py:24
  22.2 5.4 %collective-permute-done.13 = bf16[2,256,256]{2,1,0:T(8,128)(2,1)S(1)} collective-permute-done((bf16[2,256,256]{2,1,0:T(8,128)(2,1)S(1)}, bf16[2,256,256]{2,1,0:T(8,128)(2,1)S(1)}, u32[]{:S(2)}, u32[]{:S(2)}) %collective-permute-start.13) | collective-permute-done | bytes 262176 | tf_op jit(solution)/shard_map/ppermute | solution.py:23
  27.6 3.2 %collective-permute-start.11 = (bf16[2,256,256]{2,1,0:T(8,128)(2,1)S(1)}, bf16[2,256,256]{2,1,0:T(8,128)(2,1)S(1)}, u32[]{:S(2)}, u32[]{:S(2)}) collective-permute-start(bf16[2,256,256]{2,1,0:T(8,128)(2,1)S(1)} %collective-permute-done.10), channel_id=1, source_target_pairs={{0,7},{1,0},{2,1},{3,2},{4,3},{5,4},{6,5},{7,6},{8,15},{9,8},{10,9... | collective-permute-start | bytes 786440 | tf_op jit(solution)/shard_map/ppermute | solution.py:24
  30.8 4.6 %collective-permute-done.14 = bf16[2,256,256]{2,1,0:T(8,128)(2,1)S(1)} collective-permute-done((bf16[2,256,256]{2,1,0:T(8,128)(2,1)S(1)}, bf16[2,256,256]{2,1,0:T(8,128)(2,1)S(1)}, u32[]{:S(2)}, u32[]{:S(2)}) %collective-permute-start.14) | collective-permute-done | bytes 262176 | tf_op jit(solution)/shard_map/ppermute | solution.py:23
  35.4 3.2 %collective-permute-start.12 = (bf16[2,256,256]{2,1,0:T(8,128)(2,1)S(1)}, bf16[2,256,256]{2,1,0:T(8,128)(2,1)S(1)}, u32[]{:S(2)}, u32[]{:S(2)}) collective-permute-start(bf16[2,256,256]{2,1,0:T(8,128)(2,1)S(1)} %collective-permute-done.11), channel_id=1, source_target_pairs={{0,7},{1,0},{2,1},{3,2},{4,3},{5,4},{6,5},{7,6},{8,15},{9,8},{10,9... | collective-permute-start | bytes 786440 | tf_op jit(solution)/shard_map/ppermute | solution.py:24
  43.1 3.5 %collective-permute-start.17 = (bf16[1,256,256]{2,1,0:T(8,128)(2,1)S(1)}, bf16[1,256,256]{2,1,0:T(8,128)(2,1)}, u32[]{:S(2)}, u32[]{:S(2)}) collective-permute-start(bf16[1,256,256]{2,1,0:T(8,128)(2,1)S(1)} %slice.97), channel_id=1, source_target_pairs={{0,7},{1,0},{2,1},{3,2},{4,3},{5,4},{6,5},{7,6},{8,15},{9,8},{10,9... | collective-permute-start | bytes 393224 | tf_op jit(solution)/shard_map/ppermute | solution.py:33
  46.6 3.3 %all-gather.2.cloned.1.call-done = bf16[4,48,64,64]{3,2,1,0:T(8,128)(2,1)} async-done(((bf16[4,3,64,64]{3,2,1,0:T(8,128)(2,1)}), bf16[4,48,64,64]{3,2,1,0:T(8,128)(2,1)}) %all-gather.2.cloned.1.call-update) | async-done | bytes 1572880 | tf_op jit(solution)/shard_map/all_gather | solution.py:100
  49.9 4.5 %shard_map.46 = bf16[4160,256]{1,0:T(8,128)(2,1)} custom-call(s32[192]{0:T(256)} %reshape.43.dest_ref, bf16[1,4,48,64,64]{4,3,2,1,0:T(8,128)(2,1)} %bitcast.183), custom_call_target="tpu_custom_call" | custom-call | tf_op jit(solution)/shard_map/pallas_call | solution.py:77
  59.1 82.6 %while.12 = (s32[]{:T(128)}, bf16[256,256]{1,0:T(8,128)(2,1)S(1)}, bf16[256,256]{1,0:T(8,128)(2,1)S(1)}, bf16[8,2,256,256]{3,2,1,0:T(8,128)(2,1)S(1)}, s32[]{:T(...) while((s32[]{:T(128)}, bf16[256,256]{1,0:T(8,128)(2,1)S(1)}, ...), condition=%wide.region_2.4_spmd, body=%wide.region_1.3_spmd.sunk | while | flops 538116096 | bytes 17564300 | solution.py:128
  59.1 2.9 %collective-permute-start = (bf16[256,256]{1,0:T(8,128)(2,1)S(1)}, bf16[256,256]{1,0:T(8,128)(2,1)S(1)}, u32[]{:S(2)}, u32[]{:S(2)}) collective-permute-start(bf16[256,256]{1,0:T(8,128)(2,1)S(1)} %copy.12), channel_id=1, source_target_pairs={{0,8},{8,0},{1,9},{9,1},{2,10},{10,2},{3,11},{11,3},{4,12},{12,4},... | collective-permute-start | bytes 393224 | tf_op jit(solution)/shard_map/while/body/eval_jaxpr/ppermute | solution.py:29
  62.0 4.3 %collective-permute-done = bf16[256,256]{1,0:T(8,128)(2,1)S(1)} collective-permute-done((bf16[256,256]{1,0:T(8,128)(2,1)S(1)}, bf16[256,256]{1,0:T(8,128)(2,1)S(1)}, u32[]{:S(2)}, u32[]{:S(2)}) %collective-permute-start) | collective-permute-done | bytes 131104 | tf_op jit(solution)/shard_map/while/body/eval_jaxpr/ppermute | solution.py:29
  66.6 3.4 %collective-permute-start.4 = (bf16[2,256,256]{2,1,0:T(8,128)(2,1)S(1)}, bf16[2,256,256]{2,1,0:T(8,128)(2,1)S(1)}, u32[]{:S(2)}, u32[]{:S(2)}) collective-permute-start(bf16[2,256,256]{2,1,0:T(8,128)(2,1)S(1)} %fusion.117), channel_id=1, source_target_pairs={{0,7},{1,0},{2,1},{3,2},{4,3},{5,4},{6,5},{7,6},{8,15},{9,8},{10,9... | collective-permute-start | bytes 786440 | tf_op jit(solution)/shard_map/while/body/eval_jaxpr/ppermute | solution.py:24
  70.2 4.9 %collective-permute-done.4 = bf16[2,256,256]{2,1,0:T(8,128)(2,1)S(1)} collective-permute-done((bf16[2,256,256]{2,1,0:T(8,128)(2,1)S(1)}, bf16[2,256,256]{2,1,0:T(8,128)(2,1)S(1)}, u32[]{:S(2)}, u32[]{:S(2)}) %collective-permute-start.4) | collective-permute-done | bytes 262176 | tf_op jit(solution)/shard_map/while/body/eval_jaxpr/ppermute | solution.py:24
  75.0 3.7 %collective-permute-start.5 = (bf16[2,256,256]{2,1,0:T(8,128)(2,1)S(1)}, bf16[2,256,256]{2,1,0:T(8,128)(2,1)S(1)}, u32[]{:S(2)}, u32[]{:S(2)}) collective-permute-start(bf16[2,256,256]{2,1,0:T(8,128)(2,1)S(1)} %collective-permute-done.4), channel_id=1, source_target_pairs={{0,7},{1,0},{2,1},{3,2},{4,3},{5,4},{6,5},{7,6},{8,15},{9,8},{10,9... | collective-permute-start | bytes 786440 | tf_op jit(solution)/shard_map/while/body/eval_jaxpr/ppermute | solution.py:24
  79.2 3.8 %collective-permute-done.5 = bf16[2,256,256]{2,1,0:T(8,128)(2,1)S(1)} collective-permute-done((bf16[2,256,256]{2,1,0:T(8,128)(2,1)S(1)}, bf16[2,256,256]{2,1,0:T(8,128)(2,1)S(1)}, u32[]{:S(2)}, u32[]{:S(2)}) %collective-permute-start.5) | collective-permute-done | bytes 262176 | tf_op jit(solution)/shard_map/while/body/eval_jaxpr/ppermute | solution.py:24
  83.0 3.7 %collective-permute-start.6 = (bf16[2,256,256]{2,1,0:T(8,128)(2,1)S(1)}, bf16[2,256,256]{2,1,0:T(8,128)(2,1)S(1)}, u32[]{:S(2)}, u32[]{:S(2)}) collective-permute-start(bf16[2,256,256]{2,1,0:T(8,128)(2,1)S(1)} %collective-permute-done.5), channel_id=1, source_target_pairs={{0,7},{1,0},{2,1},{3,2},{4,3},{5,4},{6,5},{7,6},{8,15},{9,8},{10,9... | collective-permute-start | bytes 786440 | tf_op jit(solution)/shard_map/while/body/eval_jaxpr/ppermute | solution.py:24
  87.1 3.4 %collective-permute-done.6 = bf16[2,256,256]{2,1,0:T(8,128)(2,1)S(1)} collective-permute-done((bf16[2,256,256]{2,1,0:T(8,128)(2,1)S(1)}, bf16[2,256,256]{2,1,0:T(8,128)(2,1)S(1)}, u32[]{:S(2)}, u32[]{:S(2)}) %collective-permute-start.6) | collective-permute-done | bytes 262176 | tf_op jit(solution)/shard_map/while/body/eval_jaxpr/ppermute | solution.py:24
  90.6 3.8 %collective-permute-start.7 = (bf16[1,256,256]{2,1,0:T(8,128)(2,1)S(1)}, bf16[1,256,256]{2,1,0:T(8,128)(2,1)S(1)}, u32[]{:S(2)}, u32[]{:S(2)}) collective-permute-start(bf16[1,256,256]{2,1,0:T(8,128)(2,1)S(1)} %slice.161), channel_id=1, source_target_pairs={{0,7},{1,0},{2,1},{3,2},{4,3},{5,4},{6,5},{7,6},{8,15},{9,8},{10,9... | collective-permute-start | bytes 393224 | tf_op jit(solution)/shard_map/while/body/eval_jaxpr/ppermute | solution.py:33
  94.7 2.2 %collective-permute-done.7 = bf16[1,256,256]{2,1,0:T(8,128)(2,1)S(1)} collective-permute-done((bf16[1,256,256]{2,1,0:T(8,128)(2,1)S(1)}, bf16[1,256,256]{2,1,0:T(8,128)(2,1)S(1)}, u32[]{:S(2)}, u32[]{:S(2)}) %collective-permute-start.7) | collective-permute-done | bytes 131104 | tf_op jit(solution)/shard_map/while/body/eval_jaxpr/ppermute | solution.py:33
  96.9 3.8 %collective-permute-done.8 = bf16[1,256,256]{2,1,0:T(8,128)(2,1)S(1)} collective-permute-done((bf16[1,256,256]{2,1,0:T(8,128)(2,1)S(1)}, bf16[1,256,256]{2,1,0:T(8,128)(2,1)S(1)}, u32[]{:S(2)}, u32[]{:S(2)}) %collective-permute-start.8) | collective-permute-done | bytes 131104 | tf_op jit(solution)/shard_map/while/body/eval_jaxpr/ppermute | solution.py:32
  101.2 2.9 %collective-permute-start = (bf16[256,256]{1,0:T(8,128)(2,1)S(1)}, bf16[256,256]{1,0:T(8,128)(2,1)S(1)}, u32[]{:S(2)}, u32[]{:S(2)}) collective-permute-start(bf16[256,256]{1,0:T(8,128)(2,1)S(1)} %copy.12), channel_id=1, source_target_pairs={{0,8},{8,0},{1,9},{9,1},{2,10},{10,2},{3,11},{11,3},{4,12},{12,4},... | collective-permute-start | bytes 393224 | tf_op jit(solution)/shard_map/while/body/eval_jaxpr/ppermute | solution.py:29
  104.0 3.7 %collective-permute-done = bf16[256,256]{1,0:T(8,128)(2,1)S(1)} collective-permute-done((bf16[256,256]{1,0:T(8,128)(2,1)S(1)}, bf16[256,256]{1,0:T(8,128)(2,1)S(1)}, u32[]{:S(2)}, u32[]{:S(2)}) %collective-permute-start) | collective-permute-done | bytes 131104 | tf_op jit(solution)/shard_map/while/body/eval_jaxpr/ppermute | solution.py:29
  110.2 5.4 %collective-permute-done.4 = bf16[2,256,256]{2,1,0:T(8,128)(2,1)S(1)} collective-permute-done((bf16[2,256,256]{2,1,0:T(8,128)(2,1)S(1)}, bf16[2,256,256]{2,1,0:T(8,128)(2,1)S(1)}, u32[]{:S(2)}, u32[]{:S(2)}) %collective-permute-start.4) | collective-permute-done | bytes 262176 | tf_op jit(solution)/shard_map/while/body/eval_jaxpr/ppermute | solution.py:24
  115.6 2.4 %collective-permute-start.5 = (bf16[2,256,256]{2,1,0:T(8,128)(2,1)S(1)}, bf16[2,256,256]{2,1,0:T(8,128)(2,1)S(1)}, u32[]{:S(2)}, u32[]{:S(2)}) collective-permute-start(bf16[2,256,256]{2,1,0:T(8,128)(2,1)S(1)} %collective-permute-done.4), channel_id=1, source_target_pairs={{0,7},{1,0},{2,1},{3,2},{4,3},{5,4},{6,5},{7,6},{8,15},{9,8},{10,9... | collective-permute-start | bytes 786440 | tf_op jit(solution)/shard_map/while/body/eval_jaxpr/ppermute | solution.py:24
  118.5 5.0 %collective-permute-done.5 = bf16[2,256,256]{2,1,0:T(8,128)(2,1)S(1)} collective-permute-done((bf16[2,256,256]{2,1,0:T(8,128)(2,1)S(1)}, bf16[2,256,256]{2,1,0:T(8,128)(2,1)S(1)}, u32[]{:S(2)}, u32[]{:S(2)}) %collective-permute-start.5) | collective-permute-done | bytes 262176 | tf_op jit(solution)/shard_map/while/body/eval_jaxpr/ppermute | solution.py:24
  123.6 3.7 %collective-permute-start.6 = (bf16[2,256,256]{2,1,0:T(8,128)(2,1)S(1)}, bf16[2,256,256]{2,1,0:T(8,128)(2,1)S(1)}, u32[]{:S(2)}, u32[]{:S(2)}) collective-permute-start(bf16[2,256,256]{2,1,0:T(8,128)(2,1)S(1)} %collective-permute-done.5), channel_id=1, source_target_pairs={{0,7},{1,0},{2,1},{3,2},{4,3},{5,4},{6,5},{7,6},{8,15},{9,8},{10,9... | collective-permute-start | bytes 786440 | tf_op jit(solution)/shard_map/while/body/eval_jaxpr/ppermute | solution.py:24
  127.7 3.4 %collective-permute-done.6 = bf16[2,256,256]{2,1,0:T(8,128)(2,1)S(1)} collective-permute-done((bf16[2,256,256]{2,1,0:T(8,128)(2,1)S(1)}, bf16[2,256,256]{2,1,0:T(8,128)(2,1)S(1)}, u32[]{:S(2)}, u32[]{:S(2)}) %collective-permute-start.6) | collective-permute-done | bytes 262176 | tf_op jit(solution)/shard_map/while/body/eval_jaxpr/ppermute | solution.py:24
  131.1 3.8 %collective-permute-start.7 = (bf16[1,256,256]{2,1,0:T(8,128)(2,1)S(1)}, bf16[1,256,256]{2,1,0:T(8,128)(2,1)S(1)}, u32[]{:S(2)}, u32[]{:S(2)}) collective-permute-start(bf16[1,256,256]{2,1,0:T(8,128)(2,1)S(1)} %slice.161), channel_id=1, source_target_pairs={{0,7},{1,0},{2,1},{3,2},{4,3},{5,4},{6,5},{7,6},{8,15},{9,8},{10,9... | collective-permute-start | bytes 393224 | tf_op jit(solution)/shard_map/while/body/eval_jaxpr/ppermute | solution.py:33
  135.3 2.2 %collective-permute-done.7 = bf16[1,256,256]{2,1,0:T(8,128)(2,1)S(1)} collective-permute-done((bf16[1,256,256]{2,1,0:T(8,128)(2,1)S(1)}, bf16[1,256,256]{2,1,0:T(8,128)(2,1)S(1)}, u32[]{:S(2)}, u32[]{:S(2)}) %collective-permute-start.7) | collective-permute-done | bytes 131104 | tf_op jit(solution)/shard_map/while/body/eval_jaxpr/ppermute | solution.py:33
  137.4 3.8 %collective-permute-done.8 = bf16[1,256,256]{2,1,0:T(8,128)(2,1)S(1)} collective-permute-done((bf16[1,256,256]{2,1,0:T(8,128)(2,1)S(1)}, bf16[1,256,256]{2,1,0:T(8,128)(2,1)S(1)}, u32[]{:S(2)}, u32[]{:S(2)}) %collective-permute-start.8) | collective-permute-done | bytes 131104 | tf_op jit(solution)/shard_map/while/body/eval_jaxpr/ppermute | solution.py:32
  (83 shorter events, 21.0 us)
Async XLA Ops:
  6.5 43.4 %all-gather.2.cloned.1.call-start = ((), (), s32[]{:S(2)}) async-start(), calls=%async_computation | async-start | bytes 3342336 | tf_op jit(solution)/shard_map/all_gather | solution.py:100
  9.2 6.8 %collective-permute-start.9 = (bf16[256,256]{1,0:T(8,128)(2,1)S(1)}, bf16[256,256]{1,0:T(8,128)(2,1)S(1)}, u32[]{:S(2)}, u32[]{:S(2)}) collective-permute-start(bf16[256,256]{1,0:T(8,128)(2,1)S(1)} %copy.17), channel_id=1, source_target_pairs={{0,8},{8,0},{1,9},{9,1},{2,10},{10,2},{3,11},{11,3},{4,12},{12,4},... | collective-permute-start | bytes 393224 | tf_op jit(solution)/shard_map/ppermute | solution.py:29
  16.2 11.4 %collective-permute-start.13 = (bf16[2,256,256]{2,1,0:T(8,128)(2,1)S(1)}, bf16[2,256,256]{2,1,0:T(8,128)(2,1)S(1)}, u32[]{:S(2)}, u32[]{:S(2)}) collective-permute-start(bf16[2,256,256]{2,1,0:T(8,128)(2,1)S(1)} %fusion.42), channel_id=1, source_target_pairs={{0,1},{1,2},{2,3},{3,4},{4,5},{5,6},{6,7},{7,0},{8,9},{9,10},{10,1... | collective-permute-start | bytes 786440 | tf_op jit(solution)/shard_map/ppermute | solution.py:23
  18.2 9.4 %collective-permute-start.10 = (bf16[2,256,256]{2,1,0:T(8,128)(2,1)S(1)}, bf16[2,256,256]{2,1,0:T(8,128)(2,1)S(1)}, u32[]{:S(2)}, u32[]{:S(2)}) collective-permute-start(bf16[2,256,256]{2,1,0:T(8,128)(2,1)S(1)} %fusion.42), channel_id=1, source_target_pairs={{0,7},{1,0},{2,1},{3,2},{4,3},{5,4},{6,5},{7,6},{8,15},{9,8},{10,9... | collective-permute-start | bytes 786440 | tf_op jit(solution)/shard_map/ppermute | solution.py:24
  27.6 22.3 %copy-start.1 = (bf16[2,256,256]{2,1,0:T(8,128)(2,1)}, bf16[2,256,256]{2,1,0:T(8,128)(2,1)S(1)}, u32[]{:S(2)}) copy-start(bf16[2,256,256]{2,1,0:T(8,128)(2,1)S(1)} %collective-permute-done.13) | copy-start | bytes 786436
  27.6 7.8 %collective-permute-start.14 = (bf16[2,256,256]{2,1,0:T(8,128)(2,1)S(1)}, bf16[2,256,256]{2,1,0:T(8,128)(2,1)S(1)}, u32[]{:S(2)}, u32[]{:S(2)}) collective-permute-start(bf16[2,256,256]{2,1,0:T(8,128)(2,1)S(1)} %collective-permute-done.13), channel_id=1, source_target_pairs={{0,1},{1,2},{2,3},{3,4},{4,5},{5,6},{6,7},{7,0},{8,9},{9,10},{10,1... | collective-permute-start | bytes 786440 | tf_op jit(solution)/shard_map/ppermute | solution.py:23
  27.6 7.8 %collective-permute-start.11 = (bf16[2,256,256]{2,1,0:T(8,128)(2,1)S(1)}, bf16[2,256,256]{2,1,0:T(8,128)(2,1)S(1)}, u32[]{:S(2)}, u32[]{:S(2)}) collective-permute-start(bf16[2,256,256]{2,1,0:T(8,128)(2,1)S(1)} %collective-permute-done.10), channel_id=1, source_target_pairs={{0,7},{1,0},{2,1},{3,2},{4,3},{5,4},{6,5},{7,6},{8,15},{9,8},{10,9... | collective-permute-start | bytes 786440 | tf_op jit(solution)/shard_map/ppermute | solution.py:24
  35.4 7.6 %collective-permute-start.15 = (bf16[2,256,256]{2,1,0:T(8,128)(2,1)S(1)}, bf16[2,256,256]{2,1,0:T(8,128)(2,1)S(1)}, u32[]{:S(2)}, u32[]{:S(2)}) collective-permute-start(bf16[2,256,256]{2,1,0:T(8,128)(2,1)S(1)} %collective-permute-done.14), channel_id=1, source_target_pairs={{0,1},{1,2},{2,3},{3,4},{4,5},{5,6},{6,7},{7,0},{8,9},{9,10},{10,1... | collective-permute-start | bytes 786440 | tf_op jit(solution)/shard_map/ppermute | solution.py:23
  35.4 19.0 %copy-start.3 = (bf16[2,256,256]{2,1,0:T(8,128)(2,1)}, bf16[2,256,256]{2,1,0:T(8,128)(2,1)S(1)}, u32[]{:S(2)}) copy-start(bf16[2,256,256]{2,1,0:T(8,128)(2,1)S(1)} %collective-permute-done.11) | copy-start | bytes 786436
  35.4 7.7 %collective-permute-start.12 = (bf16[2,256,256]{2,1,0:T(8,128)(2,1)S(1)}, bf16[2,256,256]{2,1,0:T(8,128)(2,1)S(1)}, u32[]{:S(2)}, u32[]{:S(2)}) collective-permute-start(bf16[2,256,256]{2,1,0:T(8,128)(2,1)S(1)} %collective-permute-done.11), channel_id=1, source_target_pairs={{0,7},{1,0},{2,1},{3,2},{4,3},{5,4},{6,5},{7,6},{8,15},{9,8},{10,9... | collective-permute-start | bytes 786440 | tf_op jit(solution)/shard_map/ppermute | solution.py:24
  43.0 14.5 %collective-permute-start.16 = (bf16[1,256,256]{2,1,0:T(8,128)(2,1)S(1)}, bf16[1,256,256]{2,1,0:T(8,128)(2,1)}, u32[]{:S(2)}, u32[]{:S(2)}) collective-permute-start(bf16[1,256,256]{2,1,0:T(8,128)(2,1)S(1)} %slice.96), channel_id=1, source_target_pairs={{0,1},{1,2},{2,3},{3,4},{4,5},{5,6},{6,7},{7,0},{8,9},{9,10},{10,1... | collective-permute-start | bytes 393224 | tf_op jit(solution)/shard_map/ppermute | solution.py:32
  43.1 14.4 %collective-permute-start.17 = (bf16[1,256,256]{2,1,0:T(8,128)(2,1)S(1)}, bf16[1,256,256]{2,1,0:T(8,128)(2,1)}, u32[]{:S(2)}, u32[]{:S(2)}) collective-permute-start(bf16[1,256,256]{2,1,0:T(8,128)(2,1)S(1)} %slice.97), channel_id=1, source_target_pairs={{0,7},{1,0},{2,1},{3,2},{4,3},{5,4},{6,5},{7,6},{8,15},{9,8},{10,9... | collective-permute-start | bytes 393224 | tf_op jit(solution)/shard_map/ppermute | solution.py:33
  56.1 1.2 copy-start.2
  57.0 2.1 %slice-start = ((bf16[4160,256]{1,0:T(8,128)(2,1)}), bf16[4096,256]{1,0:T(8,128)(2,1)S(1)}, s32[]{:S(2)}) async-start(bf16[4160,256]{1,0:T(8,128)(2,1)} %shard_map.46), calls=%async_computation.1 | async-start | bytes 4194304 | tf_op jit(solution)/shard_map/slice | solution.py:109
  59.1 7.2 %collective-permute-start = (bf16[256,256]{1,0:T(8,128)(2,1)S(1)}, bf16[256,256]{1,0:T(8,128)(2,1)S(1)}, u32[]{:S(2)}, u32[]{:S(2)}) collective-permute-start(bf16[256,256]{1,0:T(8,128)(2,1)S(1)} %copy.12), channel_id=1, source_target_pairs={{0,8},{8,0},{1,9},{9,1},{2,10},{10,2},{3,11},{11,3},{4,12},{12,4},... | collective-permute-start | bytes 393224 | tf_op jit(solution)/shard_map/while/body/eval_jaxpr/ppermute | solution.py:29
  66.6 8.5 %collective-permute-start.4 = (bf16[2,256,256]{2,1,0:T(8,128)(2,1)S(1)}, bf16[2,256,256]{2,1,0:T(8,128)(2,1)S(1)}, u32[]{:S(2)}, u32[]{:S(2)}) collective-permute-start(bf16[2,256,256]{2,1,0:T(8,128)(2,1)S(1)} %fusion.117), channel_id=1, source_target_pairs={{0,7},{1,0},{2,1},{3,2},{4,3},{5,4},{6,5},{7,6},{8,15},{9,8},{10,9... | collective-permute-start | bytes 786440 | tf_op jit(solution)/shard_map/while/body/eval_jaxpr/ppermute | solution.py:24
  69.9 8.8 %collective-permute-start.1 = (bf16[2,256,256]{2,1,0:T(8,128)(2,1)S(1)}, bf16[2,256,256]{2,1,0:T(8,128)(2,1)S(1)}, u32[]{:S(2)}, u32[]{:S(2)}) collective-permute-start(bf16[2,256,256]{2,1,0:T(8,128)(2,1)S(1)} %fusion.117), channel_id=1, source_target_pairs={{0,1},{1,2},{2,3},{3,4},{4,5},{5,6},{6,7},{7,0},{8,9},{9,10},{10,1... | collective-permute-start | bytes 786440 | tf_op jit(solution)/shard_map/while/body/eval_jaxpr/ppermute | solution.py:23
  75.0 7.9 %collective-permute-start.5 = (bf16[2,256,256]{2,1,0:T(8,128)(2,1)S(1)}, bf16[2,256,256]{2,1,0:T(8,128)(2,1)S(1)}, u32[]{:S(2)}, u32[]{:S(2)}) collective-permute-start(bf16[2,256,256]{2,1,0:T(8,128)(2,1)S(1)} %collective-permute-done.4), channel_id=1, source_target_pairs={{0,7},{1,0},{2,1},{3,2},{4,3},{5,4},{6,5},{7,6},{8,15},{9,8},{10,9... | collective-permute-start | bytes 786440 | tf_op jit(solution)/shard_map/while/body/eval_jaxpr/ppermute | solution.py:24
  78.7 7.9 %collective-permute-start.2 = (bf16[2,256,256]{2,1,0:T(8,128)(2,1)S(1)}, bf16[2,256,256]{2,1,0:T(8,128)(2,1)S(1)}, u32[]{:S(2)}, u32[]{:S(2)}) collective-permute-start(bf16[2,256,256]{2,1,0:T(8,128)(2,1)S(1)} %collective-permute-done.1), channel_id=1, source_target_pairs={{0,1},{1,2},{2,3},{3,4},{4,5},{5,6},{6,7},{7,0},{8,9},{9,10},{10,1... | collective-permute-start | bytes 786440 | tf_op jit(solution)/shard_map/while/body/eval_jaxpr/ppermute | solution.py:23
  83.0 7.6 %collective-permute-start.6 = (bf16[2,256,256]{2,1,0:T(8,128)(2,1)S(1)}, bf16[2,256,256]{2,1,0:T(8,128)(2,1)S(1)}, u32[]{:S(2)}, u32[]{:S(2)}) collective-permute-start(bf16[2,256,256]{2,1,0:T(8,128)(2,1)S(1)} %collective-permute-done.5), channel_id=1, source_target_pairs={{0,7},{1,0},{2,1},{3,2},{4,3},{5,4},{6,5},{7,6},{8,15},{9,8},{10,9... | collective-permute-start | bytes 786440 | tf_op jit(solution)/shard_map/while/body/eval_jaxpr/ppermute | solution.py:24
  86.7 7.7 %collective-permute-start.3 = (bf16[2,256,256]{2,1,0:T(8,128)(2,1)S(1)}, bf16[2,256,256]{2,1,0:T(8,128)(2,1)S(1)}, u32[]{:S(2)}, u32[]{:S(2)}) collective-permute-start(bf16[2,256,256]{2,1,0:T(8,128)(2,1)S(1)} %collective-permute-done.2), channel_id=1, source_target_pairs={{0,1},{1,2},{2,3},{3,4},{4,5},{5,6},{6,7},{7,0},{8,9},{9,10},{10,1... | collective-permute-start | bytes 786440 | tf_op jit(solution)/shard_map/while/body/eval_jaxpr/ppermute | solution.py:23
  90.6 6.3 %collective-permute-start.7 = (bf16[1,256,256]{2,1,0:T(8,128)(2,1)S(1)}, bf16[1,256,256]{2,1,0:T(8,128)(2,1)S(1)}, u32[]{:S(2)}, u32[]{:S(2)}) collective-permute-start(bf16[1,256,256]{2,1,0:T(8,128)(2,1)S(1)} %slice.161), channel_id=1, source_target_pairs={{0,7},{1,0},{2,1},{3,2},{4,3},{5,4},{6,5},{7,6},{8,15},{9,8},{10,9... | collective-permute-start | bytes 393224 | tf_op jit(solution)/shard_map/while/body/eval_jaxpr/ppermute | solution.py:33
  94.4 6.3 %collective-permute-start.8 = (bf16[1,256,256]{2,1,0:T(8,128)(2,1)S(1)}, bf16[1,256,256]{2,1,0:T(8,128)(2,1)S(1)}, u32[]{:S(2)}, u32[]{:S(2)}) collective-permute-start(bf16[1,256,256]{2,1,0:T(8,128)(2,1)S(1)} %slice.162), channel_id=1, source_target_pairs={{0,1},{1,2},{2,3},{3,4},{4,5},{5,6},{6,7},{7,0},{8,9},{9,10},{10,1... | collective-permute-start | bytes 393224 | tf_op jit(solution)/shard_map/while/body/eval_jaxpr/ppermute | solution.py:32
  101.2 6.6 %collective-permute-start = (bf16[256,256]{1,0:T(8,128)(2,1)S(1)}, bf16[256,256]{1,0:T(8,128)(2,1)S(1)}, u32[]{:S(2)}, u32[]{:S(2)}) collective-permute-start(bf16[256,256]{1,0:T(8,128)(2,1)S(1)} %copy.12), channel_id=1, source_target_pairs={{0,8},{8,0},{1,9},{9,1},{2,10},{10,2},{3,11},{11,3},{4,12},{12,4},... | collective-permute-start | bytes 393224 | tf_op jit(solution)/shard_map/while/body/eval_jaxpr/ppermute | solution.py:29
  107.9 7.7 %collective-permute-start.4 = (bf16[2,256,256]{2,1,0:T(8,128)(2,1)S(1)}, bf16[2,256,256]{2,1,0:T(8,128)(2,1)S(1)}, u32[]{:S(2)}, u32[]{:S(2)}) collective-permute-start(bf16[2,256,256]{2,1,0:T(8,128)(2,1)S(1)} %fusion.117), channel_id=1, source_target_pairs={{0,7},{1,0},{2,1},{3,2},{4,3},{5,4},{6,5},{7,6},{8,15},{9,8},{10,9... | collective-permute-start | bytes 786440 | tf_op jit(solution)/shard_map/while/body/eval_jaxpr/ppermute | solution.py:24
  108.0 10.1 %collective-permute-start.1 = (bf16[2,256,256]{2,1,0:T(8,128)(2,1)S(1)}, bf16[2,256,256]{2,1,0:T(8,128)(2,1)S(1)}, u32[]{:S(2)}, u32[]{:S(2)}) collective-permute-start(bf16[2,256,256]{2,1,0:T(8,128)(2,1)S(1)} %fusion.117), channel_id=1, source_target_pairs={{0,1},{1,2},{2,3},{3,4},{4,5},{5,6},{6,7},{7,0},{8,9},{9,10},{10,1... | collective-permute-start | bytes 786440 | tf_op jit(solution)/shard_map/while/body/eval_jaxpr/ppermute | solution.py:23
  115.6 7.9 %collective-permute-start.5 = (bf16[2,256,256]{2,1,0:T(8,128)(2,1)S(1)}, bf16[2,256,256]{2,1,0:T(8,128)(2,1)S(1)}, u32[]{:S(2)}, u32[]{:S(2)}) collective-permute-start(bf16[2,256,256]{2,1,0:T(8,128)(2,1)S(1)} %collective-permute-done.4), channel_id=1, source_target_pairs={{0,7},{1,0},{2,1},{3,2},{4,3},{5,4},{6,5},{7,6},{8,15},{9,8},{10,9... | collective-permute-start | bytes 786440 | tf_op jit(solution)/shard_map/while/body/eval_jaxpr/ppermute | solution.py:24
  118.0 9.2 %collective-permute-start.2 = (bf16[2,256,256]{2,1,0:T(8,128)(2,1)S(1)}, bf16[2,256,256]{2,1,0:T(8,128)(2,1)S(1)}, u32[]{:S(2)}, u32[]{:S(2)}) collective-permute-start(bf16[2,256,256]{2,1,0:T(8,128)(2,1)S(1)} %collective-permute-done.1), channel_id=1, source_target_pairs={{0,1},{1,2},{2,3},{3,4},{4,5},{5,6},{6,7},{7,0},{8,9},{9,10},{10,1... | collective-permute-start | bytes 786440 | tf_op jit(solution)/shard_map/while/body/eval_jaxpr/ppermute | solution.py:23
  123.6 7.6 %collective-permute-start.6 = (bf16[2,256,256]{2,1,0:T(8,128)(2,1)S(1)}, bf16[2,256,256]{2,1,0:T(8,128)(2,1)S(1)}, u32[]{:S(2)}, u32[]{:S(2)}) collective-permute-start(bf16[2,256,256]{2,1,0:T(8,128)(2,1)S(1)} %collective-permute-done.5), channel_id=1, source_target_pairs={{0,7},{1,0},{2,1},{3,2},{4,3},{5,4},{6,5},{7,6},{8,15},{9,8},{10,9... | collective-permute-start | bytes 786440 | tf_op jit(solution)/shard_map/while/body/eval_jaxpr/ppermute | solution.py:24
  127.2 7.7 %collective-permute-start.3 = (bf16[2,256,256]{2,1,0:T(8,128)(2,1)S(1)}, bf16[2,256,256]{2,1,0:T(8,128)(2,1)S(1)}, u32[]{:S(2)}, u32[]{:S(2)}) collective-permute-start(bf16[2,256,256]{2,1,0:T(8,128)(2,1)S(1)} %collective-permute-done.2), channel_id=1, source_target_pairs={{0,1},{1,2},{2,3},{3,4},{4,5},{5,6},{6,7},{7,0},{8,9},{9,10},{10,1... | collective-permute-start | bytes 786440 | tf_op jit(solution)/shard_map/while/body/eval_jaxpr/ppermute | solution.py:23
  131.1 6.3 %collective-permute-start.7 = (bf16[1,256,256]{2,1,0:T(8,128)(2,1)S(1)}, bf16[1,256,256]{2,1,0:T(8,128)(2,1)S(1)}, u32[]{:S(2)}, u32[]{:S(2)}) collective-permute-start(bf16[1,256,256]{2,1,0:T(8,128)(2,1)S(1)} %slice.161), channel_id=1, source_target_pairs={{0,7},{1,0},{2,1},{3,2},{4,3},{5,4},{6,5},{7,6},{8,15},{9,8},{10,9... | collective-permute-start | bytes 393224 | tf_op jit(solution)/shard_map/while/body/eval_jaxpr/ppermute | solution.py:33
  134.9 6.3 %collective-permute-start.8 = (bf16[1,256,256]{2,1,0:T(8,128)(2,1)S(1)}, bf16[1,256,256]{2,1,0:T(8,128)(2,1)S(1)}, u32[]{:S(2)}, u32[]{:S(2)}) collective-permute-start(bf16[1,256,256]{2,1,0:T(8,128)(2,1)S(1)} %slice.162), channel_id=1, source_target_pairs={{0,1},{1,2},{2,3},{3,4},{4,5},{5,6},{6,7},{7,0},{8,9},{9,10},{10,1... | collective-permute-start | bytes 393224 | tf_op jit(solution)/shard_map/while/body/eval_jaxpr/ppermute | solution.py:32
  (2 other events, 1.6 us)
Sparse Core Ops, SparseCore 0:
  9.3 40.5 all-gather.1

commit v14 on v13

--- a/solution.py
+++ b/solution.py
@@ -106,13 +106,14 @@
     target = (offset * y_count + owner // z_count) * per_col + ring_neighbours % per_col
     dest = jnp.where(ring_live, target, -1)
     dense = place_tiles(dest, tiles, total_blocks)
-    dense = dense[: total_blocks * block_size].reshape(z_count, y_count, local_width, local_width)
+    chunk_rows = y_count * local_width
 
     def apply_hamiltonian(field):
         blocks = gather_col(field, y_count, z_count)
         total = None
         for d, chunk in enumerate(blocks):
-            part = jnp.einsum("ymj,yjo->mo", chunk, dense[d], preferred_element_type=jnp.float32)
+            operator = lax.slice_in_dim(dense, d * chunk_rows, (d + 1) * chunk_rows).reshape(y_count, local_width, -1)
+            part = jnp.einsum("ymj,yjo->mo", chunk, operator, preferred_element_type=jnp.float32)
             total = part if total is None else total + part
         return total
 

time: 149 us -> 149 us (level)
  waiting for transfers between devices: 64.7 us -> 56 us
  matrix products: 6.6 us -> 12.6 us
  local copies, waits for them, and re-layouts: 5.67 us -> 7.92 us
    ppermute x9, waiting for transfers between devices: 25.9 us -> 18.6 us  [ring_blocks(): left = lax.ppermute(left, axis, bwd)]
    dot_general x24, matrix products: 6.6 us -> 12.6 us  [apply_hamiltonian(): jnp.einsum('ymj,yjo->mo', chunk, operator, preferred_element_type=jnp.flo...]
    unnamed x12 -> x32, local copies, waits for them, and re-layouts: 3.28 us -> 4.09 us
  transfers between devices with their start and end apart: 28 -> 28, of which waited for: 17 -> 17; matrix products, arithmetic and copies ran while one was open for 6% -> 11% of each run, Pallas kernels for 3% -> 2%
where the time goes in v14:
time: 149 us; the launch traced here: 148 us
  waiting for transfers between devices  56 us (38%)
  starting transfers between devices  52.5 us (35%)
  between operations  13.7 us (9%)
  matrix products  12.6 us (8%)
  local copies, waits for them, and re-layouts  7.92 us (5%)
  Pallas kernels  3.1 us (2%)
  other arithmetic  2.18 us (1%)
    ppermute x9, starting transfers between devices, ring_blocks(): left = lax.ppermute(left, axis, bwd)  28.4 us
    ppermute x9, waiting for transfers between devices, ring_blocks(): left = lax.ppermute(left, axis, bwd)  18.6 us
    dot_general x24, matrix products, apply_hamiltonian(): jnp.einsum('ymj,yjo->mo', chunk, operator, preferred_element_type=jnp.flo...  12.6 us
    ppermute x3, waiting for transfers between devices, ring_blocks(): blocks[1] = lax.ppermute(piece, axis, fwd)  11.6 us
    ppermute x9, waiting for transfers between devices, ring_blocks(): right = lax.ppermute(right, axis, fwd)  11.1 us
    ppermute x3, starting transfers between devices, ring_blocks(): lax.ppermute(lax.slice_in_dim(left, split, None, axis=split_dim), axis, bwd)  10.7 us
    ppermute x3, starting transfers between devices, ring_blocks(): blocks[1] = lax.ppermute(piece, axis, fwd)  9.02 us
    ppermute x3, waiting for transfers between devices, ring_blocks(): lax.ppermute(lax.slice_in_dim(right, 0, split, axis=split_dim), axis, fwd)  7.5 us
  transfers between devices with their start and end apart: 28, of which 17 were waited for; matrix products, arithmetic and copies ran while one was open for 11% of the time, Pallas kernels for 2%

profile of v14, /device:TPU:2, one launch (start us, length us, event | category | flops | bytes accessed | tf_op | source)
XLA Modules:
  0.0 148.2 jit_solution(11184764997983932935)
XLA Ops:
  9.2 3.3 %collective-permute-start.9 = (bf16[256,256]{1,0:T(8,128)(2,1)S(1)}, bf16[256,256]{1,0:T(8,128)(2,1)S(1)}, u32[]{:S(2)}, u32[]{:S(2)}) collective-permute-start(bf16[256,256]{1,0:T(8,128)(2,1)S(1)} %copy.17), channel_id=1, source_target_pairs={{0,8},{8,0},{1,9},{9,1},{2,10},{10,2},{3,11},{11,3},{4,12},{12,4},... | collective-permute-start | bytes 393224 | tf_op jit(solution)/shard_map/ppermute | solution.py:29
  12.5 3.5 %collective-permute-done.9 = bf16[256,256]{1,0:T(8,128)(2,1)S(1)} collective-permute-done((bf16[256,256]{1,0:T(8,128)(2,1)S(1)}, bf16[256,256]{1,0:T(8,128)(2,1)S(1)}, u32[]{:S(2)}, u32[]{:S(2)}) %collective-permute-start.9) | collective-permute-done | bytes 131104 | tf_op jit(solution)/shard_map/ppermute | solution.py:29
  18.2 4.6 %collective-permute-start.10 = (bf16[2,256,256]{2,1,0:T(8,128)(2,1)S(1)}, bf16[2,256,256]{2,1,0:T(8,128)(2,1)S(1)}, u32[]{:S(2)}, u32[]{:S(2)}) collective-permute-start(bf16[2,256,256]{2,1,0:T(8,128)(2,1)S(1)} %fusion.26), channel_id=1, source_target_pairs={{0,7},{1,0},{2,1},{3,2},{4,3},{5,4},{6,5},{7,6},{8,15},{9,8},{10,9... | collective-permute-start | bytes 786440 | tf_op jit(solution)/shard_map/ppermute | solution.py:24
  22.8 4.8 %collective-permute-done.13 = bf16[2,256,256]{2,1,0:T(8,128)(2,1)S(1)} collective-permute-done((bf16[2,256,256]{2,1,0:T(8,128)(2,1)S(1)}, bf16[2,256,256]{2,1,0:T(8,128)(2,1)S(1)}, u32[]{:S(2)}, u32[]{:S(2)}) %collective-permute-start.13) | collective-permute-done | bytes 262176 | tf_op jit(solution)/shard_map/ppermute | solution.py:23
  27.6 3.6 %collective-permute-start.11 = (bf16[2,256,256]{2,1,0:T(8,128)(2,1)S(1)}, bf16[2,256,256]{2,1,0:T(8,128)(2,1)S(1)}, u32[]{:S(2)}, u32[]{:S(2)}) collective-permute-start(bf16[2,256,256]{2,1,0:T(8,128)(2,1)S(1)} %collective-permute-done.10), channel_id=1, source_target_pairs={{0,7},{1,0},{2,1},{3,2},{4,3},{5,4},{6,5},{7,6},{8,15},{9,8},{10,9... | collective-permute-start | bytes 786440 | tf_op jit(solution)/shard_map/ppermute | solution.py:24
  31.2 4.2 %collective-permute-done.14 = bf16[2,256,256]{2,1,0:T(8,128)(2,1)S(1)} collective-permute-done((bf16[2,256,256]{2,1,0:T(8,128)(2,1)S(1)}, bf16[2,256,256]{2,1,0:T(8,128)(2,1)S(1)}, u32[]{:S(2)}, u32[]{:S(2)}) %collective-permute-start.14) | collective-permute-done | bytes 262176 | tf_op jit(solution)/shard_map/ppermute | solution.py:23
  35.5 3.3 %collective-permute-start.12 = (bf16[2,256,256]{2,1,0:T(8,128)(2,1)S(1)}, bf16[2,256,256]{2,1,0:T(8,128)(2,1)S(1)}, u32[]{:S(2)}, u32[]{:S(2)}) collective-permute-start(bf16[2,256,256]{2,1,0:T(8,128)(2,1)S(1)} %collective-permute-done.11), channel_id=1, source_target_pairs={{0,7},{1,0},{2,1},{3,2},{4,3},{5,4},{6,5},{7,6},{8,15},{9,8},{10,9... | collective-permute-start | bytes 786440 | tf_op jit(solution)/shard_map/ppermute | solution.py:24
  43.9 3.2 %collective-permute-start.17 = (bf16[1,256,256]{2,1,0:T(8,128)(2,1)}, bf16[1,256,256]{2,1,0:T(8,128)(2,1)}, u32[]{:S(2)}, u32[]{:S(2)}) collective-permute-start(bf16[1,256,256]{2,1,0:T(8,128)(2,1)} %slice.77), channel_id=1, source_target_pairs={{0,7},{1,0},{2,1},{3,2},{4,3},{5,4},{6,5},{7,6},{8,15},{9,8},{10,9... | collective-permute-start | bytes 393224 | tf_op jit(solution)/shard_map/ppermute | solution.py:33
  47.1 2.9 %all-gather.2.cloned.1.call-done = bf16[4,48,64,64]{3,2,1,0:T(8,128)(2,1)} async-done(((bf16[4,3,64,64]{3,2,1,0:T(8,128)(2,1)}), bf16[4,48,64,64]{3,2,1,0:T(8,128)(2,1)}) %all-gather.2.cloned.1.call-update) | async-done | bytes 1572880 | tf_op jit(solution)/shard_map/all_gather | solution.py:100
  50.0 3.1 %shard_map.46 = bf16[4160,256]{1,0:T(8,128)(2,1)S(1)} custom-call(s32[192]{0:T(256)} %reshape.72.dest_ref, bf16[1,4,48,64,64]{4,3,2,1,0:T(8,128)(2,1)} %bitcast.197), custom_call_target="tpu_custom_call" | custom-call | tf_op jit(solution)/shard_map/pallas_call | solution.py:77
  57.0 83.7 %while.12 = (s32[]{:T(128)}, bf16[256,256]{1,0:T(8,128)(2,1)S(1)}, bf16[256,256]{1,0:T(8,128)(2,1)S(1)}, bf16[4160,256]{1,0:T(8,128)(2,1)S(1)}, s32[]{:T(128)}, ...) while((s32[]{:T(128)}, bf16[256,256]{1,0:T(8,128)(2,1)S(1)}, ...), condition=%wide.region_2.4_spmd, body=%wide.region_1.3_spmd.sunk | while | flops 538116096 | bytes 23855812 | solution.py:129
  57.0 2.9 %collective-permute-start = (bf16[256,256]{1,0:T(8,128)(2,1)S(1)}, bf16[256,256]{1,0:T(8,128)(2,1)S(1)}, u32[]{:S(2)}, u32[]{:S(2)}) collective-permute-start(bf16[256,256]{1,0:T(8,128)(2,1)S(1)} %copy.12), channel_id=1, source_target_pairs={{0,8},{8,0},{1,9},{9,1},{2,10},{10,2},{3,11},{11,3},{4,12},{12,4},... | collective-permute-start | bytes 393224 | tf_op jit(solution)/shard_map/while/body/eval_jaxpr/ppermute | solution.py:29
  59.9 4.3 %collective-permute-done = bf16[256,256]{1,0:T(8,128)(2,1)S(1)} collective-permute-done((bf16[256,256]{1,0:T(8,128)(2,1)S(1)}, bf16[256,256]{1,0:T(8,128)(2,1)S(1)}, u32[]{:S(2)}, u32[]{:S(2)}) %collective-permute-start) | collective-permute-done | bytes 131104 | tf_op jit(solution)/shard_map/while/body/eval_jaxpr/ppermute | solution.py:29
  64.4 3.4 %collective-permute-start.4 = (bf16[2,256,256]{2,1,0:T(8,128)(2,1)S(1)}, bf16[2,256,256]{2,1,0:T(8,128)(2,1)}, u32[]{:S(2)}, u32[]{:S(2)}) collective-permute-start(bf16[2,256,256]{2,1,0:T(8,128)(2,1)S(1)} %fusion.111), channel_id=1, source_target_pairs={{0,7},{1,0},{2,1},{3,2},{4,3},{5,4},{6,5},{7,6},{8,15},{9,8},{10,9... | collective-permute-start | bytes 786440 | tf_op jit(solution)/shard_map/while/body/eval_jaxpr/ppermute | solution.py:24
  70.2 2.8 %collective-permute-done.4 = bf16[2,256,256]{2,1,0:T(8,128)(2,1)} collective-permute-done((bf16[2,256,256]{2,1,0:T(8,128)(2,1)S(1)}, bf16[2,256,256]{2,1,0:T(8,128)(2,1)}, u32[]{:S(2)}, u32[]{:S(2)}) %collective-permute-start.4) | collective-permute-done | bytes 262176 | tf_op jit(solution)/shard_map/while/body/eval_jaxpr/ppermute | solution.py:24
  73.0 3.8 %collective-permute-start.5 = (bf16[2,256,256]{2,1,0:T(8,128)(2,1)}, bf16[2,256,256]{2,1,0:T(8,128)(2,1)S(1)}, u32[]{:S(2)}, u32[]{:S(2)}) collective-permute-start(bf16[2,256,256]{2,1,0:T(8,128)(2,1)} %collective-permute-done.4), channel_id=1, source_target_pairs={{0,7},{1,0},{2,1},{3,2},{4,3},{5,4},{6,5},{7,6},{8,15},{9,8},{10,9... | collective-permute-start | bytes 786440 | tf_op jit(solution)/shard_map/while/body/eval_jaxpr/ppermute | solution.py:24
  81.3 3.6 %collective-permute-start.6 = (bf16[2,256,256]{2,1,0:T(8,128)(2,1)S(1)}, bf16[2,256,256]{2,1,0:T(8,128)(2,1)S(1)}, u32[]{:S(2)}, u32[]{:S(2)}) collective-permute-start(bf16[2,256,256]{2,1,0:T(8,128)(2,1)S(1)} %collective-permute-done.5), channel_id=1, source_target_pairs={{0,7},{1,0},{2,1},{3,2},{4,3},{5,4},{6,5},{7,6},{8,15},{9,8},{10,9... | collective-permute-start | bytes 786440 | tf_op jit(solution)/shard_map/while/body/eval_jaxpr/ppermute | solution.py:24
  85.4 3.4 %collective-permute-done.6 = bf16[2,256,256]{2,1,0:T(8,128)(2,1)S(1)} collective-permute-done((bf16[2,256,256]{2,1,0:T(8,128)(2,1)S(1)}, bf16[2,256,256]{2,1,0:T(8,128)(2,1)S(1)}, u32[]{:S(2)}, u32[]{:S(2)}) %collective-permute-start.6) | collective-permute-done | bytes 262176 | tf_op jit(solution)/shard_map/while/body/eval_jaxpr/ppermute | solution.py:24
  88.8 3.8 %collective-permute-start.7 = (bf16[1,256,256]{2,1,0:T(8,128)(2,1)S(1)}, bf16[1,256,256]{2,1,0:T(8,128)(2,1)S(1)}, u32[]{:S(2)}, u32[]{:S(2)}) collective-permute-start(bf16[1,256,256]{2,1,0:T(8,128)(2,1)S(1)} %slice.116), channel_id=1, source_target_pairs={{0,7},{1,0},{2,1},{3,2},{4,3},{5,4},{6,5},{7,6},{8,15},{9,8},{10,9... | collective-permute-start | bytes 393224 | tf_op jit(solution)/shard_map/while/body/eval_jaxpr/ppermute | solution.py:33
  92.9 2.2 %collective-permute-done.7 = bf16[1,256,256]{2,1,0:T(8,128)(2,1)S(1)} collective-permute-done((bf16[1,256,256]{2,1,0:T(8,128)(2,1)S(1)}, bf16[1,256,256]{2,1,0:T(8,128)(2,1)S(1)}, u32[]{:S(2)}, u32[]{:S(2)}) %collective-permute-start.7) | collective-permute-done | bytes 131104 | tf_op jit(solution)/shard_map/while/body/eval_jaxpr/ppermute | solution.py:33
  95.1 3.8 %collective-permute-done.8 = bf16[1,256,256]{2,1,0:T(8,128)(2,1)S(1)} collective-permute-done((bf16[1,256,256]{2,1,0:T(8,128)(2,1)S(1)}, bf16[1,256,256]{2,1,0:T(8,128)(2,1)S(1)}, u32[]{:S(2)}, u32[]{:S(2)}) %collective-permute-start.8) | collective-permute-done | bytes 131104 | tf_op jit(solution)/shard_map/while/body/eval_jaxpr/ppermute | solution.py:32
  99.4 2.9 %collective-permute-start = (bf16[256,256]{1,0:T(8,128)(2,1)S(1)}, bf16[256,256]{1,0:T(8,128)(2,1)S(1)}, u32[]{:S(2)}, u32[]{:S(2)}) collective-permute-start(bf16[256,256]{1,0:T(8,128)(2,1)S(1)} %copy.12), channel_id=1, source_target_pairs={{0,8},{8,0},{1,9},{9,1},{2,10},{10,2},{3,11},{11,3},{4,12},{12,4},... | collective-permute-start | bytes 393224 | tf_op jit(solution)/shard_map/while/body/eval_jaxpr/ppermute | solution.py:29
  102.3 3.7 %collective-permute-done = bf16[256,256]{1,0:T(8,128)(2,1)S(1)} collective-permute-done((bf16[256,256]{1,0:T(8,128)(2,1)S(1)}, bf16[256,256]{1,0:T(8,128)(2,1)S(1)}, u32[]{:S(2)}, u32[]{:S(2)}) %collective-permute-start) | collective-permute-done | bytes 131104 | tf_op jit(solution)/shard_map/while/body/eval_jaxpr/ppermute | solution.py:29
  106.2 2.0 %collective-permute-start.1 = (bf16[2,256,256]{2,1,0:T(8,128)(2,1)S(1)}, bf16[2,256,256]{2,1,0:T(8,128)(2,1)}, u32[]{:S(2)}, u32[]{:S(2)}) collective-permute-start(bf16[2,256,256]{2,1,0:T(8,128)(2,1)S(1)} %fusion.111), channel_id=1, source_target_pairs={{0,1},{1,2},{2,3},{3,4},{4,5},{5,6},{6,7},{7,0},{8,9},{9,10},{10,1... | collective-permute-start | bytes 786440 | tf_op jit(solution)/shard_map/while/body/eval_jaxpr/ppermute | solution.py:23
  110.6 3.6 %collective-permute-done.4 = bf16[2,256,256]{2,1,0:T(8,128)(2,1)} collective-permute-done((bf16[2,256,256]{2,1,0:T(8,128)(2,1)S(1)}, bf16[2,256,256]{2,1,0:T(8,128)(2,1)}, u32[]{:S(2)}, u32[]{:S(2)}) %collective-permute-start.4) | collective-permute-done | bytes 262176 | tf_op jit(solution)/shard_map/while/body/eval_jaxpr/ppermute | solution.py:24
  114.2 2.5 %collective-permute-start.5 = (bf16[2,256,256]{2,1,0:T(8,128)(2,1)}, bf16[2,256,256]{2,1,0:T(8,128)(2,1)S(1)}, u32[]{:S(2)}, u32[]{:S(2)}) collective-permute-start(bf16[2,256,256]{2,1,0:T(8,128)(2,1)} %collective-permute-done.4), channel_id=1, source_target_pairs={{0,7},{1,0},{2,1},{3,2},{4,3},{5,4},{6,5},{7,6},{8,15},{9,8},{10,9... | collective-permute-start | bytes 786440 | tf_op jit(solution)/shard_map/while/body/eval_jaxpr/ppermute | solution.py:24
  119.3 3.4 %collective-permute-done.5 = bf16[2,256,256]{2,1,0:T(8,128)(2,1)S(1)} collective-permute-done((bf16[2,256,256]{2,1,0:T(8,128)(2,1)}, bf16[2,256,256]{2,1,0:T(8,128)(2,1)S(1)}, u32[]{:S(2)}, u32[]{:S(2)}) %collective-permute-start.5) | collective-permute-done | bytes 262176 | tf_op jit(solution)/shard_map/while/body/eval_jaxpr/ppermute | solution.py:24
  122.6 3.6 %collective-permute-start.6 = (bf16[2,256,256]{2,1,0:T(8,128)(2,1)S(1)}, bf16[2,256,256]{2,1,0:T(8,128)(2,1)S(1)}, u32[]{:S(2)}, u32[]{:S(2)}) collective-permute-start(bf16[2,256,256]{2,1,0:T(8,128)(2,1)S(1)} %collective-permute-done.5), channel_id=1, source_target_pairs={{0,7},{1,0},{2,1},{3,2},{4,3},{5,4},{6,5},{7,6},{8,15},{9,8},{10,9... | collective-permute-start | bytes 786440 | tf_op jit(solution)/shard_map/while/body/eval_jaxpr/ppermute | solution.py:24
  126.7 3.4 %collective-permute-done.6 = bf16[2,256,256]{2,1,0:T(8,128)(2,1)S(1)} collective-permute-done((bf16[2,256,256]{2,1,0:T(8,128)(2,1)S(1)}, bf16[2,256,256]{2,1,0:T(8,128)(2,1)S(1)}, u32[]{:S(2)}, u32[]{:S(2)}) %collective-permute-start.6) | collective-permute-done | bytes 262176 | tf_op jit(solution)/shard_map/while/body/eval_jaxpr/ppermute | solution.py:24
  130.1 3.8 %collective-permute-start.7 = (bf16[1,256,256]{2,1,0:T(8,128)(2,1)S(1)}, bf16[1,256,256]{2,1,0:T(8,128)(2,1)S(1)}, u32[]{:S(2)}, u32[]{:S(2)}) collective-permute-start(bf16[1,256,256]{2,1,0:T(8,128)(2,1)S(1)} %slice.116), channel_id=1, source_target_pairs={{0,7},{1,0},{2,1},{3,2},{4,3},{5,4},{6,5},{7,6},{8,15},{9,8},{10,9... | collective-permute-start | bytes 393224 | tf_op jit(solution)/shard_map/while/body/eval_jaxpr/ppermute | solution.py:33
  134.2 2.2 %collective-permute-done.7 = bf16[1,256,256]{2,1,0:T(8,128)(2,1)S(1)} collective-permute-done((bf16[1,256,256]{2,1,0:T(8,128)(2,1)S(1)}, bf16[1,256,256]{2,1,0:T(8,128)(2,1)S(1)}, u32[]{:S(2)}, u32[]{:S(2)}) %collective-permute-start.7) | collective-permute-done | bytes 131104 | tf_op jit(solution)/shard_map/while/body/eval_jaxpr/ppermute | solution.py:33
  136.4 3.8 %collective-permute-done.8 = bf16[1,256,256]{2,1,0:T(8,128)(2,1)S(1)} collective-permute-done((bf16[1,256,256]{2,1,0:T(8,128)(2,1)S(1)}, bf16[1,256,256]{2,1,0:T(8,128)(2,1)S(1)}, u32[]{:S(2)}, u32[]{:S(2)}) %collective-permute-start.8) | collective-permute-done | bytes 131104 | tf_op jit(solution)/shard_map/while/body/eval_jaxpr/ppermute | solution.py:32
  (111 shorter events, 29.1 us)
Async XLA Ops:
  6.5 43.4 %all-gather.2.cloned.1.call-start = ((), (), s32[]{:S(2)}) async-start(), calls=%async_computation | async-start | bytes 3342336 | tf_op jit(solution)/shard_map/all_gather | solution.py:100
  9.2 6.8 %collective-permute-start.9 = (bf16[256,256]{1,0:T(8,128)(2,1)S(1)}, bf16[256,256]{1,0:T(8,128)(2,1)S(1)}, u32[]{:S(2)}, u32[]{:S(2)}) collective-permute-start(bf16[256,256]{1,0:T(8,128)(2,1)S(1)} %copy.17), channel_id=1, source_target_pairs={{0,8},{8,0},{1,9},{9,1},{2,10},{10,2},{3,11},{11,3},{4,12},{12,4},... | collective-permute-start | bytes 393224 | tf_op jit(solution)/shard_map/ppermute | solution.py:29
  16.2 11.4 %collective-permute-start.13 = (bf16[2,256,256]{2,1,0:T(8,128)(2,1)S(1)}, bf16[2,256,256]{2,1,0:T(8,128)(2,1)S(1)}, u32[]{:S(2)}, u32[]{:S(2)}) collective-permute-start(bf16[2,256,256]{2,1,0:T(8,128)(2,1)S(1)} %fusion.26), channel_id=1, source_target_pairs={{0,1},{1,2},{2,3},{3,4},{4,5},{5,6},{6,7},{7,0},{8,9},{9,10},{10,1... | collective-permute-start | bytes 786440 | tf_op jit(solution)/shard_map/ppermute | solution.py:23
  18.2 9.4 %collective-permute-start.10 = (bf16[2,256,256]{2,1,0:T(8,128)(2,1)S(1)}, bf16[2,256,256]{2,1,0:T(8,128)(2,1)S(1)}, u32[]{:S(2)}, u32[]{:S(2)}) collective-permute-start(bf16[2,256,256]{2,1,0:T(8,128)(2,1)S(1)} %fusion.26), channel_id=1, source_target_pairs={{0,7},{1,0},{2,1},{3,2},{4,3},{5,4},{6,5},{7,6},{8,15},{9,8},{10,9... | collective-permute-start | bytes 786440 | tf_op jit(solution)/shard_map/ppermute | solution.py:24
  27.6 7.8 %collective-permute-start.14 = (bf16[2,256,256]{2,1,0:T(8,128)(2,1)S(1)}, bf16[2,256,256]{2,1,0:T(8,128)(2,1)S(1)}, u32[]{:S(2)}, u32[]{:S(2)}) collective-permute-start(bf16[2,256,256]{2,1,0:T(8,128)(2,1)S(1)} %collective-permute-done.13), channel_id=1, source_target_pairs={{0,1},{1,2},{2,3},{3,4},{4,5},{5,6},{6,7},{7,0},{8,9},{9,10},{10,1... | collective-permute-start | bytes 786440 | tf_op jit(solution)/shard_map/ppermute | solution.py:23
  27.6 22.3 %copy-start.13 = (bf16[2,256,256]{2,1,0:T(8,128)(2,1)}, bf16[2,256,256]{2,1,0:T(8,128)(2,1)S(1)}, u32[]{:S(2)}) copy-start(bf16[2,256,256]{2,1,0:T(8,128)(2,1)S(1)} %collective-permute-done.10) | copy-start | bytes 786436
  27.6 7.8 %collective-permute-start.11 = (bf16[2,256,256]{2,1,0:T(8,128)(2,1)S(1)}, bf16[2,256,256]{2,1,0:T(8,128)(2,1)S(1)}, u32[]{:S(2)}, u32[]{:S(2)}) collective-permute-start(bf16[2,256,256]{2,1,0:T(8,128)(2,1)S(1)} %collective-permute-done.10), channel_id=1, source_target_pairs={{0,7},{1,0},{2,1},{3,2},{4,3},{5,4},{6,5},{7,6},{8,15},{9,8},{10,9... | collective-permute-start | bytes 786440 | tf_op jit(solution)/shard_map/ppermute | solution.py:24
  35.5 7.6 %collective-permute-start.15 = (bf16[2,256,256]{2,1,0:T(8,128)(2,1)S(1)}, bf16[2,256,256]{2,1,0:T(8,128)(2,1)S(1)}, u32[]{:S(2)}, u32[]{:S(2)}) collective-permute-start(bf16[2,256,256]{2,1,0:T(8,128)(2,1)S(1)} %collective-permute-done.14), channel_id=1, source_target_pairs={{0,1},{1,2},{2,3},{3,4},{4,5},{5,6},{6,7},{7,0},{8,9},{9,10},{10,1... | collective-permute-start | bytes 786440 | tf_op jit(solution)/shard_map/ppermute | solution.py:23
  35.5 7.7 %collective-permute-start.12 = (bf16[2,256,256]{2,1,0:T(8,128)(2,1)S(1)}, bf16[2,256,256]{2,1,0:T(8,128)(2,1)S(1)}, u32[]{:S(2)}, u32[]{:S(2)}) collective-permute-start(bf16[2,256,256]{2,1,0:T(8,128)(2,1)S(1)} %collective-permute-done.11), channel_id=1, source_target_pairs={{0,7},{1,0},{2,1},{3,2},{4,3},{5,4},{6,5},{7,6},{8,15},{9,8},{10,9... | collective-permute-start | bytes 786440 | tf_op jit(solution)/shard_map/ppermute | solution.py:24
  43.1 12.4 %collective-permute-start.16 = (bf16[1,256,256]{2,1,0:T(8,128)(2,1)S(1)}, bf16[1,256,256]{2,1,0:T(8,128)(2,1)}, u32[]{:S(2)}, u32[]{:S(2)}) collective-permute-start(bf16[1,256,256]{2,1,0:T(8,128)(2,1)S(1)} %slice.76), channel_id=1, source_target_pairs={{0,1},{1,2},{2,3},{3,4},{4,5},{5,6},{6,7},{7,0},{8,9},{9,10},{10,1... | collective-permute-start | bytes 393224 | tf_op jit(solution)/shard_map/ppermute | solution.py:32
  43.9 11.6 %collective-permute-start.17 = (bf16[1,256,256]{2,1,0:T(8,128)(2,1)}, bf16[1,256,256]{2,1,0:T(8,128)(2,1)}, u32[]{:S(2)}, u32[]{:S(2)}) collective-permute-start(bf16[1,256,256]{2,1,0:T(8,128)(2,1)} %slice.77), channel_id=1, source_target_pairs={{0,7},{1,0},{2,1},{3,2},{4,3},{5,4},{6,5},{7,6},{8,15},{9,8},{10,9... | collective-permute-start | bytes 393224 | tf_op jit(solution)/shard_map/ppermute | solution.py:33
  57.0 7.2 %collective-permute-start = (bf16[256,256]{1,0:T(8,128)(2,1)S(1)}, bf16[256,256]{1,0:T(8,128)(2,1)S(1)}, u32[]{:S(2)}, u32[]{:S(2)}) collective-permute-start(bf16[256,256]{1,0:T(8,128)(2,1)S(1)} %copy.12), channel_id=1, source_target_pairs={{0,8},{8,0},{1,9},{9,1},{2,10},{10,2},{3,11},{11,3},{4,12},{12,4},... | collective-permute-start | bytes 393224 | tf_op jit(solution)/shard_map/while/body/eval_jaxpr/ppermute | solution.py:29
  64.4 8.5 %collective-permute-start.4 = (bf16[2,256,256]{2,1,0:T(8,128)(2,1)S(1)}, bf16[2,256,256]{2,1,0:T(8,128)(2,1)}, u32[]{:S(2)}, u32[]{:S(2)}) collective-permute-start(bf16[2,256,256]{2,1,0:T(8,128)(2,1)S(1)} %fusion.111), channel_id=1, source_target_pairs={{0,7},{1,0},{2,1},{3,2},{4,3},{5,4},{6,5},{7,6},{8,15},{9,8},{10,9... | collective-permute-start | bytes 786440 | tf_op jit(solution)/shard_map/while/body/eval_jaxpr/ppermute | solution.py:24
  67.9 8.9 %collective-permute-start.1 = (bf16[2,256,256]{2,1,0:T(8,128)(2,1)S(1)}, bf16[2,256,256]{2,1,0:T(8,128)(2,1)}, u32[]{:S(2)}, u32[]{:S(2)}) collective-permute-start(bf16[2,256,256]{2,1,0:T(8,128)(2,1)S(1)} %fusion.111), channel_id=1, source_target_pairs={{0,1},{1,2},{2,3},{3,4},{4,5},{5,6},{6,7},{7,0},{8,9},{9,10},{10,1... | collective-permute-start | bytes 786440 | tf_op jit(solution)/shard_map/while/body/eval_jaxpr/ppermute | solution.py:23
  73.0 8.4 %collective-permute-start.5 = (bf16[2,256,256]{2,1,0:T(8,128)(2,1)}, bf16[2,256,256]{2,1,0:T(8,128)(2,1)S(1)}, u32[]{:S(2)}, u32[]{:S(2)}) collective-permute-start(bf16[2,256,256]{2,1,0:T(8,128)(2,1)} %collective-permute-done.4), channel_id=1, source_target_pairs={{0,7},{1,0},{2,1},{3,2},{4,3},{5,4},{6,5},{7,6},{8,15},{9,8},{10,9... | collective-permute-start | bytes 786440 | tf_op jit(solution)/shard_map/while/body/eval_jaxpr/ppermute | solution.py:24
  76.8 8.1 %collective-permute-start.2 = (bf16[2,256,256]{2,1,0:T(8,128)(2,1)}, bf16[2,256,256]{2,1,0:T(8,128)(2,1)S(1)}, u32[]{:S(2)}, u32[]{:S(2)}) collective-permute-start(bf16[2,256,256]{2,1,0:T(8,128)(2,1)} %collective-permute-done.1), channel_id=1, source_target_pairs={{0,1},{1,2},{2,3},{3,4},{4,5},{5,6},{6,7},{7,0},{8,9},{9,10},{10,1... | collective-permute-start | bytes 786440 | tf_op jit(solution)/shard_map/while/body/eval_jaxpr/ppermute | solution.py:23
  79.3 19.8 %copy-start.1 = (bf16[512,256]{1,0:T(8,128)(2,1)S(1)}, bf16[512,256]{1,0:T(8,128)(2,1)}, u32[]{:S(2)}) copy-start(bf16[512,256]{1,0:T(8,128)(2,1)} %get-tuple-element.93) | copy-start | bytes 786436 | tf_op jit(solution)/shard_map/while
  81.3 7.5 %collective-permute-start.6 = (bf16[2,256,256]{2,1,0:T(8,128)(2,1)S(1)}, bf16[2,256,256]{2,1,0:T(8,128)(2,1)S(1)}, u32[]{:S(2)}, u32[]{:S(2)}) collective-permute-start(bf16[2,256,256]{2,1,0:T(8,128)(2,1)S(1)} %collective-permute-done.5), channel_id=1, source_target_pairs={{0,7},{1,0},{2,1},{3,2},{4,3},{5,4},{6,5},{7,6},{8,15},{9,8},{10,9... | collective-permute-start | bytes 786440 | tf_op jit(solution)/shard_map/while/body/eval_jaxpr/ppermute | solution.py:24
  84.9 7.7 %collective-permute-start.3 = (bf16[2,256,256]{2,1,0:T(8,128)(2,1)S(1)}, bf16[2,256,256]{2,1,0:T(8,128)(2,1)S(1)}, u32[]{:S(2)}, u32[]{:S(2)}) collective-permute-start(bf16[2,256,256]{2,1,0:T(8,128)(2,1)S(1)} %collective-permute-done.2), channel_id=1, source_target_pairs={{0,1},{1,2},{2,3},{3,4},{4,5},{5,6},{6,7},{7,0},{8,9},{9,10},{10,1... | collective-permute-start | bytes 786440 | tf_op jit(solution)/shard_map/while/body/eval_jaxpr/ppermute | solution.py:23
  88.8 6.3 %collective-permute-start.7 = (bf16[1,256,256]{2,1,0:T(8,128)(2,1)S(1)}, bf16[1,256,256]{2,1,0:T(8,128)(2,1)S(1)}, u32[]{:S(2)}, u32[]{:S(2)}) collective-permute-start(bf16[1,256,256]{2,1,0:T(8,128)(2,1)S(1)} %slice.116), channel_id=1, source_target_pairs={{0,7},{1,0},{2,1},{3,2},{4,3},{5,4},{6,5},{7,6},{8,15},{9,8},{10,9... | collective-permute-start | bytes 393224 | tf_op jit(solution)/shard_map/while/body/eval_jaxpr/ppermute | solution.py:33
  92.6 6.3 %collective-permute-start.8 = (bf16[1,256,256]{2,1,0:T(8,128)(2,1)S(1)}, bf16[1,256,256]{2,1,0:T(8,128)(2,1)S(1)}, u32[]{:S(2)}, u32[]{:S(2)}) collective-permute-start(bf16[1,256,256]{2,1,0:T(8,128)(2,1)S(1)} %slice.117), channel_id=1, source_target_pairs={{0,1},{1,2},{2,3},{3,4},{4,5},{5,6},{6,7},{7,0},{8,9},{9,10},{10,1... | collective-permute-start | bytes 393224 | tf_op jit(solution)/shard_map/while/body/eval_jaxpr/ppermute | solution.py:32
  99.4 6.6 %collective-permute-start = (bf16[256,256]{1,0:T(8,128)(2,1)S(1)}, bf16[256,256]{1,0:T(8,128)(2,1)S(1)}, u32[]{:S(2)}, u32[]{:S(2)}) collective-permute-start(bf16[256,256]{1,0:T(8,128)(2,1)S(1)} %copy.12), channel_id=1, source_target_pairs={{0,8},{8,0},{1,9},{9,1},{2,10},{10,2},{3,11},{11,3},{4,12},{12,4},... | collective-permute-start | bytes 393224 | tf_op jit(solution)/shard_map/while/body/eval_jaxpr/ppermute | solution.py:29
  106.1 8.0 %collective-permute-start.4 = (bf16[2,256,256]{2,1,0:T(8,128)(2,1)S(1)}, bf16[2,256,256]{2,1,0:T(8,128)(2,1)}, u32[]{:S(2)}, u32[]{:S(2)}) collective-permute-start(bf16[2,256,256]{2,1,0:T(8,128)(2,1)S(1)} %fusion.111), channel_id=1, source_target_pairs={{0,7},{1,0},{2,1},{3,2},{4,3},{5,4},{6,5},{7,6},{8,15},{9,8},{10,9... | collective-permute-start | bytes 786440 | tf_op jit(solution)/shard_map/while/body/eval_jaxpr/ppermute | solution.py:24
  106.2 10.5 %collective-permute-start.1 = (bf16[2,256,256]{2,1,0:T(8,128)(2,1)S(1)}, bf16[2,256,256]{2,1,0:T(8,128)(2,1)}, u32[]{:S(2)}, u32[]{:S(2)}) collective-permute-start(bf16[2,256,256]{2,1,0:T(8,128)(2,1)S(1)} %fusion.111), channel_id=1, source_target_pairs={{0,1},{1,2},{2,3},{3,4},{4,5},{5,6},{6,7},{7,0},{8,9},{9,10},{10,1... | collective-permute-start | bytes 786440 | tf_op jit(solution)/shard_map/while/body/eval_jaxpr/ppermute | solution.py:23
  109.3 17.1 %copy-start = (bf16[512,256]{1,0:T(8,128)(2,1)S(1)}, bf16[512,256]{1,0:T(8,128)(2,1)}, u32[]{:S(2)}) copy-start(bf16[512,256]{1,0:T(8,128)(2,1)} %get-tuple-element.92) | copy-start | bytes 786436 | tf_op jit(solution)/shard_map/while
  114.2 8.4 %collective-permute-start.5 = (bf16[2,256,256]{2,1,0:T(8,128)(2,1)}, bf16[2,256,256]{2,1,0:T(8,128)(2,1)S(1)}, u32[]{:S(2)}, u32[]{:S(2)}) collective-permute-start(bf16[2,256,256]{2,1,0:T(8,128)(2,1)} %collective-permute-done.4), channel_id=1, source_target_pairs={{0,7},{1,0},{2,1},{3,2},{4,3},{5,4},{6,5},{7,6},{8,15},{9,8},{10,9... | collective-permute-start | bytes 786440 | tf_op jit(solution)/shard_map/while/body/eval_jaxpr/ppermute | solution.py:24
  116.7 9.5 %collective-permute-start.2 = (bf16[2,256,256]{2,1,0:T(8,128)(2,1)}, bf16[2,256,256]{2,1,0:T(8,128)(2,1)S(1)}, u32[]{:S(2)}, u32[]{:S(2)}) collective-permute-start(bf16[2,256,256]{2,1,0:T(8,128)(2,1)} %collective-permute-done.1), channel_id=1, source_target_pairs={{0,1},{1,2},{2,3},{3,4},{4,5},{5,6},{6,7},{7,0},{8,9},{9,10},{10,1... | collective-permute-start | bytes 786440 | tf_op jit(solution)/shard_map/while/body/eval_jaxpr/ppermute | solution.py:23
  119.2 21.2 %copy-start.1 = (bf16[512,256]{1,0:T(8,128)(2,1)S(1)}, bf16[512,256]{1,0:T(8,128)(2,1)}, u32[]{:S(2)}) copy-start(bf16[512,256]{1,0:T(8,128)(2,1)} %get-tuple-element.93) | copy-start | bytes 786436 | tf_op jit(solution)/shard_map/while
  122.6 7.5 %collective-permute-start.6 = (bf16[2,256,256]{2,1,0:T(8,128)(2,1)S(1)}, bf16[2,256,256]{2,1,0:T(8,128)(2,1)S(1)}, u32[]{:S(2)}, u32[]{:S(2)}) collective-permute-start(bf16[2,256,256]{2,1,0:T(8,128)(2,1)S(1)} %collective-permute-done.5), channel_id=1, source_target_pairs={{0,7},{1,0},{2,1},{3,2},{4,3},{5,4},{6,5},{7,6},{8,15},{9,8},{10,9... | collective-permute-start | bytes 786440 | tf_op jit(solution)/shard_map/while/body/eval_jaxpr/ppermute | solution.py:24
  126.2 7.7 %collective-permute-start.3 = (bf16[2,256,256]{2,1,0:T(8,128)(2,1)S(1)}, bf16[2,256,256]{2,1,0:T(8,128)(2,1)S(1)}, u32[]{:S(2)}, u32[]{:S(2)}) collective-permute-start(bf16[2,256,256]{2,1,0:T(8,128)(2,1)S(1)} %collective-permute-done.2), channel_id=1, source_target_pairs={{0,1},{1,2},{2,3},{3,4},{4,5},{5,6},{6,7},{7,0},{8,9},{9,10},{10,1... | collective-permute-start | bytes 786440 | tf_op jit(solution)/shard_map/while/body/eval_jaxpr/ppermute | solution.py:23
  130.1 6.3 %collective-permute-start.7 = (bf16[1,256,256]{2,1,0:T(8,128)(2,1)S(1)}, bf16[1,256,256]{2,1,0:T(8,128)(2,1)S(1)}, u32[]{:S(2)}, u32[]{:S(2)}) collective-permute-start(bf16[1,256,256]{2,1,0:T(8,128)(2,1)S(1)} %slice.116), channel_id=1, source_target_pairs={{0,7},{1,0},{2,1},{3,2},{4,3},{5,4},{6,5},{7,6},{8,15},{9,8},{10,9... | collective-permute-start | bytes 393224 | tf_op jit(solution)/shard_map/while/body/eval_jaxpr/ppermute | solution.py:33
  133.9 6.3 %collective-permute-start.8 = (bf16[1,256,256]{2,1,0:T(8,128)(2,1)S(1)}, bf16[1,256,256]{2,1,0:T(8,128)(2,1)S(1)}, u32[]{:S(2)}, u32[]{:S(2)}) collective-permute-start(bf16[1,256,256]{2,1,0:T(8,128)(2,1)S(1)} %slice.117), channel_id=1, source_target_pairs={{0,1},{1,2},{2,3},{3,4},{4,5},{5,6},{6,7},{7,0},{8,9},{9,10},{10,1... | collective-permute-start | bytes 393224 | tf_op jit(solution)/shard_map/while/body/eval_jaxpr/ppermute | solution.py:32
  (15 other events, 79.5 us)
Sparse Core Ops, SparseCore 0:
  9.3 40.5 all-gather.1
